TPU v7x, 32 devices: a whole 2x2x4 slice. The times are simulated.
32 devices in a mesh: row: 8 (over y, x, core), col: 4 (over z).
Axes of the slice: x: 2, y: 2, z: 4, core: 2. Of those that a mesh axis runs over, the one named last changes fastest.
Arguments:
- records: float32 [128, 6, 8192], P(('row', 'col')), may hold values from -6 to 6
- fir_taps: float32 [32], replicated, may hold values from -1 to 1
- lag_limit: int32 [128], P('row'), may hold values from 16 to 64
Outputs:
- corr: float32 [128, 4, 32, 128], P('row', 'col')
Inputs may be any that keep to these rules, and one draw needn't show every extreme that they name: lag_limit[i] is the largest lag offset |l - 64| kept for reference station i.
All inputs are finite; a program needn't handle non-finite values.
Results may differ from a plain program's by a relative error of at most 0.0031.
Values may be sent and summed in bfloat16 or wider, within the bound.
No kernel may reach another device: no remote copies, remote signals or barrier semaphores. Data moves between devices by JAX's collectives and lax.ppermute only.
A program may use at most 64 MiB of HBM per device.

v0:
```python
import math

import jax
import jax.numpy as jnp
from jax import lax
from jax.sharding import PartitionSpec as P

DECIM = 2
LAGS = 128
BAND = 64
LH = 64


def angle_table(row_count, col_count, period, offset):
    row_ids = jnp.arange(row_count, dtype=jnp.int32)[:, None] + offset
    col_ids = jnp.arange(col_count, dtype=jnp.int32)[None, :]
    phase_int = jnp.mod(row_ids * col_ids, period)
    angles = phase_int.astype(jnp.float32) * (2.0 * math.pi / period)
    return (jnp.cos(angles), jnp.sin(angles))


def decimate(records, fir_taps):
    tap_count = fir_taps.shape[0]
    out_block = 128
    in_block = DECIM * out_block
    lead_dims = records.shape[:2]
    block_count = records.shape[2] // in_block
    blocks = records.reshape(lead_dims + (block_count, in_block))
    tails = blocks[:, :, :-1, in_block - tap_count :]
    tails = jnp.concatenate([jnp.zeros(lead_dims + (1, tap_count), records.dtype), tails], axis=2)
    windows = jnp.concatenate([tails, blocks], axis=3)
    tap_ids = jnp.arange(tap_count, dtype=jnp.int32)[:, None, None]
    in_ids = jnp.arange(in_block + tap_count, dtype=jnp.int32)[None, :, None]
    out_ids = jnp.arange(out_block, dtype=jnp.int32)[None, None, :]
    onehot = (in_ids == DECIM * out_ids + tap_count - tap_ids).astype(jnp.float32)
    band_matrix = jnp.einsum("k,kij->ij", fir_taps, onehot, precision=lax.Precision.HIGHEST)
    summed = jnp.einsum("swbi,ij->swbj", windows, band_matrix, precision=lax.Precision.HIGHEST)
    return summed.reshape(lead_dims + (block_count * out_block,))


def spectrum(decimated):
    out_length = decimated.shape[-1]
    first_len = 64
    second_len = out_length // first_len
    lead_dims = decimated.shape[:-1]
    blocks = decimated.reshape(lead_dims + (first_len, second_len))
    cos_one, sin_one = angle_table(first_len, first_len, first_len, 0)
    real_z = jnp.einsum("bwnq,fn->bwfq", blocks, cos_one, precision=lax.Precision.HIGHEST)
    imag_z = -jnp.einsum("bwnq,fn->bwfq", blocks, sin_one, precision=lax.Precision.HIGHEST)
    cos_two, sin_two = angle_table(first_len, second_len, out_length, 0)
    real_t = real_z * cos_two + imag_z * sin_two
    imag_t = imag_z * cos_two - real_z * sin_two
    cos_three, sin_three = angle_table(second_len // 2, second_len, second_len, 0)
    real_x = jnp.einsum(
        "bwfq,gq->bwgf", real_t, cos_three, precision=lax.Precision.HIGHEST
    ) + jnp.einsum("bwfq,gq->bwgf", imag_t, sin_three, precision=lax.Precision.HIGHEST)
    imag_x = jnp.einsum(
        "bwfq,gq->bwgf", imag_t, cos_three, precision=lax.Precision.HIGHEST
    ) - jnp.einsum("bwfq,gq->bwgf", real_t, sin_three, precision=lax.Precision.HIGHEST)
    bin_count = out_length // 2
    return (real_x.reshape(lead_dims + (bin_count,)), imag_x.reshape(lead_dims + (bin_count,)))


def whiten(spec_real, spec_imag):
    lead_dims = spec_real.shape[:-1]
    bin_count = spec_real.shape[-1]
    banded = lead_dims + (bin_count // BAND, BAND)
    squares = (spec_real * spec_real + spec_imag * spec_imag).reshape(banded)
    band_power = jnp.mean(squares, axis=-1, keepdims=True)
    inverse = 1.0 / jnp.sqrt(band_power + 1e-06)
    white_real = (spec_real.reshape(banded) * inverse).reshape(spec_real.shape)
    white_imag = (spec_imag.reshape(banded) * inverse).reshape(spec_imag.shape)
    return jnp.concatenate([white_real, white_imag], axis=-1).astype(jnp.bfloat16)


def pair_tile(left_by_window, left_limit, visiting, lag_table):
    visit_count = visiting.shape[1]
    lag_count = lag_table.shape[1]
    window_count = visiting.shape[0]
    bin_count = visiting.shape[2] // 2
    left_count = left_by_window.shape[1]

    def add_window(sums, window_pair):
        left_w, visit_w = window_pair
        left_c = left_w[:, None, :bin_count].astype(jnp.float32)
        left_d = left_w[:, None, bin_count:].astype(jnp.float32)
        vis_c = visit_w[None, :, :bin_count].astype(jnp.float32)
        vis_d = visit_w[None, :, bin_count:].astype(jnp.float32)
        new_real = sums[0] + (left_c * vis_c + left_d * vis_d)
        new_imag = sums[1] + (left_c * vis_d - left_d * vis_c)
        return ((new_real, new_imag), None)

    zero_sum = jnp.zeros((left_count, visit_count, bin_count), jnp.float32)
    sums, ignored = lax.scan(add_window, (zero_sum, zero_sum), (left_by_window, visiting))
    cross = jnp.concatenate([sums[0], sums[1]], axis=-1).astype(jnp.bfloat16)
    pair_block = jnp.dot(
        cross.reshape(left_count * visit_count, 2 * bin_count),
        lag_table,
        preferred_element_type=jnp.float32,
    )
    norm_scale = 1.0 / math.sqrt(window_count * bin_count)
    pair_block = pair_block.reshape(left_count, visit_count, lag_count) * norm_scale
    lag_offset = jnp.abs(jnp.arange(lag_count, dtype=jnp.int32) - lag_count // 2)
    keep_mask = lag_offset[None, :] <= left_limit[:, None]
    return jnp.where(keep_mask[:, None, :], pair_block, 0.0)


def on_device(records, fir_taps, lag_limit):
    block_size = records.shape[0]
    decimated = decimate(records, fir_taps)
    out_length = decimated.shape[-1]
    bin_count = out_length // 2
    spec_real, spec_imag = spectrum(decimated)
    white = whiten(spec_real, spec_imag)
    white_by_window = jnp.moveaxis(white, 1, 0)
    left_by_window = lax.all_gather(white_by_window, "col", axis=1, tiled=True)
    cos_lag, sin_lag = angle_table(LAGS, bin_count, out_length, -LH)
    lag_table = jnp.concatenate([cos_lag.T, sin_lag.T], axis=0).astype(jnp.bfloat16)
    group_rows = left_by_window.shape[1]
    piece_rows = lax.all_gather(white_by_window, "row", axis=1, tiled=True)
    visit_count = piece_rows.shape[1]
    group_size = math.gcd(visit_count, block_size)
    grouped = piece_rows.reshape(
        (piece_rows.shape[0], visit_count // group_size, group_size, piece_rows.shape[2])
    )
    grouped = jnp.moveaxis(grouped, 1, 0)

    def one_group(sub_block):
        return pair_tile(left_by_window, lag_limit, sub_block, lag_table)

    tile_stack = lax.map(one_group, grouped)
    tile_stack = jnp.moveaxis(tile_stack, 0, 1).reshape(group_rows, visit_count, LAGS)
    return tile_stack[:, None]


def solution(mesh):
    placed = (P(("row", "col"), None, None), P(), P("row"))
    return jax.shard_map(
        on_device,
        mesh=mesh,
        in_specs=placed,
        out_specs=P("row", "col", None, None),
        check_vma=False,
    )
```

profile of v0, /device:TPU:0, one launch (start us, length us, event | category | flops | bytes accessed | tf_op | source)
XLA Modules:
  0.0 118.9 jit_solution(3765991084609973190)
XLA Ops:
  6.5 1.7 %reshape.142 = f32[4,6,32,256]{3,2,0,1:T(8,128)S(1)} reshape(f32[4,6,8192]{2,0,1:T(4,128)} %param.7) | data formatting | bytes 1572864 | tf_op jit(solution)/shard_map/reshape | solution.py:28
  9.1 1.3 %fusion.8 = f32[1,288,128]{2,0,1:T(1,128)S(1)} fusion(pred[32,288,128]{2,1,0:T(32,128)(4,1)S(1)} %iota_compare_fusion, f32[32]{0:T(128)S(1)} %copy-done), kind=kOutput, calls=%fused_computation.23 | convolution fusion | flops 14155776 | bytes 1327232 | tf_op jit(solution)/shard_map/k,kij->ij/dot_general | solution.py:36
  10.5 1.3 %fusion.12 = f32[4,6,32,128]{3,2,1,0:T(8,128)S(1)} fusion(f32[288,128,1,1]{1,0,3,2:T(8,128)S(1)} %bitcast.96, f32[4,6,31,32]{3,2,1,0:T(8,128)S(1)} %copy.50, f32[4,6,32,256]{3,2,0,1:T(8,128)S(1)} %reshape.142), kind=kOutput, calls=%fused_computation.35 | convolution fusion | flops 340402176 | bytes 1422336 | tf_op jit(solution)/shard_map/swbi,ij->swbj/dot_general | solution.py:37
  14.0 2.3 %fusion.25 = f32[32,4,6,64]{3,0,2,1:T(8,128)S(1)} fusion(f32[64,4,6,64]{3,0,2,1:T(8,128)S(1)} %convolution_negate_fusion, f32[64,4,6,64]{3,0,2,1:T(8,128)S(1)} %fusion.34, f32[64,64]{1,0:T(8,128)S(1)} %get-tuple-element.169, f32[64,64]{1,0:T(8,128)S(1)} %get-tuple-element.170), kind=kOutput, calls=%fused_computation.52 | convolution fusion | flops 38072320 | bytes 1015808 | tf_op jit(solution)/shard_map/bwfq,gq->bwgf/dot_general | solution.py:54
  16.3 2.3 %fusion.21 = f32[32,4,6,64]{3,0,2,1:T(8,128)S(1)} fusion(f32[64,4,6,64]{3,0,2,1:T(8,128)S(1)} %fusion.34, f32[64,4,6,64]{3,0,2,1:T(8,128)S(1)} %convolution_negate_fusion, f32[64,64]{1,0:T(8,128)S(1)} %get-tuple-element.169, f32[64,64]{1,0:T(8,128)S(1)} %get-tuple-element.170), kind=kOutput, calls=%fused_computation.48 | convolution fusion | flops 38072320 | bytes 1015808 | tf_op jit(solution)/shard_map/bwfq,gq->bwgf/dot_general | solution.py:57
  18.5 2.3 %fusion.11 = f32[4,6,32,64]{3,2,1,0:T(8,128)S(1)} fusion(f32[32,4,6,64]{3,0,2,1:T(8,128)S(1)} %fusion.25, f32[64,4,6,64]{3,0,2,1:T(8,128)S(1)} %fusion.34, f32[64,4,6,64]{3,0,2,1:T(8,128)S(1)} %convolution_negate_fusion, f32[64,64]{1,0:T(8,128)S(1)} %get-tuple-element.169, f32[64,64]{1,0:T(8,128)S(1)} %get-tuple-element.170), kind=kOutput, calls=%fused_computation.33 | convolution fusion | flops 38121472 | bytes 1212416 | tf_op jit(solution)/shard_map/bwfq,gq->bwgf/dot_general | solution.py:56
  20.8 2.5 %add_reduce_fusion = (f32[4,6,32]{2,1,0:T(8,128)S(1)}, f32[4,6,32,64]{3,2,1,0:T(8,128)S(1)}) fusion(f32[4,6,32,64]{3,2,1,0:T(8,128)S(1)} %fusion.11, f32[32,4,6,64]{3,0,2,1:T(8,128)S(1)} %fusion.21, f32[64,4,6,64]{3,0,2,1:T(8,128)S(1)} %convolution_negate_fusion, f32[64,64]{1,0:T(8,128)S(1)} %get-tuple-element.169, f32[64,4,6,64]{3,0,2,1:T(8,128)S(1)} %fusion.34, ...), kind=kOutput, calls=%fused_computation.60 | convolution fusion | flops 38317312 | bytes 1412096 | tf_op jit(solution)/shard_map/bwfq,gq->bwgf/dot_general | solution.py:59
  25.1 24.4 %all_gather.7 = bf16[6,16,4096]{2,0,1:T(8,128)(2,1)S(1)} all-gather(bf16[6,4,4096]{2,0,1:T(8,128)(2,1)} %copy.25), channel_id=1, replica_groups=mesh['row'=8,'col'=4] {'col'}, dimensions={1}, use_global_device_ids=true | all-gather | bytes 983040 | tf_op jit(solution)/shard_map/all_gather | solution.py:116
  49.9 4.4 %cosine_convert_fusion = (bf16[2048,128]{1,0:T(8,128)(2,1)S(1)}, bf16[2048,128]{1,0:T(8,128)(2,1)S(1)}) fusion(s32[128]{0:T(128)S(1)} %iota_add_fusion), kind=kLoop, calls=%fused_computation.44 | loop fusion | flops 4194304 | bytes 1049088 | tf_op jit(solution)/shard_map/convert.2
  54.4 1.4 %all-gather.2.cloned.1.call-done = bf16[6,32,4096]{2,0,1:T(8,128)(2,1)} async-done(((bf16[6,4,4096]{2,0,1:T(8,128)(2,1)}), bf16[6,32,4096]{2,0,1:T(8,128)(2,1)}) %all-gather.2.cloned.1.call-update) | async-done | bytes 1572880 | tf_op jit(solution)/shard_map/all_gather | solution.py:120
  55.8 4.0 %copy.49 = bf16[6,8,4,4096]{3,2,0,1:T(4,128)(2,1)} copy(bf16[6,8,4,4096]{3,0,2,1:T(8,128)(2,1)} %bitcast.94) | data formatting | bytes 3145728 | tf_op jit(solution)/shard_map/reshape | solution.py:123
  59.8 50.5 %while.38 = (s32[]{:T(128)}, f32[8,16,4,128]{3,1,2,0:T(8,128)}, s32[16]{0:T(128)S(1)}, bf16[8,6,4,4096]{3,2,1,0:T(4,128)(2,1)}, bf16[6,16,4096]{2,1,0:T(8,128)(2...) while((s32[]{:T(128)}, f32[8,16,4,128]{3,1,2,0:T(8,128)}, ...), condition=%wide.region_4.5_spmd, body=%wide.region_1.4_spmd.sunk | while | flops 69568768 | bytes 6821704 | solution.py:131
  59.8 1.0 dynamic-slice_bitcast_fusion.6
  60.8 3.7 %while.39 = (s32[]{:T(128)}, f32[16,4,2048]{2,1,0:T(4,128)S(1)}, f32[16,4,2048]{2,1,0:T(4,128)S(1)}, bf16[6,16,4096]{2,1,0:T(8,128)(2,1)S(1)}, bf16[6,4,4096]{2,1,0:T(4,128)(2,1)S(1)}, /*index=5*/s32[]{:T(128)}, s32[]{:T(128)}) while((s32[]{:T(128)}, f32[16,4,2048]{2,1,0:T(4,128)S(1)}, f32[16,4,2048]{2,1,0:T(4,128)S(1)}, ...), condition=%wide.region_3.3_spmd.clone, body=%wide.region_2.2_spmd.clone.sunk | while | flops 1392643 | bytes 3244127 | solution.py:94
  66.1 1.0 dynamic-slice_bitcast_fusion.6
  67.1 3.7 %while.39 = (s32[]{:T(128)}, f32[16,4,2048]{2,1,0:T(4,128)S(1)}, f32[16,4,2048]{2,1,0:T(4,128)S(1)}, bf16[6,16,4096]{2,1,0:T(8,128)(2,1)S(1)}, bf16[6,4,4096]{2,1,0:T(4,128)(2,1)S(1)}, /*index=5*/s32[]{:T(128)}, s32[]{:T(128)}) while((s32[]{:T(128)}, f32[16,4,2048]{2,1,0:T(4,128)S(1)}, f32[16,4,2048]{2,1,0:T(4,128)S(1)}, ...), condition=%wide.region_3.3_spmd.clone, body=%wide.region_2.2_spmd.clone.sunk | while | flops 1392643 | bytes 3244127 | solution.py:94
  73.5 3.7 %while.39 = (s32[]{:T(128)}, f32[16,4,2048]{2,1,0:T(4,128)S(1)}, f32[16,4,2048]{2,1,0:T(4,128)S(1)}, bf16[6,16,4096]{2,1,0:T(8,128)(2,1)S(1)}, bf16[6,4,4096]{2,1,0:T(4,128)(2,1)S(1)}, /*index=5*/s32[]{:T(128)}, s32[]{:T(128)}) while((s32[]{:T(128)}, f32[16,4,2048]{2,1,0:T(4,128)S(1)}, f32[16,4,2048]{2,1,0:T(4,128)S(1)}, ...), condition=%wide.region_3.3_spmd.clone, body=%wide.region_2.2_spmd.clone.sunk | while | flops 1392643 | bytes 3244127 | solution.py:94
  78.8 1.0 dynamic-slice_bitcast_fusion.6
  79.8 3.7 %while.39 = (s32[]{:T(128)}, f32[16,4,2048]{2,1,0:T(4,128)S(1)}, f32[16,4,2048]{2,1,0:T(4,128)S(1)}, bf16[6,16,4096]{2,1,0:T(8,128)(2,1)S(1)}, bf16[6,4,4096]{2,1,0:T(4,128)(2,1)S(1)}, /*index=5*/s32[]{:T(128)}, s32[]{:T(128)}) while((s32[]{:T(128)}, f32[16,4,2048]{2,1,0:T(4,128)S(1)}, f32[16,4,2048]{2,1,0:T(4,128)S(1)}, ...), condition=%wide.region_3.3_spmd.clone, body=%wide.region_2.2_spmd.clone.sunk | while | flops 1392643 | bytes 3244127 | solution.py:94
  86.1 3.7 %while.39 = (s32[]{:T(128)}, f32[16,4,2048]{2,1,0:T(4,128)S(1)}, f32[16,4,2048]{2,1,0:T(4,128)S(1)}, bf16[6,16,4096]{2,1,0:T(8,128)(2,1)S(1)}, bf16[6,4,4096]{2,1,0:T(4,128)(2,1)S(1)}, /*index=5*/s32[]{:T(128)}, s32[]{:T(128)}) while((s32[]{:T(128)}, f32[16,4,2048]{2,1,0:T(4,128)S(1)}, f32[16,4,2048]{2,1,0:T(4,128)S(1)}, ...), condition=%wide.region_3.3_spmd.clone, body=%wide.region_2.2_spmd.clone.sunk | while | flops 1392643 | bytes 3244127 | solution.py:94
  92.4 3.7 %while.39 = (s32[]{:T(128)}, f32[16,4,2048]{2,1,0:T(4,128)S(1)}, f32[16,4,2048]{2,1,0:T(4,128)S(1)}, bf16[6,16,4096]{2,1,0:T(8,128)(2,1)S(1)}, bf16[6,4,4096]{2,1,0:T(4,128)(2,1)S(1)}, /*index=5*/s32[]{:T(128)}, s32[]{:T(128)}) while((s32[]{:T(128)}, f32[16,4,2048]{2,1,0:T(4,128)S(1)}, f32[16,4,2048]{2,1,0:T(4,128)S(1)}, ...), condition=%wide.region_3.3_spmd.clone, body=%wide.region_2.2_spmd.clone.sunk | while | flops 1392643 | bytes 3244127 | solution.py:94
  98.7 3.7 %while.39 = (s32[]{:T(128)}, f32[16,4,2048]{2,1,0:T(4,128)S(1)}, f32[16,4,2048]{2,1,0:T(4,128)S(1)}, bf16[6,16,4096]{2,1,0:T(8,128)(2,1)S(1)}, bf16[6,4,4096]{2,1,0:T(4,128)(2,1)S(1)}, /*index=5*/s32[]{:T(128)}, s32[]{:T(128)}) while((s32[]{:T(128)}, f32[16,4,2048]{2,1,0:T(4,128)S(1)}, f32[16,4,2048]{2,1,0:T(4,128)S(1)}, ...), condition=%wide.region_3.3_spmd.clone, body=%wide.region_2.2_spmd.clone.sunk | while | flops 1392643 | bytes 3244127 | solution.py:94
  105.0 3.7 %while.39 = (s32[]{:T(128)}, f32[16,4,2048]{2,1,0:T(4,128)S(1)}, f32[16,4,2048]{2,1,0:T(4,128)S(1)}, bf16[6,16,4096]{2,1,0:T(8,128)(2,1)S(1)}, bf16[6,4,4096]{2,1,0:T(4,128)(2,1)S(1)}, /*index=5*/s32[]{:T(128)}, s32[]{:T(128)}) while((s32[]{:T(128)}, f32[16,4,2048]{2,1,0:T(4,128)S(1)}, f32[16,4,2048]{2,1,0:T(4,128)S(1)}, ...), condition=%wide.region_3.3_spmd.clone, body=%wide.region_2.2_spmd.clone.sunk | while | flops 1392643 | bytes 3244127 | solution.py:94
  110.3 1.8 %copy.29 = f32[16,8,4,128]{3,2,1,0:T(4,128)} copy(f32[16,8,4,128]{3,0,2,1:T(8,128)} %bitcast.95) | data formatting | bytes 524288 | tf_op jit(solution)/shard_map/transpose | solution.py:132
  (328 shorter events, 49.9 us)
Async XLA Ops:
  6.5 2.6 %copy-start = (f32[32]{0:T(128)S(1)}, f32[32]{0:T(128)}, u32[]{:S(2)}) copy-start(f32[32]{0:T(128)} %param.8) | copy-start | bytes 388
  6.5 49.3 %all-gather.2.cloned.1.call-start = ((), (), s32[]{:S(2)}) async-start(), calls=%async_computation | async-start | bytes 2359296 | tf_op jit(solution)/shard_map/all_gather | solution.py:120
  55.8 4.0 %copy-start.1 = (s32[16]{0:T(128)S(1)}, s32[16]{0:T(128)}, u32[]{:S(2)}) copy-start(s32[16]{0:T(128)} %param.9) | copy-start | bytes 196
Sparse Core Ops, SparseCore 0:
  25.2 30.5 all-gather.1
where the time goes:
time: 119 us
  other arithmetic  31.4 us (26%)
  blocking collectives  24.4 us (21%)
  local copies, waits for them, and re-layouts  24 us (20%)
  matrix products  21.3 us (18%)
  between operations  13.6 us (11%)
  loops' own time  2.85 us (2%)
  waiting for transfers between devices  1.44 us (1%)
    all_gather x1, blocking collectives, on_device(): left_by_window = lax.all_gather(white_by_window, 'col', axis=1, tiled=True)  24.4 us
    add x48, other arithmetic, add_window(): new_imag = sums[1] + (left_c * vis_d - left_d * vis_c)  23.8 us
    squeeze x8, local copies, waits for them, and re-layouts, on_device(): tile_stack = lax.map(one_group, grouped)  7.96 us
    dot_general x8, matrix products, pair_tile(): jnp.dot(cross.reshape(left_count * visit_count, 2 * bin_count), lag_table...  7.49 us
    while x16, local copies, waits for them, and re-layouts, pair_tile(): lax.scan(add_window, (zero_sum, zero_sum), (left_by_window, visiting))  4.61 us
    another operation x2, other arithmetic  4.55 us
    reshape x1, local copies, waits for them, and re-layouts, on_device(): piece_rows.reshape((piece_rows.shape[0], visit_count // group_size, group...  4 us
    dot_general x1, matrix products, spectrum(): jnp.einsum('bwfq,gq->bwgf', real_t, sin_three, precision=lax.Precision.HI...  2.53 us
  transfers between devices with their start and end apart: 1, of which 1 were waited for; matrix products, arithmetic and copies ran while one was open for 4% of the time, Pallas kernels for 0%

commit v1 on v0

--- a/solution.py
+++ b/solution.py
@@ -3,6 +3,8 @@
 import jax
 import jax.numpy as jnp
 from jax import lax
+from jax.experimental import pallas as pl
+from jax.experimental.pallas import tpu as pltpu
 from jax.sharding import PartitionSpec as P
 
 DECIM = 2
@@ -73,36 +75,72 @@
     return jnp.concatenate([white_real, white_imag], axis=-1).astype(jnp.bfloat16)
 
 
-def pair_tile(left_by_window, left_limit, visiting, lag_table):
+def cross_kernel(left_ref, visit_ref, table_ref, out_ref, left_f32, visit_f32, cross_ref):
+    window_count, left_count, width = left_ref.shape
+    group = visit_ref.shape[1]
+    bin_count = width // 2
+    chunk = max(128, min(512, 8192 // left_count))
+    chunks = bin_count // chunk
+
+    @pl.when(pl.program_id(0) == 0)
+    def _():
+        left_f32[...] = left_ref[...].astype(jnp.float32)
+
+    visit_f32[...] = visit_ref[...].astype(jnp.float32)
+
+    def one_chunk(step, carry):
+        partner = step // chunks
+        off = pl.multiple_of((step % chunks) * chunk, chunk)
+        acc_re = jnp.zeros((left_count, chunk), jnp.float32)
+        acc_im = jnp.zeros((left_count, chunk), jnp.float32)
+        for window in range(window_count):
+            left_c = left_f32[window, :, pl.ds(off, chunk)]
+            left_d = left_f32[window, :, pl.ds(off + bin_count, chunk)]
+            vis_c = visit_f32[window, pl.ds(partner, 1), pl.ds(off, chunk)]
+            vis_d = visit_f32[window, pl.ds(partner, 1), pl.ds(off + bin_count, chunk)]
+            acc_re = acc_re + (left_c * vis_c + left_d * vis_d)
+            acc_im = acc_im + (left_c * vis_d - left_d * vis_c)
+        row = pl.multiple_of(partner * left_count, left_count)
+        cross_ref[pl.ds(row, left_count), pl.ds(off, chunk)] = acc_re.astype(jnp.bfloat16)
+        cross_ref[pl.ds(row, left_count), pl.ds(off + bin_count, chunk)] = acc_im.astype(jnp.bfloat16)
+        return carry
+
+    lax.fori_loop(0, group * chunks, one_chunk, 0)
+    out_ref[...] = jnp.dot(cross_ref[...], table_ref[...], preferred_element_type=jnp.float32)
+
+
+def pair_block(left_by_window, visiting, lag_table):
+    window_count, left_count, width = left_by_window.shape
     visit_count = visiting.shape[1]
     lag_count = lag_table.shape[1]
-    window_count = visiting.shape[0]
-    bin_count = visiting.shape[2] // 2
-    left_count = left_by_window.shape[1]
-
-    def add_window(sums, window_pair):
-        left_w, visit_w = window_pair
-        left_c = left_w[:, None, :bin_count].astype(jnp.float32)
-        left_d = left_w[:, None, bin_count:].astype(jnp.float32)
-        vis_c = visit_w[None, :, :bin_count].astype(jnp.float32)
-        vis_d = visit_w[None, :, bin_count:].astype(jnp.float32)
-        new_real = sums[0] + (left_c * vis_c + left_d * vis_d)
-        new_imag = sums[1] + (left_c * vis_d - left_d * vis_c)
-        return ((new_real, new_imag), None)
-
-    zero_sum = jnp.zeros((left_count, visit_count, bin_count), jnp.float32)
-    sums, ignored = lax.scan(add_window, (zero_sum, zero_sum), (left_by_window, visiting))
-    cross = jnp.concatenate([sums[0], sums[1]], axis=-1).astype(jnp.bfloat16)
-    pair_block = jnp.dot(
-        cross.reshape(left_count * visit_count, 2 * bin_count),
-        lag_table,
-        preferred_element_type=jnp.float32,
-    )
-    norm_scale = 1.0 / math.sqrt(window_count * bin_count)
-    pair_block = pair_block.reshape(left_count, visit_count, lag_count) * norm_scale
-    lag_offset = jnp.abs(jnp.arange(lag_count, dtype=jnp.int32) - lag_count // 2)
-    keep_mask = lag_offset[None, :] <= left_limit[:, None]
-    return jnp.where(keep_mask[:, None, :], pair_block, 0.0)
+    group = min(8, visit_count)
+    while visit_count % group:
+        group -= 1
+    rows = group * left_count
+    flops = visit_count * left_count * width * (4 * window_count + 2 * lag_count)
+    return pl.pallas_call(
+        cross_kernel,
+        out_shape=jax.ShapeDtypeStruct((visit_count * left_count, lag_count), jnp.float32),
+        grid=(visit_count // group,),
+        in_specs=[
+            pl.BlockSpec((window_count, left_count, width), lambda g: (0, 0, 0)),
+            pl.BlockSpec((window_count, group, width), lambda g: (0, g, 0)),
+            pl.BlockSpec((width, lag_count), lambda g: (0, 0)),
+        ],
+        out_specs=pl.BlockSpec((rows, lag_count), lambda g: (g, 0)),
+        scratch_shapes=[
+            pltpu.VMEM((window_count, left_count, width), jnp.float32),
+            pltpu.VMEM((window_count, group, width), jnp.float32),
+            pltpu.VMEM((rows, width), jnp.bfloat16),
+        ],
+        compiler_params=pltpu.CompilerParams(dimension_semantics=("arbitrary",)),
+        cost_estimate=pl.CostEstimate(
+            flops=flops,
+            transcendentals=0,
+            bytes_accessed=2 * width * (window_count * (left_count + visit_count) + lag_count)
+            + 4 * visit_count * left_count * lag_count,
+        ),
+    )(left_by_window, visiting, lag_table)
 
 
 def on_device(records, fir_taps, lag_limit):
@@ -119,17 +157,13 @@
     group_rows = left_by_window.shape[1]
     piece_rows = lax.all_gather(white_by_window, "row", axis=1, tiled=True)
     visit_count = piece_rows.shape[1]
-    group_size = math.gcd(visit_count, block_size)
-    grouped = piece_rows.reshape(
-        (piece_rows.shape[0], visit_count // group_size, group_size, piece_rows.shape[2])
-    )
-    grouped = jnp.moveaxis(grouped, 1, 0)
-
-    def one_group(sub_block):
-        return pair_tile(left_by_window, lag_limit, sub_block, lag_table)
-
-    tile_stack = lax.map(one_group, grouped)
-    tile_stack = jnp.moveaxis(tile_stack, 0, 1).reshape(group_rows, visit_count, LAGS)
+    pair = pair_block(left_by_window, piece_rows, lag_table)
+    pair = jnp.swapaxes(pair.reshape(visit_count, group_rows, LAGS), 0, 1)
+    norm_scale = 1.0 / math.sqrt(white.shape[1] * bin_count)
+    pair = pair * norm_scale
+    lag_offset = jnp.abs(jnp.arange(LAGS, dtype=jnp.int32) - LH)
+    keep_mask = lag_offset[None, :] <= lag_limit[:, None]
+    tile_stack = jnp.where(keep_mask[:, None, :], pair, 0.0)
     return tile_stack[:, None]
 
 

time: 119 us -> 81.4 us (0.68)
  other arithmetic: 31.4 us -> 8.35 us
  local copies, waits for them, and re-layouts: 24 us -> 8.37 us
  Pallas kernels: 0 us -> 12.6 us
  matrix products: 21.3 us -> 13.8 us
  loops' own time: 2.85 us -> 0 us
  waiting for transfers between devices: 1.44 us -> 0.02 us
    add x49 -> x0, other arithmetic: 23.8 us -> none  [the longest x48 23.8 us: add_window(): new_imag = sums[1] + (left_c * vis_d - left_d * vis_c)]
    pallas_call x0 -> x1, Pallas kernels: none -> 12.6 us  [pair_block(): pl.pallas_call(cross_kernel, out_shape=jax.ShapeDtypeStruct((visit_count...]
    squeeze x104 -> x0, local copies, waits for them, and re-layouts: 9.73 us -> none  [the longest x8 7.96 us: on_device(): tile_stack = lax.map(one_group, grouped)]
    dot_general x8 -> x0, matrix products: 7.49 us -> none  [pair_tile(): jnp.dot(cross.reshape(left_count * visit_count, 2 * bin_count), lag_table...]
    while x17 -> x0, local copies, waits for them, and re-layouts: 5.05 us -> none  [the longest x16 4.61 us: pair_tile(): lax.scan(add_window, (zero_sum, zero_sum), (left_by_window, visiting))]
    all_gather x0 -> x2, local copies, waits for them, and re-layouts: none -> 4.96 us  [the longest x1 3.61 us: on_device(): piece_rows = lax.all_gather(white_by_window, 'row', axis=1, tiled=True)]
    reshape x1 -> x0, local copies, waits for them, and re-layouts: 4 us -> none  [on_device(): piece_rows.reshape((piece_rows.shape[0], visit_count // group_size, group...]
    another operation x9 -> x0, loops' own time: 2.85 us -> none  [the longest x8 2.47 us: pair_tile(): lax.scan(add_window, (zero_sum, zero_sum), (left_by_window, visiting))]
  transfers between devices with their start and end apart: 1 -> 1, of which waited for: 1 -> 0; matrix products, arithmetic and copies ran while one was open for 4% -> 8% of each run, Pallas kernels for 0% -> 0%
where the time goes in v1:
time: 81.4 us; the launch traced here: 81.2 us
  blocking collectives  24.4 us (30%)
  matrix products  13.8 us (17%)
  between operations  13.6 us (17%)
  Pallas kernels  12.6 us (15%)
  local copies, waits for them, and re-layouts  8.37 us (10%)
  other arithmetic  8.35 us (10%)
    all_gather x1, blocking collectives, on_device(): left_by_window = lax.all_gather(white_by_window, 'col', axis=1, tiled=True)  24.4 us
    pallas_call x1, Pallas kernels, pair_block(): pl.pallas_call(cross_kernel, out_shape=jax.ShapeDtypeStruct((visit_count...  12.6 us
    another operation x2, other arithmetic  4.53 us
    all_gather x1, local copies, waits for them, and re-layouts, on_device(): piece_rows = lax.all_gather(white_by_window, 'row', axis=1, tiled=True)  3.61 us
    dot_general x1, matrix products, spectrum(): jnp.einsum('bwfq,gq->bwgf', real_t, sin_three, precision=lax.Precision.HI...  2.53 us
    dot_general x1, matrix products, spectrum(): jnp.einsum('bwfq,gq->bwgf', imag_t, cos_three, precision=lax.Precision.HI...  2.27 us
    dot_general x1, matrix products, spectrum(): jnp.einsum('bwfq,gq->bwgf', imag_t, sin_three, precision=lax.Precision.HI...  2.27 us
    dot_general x1, matrix products, spectrum(): jnp.einsum('bwfq,gq->bwgf', real_t, cos_three, precision=lax.Precision.HI...  2.27 us
  transfers between devices with their start and end apart: 1, of which 0 were waited for; matrix products, arithmetic and copies ran while one was open for 8% of the time, Pallas kernels for 0%

profile of v1, /device:TPU:0, one launch (start us, length us, event | category | flops | bytes accessed | tf_op | source)
XLA Modules:
  0.0 81.2 jit_solution(17937610034400174133)
XLA Ops:
  6.5 1.7 %reshape.124 = f32[4,6,32,256]{3,2,0,1:T(8,128)S(1)} reshape(f32[4,6,8192]{2,0,1:T(4,128)} %param.3) | data formatting | bytes 1572864 | tf_op jit(solution)/shard_map/reshape | solution.py:30
  8.2 0.2 slice.4
  8.4 0.7 iota_compare_fusion
  9.1 1.3 %fusion = f32[1,288,128]{2,0,1:T(1,128)S(1)} fusion(pred[32,288,128]{2,1,0:T(32,128)(4,1)S(1)} %iota_compare_fusion, f32[32]{0:T(128)S(1)} %copy-done), kind=kOutput, calls=%fused_computation.1 | convolution fusion | flops 14155776 | bytes 1327232 | tf_op jit(solution)/shard_map/k,kij->ij/dot_general | solution.py:38
  10.5 1.3 %fusion.4 = f32[4,6,32,128]{3,2,1,0:T(8,128)S(1)} fusion(f32[288,128,1,1]{1,0,3,2:T(8,128)S(1)} %bitcast.70, f32[4,6,31,32]{3,2,1,0:T(8,128)S(1)} %copy.44, f32[4,6,32,256]{3,2,0,1:T(8,128)S(1)} %reshape.124), kind=kOutput, calls=%fused_computation.12 | convolution fusion | flops 340402176 | bytes 1422336 | tf_op jit(solution)/shard_map/swbi,ij->swbj/dot_general | solution.py:39
  11.8 0.2 reshape_reshape.3
  12.0 0.9 %convolution_negate_fusion = f32[64,4,6,64]{3,0,2,1:T(8,128)S(1)} fusion(f32[4,6,64,64]{3,2,1,0:T(8,128)S(1)} %reshape_reshape.3), kind=kOutput, calls=%fused_computation.6 | convolution fusion | flops 75653120 | bytes 786432 | tf_op jit(solution)/shard_map/bwnq,fn->bwfq/dot_general | solution.py:51
  12.9 0.9 %fusion.27 = f32[64,4,6,64]{3,0,2,1:T(8,128)S(1)} fusion(f32[4,6,64,64]{3,2,1,0:T(8,128)S(1)} %reshape_reshape.3), kind=kOutput, calls=%fused_computation.52 | convolution fusion | flops 75554816 | bytes 786432 | tf_op jit(solution)/shard_map/bwnq,fn->bwfq/dot_general | solution.py:50
  14.0 2.3 %fusion.17 = f32[32,4,6,64]{3,0,2,1:T(8,128)S(1)} fusion(f32[64,4,6,64]{3,0,2,1:T(8,128)S(1)} %convolution_negate_fusion, f32[64,4,6,64]{3,0,2,1:T(8,128)S(1)} %fusion.27, f32[64,64]{1,0:T(8,128)S(1)} %get-tuple-element.11, f32[64,64]{1,0:T(8,128)S(1)} %get-tuple-element.12), kind=kOutput, calls=%fused_computation.29 | convolution fusion | flops 38072320 | bytes 1015808 | tf_op jit(solution)/shard_map/bwfq,gq->bwgf/dot_general | solution.py:56
  16.3 2.3 %fusion.13 = f32[32,4,6,64]{3,0,2,1:T(8,128)S(1)} fusion(f32[64,4,6,64]{3,0,2,1:T(8,128)S(1)} %fusion.27, f32[64,4,6,64]{3,0,2,1:T(8,128)S(1)} %convolution_negate_fusion, f32[64,64]{1,0:T(8,128)S(1)} %get-tuple-element.11, f32[64,64]{1,0:T(8,128)S(1)} %get-tuple-element.12), kind=kOutput, calls=%fused_computation.25 | convolution fusion | flops 38072320 | bytes 1015808 | tf_op jit(solution)/shard_map/bwfq,gq->bwgf/dot_general | solution.py:59
  18.5 2.3 %fusion.3 = f32[4,6,32,64]{3,2,1,0:T(8,128)S(1)} fusion(f32[32,4,6,64]{3,0,2,1:T(8,128)S(1)} %fusion.17, f32[64,4,6,64]{3,0,2,1:T(8,128)S(1)} %fusion.27, f32[64,4,6,64]{3,0,2,1:T(8,128)S(1)} %convolution_negate_fusion, f32[64,64]{1,0:T(8,128)S(1)} %get-tuple-element.11, f32[64,64]{1,0:T(8,128)S(1)} %get-tuple-element.12), kind=kOutput, calls=%fused_computation.10 | convolution fusion | flops 38121472 | bytes 1212416 | tf_op jit(solution)/shard_map/bwfq,gq->bwgf/dot_general | solution.py:58
  20.8 2.5 %add_reduce_fusion = (f32[4,6,32]{2,1,0:T(8,128)S(1)}, f32[4,6,32,64]{3,2,1,0:T(8,128)S(1)}) fusion(f32[4,6,32,64]{3,2,1,0:T(8,128)S(1)} %fusion.3, f32[32,4,6,64]{3,0,2,1:T(8,128)S(1)} %fusion.13, f32[64,4,6,64]{3,0,2,1:T(8,128)S(1)} %convolution_negate_fusion, f32[64,64]{1,0:T(8,128)S(1)} %get-tuple-element.11, f32[64,4,6,64]{3,0,2,1:T(8,128)S(1)} %fusion.27, ...), kind=kOutput, calls=%fused_computation.37 | convolution fusion | flops 38317312 | bytes 1412096 | tf_op jit(solution)/shard_map/bwfq,gq->bwgf/dot_general | solution.py:61
  23.4 0.2 multiply_convert_fusion.1
  23.6 0.2 reshape.134
  23.8 0.2 reshape.135
  24.2 0.8 %copy.22 = bf16[6,4,4096]{2,0,1:T(8,128)(2,1)} copy(bf16[6,4,4096]{2,1,0:T(4,128)(2,1)S(1)} %maximum_bitcast_fusion) | data formatting | bytes 393216 | tf_op jit(solution)/shard_map/transpose | solution.py:153
  25.0 24.4 %all_gather.6 = bf16[6,16,4096]{2,0,1:T(8,128)(2,1)S(1)} all-gather(bf16[6,4,4096]{2,0,1:T(8,128)(2,1)} %copy.22), channel_id=1, replica_groups=mesh['row'=8,'col'=4] {'col'}, dimensions={1}, use_global_device_ids=true | all-gather | bytes 983040 | tf_op jit(solution)/shard_map/all_gather | solution.py:154
  49.4 1.3 %copy.24.left_ref = bf16[6,16,4096]{2,1,0:T(8,128)(2,1)} copy(bf16[6,16,4096]{2,0,1:T(8,128)(2,1)S(1)} %all_gather.6) | data formatting | bytes 1572864 | tf_op jit(solution)/shard_map/all_gather | solution.py:154
  50.9 4.4 %cosine_convert_fusion = (bf16[2048,128]{1,0:T(8,128)(2,1)S(1)}, bf16[2048,128]{1,0:T(8,128)(2,1)S(1)}) fusion(s32[128]{0:T(128)S(1)} %iota_add_fusion), kind=kLoop, calls=%fused_computation.21 | loop fusion | flops 4194304 | bytes 1049088 | tf_op jit(solution)/shard_map/convert
  55.2 1.1 %pad_maximum_fusion.table_ref = bf16[4096,128]{1,0:T(8,128)(2,1)} fusion(bf16[2048,128]{1,0:T(8,128)(2,1)S(1)} %get-tuple-element.8, bf16[2048,128]{1,0:T(8,128)(2,1)S(1)} %get-tuple-element.7), kind=kLoop, calls=%fused_computation.19 | loop fusion | flops 2097152 | bytes 2097152 | tf_op jit(solution)/shard_map/concatenate | solution.py:156
  56.3 3.6 %copy.25.visit_ref = bf16[6,32,4096]{2,1,0:T(8,128)(2,1)} copy(bf16[6,32,4096]{2,0,1:T(8,128)(2,1)} %all-gather.2.cloned.1.call-done) | data formatting | bytes 3145728 | tf_op jit(solution)/shard_map/all_gather | solution.py:158
  59.9 12.6 %shard_map.37 = f32[512,128]{1,0:T(8,128)} custom-call(bf16[6,16,4096]{2,1,0:T(8,128)(2,1)} %copy.24.left_ref, bf16[6,32,4096]{2,1,0:T(8,128)(2,1)} %copy.25.visit_ref, bf16[4096,128]{1,0:T(8,128)(2,1)} %pad_maximum_fusion.table_ref), custom_call_target="tpu_custom_call" | custom-call | flops 587202560 | bytes 3670016 | tf_op jit(solution)/shard_map/pallas_call | solution.py:121
  72.5 1.0 %broadcast_multiply_fusion = f32[512,128]{1,0:T(8,128)S(1)} fusion(f32[512,128]{1,0:T(8,128)} %shard_map.37), kind=kLoop, calls=%fused_computation.41 | loop fusion | flops 65536 | bytes 524288 | tf_op jit(solution)/shard_map/mul | solution.py:163
  73.5 0.8 fusion.21
  (18 shorter events, 0.5 us)
Async XLA Ops:
  6.5 2.6 %copy-start = (f32[32]{0:T(128)S(1)}, f32[32]{0:T(128)}, u32[]{:S(2)}) copy-start(f32[32]{0:T(128)} %param.4) | copy-start | bytes 388
  6.5 49.8 %all-gather.2.cloned.1.call-start = ((), (), s32[]{:S(2)}) async-start(), calls=%async_computation | async-start | bytes 2359296 | tf_op jit(solution)/shard_map/all_gather | solution.py:158
  49.4 1.4 %copy-start.1 = (s32[16]{0:T(128)S(1)}, s32[16]{0:T(128)}, u32[]{:S(2)}) copy-start(s32[16]{0:T(128)} %param.5) | copy-start | bytes 196
Sparse Core Ops, SparseCore 0:
  25.2 30.5 all-gather.1

commit v2 on v1

--- a/solution.py
+++ b/solution.py
@@ -143,6 +143,17 @@
     )(left_by_window, visiting, lag_table)
 
 
+def xor_gather(block, axis_name, size):
+    if size & (size - 1):
+        return lax.all_gather(block, axis_name, axis=1, tiled=True), None
+    pieces = [block]
+    for step in range(1, size):
+        pairs = [(source, source ^ step) for source in range(size)]
+        pieces.append(lax.ppermute(block, axis_name, pairs))
+    order = lax.axis_index(axis_name) ^ jnp.arange(size, dtype=jnp.int32)
+    return jnp.concatenate(pieces, axis=1), order
+
+
 def on_device(records, fir_taps, lag_limit):
     block_size = records.shape[0]
     decimated = decimate(records, fir_taps)
@@ -151,14 +162,22 @@
     spec_real, spec_imag = spectrum(decimated)
     white = whiten(spec_real, spec_imag)
     white_by_window = jnp.moveaxis(white, 1, 0)
-    left_by_window = lax.all_gather(white_by_window, "col", axis=1, tiled=True)
+    col_size = lax.axis_size("col")
+    row_size = lax.axis_size("row")
+    left_by_window, left_order = xor_gather(white_by_window, "col", col_size)
     cos_lag, sin_lag = angle_table(LAGS, bin_count, out_length, -LH)
     lag_table = jnp.concatenate([cos_lag.T, sin_lag.T], axis=0).astype(jnp.bfloat16)
     group_rows = left_by_window.shape[1]
-    piece_rows = lax.all_gather(white_by_window, "row", axis=1, tiled=True)
+    piece_rows, visit_order = xor_gather(white_by_window, "row", row_size)
     visit_count = piece_rows.shape[1]
     pair = pair_block(left_by_window, piece_rows, lag_table)
     pair = jnp.swapaxes(pair.reshape(visit_count, group_rows, LAGS), 0, 1)
+    if visit_order is not None:
+        pair = pair.reshape(group_rows, row_size, block_size, LAGS)
+        pair = jnp.take(pair, visit_order, axis=1).reshape(group_rows, visit_count, LAGS)
+    if left_order is not None:
+        pair = pair.reshape(col_size, block_size, visit_count, LAGS)
+        pair = jnp.take(pair, left_order, axis=0).reshape(group_rows, visit_count, LAGS)
     norm_scale = 1.0 / math.sqrt(white.shape[1] * bin_count)
     pair = pair * norm_scale
     lag_offset = jnp.abs(jnp.arange(LAGS, dtype=jnp.int32) - LH)

time: 81.4 us -> 70.4 us (0.86)
  blocking collectives: 24.4 us -> 0 us
  between operations: 13.6 us -> 0.26 us
  starting transfers between devices: 0.01 us -> 12.8 us
  waiting for transfers between devices: 0.02 us -> 10.9 us
  local copies, waits for them, and re-layouts: 8.37 us -> 11 us
    all_gather x1 -> x0, blocking collectives: 24.4 us -> none  [on_device(): left_by_window = lax.all_gather(white_by_window, 'col', axis=1, tiled=True)]
    ppermute x0 -> x10, starting transfers between devices: none -> 12.8 us  [xor_gather(): pieces.append(lax.ppermute(block, axis_name, pairs))]
    ppermute x0 -> x10, waiting for transfers between devices: none -> 10.9 us  [xor_gather(): pieces.append(lax.ppermute(block, axis_name, pairs))]
    concatenate x0 -> x1, local copies, waits for them, and re-layouts: none -> 5.95 us  [xor_gather(): return (jnp.concatenate(pieces, axis=1), order)]
    all_gather x2 -> x0, local copies, waits for them, and re-layouts: 4.96 us -> none  [the longest x1 3.61 us: on_device(): piece_rows = lax.all_gather(white_by_window, 'row', axis=1, tiled=True)]
    gather x0 -> x2, local copies, waits for them, and re-layouts: none -> 2.08 us  [the longest x1 1.51 us: on_device(): jnp.take(pair, visit_order, axis=1).reshape(group_rows, visit_count, LAGS)]
    concatenate x0 -> x1, other arithmetic: none -> 1.34 us  [xor_gather(): return (jnp.concatenate(pieces, axis=1), order)]
    mul x1 -> x0, other arithmetic: 0.97 us -> none  [on_device(): pair = pair * norm_scale]
  transfers between devices with their start and end apart: 1 -> 10, of which waited for: 0 -> 2; matrix products, arithmetic and copies ran while one was open for 8% -> 10% of each run, Pallas kernels for 0% -> 0%
where the time goes in v2:
time: 70.4 us; the launch traced here: 70.2 us
  matrix products  13.9 us (20%)
  starting transfers between devices  12.8 us (18%)
  Pallas kernels  12.6 us (18%)
  local copies, waits for them, and re-layouts  11 us (16%)
  waiting for transfers between devices  10.9 us (15%)
  other arithmetic  8.89 us (13%)
    ppermute x10, starting transfers between devices, xor_gather(): pieces.append(lax.ppermute(block, axis_name, pairs))  12.8 us
    pallas_call x1, Pallas kernels, pair_block(): pl.pallas_call(cross_kernel, out_shape=jax.ShapeDtypeStruct((visit_count...  12.6 us
    ppermute x10, waiting for transfers between devices, xor_gather(): pieces.append(lax.ppermute(block, axis_name, pairs))  10.9 us
    concatenate x1, local copies, waits for them, and re-layouts, xor_gather(): return (jnp.concatenate(pieces, axis=1), order)  5.95 us
    another operation x2, other arithmetic  4.54 us
    dot_general x1, matrix products, spectrum(): jnp.einsum('bwfq,gq->bwgf', real_t, sin_three, precision=lax.Precision.HI...  2.54 us
    dot_general x1, matrix products, spectrum(): jnp.einsum('bwfq,gq->bwgf', real_t, cos_three, precision=lax.Precision.HI...  2.27 us
    dot_general x1, matrix products, spectrum(): jnp.einsum('bwfq,gq->bwgf', imag_t, sin_three, precision=lax.Precision.HI...  2.27 us
  transfers between devices with their start and end apart: 10, of which 2 were waited for; matrix products, arithmetic and copies ran while one was open for 10% of the time, Pallas kernels for 0%

profile of v2, /device:TPU:0, one launch (start us, length us, event | category | flops | bytes accessed | tf_op | source)
XLA Modules:
  0.0 70.2 jit_solution(17955390643171868691)
XLA Ops:
  0.2 1.7 %reshape.190 = f32[4,6,32,256]{3,2,0,1:T(8,128)S(1)} reshape(f32[4,6,8192]{2,0,1:T(4,128)} %param.3) | data formatting | bytes 1572864 | tf_op jit(solution)/shard_map/reshape | solution.py:30
  2.7 1.3 %fusion = f32[1,288,128]{2,0,1:T(1,128)S(1)} fusion(pred[32,288,128]{2,1,0:T(32,128)(4,1)S(1)} %iota_compare_fusion, f32[32]{0:T(128)S(1)} %copy-done), kind=kOutput, calls=%fused_computation.3 | convolution fusion | flops 14155776 | bytes 1327232 | tf_op jit(solution)/shard_map/k,kij->ij/dot_general | solution.py:38
  4.1 1.3 %fusion.4 = f32[4,6,32,128]{3,2,1,0:T(8,128)S(1)} fusion(f32[288,128,1,1]{1,0,3,2:T(8,128)S(1)} %bitcast.82, f32[4,6,31,32]{3,2,1,0:T(8,128)S(1)} %copy.33, f32[4,6,32,256]{3,2,0,1:T(8,128)S(1)} %reshape.190), kind=kOutput, calls=%fused_computation.14 | convolution fusion | flops 340402176 | bytes 1422336 | tf_op jit(solution)/shard_map/swbi,ij->swbj/dot_general | solution.py:39
  5.6 0.9 %convolution_negate_fusion = f32[64,4,6,64]{3,0,2,1:T(8,128)S(1)} fusion(f32[4,6,64,64]{3,2,1,0:T(8,128)S(1)} %reshape_reshape.4), kind=kOutput, calls=%fused_computation.8 | convolution fusion | flops 75653120 | bytes 786432 | tf_op jit(solution)/shard_map/bwnq,fn->bwfq/dot_general | solution.py:51
  6.5 0.9 %fusion.26 = f32[64,4,6,64]{3,0,2,1:T(8,128)S(1)} fusion(f32[4,6,64,64]{3,2,1,0:T(8,128)S(1)} %reshape_reshape.4), kind=kOutput, calls=%fused_computation.54 | convolution fusion | flops 75554816 | bytes 786432 | tf_op jit(solution)/shard_map/bwnq,fn->bwfq/dot_general | solution.py:50
  7.5 2.3 %fusion.13 = f32[32,4,6,64]{3,0,2,1:T(8,128)S(1)} fusion(f32[64,4,6,64]{3,0,2,1:T(8,128)S(1)} %fusion.26, f32[64,4,6,64]{3,0,2,1:T(8,128)S(1)} %convolution_negate_fusion, f32[64,64]{1,0:T(8,128)S(1)} %get-tuple-element.11, f32[64,64]{1,0:T(8,128)S(1)} %get-tuple-element.12), kind=kOutput, calls=%fused_computation.28 | convolution fusion | flops 38072320 | bytes 1015808 | tf_op jit(solution)/shard_map/bwfq,gq->bwgf/dot_general | solution.py:59
  9.7 2.3 %fusion.17 = f32[32,4,6,64]{3,0,2,1:T(8,128)S(1)} fusion(f32[64,4,6,64]{3,0,2,1:T(8,128)S(1)} %convolution_negate_fusion, f32[64,4,6,64]{3,0,2,1:T(8,128)S(1)} %fusion.26, f32[64,64]{1,0:T(8,128)S(1)} %get-tuple-element.11, f32[64,64]{1,0:T(8,128)S(1)} %get-tuple-element.12), kind=kOutput, calls=%fused_computation.32 | convolution fusion | flops 38072320 | bytes 1015808 | tf_op jit(solution)/shard_map/bwfq,gq->bwgf/dot_general | solution.py:56
  12.0 2.3 %fusion.3 = f32[4,6,32,64]{3,2,1,0:T(8,128)S(1)} fusion(f32[32,4,6,64]{3,0,2,1:T(8,128)S(1)} %fusion.17, f32[64,4,6,64]{3,0,2,1:T(8,128)S(1)} %fusion.26, f32[64,4,6,64]{3,0,2,1:T(8,128)S(1)} %convolution_negate_fusion, f32[64,64]{1,0:T(8,128)S(1)} %get-tuple-element.11, f32[64,64]{1,0:T(8,128)S(1)} %get-tuple-element.12), kind=kOutput, calls=%fused_computation.12 | convolution fusion | flops 38121472 | bytes 1212416 | tf_op jit(solution)/shard_map/bwfq,gq->bwgf/dot_general | solution.py:58
  14.3 2.5 %add_reduce_fusion = (f32[4,6,32]{2,1,0:T(8,128)S(1)}, f32[4,6,32,64]{3,2,1,0:T(8,128)S(1)}) fusion(f32[4,6,32,64]{3,2,1,0:T(8,128)S(1)} %fusion.3, f32[32,4,6,64]{3,0,2,1:T(8,128)S(1)} %fusion.13, f32[64,4,6,64]{3,0,2,1:T(8,128)S(1)} %convolution_negate_fusion, f32[64,64]{1,0:T(8,128)S(1)} %get-tuple-element.11, f32[64,4,6,64]{3,0,2,1:T(8,128)S(1)} %fusion.26, ...), kind=kOutput, calls=%fused_computation.40 | convolution fusion | flops 38317312 | bytes 1412096 | tf_op jit(solution)/shard_map/bwfq,gq->bwgf/dot_general | solution.py:61
  17.7 3.4 %collective-permute-start.9 = (bf16[6,4,4096]{2,1,0:T(4,128)(2,1)S(1)}, bf16[6,4,4096]{2,1,0:T(4,128)(2,1)S(1)}, u32[]{:S(2)}, u32[]{:S(2)}) collective-permute-start(bf16[6,4,4096]{2,1,0:T(4,128)(2,1)S(1)} %maximum_bitcast_fusion), channel_id=1, source_target_pairs={{0,28},{4,24},{8,20},{12,16},{16,12},{20,8},{24,4},{28,0},{1,29},{... | collective-permute-start | bytes 589832 | tf_op jit(solution)/shard_map/ppermute | solution.py:152
  21.7 3.6 %collective-permute-start.2 = (bf16[6,4,4096]{2,1,0:T(4,128)(2,1)S(1)}, bf16[6,4,4096]{2,1,0:T(4,128)(2,1)S(1)}, u32[]{:S(2)}, u32[]{:S(2)}) collective-permute-start(bf16[6,4,4096]{2,1,0:T(4,128)(2,1)S(1)} %maximum_bitcast_fusion), channel_id=1, source_target_pairs={{0,3},{1,2},{2,1},{3,0},{4,7},{5,6},{6,5},{7,4},{8,11},{9,10},{10,... | collective-permute-start | bytes 589832 | tf_op jit(solution)/shard_map/ppermute | solution.py:152
  25.3 0.8 %collective-permute-start = (bf16[6,4,4096]{2,1,0:T(4,128)(2,1)S(1)}, bf16[6,4,4096]{2,1,0:T(4,128)(2,1)S(1)}, u32[]{:S(2)}, u32[]{:S(2)}) collective-permute-start(bf16[6,4,4096]{2,1,0:T(4,128)(2,1)S(1)} %maximum_bitcast_fusion), channel_id=1, source_target_pairs={{0,1},{1,0},{2,3},{3,2},{4,5},{5,4},{6,7},{7,6},{8,9},{9,8},{10,11... | collective-permute-start | bytes 589832 | tf_op jit(solution)/shard_map/ppermute | solution.py:152
  26.6 4.4 %cosine_convert_fusion = (bf16[2048,128]{1,0:T(8,128)(2,1)S(1)}, bf16[2048,128]{1,0:T(8,128)(2,1)S(1)}) fusion(s32[128]{0:T(128)S(1)} %iota_add_fusion), kind=kLoop, calls=%fused_computation.23 | loop fusion | flops 4194304 | bytes 1049088 | tf_op jit(solution)/shard_map/convert
  30.9 1.1 %pad_maximum_fusion.table_ref = bf16[4096,128]{1,0:T(8,128)(2,1)} fusion(bf16[2048,128]{1,0:T(8,128)(2,1)S(1)} %get-tuple-element.8, bf16[2048,128]{1,0:T(8,128)(2,1)S(1)} %get-tuple-element.7), kind=kLoop, calls=%fused_computation.21 | loop fusion | flops 2097152 | bytes 2097152 | tf_op jit(solution)/shard_map/concatenate | solution.py:169
  32.7 0.9 %collective-permute-start.6 = (bf16[6,4,4096]{2,1,0:T(4,128)(2,1)S(1)}, bf16[6,4,4096]{2,1,0:T(4,128)(2,1)S(1)}, u32[]{:S(2)}, u32[]{:S(2)}) collective-permute-start(bf16[6,4,4096]{2,1,0:T(4,128)(2,1)S(1)} %maximum_bitcast_fusion), channel_id=1, source_target_pairs={{0,16},{4,20},{8,24},{12,28},{16,0},{20,4},{24,8},{28,12},{1,17},{... | collective-permute-start | bytes 589832 | tf_op jit(solution)/shard_map/ppermute | solution.py:152
  33.6 1.4 %collective-permute-start.5 = (bf16[6,4,4096]{2,1,0:T(4,128)(2,1)S(1)}, bf16[6,4,4096]{2,1,0:T(4,128)(2,1)S(1)}, u32[]{:S(2)}, u32[]{:S(2)}) collective-permute-start(bf16[6,4,4096]{2,1,0:T(4,128)(2,1)S(1)} %maximum_bitcast_fusion), channel_id=1, source_target_pairs={{0,12},{4,8},{8,4},{12,0},{16,28},{20,24},{24,20},{28,16},{1,13},{... | collective-permute-start | bytes 589832 | tf_op jit(solution)/shard_map/ppermute | solution.py:152
  34.9 7.5 %collective-permute-done.1 = bf16[6,4,4096]{2,1,0:T(4,128)(2,1)S(1)} collective-permute-done((bf16[6,4,4096]{2,1,0:T(4,128)(2,1)S(1)}, bf16[6,4,4096]{2,1,0:T(4,128)(2,1)S(1)}, u32[]{:S(2)}, u32[]{:S(2)}) %collective-permute-start.1) | collective-permute-done | bytes 196640 | tf_op jit(solution)/shard_map/ppermute | solution.py:152
  42.4 1.5 %collective-permute-start.4 = (bf16[6,4,4096]{2,1,0:T(4,128)(2,1)S(1)}, bf16[6,4,4096]{2,1,0:T(4,128)(2,1)S(1)}, u32[]{:S(2)}, u32[]{:S(2)}) collective-permute-start(bf16[6,4,4096]{2,1,0:T(4,128)(2,1)S(1)} %maximum_bitcast_fusion), channel_id=1, source_target_pairs={{0,8},{4,12},{8,0},{12,4},{16,24},{20,28},{24,16},{28,20},{1,9},{5... | collective-permute-start | bytes 589832 | tf_op jit(solution)/shard_map/ppermute | solution.py:152
  44.0 1.3 %pad_maximum_fusion.1.left_ref = bf16[6,16,4096]{2,1,0:T(8,128)(2,1)} fusion(bf16[6,4,4096]{2,1,0:T(4,128)(2,1)S(1)} %collective-permute-done.2, bf16[6,4,4096]{2,1,0:T(4,128)(2,1)S(1)} %collective-permute-done.1, bf16[6,4,4096]{2,1,0:T(4,128)(2,1)S(1)} %collective-permute-done, bf16[6,4,4096]{2,1,0:T(4,128)(2,1)S(1)} %maximum_bitcast_fusion), kind=kLoop, calls=%fused_computation.27 | loop fusion | flops 3145728 | bytes 1572864 | tf_op jit(solution)/shard_map/concatenate | solution.py:154
  45.3 3.3 %collective-permute-done.4 = bf16[6,4,4096]{2,1,0:T(4,128)(2,1)S(1)} collective-permute-done((bf16[6,4,4096]{2,1,0:T(4,128)(2,1)S(1)}, bf16[6,4,4096]{2,1,0:T(4,128)(2,1)S(1)}, u32[]{:S(2)}, u32[]{:S(2)}) %collective-permute-start.4) | collective-permute-done | bytes 196640 | tf_op jit(solution)/shard_map/ppermute | solution.py:152
  48.7 5.9 %concatenate.24.visit_ref = bf16[6,32,4096]{2,1,0:T(8,128)(2,1)} concatenate(bf16[6,4,4096]{2,1,0:T(4,128)(2,1)S(1)} %maximum_bitcast_fusion, bf16[6,4,4096]{2,1,0:T(4,128)(2,1)S(1)} %collective-permute-done.3, bf16[6,4,4096]{2,1,0:T(4,128)(2,1)S(1)} %collective-permute-done.4, bf16[6,4,4096]{2,1,0:T(4,128)(2,1)S(1)} %collective-permute-done.5, ...), dimensions={1} | concatenate | bytes 3145728 | tf_op jit(solution)/shard_map/concatenate | solution.py:154
  54.6 12.6 %shard_map.37 = f32[512,128]{1,0:T(8,128)} custom-call(bf16[6,16,4096]{2,1,0:T(8,128)(2,1)} %pad_maximum_fusion.1.left_ref, bf16[6,32,4096]{2,1,0:T(8,128)(2,1)} %concatenate.24.visit_ref, bf16[4096,128]{1,0:T(8,128)(2,1)} %pad_maximum_fusion.table_ref), custom_call_target="tpu_custom_call" | custom-call | flops 587202560 | bytes 3670016 | tf_op jit(solution)/shard_map/pallas_call | solution.py:121
  67.2 1.5 %gather_fusion = f32[8,16,4,128]{3,1,2,0:T(8,128)S(1)} fusion(f32[16,8,4,128]{3,0,2,1:T(8,128)} %bitcast.79, s32[1024]{0:T(1024)S(1)} %pad_clamp_fusion.1), kind=kCustom, calls=%fused_computation | custom fusion | bytes 524320 | tf_op jit(solution)/shard_map/jit(_take)/gather | solution.py:177
  69.4 0.8 %multiply_select_fusion = f32[16,1,32,128]{3,2,1,0:T(8,128)} fusion(f32[16,1,32,128]{3,2,1,0:T(8,128)S(1)} %bitcast.80, pred[16]{0:T(512)(128)(4,1)S(1)} %broadcast_in_dim.63, pred[16,128]{1,0:T(8,128)(4,1)S(1)} %broadcast_compare_fusion), kind=kLoop, calls=%fused_computation.42 | loop fusion | flops 196608 | bytes 526352 | tf_op jit(solution)/shard_map/jit(_where)/select_n | solution.py:185
  (45 shorter events, 4.4 us)
Async XLA Ops:
  0.0 2.7 %copy-start = (f32[32]{0:T(128)S(1)}, f32[32]{0:T(128)}, u32[]{:S(2)}) copy-start(f32[32]{0:T(128)} %param.4) | copy-start | bytes 388
  17.7 14.4 %collective-permute-start.9 = (bf16[6,4,4096]{2,1,0:T(4,128)(2,1)S(1)}, bf16[6,4,4096]{2,1,0:T(4,128)(2,1)S(1)}, u32[]{:S(2)}, u32[]{:S(2)}) collective-permute-start(bf16[6,4,4096]{2,1,0:T(4,128)(2,1)S(1)} %maximum_bitcast_fusion), channel_id=1, source_target_pairs={{0,28},{4,24},{8,20},{12,16},{16,12},{20,8},{24,4},{28,0},{1,29},{... | collective-permute-start | bytes 589832 | tf_op jit(solution)/shard_map/ppermute | solution.py:152
  21.1 11.6 %collective-permute-start.8 = (bf16[6,4,4096]{2,1,0:T(4,128)(2,1)S(1)}, bf16[6,4,4096]{2,1,0:T(4,128)(2,1)S(1)}, u32[]{:S(2)}, u32[]{:S(2)}) collective-permute-start(bf16[6,4,4096]{2,1,0:T(4,128)(2,1)S(1)} %maximum_bitcast_fusion), channel_id=1, source_target_pairs={{0,24},{4,28},{8,16},{12,20},{16,8},{20,12},{24,0},{28,4},{1,25},{... | collective-permute-start | bytes 589832 | tf_op jit(solution)/shard_map/ppermute | solution.py:152
  21.7 11.8 %collective-permute-start.2 = (bf16[6,4,4096]{2,1,0:T(4,128)(2,1)S(1)}, bf16[6,4,4096]{2,1,0:T(4,128)(2,1)S(1)}, u32[]{:S(2)}, u32[]{:S(2)}) collective-permute-start(bf16[6,4,4096]{2,1,0:T(4,128)(2,1)S(1)} %maximum_bitcast_fusion), channel_id=1, source_target_pairs={{0,3},{1,2},{2,1},{3,0},{4,7},{5,6},{6,5},{7,4},{8,11},{9,10},{10,... | collective-permute-start | bytes 589832 | tf_op jit(solution)/shard_map/ppermute | solution.py:152
  25.3 17.1 %collective-permute-start.1 = (bf16[6,4,4096]{2,1,0:T(4,128)(2,1)S(1)}, bf16[6,4,4096]{2,1,0:T(4,128)(2,1)S(1)}, u32[]{:S(2)}, u32[]{:S(2)}) collective-permute-start(bf16[6,4,4096]{2,1,0:T(4,128)(2,1)S(1)} %maximum_bitcast_fusion), channel_id=1, source_target_pairs={{0,2},{1,3},{2,0},{3,1},{4,6},{5,7},{6,4},{7,5},{8,10},{9,11},{10,... | collective-permute-start | bytes 589832 | tf_op jit(solution)/shard_map/ppermute | solution.py:152
  25.3 18.6 %collective-permute-start = (bf16[6,4,4096]{2,1,0:T(4,128)(2,1)S(1)}, bf16[6,4,4096]{2,1,0:T(4,128)(2,1)S(1)}, u32[]{:S(2)}, u32[]{:S(2)}) collective-permute-start(bf16[6,4,4096]{2,1,0:T(4,128)(2,1)S(1)} %maximum_bitcast_fusion), channel_id=1, source_target_pairs={{0,1},{1,0},{2,3},{3,2},{4,5},{5,4},{6,7},{7,6},{8,9},{9,8},{10,11... | collective-permute-start | bytes 589832 | tf_op jit(solution)/shard_map/ppermute | solution.py:152
  30.9 1.1 %copy-start.1 = (s32[16]{0:T(128)S(1)}, s32[16]{0:T(128)}, u32[]{:S(2)}) copy-start(s32[16]{0:T(128)} %param.5) | copy-start | bytes 196
  32.1 13.2 %collective-permute-start.7 = (bf16[6,4,4096]{2,1,0:T(4,128)(2,1)S(1)}, bf16[6,4,4096]{2,1,0:T(4,128)(2,1)S(1)}, u32[]{:S(2)}, u32[]{:S(2)}) collective-permute-start(bf16[6,4,4096]{2,1,0:T(4,128)(2,1)S(1)} %maximum_bitcast_fusion), channel_id=1, source_target_pairs={{0,20},{4,16},{8,28},{12,24},{16,4},{20,0},{24,12},{28,8},{1,21},{... | collective-permute-start | bytes 589832 | tf_op jit(solution)/shard_map/ppermute | solution.py:152
  32.7 12.6 %collective-permute-start.6 = (bf16[6,4,4096]{2,1,0:T(4,128)(2,1)S(1)}, bf16[6,4,4096]{2,1,0:T(4,128)(2,1)S(1)}, u32[]{:S(2)}, u32[]{:S(2)}) collective-permute-start(bf16[6,4,4096]{2,1,0:T(4,128)(2,1)S(1)} %maximum_bitcast_fusion), channel_id=1, source_target_pairs={{0,16},{4,20},{8,24},{12,28},{16,0},{20,4},{24,8},{28,12},{1,17},{... | collective-permute-start | bytes 589832 | tf_op jit(solution)/shard_map/ppermute | solution.py:152
  33.6 11.8 %collective-permute-start.5 = (bf16[6,4,4096]{2,1,0:T(4,128)(2,1)S(1)}, bf16[6,4,4096]{2,1,0:T(4,128)(2,1)S(1)}, u32[]{:S(2)}, u32[]{:S(2)}) collective-permute-start(bf16[6,4,4096]{2,1,0:T(4,128)(2,1)S(1)} %maximum_bitcast_fusion), channel_id=1, source_target_pairs={{0,12},{4,8},{8,4},{12,0},{16,28},{20,24},{24,20},{28,16},{1,13},{... | collective-permute-start | bytes 589832 | tf_op jit(solution)/shard_map/ppermute | solution.py:152
  42.4 6.2 %collective-permute-start.4 = (bf16[6,4,4096]{2,1,0:T(4,128)(2,1)S(1)}, bf16[6,4,4096]{2,1,0:T(4,128)(2,1)S(1)}, u32[]{:S(2)}, u32[]{:S(2)}) collective-permute-start(bf16[6,4,4096]{2,1,0:T(4,128)(2,1)S(1)} %maximum_bitcast_fusion), channel_id=1, source_target_pairs={{0,8},{4,12},{8,0},{12,4},{16,24},{20,28},{24,16},{28,20},{1,9},{5... | collective-permute-start | bytes 589832 | tf_op jit(solution)/shard_map/ppermute | solution.py:152
  44.0 4.7 %collective-permute-start.3 = (bf16[6,4,4096]{2,1,0:T(4,128)(2,1)S(1)}, bf16[6,4,4096]{2,1,0:T(4,128)(2,1)S(1)}, u32[]{:S(2)}, u32[]{:S(2)}) collective-permute-start(bf16[6,4,4096]{2,1,0:T(4,128)(2,1)S(1)} %maximum_bitcast_fusion), channel_id=1, source_target_pairs={{0,4},{4,0},{8,12},{12,8},{16,20},{20,16},{24,28},{28,24},{1,5},{5... | collective-permute-start | bytes 589832 | tf_op jit(solution)/shard_map/ppermute | solution.py:152

commit v3 on v2

--- a/solution.py
+++ b/solution.py
@@ -1,3 +1,4 @@
+import functools
 import math
 
 import jax
@@ -75,83 +76,91 @@
     return jnp.concatenate([white_real, white_imag], axis=-1).astype(jnp.bfloat16)
 
 
-def cross_kernel(left_ref, visit_ref, table_ref, out_ref, left_f32, visit_f32, cross_ref):
-    window_count, left_count, width = left_ref.shape
-    group = visit_ref.shape[1]
+def cross_kernel(left_count, visit_count, *refs):
+    left_refs = refs[:left_count]
+    visit_refs = refs[left_count:left_count + visit_count]
+    table_ref, out_ref, left_f32, visit_f32, cross_ref = refs[left_count + visit_count:]
+    window_count, piece, width = left_refs[0].shape
+    rows_left = left_f32.shape[1]
     bin_count = width // 2
-    chunk = max(128, min(512, 8192 // left_count))
+    chunk = max(128, min(512, 8192 // rows_left))
     chunks = bin_count // chunk
-
-    @pl.when(pl.program_id(0) == 0)
-    def _():
-        left_f32[...] = left_ref[...].astype(jnp.float32)
-
-    visit_f32[...] = visit_ref[...].astype(jnp.float32)
-
-    def one_chunk(step, carry):
-        partner = step // chunks
-        off = pl.multiple_of((step % chunks) * chunk, chunk)
-        acc_re = jnp.zeros((left_count, chunk), jnp.float32)
-        acc_im = jnp.zeros((left_count, chunk), jnp.float32)
-        for window in range(window_count):
-            left_c = left_f32[window, :, pl.ds(off, chunk)]
-            left_d = left_f32[window, :, pl.ds(off + bin_count, chunk)]
-            vis_c = visit_f32[window, pl.ds(partner, 1), pl.ds(off, chunk)]
-            vis_d = visit_f32[window, pl.ds(partner, 1), pl.ds(off + bin_count, chunk)]
-            acc_re = acc_re + (left_c * vis_c + left_d * vis_d)
-            acc_im = acc_im + (left_c * vis_d - left_d * vis_c)
-        row = pl.multiple_of(partner * left_count, left_count)
-        cross_ref[pl.ds(row, left_count), pl.ds(off, chunk)] = acc_re.astype(jnp.bfloat16)
-        cross_ref[pl.ds(row, left_count), pl.ds(off + bin_count, chunk)] = acc_im.astype(jnp.bfloat16)
-        return carry
-
-    lax.fori_loop(0, group * chunks, one_chunk, 0)
-    out_ref[...] = jnp.dot(cross_ref[...], table_ref[...], preferred_element_type=jnp.float32)
-
-
-def pair_block(left_by_window, visiting, lag_table):
-    window_count, left_count, width = left_by_window.shape
-    visit_count = visiting.shape[1]
+    group_rows = cross_ref.shape[0]
+    group = group_rows // (piece * rows_left)
+
+    for index, ref in enumerate(left_refs):
+        left_f32[:, index * piece:(index + 1) * piece, :] = ref[...].astype(jnp.float32)
+    for index, ref in enumerate(visit_refs):
+        visit_f32[:, index * piece:(index + 1) * piece, :] = ref[...].astype(jnp.float32)
+
+    for first in range(0, visit_count, group):
+        base = first * piece
+
+        def one_chunk(step, carry):
+            local = step // chunks
+            partner = base + local
+            off = pl.multiple_of((step % chunks) * chunk, chunk)
+            acc_re = jnp.zeros((rows_left, chunk), jnp.float32)
+            acc_im = jnp.zeros((rows_left, chunk), jnp.float32)
+            for window in range(window_count):
+                left_c = left_f32[window, :, pl.ds(off, chunk)]
+                left_d = left_f32[window, :, pl.ds(off + bin_count, chunk)]
+                vis_c = visit_f32[window, pl.ds(partner, 1), pl.ds(off, chunk)]
+                vis_d = visit_f32[window, pl.ds(partner, 1), pl.ds(off + bin_count, chunk)]
+                acc_re = acc_re + (left_c * vis_c + left_d * vis_d)
+                acc_im = acc_im + (left_c * vis_d - left_d * vis_c)
+            row = pl.multiple_of(local * rows_left, rows_left)
+            cross_ref[pl.ds(row, rows_left), pl.ds(off, chunk)] = acc_re.astype(jnp.bfloat16)
+            cross_ref[pl.ds(row, rows_left), pl.ds(off + bin_count, chunk)] = acc_im.astype(jnp.bfloat16)
+            return carry
+
+        lax.fori_loop(0, group * piece * chunks, one_chunk, 0)
+        out_ref[base * rows_left:base * rows_left + group_rows, :] = jnp.dot(
+            cross_ref[...], table_ref[...], preferred_element_type=jnp.float32
+        )
+
+
+def pair_block(left_pieces, visit_pieces, lag_table):
+    window_count, piece, width = left_pieces[0].shape
+    left_count = len(left_pieces)
+    visit_count = len(visit_pieces)
+    rows_left = left_count * piece
+    visit_rows = visit_count * piece
     lag_count = lag_table.shape[1]
-    group = min(8, visit_count)
+    group = max(1, min(visit_count, 256 // (piece * rows_left)))
     while visit_count % group:
         group -= 1
-    rows = group * left_count
-    flops = visit_count * left_count * width * (4 * window_count + 2 * lag_count)
+    flops = visit_rows * rows_left * width * (4 * window_count + 2 * lag_count)
+    vmem = pltpu.VMEM
     return pl.pallas_call(
-        cross_kernel,
-        out_shape=jax.ShapeDtypeStruct((visit_count * left_count, lag_count), jnp.float32),
-        grid=(visit_count // group,),
-        in_specs=[
-            pl.BlockSpec((window_count, left_count, width), lambda g: (0, 0, 0)),
-            pl.BlockSpec((window_count, group, width), lambda g: (0, g, 0)),
-            pl.BlockSpec((width, lag_count), lambda g: (0, 0)),
+        functools.partial(cross_kernel, left_count, visit_count),
+        out_shape=jax.ShapeDtypeStruct((visit_rows * rows_left, lag_count), jnp.float32),
+        in_specs=[pl.BlockSpec(memory_space=vmem)] * (left_count + visit_count + 1),
+        out_specs=pl.BlockSpec(memory_space=vmem),
+        scratch_shapes=[
+            vmem((window_count, rows_left, width), jnp.float32),
+            vmem((window_count, visit_rows, width), jnp.float32),
+            vmem((group * piece * rows_left, width), jnp.bfloat16),
         ],
-        out_specs=pl.BlockSpec((rows, lag_count), lambda g: (g, 0)),
-        scratch_shapes=[
-            pltpu.VMEM((window_count, left_count, width), jnp.float32),
-            pltpu.VMEM((window_count, group, width), jnp.float32),
-            pltpu.VMEM((rows, width), jnp.bfloat16),
-        ],
-        compiler_params=pltpu.CompilerParams(dimension_semantics=("arbitrary",)),
+        compiler_params=pltpu.CompilerParams(vmem_limit_bytes=60 * 1024 * 1024),
         cost_estimate=pl.CostEstimate(
             flops=flops,
             transcendentals=0,
-            bytes_accessed=2 * width * (window_count * (left_count + visit_count) + lag_count)
-            + 4 * visit_count * left_count * lag_count,
+            bytes_accessed=2 * width * (window_count * (rows_left + visit_rows) + lag_count)
+            + 4 * visit_rows * rows_left * lag_count,
         ),
-    )(left_by_window, visiting, lag_table)
+    )(*left_pieces, *visit_pieces, lag_table)
 
 
 def xor_gather(block, axis_name, size):
     if size & (size - 1):
-        return lax.all_gather(block, axis_name, axis=1, tiled=True), None
+        return [lax.all_gather(block, axis_name, axis=1, tiled=True)], None
     pieces = [block]
     for step in range(1, size):
         pairs = [(source, source ^ step) for source in range(size)]
         pieces.append(lax.ppermute(block, axis_name, pairs))
     order = lax.axis_index(axis_name) ^ jnp.arange(size, dtype=jnp.int32)
-    return jnp.concatenate(pieces, axis=1), order
+    return pieces, order
 
 
 def on_device(records, fir_taps, lag_limit):
@@ -167,9 +176,9 @@
     left_by_window, left_order = xor_gather(white_by_window, "col", col_size)
     cos_lag, sin_lag = angle_table(LAGS, bin_count, out_length, -LH)
     lag_table = jnp.concatenate([cos_lag.T, sin_lag.T], axis=0).astype(jnp.bfloat16)
-    group_rows = left_by_window.shape[1]
+    group_rows = sum(piece.shape[1] for piece in left_by_window)
     piece_rows, visit_order = xor_gather(white_by_window, "row", row_size)
-    visit_count = piece_rows.shape[1]
+    visit_count = sum(piece.shape[1] for piece in piece_rows)
     pair = pair_block(left_by_window, piece_rows, lag_table)
     pair = jnp.swapaxes(pair.reshape(visit_count, group_rows, LAGS), 0, 1)
     if visit_order is not None:

time: 70.4 us -> 74.1 us (1.053)
  waiting for transfers between devices: 10.9 us -> 15.9 us
  local copies, waits for them, and re-layouts: 11 us -> 6.33 us
  starting transfers between devices: 12.8 us -> 16.8 us
  other arithmetic: 8.89 us -> 7.55 us
    concatenate x1 -> x0, local copies, waits for them, and re-layouts: 5.95 us -> none  [xor_gather(): return (jnp.concatenate(pieces, axis=1), order)]
    ppermute x10, waiting for transfers between devices: 10.9 us -> 15.9 us  [xor_gather(): pieces.append(lax.ppermute(block, axis_name, pairs))]
    ppermute x10, starting transfers between devices: 12.8 us -> 16.8 us  [xor_gather(): pieces.append(lax.ppermute(block, axis_name, pairs))]
    concatenate x1 -> x0, other arithmetic: 1.34 us -> none  [xor_gather(): return (jnp.concatenate(pieces, axis=1), order)]
    unnamed x5 -> x27, local copies, waits for them, and re-layouts: 0.04 us -> 1.37 us
  transfers between devices with their start and end apart: 10 -> 10, of which waited for: 2 -> 4; matrix products, arithmetic and copies ran while one was open for 10% -> 8% of each run, Pallas kernels for 0% -> 0%
where the time goes in v3:
time: 74.1 us; the launch traced here: 73.9 us
  starting transfers between devices  16.8 us (23%)
  waiting for transfers between devices  15.9 us (21%)
  matrix products  13.9 us (19%)
  Pallas kernels  13.2 us (18%)
  other arithmetic  7.55 us (10%)
  local copies, waits for them, and re-layouts  6.33 us (9%)
    ppermute x10, starting transfers between devices, xor_gather(): pieces.append(lax.ppermute(block, axis_name, pairs))  16.8 us
    ppermute x10, waiting for transfers between devices, xor_gather(): pieces.append(lax.ppermute(block, axis_name, pairs))  15.9 us
    pallas_call x1, Pallas kernels, pair_block(): pl.pallas_call(functools.partial(cross_kernel, left_count, visit_count),...  13.2 us
    another operation x2, other arithmetic  4.54 us
    dot_general x1, matrix products, spectrum(): jnp.einsum('bwfq,gq->bwgf', real_t, sin_three, precision=lax.Precision.HI...  2.54 us
    dot_general x1, matrix products, spectrum(): jnp.einsum('bwfq,gq->bwgf', real_t, cos_three, precision=lax.Precision.HI...  2.27 us
    dot_general x1, matrix products, spectrum(): jnp.einsum('bwfq,gq->bwgf', imag_t, sin_three, precision=lax.Precision.HI...  2.27 us
    dot_general x1, matrix products, spectrum(): jnp.einsum('bwfq,gq->bwgf', imag_t, cos_three, precision=lax.Precision.HI...  2.27 us
  transfers between devices with their start and end apart: 10, of which 4 were waited for; matrix products, arithmetic and copies ran while one was open for 8% of the time, Pallas kernels for 0%

profile of v3, /device:TPU:0, one launch (start us, length us, event | category | flops | bytes accessed | tf_op | source)
XLA Modules:
  0.0 73.9 jit_solution(2925953127562973430)
XLA Ops:
  0.2 1.7 %reshape.190 = f32[4,6,32,256]{3,2,0,1:T(8,128)S(1)} reshape(f32[4,6,8192]{2,0,1:T(4,128)} %param.3) | data formatting | bytes 1572864 | tf_op jit(solution)/shard_map/reshape | solution.py:31
  2.7 1.3 %fusion = f32[1,288,128]{2,0,1:T(1,128)S(1)} fusion(pred[32,288,128]{2,1,0:T(32,128)(4,1)S(1)} %iota_compare_fusion, f32[32]{0:T(128)S(1)} %copy-done), kind=kOutput, calls=%fused_computation.3 | convolution fusion | flops 14155776 | bytes 1327232 | tf_op jit(solution)/shard_map/k,kij->ij/dot_general | solution.py:39
  4.1 1.3 %fusion.4 = f32[4,6,32,128]{3,2,1,0:T(8,128)S(1)} fusion(f32[288,128,1,1]{1,0,3,2:T(8,128)S(1)} %bitcast.82, f32[4,6,31,32]{3,2,1,0:T(8,128)S(1)} %copy.33, f32[4,6,32,256]{3,2,0,1:T(8,128)S(1)} %reshape.190), kind=kOutput, calls=%fused_computation.14 | convolution fusion | flops 340402176 | bytes 1422336 | tf_op jit(solution)/shard_map/swbi,ij->swbj/dot_general | solution.py:40
  5.6 0.9 %convolution_negate_fusion = f32[64,4,6,64]{3,0,2,1:T(8,128)S(1)} fusion(f32[4,6,64,64]{3,2,1,0:T(8,128)S(1)} %reshape_reshape.4), kind=kOutput, calls=%fused_computation.8 | convolution fusion | flops 75653120 | bytes 786432 | tf_op jit(solution)/shard_map/bwnq,fn->bwfq/dot_general | solution.py:52
  6.5 0.9 %fusion.26 = f32[64,4,6,64]{3,0,2,1:T(8,128)S(1)} fusion(f32[4,6,64,64]{3,2,1,0:T(8,128)S(1)} %reshape_reshape.4), kind=kOutput, calls=%fused_computation.53 | convolution fusion | flops 75554816 | bytes 786432 | tf_op jit(solution)/shard_map/bwnq,fn->bwfq/dot_general | solution.py:51
  7.5 2.3 %fusion.13 = f32[32,4,6,64]{3,0,2,1:T(8,128)S(1)} fusion(f32[64,4,6,64]{3,0,2,1:T(8,128)S(1)} %fusion.26, f32[64,4,6,64]{3,0,2,1:T(8,128)S(1)} %convolution_negate_fusion, f32[64,64]{1,0:T(8,128)S(1)} %get-tuple-element.11, f32[64,64]{1,0:T(8,128)S(1)} %get-tuple-element.12), kind=kOutput, calls=%fused_computation.27 | convolution fusion | flops 38072320 | bytes 1015808 | tf_op jit(solution)/shard_map/bwfq,gq->bwgf/dot_general | solution.py:60
  9.7 2.3 %fusion.17 = f32[32,4,6,64]{3,0,2,1:T(8,128)S(1)} fusion(f32[64,4,6,64]{3,0,2,1:T(8,128)S(1)} %convolution_negate_fusion, f32[64,4,6,64]{3,0,2,1:T(8,128)S(1)} %fusion.26, f32[64,64]{1,0:T(8,128)S(1)} %get-tuple-element.11, f32[64,64]{1,0:T(8,128)S(1)} %get-tuple-element.12), kind=kOutput, calls=%fused_computation.31 | convolution fusion | flops 38072320 | bytes 1015808 | tf_op jit(solution)/shard_map/bwfq,gq->bwgf/dot_general | solution.py:57
  12.0 2.3 %fusion.3 = f32[4,6,32,64]{3,2,1,0:T(8,128)S(1)} fusion(f32[32,4,6,64]{3,0,2,1:T(8,128)S(1)} %fusion.17, f32[64,4,6,64]{3,0,2,1:T(8,128)S(1)} %fusion.26, f32[64,4,6,64]{3,0,2,1:T(8,128)S(1)} %convolution_negate_fusion, f32[64,64]{1,0:T(8,128)S(1)} %get-tuple-element.11, f32[64,64]{1,0:T(8,128)S(1)} %get-tuple-element.12), kind=kOutput, calls=%fused_computation.12 | convolution fusion | flops 38121472 | bytes 1212416 | tf_op jit(solution)/shard_map/bwfq,gq->bwgf/dot_general | solution.py:59
  14.3 2.5 %add_reduce_fusion = (f32[4,6,32]{2,1,0:T(8,128)S(1)}, f32[4,6,32,64]{3,2,1,0:T(8,128)S(1)}) fusion(f32[4,6,32,64]{3,2,1,0:T(8,128)S(1)} %fusion.3, f32[32,4,6,64]{3,0,2,1:T(8,128)S(1)} %fusion.13, f32[64,4,6,64]{3,0,2,1:T(8,128)S(1)} %convolution_negate_fusion, f32[64,64]{1,0:T(8,128)S(1)} %get-tuple-element.11, f32[64,4,6,64]{3,0,2,1:T(8,128)S(1)} %fusion.26, ...), kind=kOutput, calls=%fused_computation.39 | convolution fusion | flops 38317312 | bytes 1412096 | tf_op jit(solution)/shard_map/bwfq,gq->bwgf/dot_general | solution.py:62
  17.7 3.4 %collective-permute-start.9 = (bf16[6,4,4096]{2,1,0:T(4,128)(2,1)S(1)}, bf16[6,4,4096]{2,1,0:T(4,128)(2,1)S(1)}, u32[]{:S(2)}, u32[]{:S(2)}) collective-permute-start(bf16[6,4,4096]{2,1,0:T(4,128)(2,1)S(1)} %maximum_bitcast_fusion.refs_0_.refs_4_), channel_id=1, source_target_pairs={{0,28},{4,24},{8,20},{12,16},{16,12},{20,8},{24,4},{28,0},{1,29},{... | collective-permute-start | bytes 589832 | tf_op jit(solution)/shard_map/ppermute | solution.py:161
  21.8 1.4 %collective-permute-start.7 = (bf16[6,4,4096]{2,1,0:T(4,128)(2,1)S(1)}, bf16[6,4,4096]{2,1,0:T(4,128)(2,1)S(1)}, u32[]{:S(2)}, u32[]{:S(2)}) collective-permute-start(bf16[6,4,4096]{2,1,0:T(4,128)(2,1)S(1)} %maximum_bitcast_fusion.refs_0_.refs_4_), channel_id=1, source_target_pairs={{0,20},{4,16},{8,28},{12,24},{16,4},{20,0},{24,12},{28,8},{1,21},{... | collective-permute-start | bytes 589832 | tf_op jit(solution)/shard_map/ppermute | solution.py:161
  23.4 1.1 %collective-permute-start.5 = (bf16[6,4,4096]{2,1,0:T(4,128)(2,1)S(1)}, bf16[6,4,4096]{2,1,0:T(4,128)(2,1)S(1)}, u32[]{:S(2)}, u32[]{:S(2)}) collective-permute-start(bf16[6,4,4096]{2,1,0:T(4,128)(2,1)S(1)} %maximum_bitcast_fusion.refs_0_.refs_4_), channel_id=1, source_target_pairs={{0,12},{4,8},{8,4},{12,0},{16,28},{20,24},{24,20},{28,16},{1,13},{... | collective-permute-start | bytes 589832 | tf_op jit(solution)/shard_map/ppermute | solution.py:161
  24.9 4.4 %cosine_convert_fusion = (bf16[2048,128]{1,0:T(8,128)(2,1)S(1)}, bf16[2048,128]{1,0:T(8,128)(2,1)S(1)}) fusion(s32[128]{0:T(128)S(1)} %iota_add_fusion), kind=kLoop, calls=%fused_computation.23 | loop fusion | flops 4194304 | bytes 1049088 | tf_op jit(solution)/shard_map/convert
  29.3 1.1 %pad_maximum_fusion.refs_12_ = bf16[4096,128]{1,0:T(8,128)(2,1)} fusion(bf16[2048,128]{1,0:T(8,128)(2,1)S(1)} %get-tuple-element.8, bf16[2048,128]{1,0:T(8,128)(2,1)S(1)} %get-tuple-element.7), kind=kLoop, calls=%fused_computation.21 | loop fusion | flops 2097152 | bytes 2097152 | tf_op jit(solution)/shard_map/concatenate | solution.py:178
  30.4 0.8 %collective-permute-start.4 = (bf16[6,4,4096]{2,1,0:T(4,128)(2,1)S(1)}, bf16[6,4,4096]{2,1,0:T(4,128)(2,1)S(1)}, u32[]{:S(2)}, u32[]{:S(2)}) collective-permute-start(bf16[6,4,4096]{2,1,0:T(4,128)(2,1)S(1)} %maximum_bitcast_fusion.refs_0_.refs_4_), channel_id=1, source_target_pairs={{0,8},{4,12},{8,0},{12,4},{16,24},{20,28},{24,16},{28,20},{1,9},{5... | collective-permute-start | bytes 589832 | tf_op jit(solution)/shard_map/ppermute | solution.py:161
  31.7 3.3 %collective-permute-done.7.refs_9_ = bf16[6,4,4096]{2,1,0:T(4,128)(2,1)S(1)} collective-permute-done((bf16[6,4,4096]{2,1,0:T(4,128)(2,1)S(1)}, bf16[6,4,4096]{2,1,0:T(4,128)(2,1)S(1)}, u32[]{:S(2)}, u32[]{:S(2)}) %collective-permute-start.7) | collective-permute-done | bytes 196640 | tf_op jit(solution)/shard_map/ppermute | solution.py:161
  35.0 4.3 %collective-permute-start.2 = (bf16[6,4,4096]{2,1,0:T(4,128)(2,1)S(1)}, bf16[6,4,4096]{2,1,0:T(4,128)(2,1)S(1)}, u32[]{:S(2)}, u32[]{:S(2)}) collective-permute-start(bf16[6,4,4096]{2,1,0:T(4,128)(2,1)S(1)} %maximum_bitcast_fusion.refs_0_.refs_4_), channel_id=1, source_target_pairs={{0,3},{1,2},{2,1},{3,0},{4,7},{5,6},{6,5},{7,4},{8,11},{9,10},{10,... | collective-permute-start | bytes 589832 | tf_op jit(solution)/shard_map/ppermute | solution.py:161
  39.3 3.2 %collective-permute-start.1 = (bf16[6,4,4096]{2,1,0:T(4,128)(2,1)S(1)}, bf16[6,4,4096]{2,1,0:T(4,128)(2,1)S(1)}, u32[]{:S(2)}, u32[]{:S(2)}) collective-permute-start(bf16[6,4,4096]{2,1,0:T(4,128)(2,1)S(1)} %maximum_bitcast_fusion.refs_0_.refs_4_), channel_id=1, source_target_pairs={{0,2},{1,3},{2,0},{3,1},{4,6},{5,7},{6,4},{7,5},{8,10},{9,11},{10,... | collective-permute-start | bytes 589832 | tf_op jit(solution)/shard_map/ppermute | solution.py:161
  42.6 1.6 %collective-permute-start = (bf16[6,4,4096]{2,1,0:T(4,128)(2,1)S(1)}, bf16[6,4,4096]{2,1,0:T(4,128)(2,1)S(1)}, u32[]{:S(2)}, u32[]{:S(2)}) collective-permute-start(bf16[6,4,4096]{2,1,0:T(4,128)(2,1)S(1)} %maximum_bitcast_fusion.refs_0_.refs_4_), channel_id=1, source_target_pairs={{0,1},{1,0},{2,3},{3,2},{4,5},{5,4},{6,7},{7,6},{8,9},{9,8},{10,11... | collective-permute-start | bytes 589832 | tf_op jit(solution)/shard_map/ppermute | solution.py:161
  44.7 11.7 %collective-permute-done.1.refs_2_ = bf16[6,4,4096]{2,1,0:T(4,128)(2,1)S(1)} collective-permute-done((bf16[6,4,4096]{2,1,0:T(4,128)(2,1)S(1)}, bf16[6,4,4096]{2,1,0:T(4,128)(2,1)S(1)}, u32[]{:S(2)}, u32[]{:S(2)}) %collective-permute-start.1) | collective-permute-done | bytes 196640 | tf_op jit(solution)/shard_map/ppermute | solution.py:161
  57.1 0.7 copy-done.11
  57.7 13.2 %shard_map.37 = f32[512,128]{1,0:T(8,128)} custom-call(bf16[6,4,4096]{2,1,0:T(4,128)(2,1)} %copy-done.1, bf16[6,4,4096]{2,1,0:T(4,128)(2,1)} %copy-done.11, bf16[6,4,4096]{2,1,0:T(4,128)(2,1)} %copy-done.10, bf16[6,4,4096]{2,1,0:T(4,128)(2,1)} %copy-done.9, bf16[6,4,4096]{2,1,0:T(4,128)(2,1)} %copy-done.1, bf16[6,4,4096]{2,1,0:T(4,128)(2,1)} %copy-done.8, ...), custom_call_target="tpu_custom_call" | custom-call | flops 587202560 | bytes 3670016 | tf_op jit(solution)/shard_map/pallas_call | solution.py:135
  70.9 1.5 %gather_fusion = f32[8,16,4,128]{3,1,2,0:T(8,128)S(1)} fusion(f32[16,8,4,128]{3,0,2,1:T(8,128)} %bitcast.79, s32[1024]{0:T(1024)S(1)} %pad_clamp_fusion.1), kind=kCustom, calls=%fused_computation | custom fusion | bytes 524320 | tf_op jit(solution)/shard_map/jit(_take)/gather | solution.py:186
  73.1 0.8 %multiply_select_fusion = f32[16,1,32,128]{3,2,1,0:T(8,128)} fusion(f32[16,1,32,128]{3,2,1,0:T(8,128)S(1)} %bitcast.80, pred[16]{0:T(512)(128)(4,1)S(1)} %broadcast_in_dim.63, pred[16,128]{1,0:T(8,128)(4,1)S(1)} %broadcast_compare_fusion), kind=kLoop, calls=%fused_computation.41 | loop fusion | flops 196608 | bytes 526352 | tf_op jit(solution)/shard_map/jit(_where)/select_n | solution.py:194
  (65 shorter events, 5.5 us)
Async XLA Ops:
  0.0 2.7 %copy-start = (f32[32]{0:T(128)S(1)}, f32[32]{0:T(128)}, u32[]{:S(2)}) copy-start(f32[32]{0:T(128)} %param.4) | copy-start | bytes 388
  17.7 24.9 %copy-start.1 = (bf16[6,4,4096]{2,1,0:T(4,128)(2,1)}, bf16[6,4,4096]{2,1,0:T(4,128)(2,1)S(1)}, u32[]{:S(2)}) copy-start(bf16[6,4,4096]{2,1,0:T(4,128)(2,1)S(1)} %maximum_bitcast_fusion.refs_0_.refs_4_) | copy-start | bytes 589828
  17.7 12.7 %collective-permute-start.9 = (bf16[6,4,4096]{2,1,0:T(4,128)(2,1)S(1)}, bf16[6,4,4096]{2,1,0:T(4,128)(2,1)S(1)}, u32[]{:S(2)}, u32[]{:S(2)}) collective-permute-start(bf16[6,4,4096]{2,1,0:T(4,128)(2,1)S(1)} %maximum_bitcast_fusion.refs_0_.refs_4_), channel_id=1, source_target_pairs={{0,28},{4,24},{8,20},{12,16},{16,12},{20,8},{24,4},{28,0},{1,29},{... | collective-permute-start | bytes 589832 | tf_op jit(solution)/shard_map/ppermute | solution.py:161
  21.1 10.5 %collective-permute-start.8 = (bf16[6,4,4096]{2,1,0:T(4,128)(2,1)S(1)}, bf16[6,4,4096]{2,1,0:T(4,128)(2,1)S(1)}, u32[]{:S(2)}, u32[]{:S(2)}) collective-permute-start(bf16[6,4,4096]{2,1,0:T(4,128)(2,1)S(1)} %maximum_bitcast_fusion.refs_0_.refs_4_), channel_id=1, source_target_pairs={{0,24},{4,28},{8,16},{12,20},{16,8},{20,12},{24,0},{28,4},{1,25},{... | collective-permute-start | bytes 589832 | tf_op jit(solution)/shard_map/ppermute | solution.py:161
  21.8 13.2 %collective-permute-start.7 = (bf16[6,4,4096]{2,1,0:T(4,128)(2,1)S(1)}, bf16[6,4,4096]{2,1,0:T(4,128)(2,1)S(1)}, u32[]{:S(2)}, u32[]{:S(2)}) collective-permute-start(bf16[6,4,4096]{2,1,0:T(4,128)(2,1)S(1)} %maximum_bitcast_fusion.refs_0_.refs_4_), channel_id=1, source_target_pairs={{0,20},{4,16},{8,28},{12,24},{16,4},{20,0},{24,12},{28,8},{1,21},{... | collective-permute-start | bytes 589832 | tf_op jit(solution)/shard_map/ppermute | solution.py:161
  23.1 16.2 %collective-permute-start.6 = (bf16[6,4,4096]{2,1,0:T(4,128)(2,1)S(1)}, bf16[6,4,4096]{2,1,0:T(4,128)(2,1)S(1)}, u32[]{:S(2)}, u32[]{:S(2)}) collective-permute-start(bf16[6,4,4096]{2,1,0:T(4,128)(2,1)S(1)} %maximum_bitcast_fusion.refs_0_.refs_4_), channel_id=1, source_target_pairs={{0,16},{4,20},{8,24},{12,28},{16,0},{20,4},{24,8},{28,12},{1,17},{... | collective-permute-start | bytes 589832 | tf_op jit(solution)/shard_map/ppermute | solution.py:161
  23.4 19.1 %collective-permute-start.5 = (bf16[6,4,4096]{2,1,0:T(4,128)(2,1)S(1)}, bf16[6,4,4096]{2,1,0:T(4,128)(2,1)S(1)}, u32[]{:S(2)}, u32[]{:S(2)}) collective-permute-start(bf16[6,4,4096]{2,1,0:T(4,128)(2,1)S(1)} %maximum_bitcast_fusion.refs_0_.refs_4_), channel_id=1, source_target_pairs={{0,12},{4,8},{8,4},{12,0},{16,28},{20,24},{24,20},{28,16},{1,13},{... | collective-permute-start | bytes 589832 | tf_op jit(solution)/shard_map/ppermute | solution.py:161
  29.3 14.9 %copy-start.12 = (s32[16]{0:T(128)S(1)}, s32[16]{0:T(128)}, u32[]{:S(2)}) copy-start(s32[16]{0:T(128)} %param.5) | copy-start | bytes 196
  30.4 26.0 %copy-start.2 = (bf16[6,4,4096]{2,1,0:T(4,128)(2,1)}, bf16[6,4,4096]{2,1,0:T(4,128)(2,1)S(1)}, u32[]{:S(2)}) copy-start(bf16[6,4,4096]{2,1,0:T(4,128)(2,1)S(1)} %collective-permute-done.9.refs_11_) | copy-start | bytes 589828
  30.4 13.9 %collective-permute-start.4 = (bf16[6,4,4096]{2,1,0:T(4,128)(2,1)S(1)}, bf16[6,4,4096]{2,1,0:T(4,128)(2,1)S(1)}, u32[]{:S(2)}, u32[]{:S(2)}) collective-permute-start(bf16[6,4,4096]{2,1,0:T(4,128)(2,1)S(1)} %maximum_bitcast_fusion.refs_0_.refs_4_), channel_id=1, source_target_pairs={{0,8},{4,12},{8,0},{12,4},{16,24},{20,28},{24,16},{28,20},{1,9},{5... | collective-permute-start | bytes 589832 | tf_op jit(solution)/shard_map/ppermute | solution.py:161
  31.7 24.7 %copy-start.3 = (bf16[6,4,4096]{2,1,0:T(4,128)(2,1)}, bf16[6,4,4096]{2,1,0:T(4,128)(2,1)S(1)}, u32[]{:S(2)}) copy-start(bf16[6,4,4096]{2,1,0:T(4,128)(2,1)S(1)} %collective-permute-done.8.refs_10_) | copy-start | bytes 589828
  31.7 12.6 %collective-permute-start.3 = (bf16[6,4,4096]{2,1,0:T(4,128)(2,1)S(1)}, bf16[6,4,4096]{2,1,0:T(4,128)(2,1)S(1)}, u32[]{:S(2)}, u32[]{:S(2)}) collective-permute-start(bf16[6,4,4096]{2,1,0:T(4,128)(2,1)S(1)} %maximum_bitcast_fusion.refs_0_.refs_4_), channel_id=1, source_target_pairs={{0,4},{4,0},{8,12},{12,8},{16,20},{20,16},{24,28},{28,24},{1,5},{5... | collective-permute-start | bytes 589832 | tf_op jit(solution)/shard_map/ppermute | solution.py:161
  35.0 21.4 %copy-start.4 = (bf16[6,4,4096]{2,1,0:T(4,128)(2,1)}, bf16[6,4,4096]{2,1,0:T(4,128)(2,1)S(1)}, u32[]{:S(2)}) copy-start(bf16[6,4,4096]{2,1,0:T(4,128)(2,1)S(1)} %collective-permute-done.7.refs_9_) | copy-start | bytes 589828
  35.0 9.7 %collective-permute-start.2 = (bf16[6,4,4096]{2,1,0:T(4,128)(2,1)S(1)}, bf16[6,4,4096]{2,1,0:T(4,128)(2,1)S(1)}, u32[]{:S(2)}, u32[]{:S(2)}) collective-permute-start(bf16[6,4,4096]{2,1,0:T(4,128)(2,1)S(1)} %maximum_bitcast_fusion.refs_0_.refs_4_), channel_id=1, source_target_pairs={{0,3},{1,2},{2,1},{3,0},{4,7},{5,6},{6,5},{7,4},{8,11},{9,10},{10,... | collective-permute-start | bytes 589832 | tf_op jit(solution)/shard_map/ppermute | solution.py:161
  39.3 17.1 %copy-start.5 = (bf16[6,4,4096]{2,1,0:T(4,128)(2,1)}, bf16[6,4,4096]{2,1,0:T(4,128)(2,1)S(1)}, u32[]{:S(2)}) copy-start(bf16[6,4,4096]{2,1,0:T(4,128)(2,1)S(1)} %collective-permute-done.6.refs_8_) | copy-start | bytes 589828
  39.3 17.0 %collective-permute-start.1 = (bf16[6,4,4096]{2,1,0:T(4,128)(2,1)S(1)}, bf16[6,4,4096]{2,1,0:T(4,128)(2,1)S(1)}, u32[]{:S(2)}, u32[]{:S(2)}) collective-permute-start(bf16[6,4,4096]{2,1,0:T(4,128)(2,1)S(1)} %maximum_bitcast_fusion.refs_0_.refs_4_), channel_id=1, source_target_pairs={{0,2},{1,3},{2,0},{3,1},{4,6},{5,7},{6,4},{7,5},{8,10},{9,11},{10,... | collective-permute-start | bytes 589832 | tf_op jit(solution)/shard_map/ppermute | solution.py:161
  42.6 13.8 %copy-start.6 = (bf16[6,4,4096]{2,1,0:T(4,128)(2,1)}, bf16[6,4,4096]{2,1,0:T(4,128)(2,1)S(1)}, u32[]{:S(2)}) copy-start(bf16[6,4,4096]{2,1,0:T(4,128)(2,1)S(1)} %collective-permute-done.5.refs_7_) | copy-start | bytes 589828
  42.6 13.8 %collective-permute-start = (bf16[6,4,4096]{2,1,0:T(4,128)(2,1)S(1)}, bf16[6,4,4096]{2,1,0:T(4,128)(2,1)S(1)}, u32[]{:S(2)}, u32[]{:S(2)}) collective-permute-start(bf16[6,4,4096]{2,1,0:T(4,128)(2,1)S(1)} %maximum_bitcast_fusion.refs_0_.refs_4_), channel_id=1, source_target_pairs={{0,1},{1,0},{2,3},{3,2},{4,5},{5,4},{6,7},{7,6},{8,9},{9,8},{10,11... | collective-permute-start | bytes 589832 | tf_op jit(solution)/shard_map/ppermute | solution.py:161
  44.3 12.1 %copy-start.7 = (bf16[6,4,4096]{2,1,0:T(4,128)(2,1)}, bf16[6,4,4096]{2,1,0:T(4,128)(2,1)S(1)}, u32[]{:S(2)}) copy-start(bf16[6,4,4096]{2,1,0:T(4,128)(2,1)S(1)} %collective-permute-done.4.refs_6_) | copy-start | bytes 589828
  44.3 12.1 %copy-start.8 = (bf16[6,4,4096]{2,1,0:T(4,128)(2,1)}, bf16[6,4,4096]{2,1,0:T(4,128)(2,1)S(1)}, u32[]{:S(2)}) copy-start(bf16[6,4,4096]{2,1,0:T(4,128)(2,1)S(1)} %collective-permute-done.3.refs_5_) | copy-start | bytes 589828
  44.7 11.8 %copy-start.9 = (bf16[6,4,4096]{2,1,0:T(4,128)(2,1)}, bf16[6,4,4096]{2,1,0:T(4,128)(2,1)S(1)}, u32[]{:S(2)}) copy-start(bf16[6,4,4096]{2,1,0:T(4,128)(2,1)S(1)} %collective-permute-done.2.refs_3_) | copy-start | bytes 589828
  56.4 0.7 copy-start.10
  57.0 0.7 copy-start.11

commit v4 on v3

--- a/solution.py
+++ b/solution.py
@@ -177,7 +177,10 @@
     cos_lag, sin_lag = angle_table(LAGS, bin_count, out_length, -LH)
     lag_table = jnp.concatenate([cos_lag.T, sin_lag.T], axis=0).astype(jnp.bfloat16)
     group_rows = sum(piece.shape[1] for piece in left_by_window)
-    piece_rows, visit_order = xor_gather(white_by_window, "row", row_size)
+    row_block = white_by_window
+    if len(left_by_window) > 1:
+        row_block, ignored = lax.optimization_barrier((white_by_window, left_by_window[1]))
+    piece_rows, visit_order = xor_gather(row_block, "row", row_size)
     visit_count = sum(piece.shape[1] for piece in piece_rows)
     pair = pair_block(left_by_window, piece_rows, lag_table)
     pair = jnp.swapaxes(pair.reshape(visit_count, group_rows, LAGS), 0, 1)

time: 74.1 us -> 74.1 us (level)
  starting transfers between devices: 16.8 us -> 12.6 us
  waiting for transfers between devices: 15.9 us -> 20 us
    ppermute x10, starting transfers between devices: 16.8 us -> 12.6 us  [xor_gather(): pieces.append(lax.ppermute(block, axis_name, pairs))]
    ppermute x10, waiting for transfers between devices: 15.9 us -> 20 us  [xor_gather(): pieces.append(lax.ppermute(block, axis_name, pairs))]
  transfers between devices with their start and end apart: 10 -> 10, of which waited for: 4 -> 5; matrix products, arithmetic and copies ran while one was open for 8% -> 8% of each run, Pallas kernels for 0% -> 0%
where the time goes in v4:
time: 74.1 us; the launch traced here: 73.9 us
  waiting for transfers between devices  20 us (27%)
  matrix products  13.9 us (19%)
  Pallas kernels  13.2 us (18%)
  starting transfers between devices  12.6 us (17%)
  other arithmetic  7.54 us (10%)
  local copies, waits for them, and re-layouts  6.45 us (9%)
    ppermute x10, waiting for transfers between devices, xor_gather(): pieces.append(lax.ppermute(block, axis_name, pairs))  20 us
    pallas_call x1, Pallas kernels, pair_block(): pl.pallas_call(functools.partial(cross_kernel, left_count, visit_count),...  13.2 us
    ppermute x10, starting transfers between devices, xor_gather(): pieces.append(lax.ppermute(block, axis_name, pairs))  12.6 us
    another operation x2, other arithmetic  4.53 us
    dot_general x1, matrix products, spectrum(): jnp.einsum('bwfq,gq->bwgf', real_t, sin_three, precision=lax.Precision.HI...  2.54 us
    dot_general x1, matrix products, spectrum(): jnp.einsum('bwfq,gq->bwgf', real_t, cos_three, precision=lax.Precision.HI...  2.27 us
    dot_general x1, matrix products, spectrum(): jnp.einsum('bwfq,gq->bwgf', imag_t, sin_three, precision=lax.Precision.HI...  2.27 us
    dot_general x1, matrix products, spectrum(): jnp.einsum('bwfq,gq->bwgf', imag_t, cos_three, precision=lax.Precision.HI...  2.27 us
  transfers between devices with their start and end apart: 10, of which 5 were waited for; matrix products, arithmetic and copies ran while one was open for 8% of the time, Pallas kernels for 0%

profile of v4, /device:TPU:0, one launch (start us, length us, event | category | flops | bytes accessed | tf_op | source)
XLA Modules:
  0.0 73.9 jit_solution(12061974009933028429)
XLA Ops:
  0.2 1.7 %reshape.190 = f32[4,6,32,256]{3,2,0,1:T(8,128)S(1)} reshape(f32[4,6,8192]{2,0,1:T(4,128)} %param.3) | data formatting | bytes 1572864 | tf_op jit(solution)/shard_map/reshape | solution.py:31
  2.7 1.3 %fusion = f32[1,288,128]{2,0,1:T(1,128)S(1)} fusion(pred[32,288,128]{2,1,0:T(32,128)(4,1)S(1)} %iota_compare_fusion, f32[32]{0:T(128)S(1)} %copy-done), kind=kOutput, calls=%fused_computation.3 | convolution fusion | flops 14155776 | bytes 1327232 | tf_op jit(solution)/shard_map/k,kij->ij/dot_general | solution.py:39
  4.1 1.3 %fusion.4 = f32[4,6,32,128]{3,2,1,0:T(8,128)S(1)} fusion(f32[288,128,1,1]{1,0,3,2:T(8,128)S(1)} %bitcast.82, f32[4,6,31,32]{3,2,1,0:T(8,128)S(1)} %copy.33, f32[4,6,32,256]{3,2,0,1:T(8,128)S(1)} %reshape.190), kind=kOutput, calls=%fused_computation.14 | convolution fusion | flops 340402176 | bytes 1422336 | tf_op jit(solution)/shard_map/swbi,ij->swbj/dot_general | solution.py:40
  5.6 0.9 %convolution_negate_fusion = f32[64,4,6,64]{3,0,2,1:T(8,128)S(1)} fusion(f32[4,6,64,64]{3,2,1,0:T(8,128)S(1)} %reshape_reshape.4), kind=kOutput, calls=%fused_computation.8 | convolution fusion | flops 75653120 | bytes 786432 | tf_op jit(solution)/shard_map/bwnq,fn->bwfq/dot_general | solution.py:52
  6.5 0.9 %fusion.26 = f32[64,4,6,64]{3,0,2,1:T(8,128)S(1)} fusion(f32[4,6,64,64]{3,2,1,0:T(8,128)S(1)} %reshape_reshape.4), kind=kOutput, calls=%fused_computation.53 | convolution fusion | flops 75554816 | bytes 786432 | tf_op jit(solution)/shard_map/bwnq,fn->bwfq/dot_general | solution.py:51
  7.5 2.3 %fusion.13 = f32[32,4,6,64]{3,0,2,1:T(8,128)S(1)} fusion(f32[64,4,6,64]{3,0,2,1:T(8,128)S(1)} %fusion.26, f32[64,4,6,64]{3,0,2,1:T(8,128)S(1)} %convolution_negate_fusion, f32[64,64]{1,0:T(8,128)S(1)} %get-tuple-element.13, f32[64,64]{1,0:T(8,128)S(1)} %get-tuple-element.14), kind=kOutput, calls=%fused_computation.27 | convolution fusion | flops 38072320 | bytes 1015808 | tf_op jit(solution)/shard_map/bwfq,gq->bwgf/dot_general | solution.py:60
  9.7 2.3 %fusion.17 = f32[32,4,6,64]{3,0,2,1:T(8,128)S(1)} fusion(f32[64,4,6,64]{3,0,2,1:T(8,128)S(1)} %convolution_negate_fusion, f32[64,4,6,64]{3,0,2,1:T(8,128)S(1)} %fusion.26, f32[64,64]{1,0:T(8,128)S(1)} %get-tuple-element.13, f32[64,64]{1,0:T(8,128)S(1)} %get-tuple-element.14), kind=kOutput, calls=%fused_computation.31 | convolution fusion | flops 38072320 | bytes 1015808 | tf_op jit(solution)/shard_map/bwfq,gq->bwgf/dot_general | solution.py:57
  12.0 2.3 %fusion.3 = f32[4,6,32,64]{3,2,1,0:T(8,128)S(1)} fusion(f32[32,4,6,64]{3,0,2,1:T(8,128)S(1)} %fusion.17, f32[64,4,6,64]{3,0,2,1:T(8,128)S(1)} %fusion.26, f32[64,4,6,64]{3,0,2,1:T(8,128)S(1)} %convolution_negate_fusion, f32[64,64]{1,0:T(8,128)S(1)} %get-tuple-element.13, f32[64,64]{1,0:T(8,128)S(1)} %get-tuple-element.14), kind=kOutput, calls=%fused_computation.12 | convolution fusion | flops 38121472 | bytes 1212416 | tf_op jit(solution)/shard_map/bwfq,gq->bwgf/dot_general | solution.py:59
  14.3 2.5 %add_reduce_fusion = (f32[4,6,32]{2,1,0:T(8,128)S(1)}, f32[4,6,32,64]{3,2,1,0:T(8,128)S(1)}) fusion(f32[4,6,32,64]{3,2,1,0:T(8,128)S(1)} %fusion.3, f32[32,4,6,64]{3,0,2,1:T(8,128)S(1)} %fusion.13, f32[64,4,6,64]{3,0,2,1:T(8,128)S(1)} %convolution_negate_fusion, f32[64,64]{1,0:T(8,128)S(1)} %get-tuple-element.13, f32[64,4,6,64]{3,0,2,1:T(8,128)S(1)} %fusion.26, ...), kind=kOutput, calls=%fused_computation.39 | convolution fusion | flops 38317312 | bytes 1412096 | tf_op jit(solution)/shard_map/bwfq,gq->bwgf/dot_general | solution.py:62
  17.7 5.1 %collective-permute-start.2 = (bf16[6,4,4096]{2,1,0:T(4,128)(2,1)S(1)}, bf16[6,4,4096]{2,1,0:T(4,128)(2,1)S(1)}, u32[]{:S(2)}, u32[]{:S(2)}) collective-permute-start(bf16[6,4,4096]{2,1,0:T(4,128)(2,1)S(1)} %maximum_bitcast_fusion.refs_0_.refs_4_), channel_id=1, source_target_pairs={{0,3},{1,2},{2,1},{3,0},{4,7},{5,6},{6,5},{7,4},{8,11},{9,10},{10,... | collective-permute-start | bytes 589832 | tf_op jit(solution)/shard_map/ppermute | solution.py:161
  23.8 4.4 %cosine_convert_fusion = (bf16[2048,128]{1,0:T(8,128)(2,1)S(1)}, bf16[2048,128]{1,0:T(8,128)(2,1)S(1)}) fusion(s32[128]{0:T(128)S(1)} %iota_add_fusion), kind=kLoop, calls=%fused_computation.23 | loop fusion | flops 4194304 | bytes 1049088 | tf_op jit(solution)/shard_map/convert
  28.2 1.1 %pad_maximum_fusion.refs_12_ = bf16[4096,128]{1,0:T(8,128)(2,1)} fusion(bf16[2048,128]{1,0:T(8,128)(2,1)S(1)} %get-tuple-element.10, bf16[2048,128]{1,0:T(8,128)(2,1)S(1)} %get-tuple-element.9), kind=kLoop, calls=%fused_computation.21 | loop fusion | flops 2097152 | bytes 2097152 | tf_op jit(solution)/shard_map/concatenate | solution.py:178
  29.3 6.2 %collective-permute-done.refs_1_ = bf16[6,4,4096]{2,1,0:T(4,128)(2,1)S(1)} collective-permute-done((bf16[6,4,4096]{2,1,0:T(4,128)(2,1)S(1)}, bf16[6,4,4096]{2,1,0:T(4,128)(2,1)S(1)}, u32[]{:S(2)}, u32[]{:S(2)}) %collective-permute-start) | collective-permute-done | bytes 196640 | tf_op jit(solution)/shard_map/ppermute | solution.py:161
  35.5 1.1 %collective-permute-start.9 = (bf16[6,4,4096]{2,1,0:T(4,128)(2,1)S(1)}, bf16[6,4,4096]{2,1,0:T(4,128)(2,1)S(1)}, u32[]{:S(2)}, u32[]{:S(2)}) collective-permute-start(bf16[6,4,4096]{2,1,0:T(4,128)(2,1)S(1)} %maximum_bitcast_fusion.refs_0_.refs_4_), channel_id=1, source_target_pairs={{0,28},{4,24},{8,20},{12,16},{16,12},{20,8},{24,4},{28,0},{1,29},{... | collective-permute-start | bytes 589832 | tf_op jit(solution)/shard_map/ppermute | solution.py:161
  36.6 1.4 %collective-permute-start.8 = (bf16[6,4,4096]{2,1,0:T(4,128)(2,1)S(1)}, bf16[6,4,4096]{2,1,0:T(4,128)(2,1)S(1)}, u32[]{:S(2)}, u32[]{:S(2)}) collective-permute-start(bf16[6,4,4096]{2,1,0:T(4,128)(2,1)S(1)} %maximum_bitcast_fusion.refs_0_.refs_4_), channel_id=1, source_target_pairs={{0,24},{4,28},{8,16},{12,20},{16,8},{20,12},{24,0},{28,4},{1,25},{... | collective-permute-start | bytes 589832 | tf_op jit(solution)/shard_map/ppermute | solution.py:161
  38.0 1.5 %collective-permute-start.7 = (bf16[6,4,4096]{2,1,0:T(4,128)(2,1)S(1)}, bf16[6,4,4096]{2,1,0:T(4,128)(2,1)S(1)}, u32[]{:S(2)}, u32[]{:S(2)}) collective-permute-start(bf16[6,4,4096]{2,1,0:T(4,128)(2,1)S(1)} %maximum_bitcast_fusion.refs_0_.refs_4_), channel_id=1, source_target_pairs={{0,20},{4,16},{8,28},{12,24},{16,4},{20,0},{24,12},{28,8},{1,21},{... | collective-permute-start | bytes 589832 | tf_op jit(solution)/shard_map/ppermute | solution.py:161
  40.8 2.8 %collective-permute-done.9.refs_11_ = bf16[6,4,4096]{2,1,0:T(4,128)(2,1)S(1)} collective-permute-done((bf16[6,4,4096]{2,1,0:T(4,128)(2,1)S(1)}, bf16[6,4,4096]{2,1,0:T(4,128)(2,1)S(1)}, u32[]{:S(2)}, u32[]{:S(2)}) %collective-permute-start.9) | collective-permute-done | bytes 196640 | tf_op jit(solution)/shard_map/ppermute | solution.py:161
  43.6 1.6 %collective-permute-start.4 = (bf16[6,4,4096]{2,1,0:T(4,128)(2,1)S(1)}, bf16[6,4,4096]{2,1,0:T(4,128)(2,1)S(1)}, u32[]{:S(2)}, u32[]{:S(2)}) collective-permute-start(bf16[6,4,4096]{2,1,0:T(4,128)(2,1)S(1)} %maximum_bitcast_fusion.refs_0_.refs_4_), channel_id=1, source_target_pairs={{0,8},{4,12},{8,0},{12,4},{16,24},{20,28},{24,16},{28,20},{1,9},{5... | collective-permute-start | bytes 589832 | tf_op jit(solution)/shard_map/ppermute | solution.py:161
  45.2 2.8 %collective-permute-done.8.refs_10_ = bf16[6,4,4096]{2,1,0:T(4,128)(2,1)S(1)} collective-permute-done((bf16[6,4,4096]{2,1,0:T(4,128)(2,1)S(1)}, bf16[6,4,4096]{2,1,0:T(4,128)(2,1)S(1)}, u32[]{:S(2)}, u32[]{:S(2)}) %collective-permute-start.8) | collective-permute-done | bytes 196640 | tf_op jit(solution)/shard_map/ppermute | solution.py:161
  48.1 3.9 %collective-permute-done.7.refs_9_ = bf16[6,4,4096]{2,1,0:T(4,128)(2,1)S(1)} collective-permute-done((bf16[6,4,4096]{2,1,0:T(4,128)(2,1)S(1)}, bf16[6,4,4096]{2,1,0:T(4,128)(2,1)S(1)}, u32[]{:S(2)}, u32[]{:S(2)}) %collective-permute-start.7) | collective-permute-done | bytes 196640 | tf_op jit(solution)/shard_map/ppermute | solution.py:161
  52.0 4.3 %collective-permute-done.6.refs_8_ = bf16[6,4,4096]{2,1,0:T(4,128)(2,1)S(1)} collective-permute-done((bf16[6,4,4096]{2,1,0:T(4,128)(2,1)S(1)}, bf16[6,4,4096]{2,1,0:T(4,128)(2,1)S(1)}, u32[]{:S(2)}, u32[]{:S(2)}) %collective-permute-start.6) | collective-permute-done | bytes 196640 | tf_op jit(solution)/shard_map/ppermute | solution.py:161
  57.8 13.2 %shard_map.37 = f32[512,128]{1,0:T(8,128)} custom-call(bf16[6,4,4096]{2,1,0:T(4,128)(2,1)} %copy-done.1, bf16[6,4,4096]{2,1,0:T(4,128)(2,1)} %copy-done.4, bf16[6,4,4096]{2,1,0:T(4,128)(2,1)} %copy-done.3, bf16[6,4,4096]{2,1,0:T(4,128)(2,1)} %copy-done.2, bf16[6,4,4096]{2,1,0:T(4,128)(2,1)} %copy-done.1, bf16[6,4,4096]{2,1,0:T(4,128)(2,1)} %copy-done.11, ...), custom_call_target="tpu_custom_call" | custom-call | flops 587202560 | bytes 3670016 | tf_op jit(solution)/shard_map/pallas_call | solution.py:135
  70.9 1.5 %gather_fusion = f32[8,16,4,128]{3,1,2,0:T(8,128)S(1)} fusion(f32[16,8,4,128]{3,0,2,1:T(8,128)} %bitcast.79, s32[1024]{0:T(1024)S(1)} %pad_clamp_fusion.1), kind=kCustom, calls=%fused_computation | custom fusion | bytes 524320 | tf_op jit(solution)/shard_map/jit(_take)/gather | solution.py:189
  73.1 0.8 %multiply_select_fusion = f32[16,1,32,128]{3,2,1,0:T(8,128)} fusion(f32[16,1,32,128]{3,2,1,0:T(8,128)S(1)} %bitcast.80, pred[16]{0:T(512)(128)(4,1)S(1)} %broadcast_in_dim.63, pred[16,128]{1,0:T(8,128)(4,1)S(1)} %broadcast_compare_fusion), kind=kLoop, calls=%fused_computation.41 | loop fusion | flops 196608 | bytes 526352 | tf_op jit(solution)/shard_map/jit(_where)/select_n | solution.py:197
  (65 shorter events, 6.5 us)
Async XLA Ops:
  0.0 2.7 %copy-start = (f32[32]{0:T(128)S(1)}, f32[32]{0:T(128)}, u32[]{:S(2)}) copy-start(f32[32]{0:T(128)} %param.4) | copy-start | bytes 388
  17.7 30.3 %copy-start.1 = (bf16[6,4,4096]{2,1,0:T(4,128)(2,1)}, bf16[6,4,4096]{2,1,0:T(4,128)(2,1)S(1)}, u32[]{:S(2)}) copy-start(bf16[6,4,4096]{2,1,0:T(4,128)(2,1)S(1)} %maximum_bitcast_fusion.refs_0_.refs_4_) | copy-start | bytes 589828
  17.7 21.8 %collective-permute-start.2 = (bf16[6,4,4096]{2,1,0:T(4,128)(2,1)S(1)}, bf16[6,4,4096]{2,1,0:T(4,128)(2,1)S(1)}, u32[]{:S(2)}, u32[]{:S(2)}) collective-permute-start(bf16[6,4,4096]{2,1,0:T(4,128)(2,1)S(1)} %maximum_bitcast_fusion.refs_0_.refs_4_), channel_id=1, source_target_pairs={{0,3},{1,2},{2,1},{3,0},{4,7},{5,6},{6,5},{7,4},{8,11},{9,10},{10,... | collective-permute-start | bytes 589832 | tf_op jit(solution)/shard_map/ppermute | solution.py:161
  22.8 17.2 %collective-permute-start.1 = (bf16[6,4,4096]{2,1,0:T(4,128)(2,1)S(1)}, bf16[6,4,4096]{2,1,0:T(4,128)(2,1)S(1)}, u32[]{:S(2)}, u32[]{:S(2)}) collective-permute-start(bf16[6,4,4096]{2,1,0:T(4,128)(2,1)S(1)} %maximum_bitcast_fusion.refs_0_.refs_4_), channel_id=1, source_target_pairs={{0,2},{1,3},{2,0},{3,1},{4,6},{5,7},{6,4},{7,5},{8,10},{9,11},{10,... | collective-permute-start | bytes 589832 | tf_op jit(solution)/shard_map/ppermute | solution.py:161
  22.8 12.7 %collective-permute-start = (bf16[6,4,4096]{2,1,0:T(4,128)(2,1)S(1)}, bf16[6,4,4096]{2,1,0:T(4,128)(2,1)S(1)}, u32[]{:S(2)}, u32[]{:S(2)}) collective-permute-start(bf16[6,4,4096]{2,1,0:T(4,128)(2,1)S(1)} %maximum_bitcast_fusion.refs_0_.refs_4_), channel_id=1, source_target_pairs={{0,1},{1,0},{2,3},{3,2},{4,5},{5,4},{6,7},{7,6},{8,9},{9,8},{10,11... | collective-permute-start | bytes 589832 | tf_op jit(solution)/shard_map/ppermute | solution.py:161
  28.2 19.8 %copy-start.12 = (s32[16]{0:T(128)S(1)}, s32[16]{0:T(128)}, u32[]{:S(2)}) copy-start(s32[16]{0:T(128)} %param.5) | copy-start | bytes 196
  35.5 20.8 %copy-start.4 = (bf16[6,4,4096]{2,1,0:T(4,128)(2,1)}, bf16[6,4,4096]{2,1,0:T(4,128)(2,1)S(1)}, u32[]{:S(2)}) copy-start(bf16[6,4,4096]{2,1,0:T(4,128)(2,1)S(1)} %collective-permute-done.refs_1_) | copy-start | bytes 589828
  35.5 8.1 %collective-permute-start.9 = (bf16[6,4,4096]{2,1,0:T(4,128)(2,1)S(1)}, bf16[6,4,4096]{2,1,0:T(4,128)(2,1)S(1)}, u32[]{:S(2)}, u32[]{:S(2)}) collective-permute-start(bf16[6,4,4096]{2,1,0:T(4,128)(2,1)S(1)} %maximum_bitcast_fusion.refs_0_.refs_4_), channel_id=1, source_target_pairs={{0,28},{4,24},{8,20},{12,16},{16,12},{20,8},{24,4},{28,0},{1,29},{... | collective-permute-start | bytes 589832 | tf_op jit(solution)/shard_map/ppermute | solution.py:161
  36.6 11.4 %collective-permute-start.8 = (bf16[6,4,4096]{2,1,0:T(4,128)(2,1)S(1)}, bf16[6,4,4096]{2,1,0:T(4,128)(2,1)S(1)}, u32[]{:S(2)}, u32[]{:S(2)}) collective-permute-start(bf16[6,4,4096]{2,1,0:T(4,128)(2,1)S(1)} %maximum_bitcast_fusion.refs_0_.refs_4_), channel_id=1, source_target_pairs={{0,24},{4,28},{8,16},{12,20},{16,8},{20,12},{24,0},{28,4},{1,25},{... | collective-permute-start | bytes 589832 | tf_op jit(solution)/shard_map/ppermute | solution.py:161
  38.0 14.0 %collective-permute-start.7 = (bf16[6,4,4096]{2,1,0:T(4,128)(2,1)S(1)}, bf16[6,4,4096]{2,1,0:T(4,128)(2,1)S(1)}, u32[]{:S(2)}, u32[]{:S(2)}) collective-permute-start(bf16[6,4,4096]{2,1,0:T(4,128)(2,1)S(1)} %maximum_bitcast_fusion.refs_0_.refs_4_), channel_id=1, source_target_pairs={{0,20},{4,16},{8,28},{12,24},{16,4},{20,0},{24,12},{28,8},{1,21},{... | collective-permute-start | bytes 589832 | tf_op jit(solution)/shard_map/ppermute | solution.py:161
  39.5 16.8 %copy-start.2 = (bf16[6,4,4096]{2,1,0:T(4,128)(2,1)}, bf16[6,4,4096]{2,1,0:T(4,128)(2,1)S(1)}, u32[]{:S(2)}) copy-start(bf16[6,4,4096]{2,1,0:T(4,128)(2,1)S(1)} %collective-permute-done.2.refs_3_) | copy-start | bytes 589828
  39.5 16.8 %collective-permute-start.6 = (bf16[6,4,4096]{2,1,0:T(4,128)(2,1)S(1)}, bf16[6,4,4096]{2,1,0:T(4,128)(2,1)S(1)}, u32[]{:S(2)}, u32[]{:S(2)}) collective-permute-start(bf16[6,4,4096]{2,1,0:T(4,128)(2,1)S(1)} %maximum_bitcast_fusion.refs_0_.refs_4_), channel_id=1, source_target_pairs={{0,16},{4,20},{8,24},{12,28},{16,0},{20,4},{24,8},{28,12},{1,17},{... | collective-permute-start | bytes 589832 | tf_op jit(solution)/shard_map/ppermute | solution.py:161
  40.0 16.3 %copy-start.3 = (bf16[6,4,4096]{2,1,0:T(4,128)(2,1)}, bf16[6,4,4096]{2,1,0:T(4,128)(2,1)S(1)}, u32[]{:S(2)}) copy-start(bf16[6,4,4096]{2,1,0:T(4,128)(2,1)S(1)} %collective-permute-done.1.refs_2_) | copy-start | bytes 589828
  40.0 16.3 %collective-permute-start.5 = (bf16[6,4,4096]{2,1,0:T(4,128)(2,1)S(1)}, bf16[6,4,4096]{2,1,0:T(4,128)(2,1)S(1)}, u32[]{:S(2)}, u32[]{:S(2)}) collective-permute-start(bf16[6,4,4096]{2,1,0:T(4,128)(2,1)S(1)} %maximum_bitcast_fusion.refs_0_.refs_4_), channel_id=1, source_target_pairs={{0,12},{4,8},{8,4},{12,0},{16,28},{20,24},{24,20},{28,16},{1,13},{... | collective-permute-start | bytes 589832 | tf_op jit(solution)/shard_map/ppermute | solution.py:161
  43.6 12.7 %copy-start.5 = (bf16[6,4,4096]{2,1,0:T(4,128)(2,1)}, bf16[6,4,4096]{2,1,0:T(4,128)(2,1)S(1)}, u32[]{:S(2)}) copy-start(bf16[6,4,4096]{2,1,0:T(4,128)(2,1)S(1)} %collective-permute-done.9.refs_11_) | copy-start | bytes 589828
  43.6 12.6 %collective-permute-start.4 = (bf16[6,4,4096]{2,1,0:T(4,128)(2,1)S(1)}, bf16[6,4,4096]{2,1,0:T(4,128)(2,1)S(1)}, u32[]{:S(2)}, u32[]{:S(2)}) collective-permute-start(bf16[6,4,4096]{2,1,0:T(4,128)(2,1)S(1)} %maximum_bitcast_fusion.refs_0_.refs_4_), channel_id=1, source_target_pairs={{0,8},{4,12},{8,0},{12,4},{16,24},{20,28},{24,16},{28,20},{1,9},{5... | collective-permute-start | bytes 589832 | tf_op jit(solution)/shard_map/ppermute | solution.py:161
  48.0 8.4 %copy-start.6 = (bf16[6,4,4096]{2,1,0:T(4,128)(2,1)}, bf16[6,4,4096]{2,1,0:T(4,128)(2,1)S(1)}, u32[]{:S(2)}) copy-start(bf16[6,4,4096]{2,1,0:T(4,128)(2,1)S(1)} %collective-permute-done.8.refs_10_) | copy-start | bytes 589828
  48.0 8.3 %collective-permute-start.3 = (bf16[6,4,4096]{2,1,0:T(4,128)(2,1)S(1)}, bf16[6,4,4096]{2,1,0:T(4,128)(2,1)S(1)}, u32[]{:S(2)}, u32[]{:S(2)}) collective-permute-start(bf16[6,4,4096]{2,1,0:T(4,128)(2,1)S(1)} %maximum_bitcast_fusion.refs_0_.refs_4_), channel_id=1, source_target_pairs={{0,4},{4,0},{8,12},{12,8},{16,20},{20,16},{24,28},{28,24},{1,5},{5... | collective-permute-start | bytes 589832 | tf_op jit(solution)/shard_map/ppermute | solution.py:161
  52.0 4.3 %copy-start.7 = (bf16[6,4,4096]{2,1,0:T(4,128)(2,1)}, bf16[6,4,4096]{2,1,0:T(4,128)(2,1)S(1)}, u32[]{:S(2)}) copy-start(bf16[6,4,4096]{2,1,0:T(4,128)(2,1)S(1)} %collective-permute-done.7.refs_9_) | copy-start | bytes 589828
  56.2 0.7 copy-start.8
  56.3 0.8 %copy-start.9 = (bf16[6,4,4096]{2,1,0:T(4,128)(2,1)}, bf16[6,4,4096]{2,1,0:T(4,128)(2,1)S(1)}, u32[]{:S(2)}) copy-start(bf16[6,4,4096]{2,1,0:T(4,128)(2,1)S(1)} %collective-permute-done.5.refs_7_) | copy-start | bytes 589828
  56.3 0.8 %copy-start.10 = (bf16[6,4,4096]{2,1,0:T(4,128)(2,1)}, bf16[6,4,4096]{2,1,0:T(4,128)(2,1)S(1)}, u32[]{:S(2)}) copy-start(bf16[6,4,4096]{2,1,0:T(4,128)(2,1)S(1)} %collective-permute-done.4.refs_6_) | copy-start | bytes 589828
  57.1 0.7 copy-start.11

commit v5 on v3

--- a/solution.py
+++ b/solution.py
@@ -83,7 +83,9 @@
     window_count, piece, width = left_refs[0].shape
     rows_left = left_f32.shape[1]
     bin_count = width // 2
-    chunk = max(128, min(512, 8192 // rows_left))
+    chunk = 512
+    while chunk > 128 and chunk * rows_left > 8192:
+        chunk //= 2
     chunks = bin_count // chunk
     group_rows = cross_ref.shape[0]
     group = group_rows // (piece * rows_left)
@@ -179,7 +181,12 @@
     group_rows = sum(piece.shape[1] for piece in left_by_window)
     piece_rows, visit_order = xor_gather(white_by_window, "row", row_size)
     visit_count = sum(piece.shape[1] for piece in piece_rows)
-    pair = pair_block(left_by_window, piece_rows, lag_table)
+    split = min(2, len(left_by_window))
+    parts = [pair_block(left_by_window[:split], piece_rows, lag_table)]
+    if len(left_by_window) > split:
+        parts.append(pair_block(left_by_window[split:], piece_rows, lag_table))
+    parts = [part.reshape(visit_count, -1, LAGS) for part in parts]
+    pair = jnp.concatenate(parts, axis=1) if len(parts) > 1 else parts[0]
     pair = jnp.swapaxes(pair.reshape(visit_count, group_rows, LAGS), 0, 1)
     if visit_order is not None:
         pair = pair.reshape(group_rows, row_size, block_size, LAGS)

time: 74.1 us -> 73.9 us (level)
  the two profiles are of different devices: /device:TPU:0 before, /device:TPU:24 now
where the time goes in v5:
time: 73.9 us; the launch traced here: 73.7 us
  Pallas kernels  18.5 us (25%)
  waiting for transfers between devices  17.9 us (24%)
  matrix products  13.9 us (19%)
  starting transfers between devices  8.52 us (12%)
  other arithmetic  8.49 us (11%)
  local copies, waits for them, and re-layouts  6.1 us (8%)
    pallas_call x2, Pallas kernels, pair_block(): pl.pallas_call(functools.partial(cross_kernel, left_count, visit_count),...  18.5 us
    ppermute x10, waiting for transfers between devices, xor_gather(): pieces.append(lax.ppermute(block, axis_name, pairs))  17.9 us
    ppermute x10, starting transfers between devices, xor_gather(): pieces.append(lax.ppermute(block, axis_name, pairs))  8.52 us
    another operation x2, other arithmetic  4.54 us
    dot_general x1, matrix products, spectrum(): jnp.einsum('bwfq,gq->bwgf', real_t, sin_three, precision=lax.Precision.HI...  2.54 us
    dot_general x1, matrix products, spectrum(): jnp.einsum('bwfq,gq->bwgf', real_t, cos_three, precision=lax.Precision.HI...  2.27 us
    dot_general x1, matrix products, spectrum(): jnp.einsum('bwfq,gq->bwgf', imag_t, sin_three, precision=lax.Precision.HI...  2.27 us
    dot_general x1, matrix products, spectrum(): jnp.einsum('bwfq,gq->bwgf', imag_t, cos_three, precision=lax.Precision.HI...  2.27 us
  transfers between devices with their start and end apart: 10, of which 5 were waited for; matrix products, arithmetic and copies ran while one was open for 8% of the time, Pallas kernels for 13%

profile of v5, /device:TPU:24, one launch (start us, length us, event | category | flops | bytes accessed | tf_op | source)
XLA Modules:
  0.0 73.7 jit_solution(13973414016719427778)
XLA Ops:
  0.2 1.7 %reshape.193 = f32[4,6,32,256]{3,2,0,1:T(8,128)S(1)} reshape(f32[4,6,8192]{2,0,1:T(4,128)} %param.3) | data formatting | bytes 1572864 | tf_op jit(solution)/shard_map/reshape | solution.py:31
  2.7 1.3 %fusion = f32[1,288,128]{2,0,1:T(1,128)S(1)} fusion(pred[32,288,128]{2,1,0:T(32,128)(4,1)S(1)} %iota_compare_fusion, f32[32]{0:T(128)S(1)} %copy-done), kind=kOutput, calls=%fused_computation.3 | convolution fusion | flops 14155776 | bytes 1327232 | tf_op jit(solution)/shard_map/k,kij->ij/dot_general | solution.py:39
  4.1 1.3 %fusion.4 = f32[4,6,32,128]{3,2,1,0:T(8,128)S(1)} fusion(f32[288,128,1,1]{1,0,3,2:T(8,128)S(1)} %bitcast.84, f32[4,6,31,32]{3,2,1,0:T(8,128)S(1)} %copy.33, f32[4,6,32,256]{3,2,0,1:T(8,128)S(1)} %reshape.193), kind=kOutput, calls=%fused_computation.14 | convolution fusion | flops 340402176 | bytes 1422336 | tf_op jit(solution)/shard_map/swbi,ij->swbj/dot_general | solution.py:40
  5.6 0.9 %convolution_negate_fusion = f32[64,4,6,64]{3,0,2,1:T(8,128)S(1)} fusion(f32[4,6,64,64]{3,2,1,0:T(8,128)S(1)} %reshape_reshape.4), kind=kOutput, calls=%fused_computation.8 | convolution fusion | flops 75653120 | bytes 786432 | tf_op jit(solution)/shard_map/bwnq,fn->bwfq/dot_general | solution.py:52
  6.5 0.9 %fusion.26 = f32[64,4,6,64]{3,0,2,1:T(8,128)S(1)} fusion(f32[4,6,64,64]{3,2,1,0:T(8,128)S(1)} %reshape_reshape.4), kind=kOutput, calls=%fused_computation.54 | convolution fusion | flops 75554816 | bytes 786432 | tf_op jit(solution)/shard_map/bwnq,fn->bwfq/dot_general | solution.py:51
  7.5 2.3 %fusion.13 = f32[32,4,6,64]{3,0,2,1:T(8,128)S(1)} fusion(f32[64,4,6,64]{3,0,2,1:T(8,128)S(1)} %fusion.26, f32[64,4,6,64]{3,0,2,1:T(8,128)S(1)} %convolution_negate_fusion, f32[64,64]{1,0:T(8,128)S(1)} %get-tuple-element.11, f32[64,64]{1,0:T(8,128)S(1)} %get-tuple-element.12), kind=kOutput, calls=%fused_computation.27 | convolution fusion | flops 38072320 | bytes 1015808 | tf_op jit(solution)/shard_map/bwfq,gq->bwgf/dot_general | solution.py:60
  9.7 2.3 %fusion.17 = f32[32,4,6,64]{3,0,2,1:T(8,128)S(1)} fusion(f32[64,4,6,64]{3,0,2,1:T(8,128)S(1)} %convolution_negate_fusion, f32[64,4,6,64]{3,0,2,1:T(8,128)S(1)} %fusion.26, f32[64,64]{1,0:T(8,128)S(1)} %get-tuple-element.11, f32[64,64]{1,0:T(8,128)S(1)} %get-tuple-element.12), kind=kOutput, calls=%fused_computation.31 | convolution fusion | flops 38072320 | bytes 1015808 | tf_op jit(solution)/shard_map/bwfq,gq->bwgf/dot_general | solution.py:57
  12.0 2.3 %fusion.3 = f32[4,6,32,64]{3,2,1,0:T(8,128)S(1)} fusion(f32[32,4,6,64]{3,0,2,1:T(8,128)S(1)} %fusion.17, f32[64,4,6,64]{3,0,2,1:T(8,128)S(1)} %fusion.26, f32[64,4,6,64]{3,0,2,1:T(8,128)S(1)} %convolution_negate_fusion, f32[64,64]{1,0:T(8,128)S(1)} %get-tuple-element.11, f32[64,64]{1,0:T(8,128)S(1)} %get-tuple-element.12), kind=kOutput, calls=%fused_computation.12 | convolution fusion | flops 38121472 | bytes 1212416 | tf_op jit(solution)/shard_map/bwfq,gq->bwgf/dot_general | solution.py:59
  14.3 2.5 %add_reduce_fusion = (f32[4,6,32]{2,1,0:T(8,128)S(1)}, f32[4,6,32,64]{3,2,1,0:T(8,128)S(1)}) fusion(f32[4,6,32,64]{3,2,1,0:T(8,128)S(1)} %fusion.3, f32[32,4,6,64]{3,0,2,1:T(8,128)S(1)} %fusion.13, f32[64,4,6,64]{3,0,2,1:T(8,128)S(1)} %convolution_negate_fusion, f32[64,64]{1,0:T(8,128)S(1)} %get-tuple-element.11, f32[64,4,6,64]{3,0,2,1:T(8,128)S(1)} %fusion.26, ...), kind=kOutput, calls=%fused_computation.39 | convolution fusion | flops 38317312 | bytes 1412096 | tf_op jit(solution)/shard_map/bwfq,gq->bwgf/dot_general | solution.py:62
  17.7 1.9 %collective-permute-start.7 = (bf16[6,4,4096]{2,1,0:T(4,128)(2,1)S(1)}, bf16[6,4,4096]{2,1,0:T(4,128)(2,1)S(1)}, u32[]{:S(2)}, u32[]{:S(2)}) collective-permute-start(bf16[6,4,4096]{2,1,0:T(4,128)(2,1)S(1)} %maximum_bitcast_fusion.refs_0_.refs_2_), channel_id=1, source_target_pairs={{0,28},{4,24},{8,20},{12,16},{16,12},{20,8},{24,4},{28,0},{1,29},{... | collective-permute-start | bytes 589832 | tf_op jit(solution)/shard_map/ppermute | solution.py:163
  20.3 1.4 %collective-permute-start.5 = (bf16[6,4,4096]{2,1,0:T(4,128)(2,1)S(1)}, bf16[6,4,4096]{2,1,0:T(4,128)(2,1)S(1)}, u32[]{:S(2)}, u32[]{:S(2)}) collective-permute-start(bf16[6,4,4096]{2,1,0:T(4,128)(2,1)S(1)} %maximum_bitcast_fusion.refs_0_.refs_2_), channel_id=1, source_target_pairs={{0,20},{4,16},{8,28},{12,24},{16,4},{20,0},{24,12},{28,8},{1,21},{... | collective-permute-start | bytes 589832 | tf_op jit(solution)/shard_map/ppermute | solution.py:163
  22.2 1.0 %collective-permute-start.3 = (bf16[6,4,4096]{2,1,0:T(4,128)(2,1)S(1)}, bf16[6,4,4096]{2,1,0:T(4,128)(2,1)S(1)}, u32[]{:S(2)}, u32[]{:S(2)}) collective-permute-start(bf16[6,4,4096]{2,1,0:T(4,128)(2,1)S(1)} %maximum_bitcast_fusion.refs_0_.refs_2_), channel_id=1, source_target_pairs={{0,12},{4,8},{8,4},{12,0},{16,28},{20,24},{24,20},{28,16},{1,13},{... | collective-permute-start | bytes 589832 | tf_op jit(solution)/shard_map/ppermute | solution.py:163
  23.5 4.4 %cosine_convert_fusion = (bf16[2048,128]{1,0:T(8,128)(2,1)S(1)}, bf16[2048,128]{1,0:T(8,128)(2,1)S(1)}) fusion(s32[128]{0:T(128)S(1)} %iota_add_fusion), kind=kLoop, calls=%fused_computation.23 | loop fusion | flops 4194304 | bytes 1049088 | tf_op jit(solution)/shard_map/convert
  27.9 1.1 %pad_maximum_fusion.refs_10_ = bf16[4096,128]{1,0:T(8,128)(2,1)} fusion(bf16[2048,128]{1,0:T(8,128)(2,1)S(1)} %get-tuple-element.8, bf16[2048,128]{1,0:T(8,128)(2,1)S(1)} %get-tuple-element.7), kind=kLoop, calls=%fused_computation.21 | loop fusion | flops 2097152 | bytes 2097152 | tf_op jit(solution)/shard_map/concatenate | solution.py:180
  29.3 1.0 %collective-permute-done.6.refs_8_ = bf16[6,4,4096]{2,1,0:T(4,128)(2,1)S(1)} collective-permute-done((bf16[6,4,4096]{2,1,0:T(4,128)(2,1)S(1)}, bf16[6,4,4096]{2,1,0:T(4,128)(2,1)S(1)}, u32[]{:S(2)}, u32[]{:S(2)}) %collective-permute-start.6) | collective-permute-done | bytes 196640 | tf_op jit(solution)/shard_map/ppermute | solution.py:163
  31.0 3.2 %collective-permute-done.5.refs_7_ = bf16[6,4,4096]{2,1,0:T(4,128)(2,1)S(1)} collective-permute-done((bf16[6,4,4096]{2,1,0:T(4,128)(2,1)S(1)}, bf16[6,4,4096]{2,1,0:T(4,128)(2,1)S(1)}, u32[]{:S(2)}, u32[]{:S(2)}) %collective-permute-start.5) | collective-permute-done | bytes 196640 | tf_op jit(solution)/shard_map/ppermute | solution.py:163
  34.3 1.5 %collective-permute-start.2 = (bf16[6,4,4096]{2,1,0:T(4,128)(2,1)S(1)}, bf16[6,4,4096]{2,1,0:T(4,128)(2,1)S(1)}, u32[]{:S(2)}, u32[]{:S(2)}) collective-permute-start(bf16[6,4,4096]{2,1,0:T(4,128)(2,1)S(1)} %maximum_bitcast_fusion.refs_0_.refs_2_), channel_id=1, source_target_pairs={{0,8},{4,12},{8,0},{12,4},{16,24},{20,28},{24,16},{28,20},{1,9},{5... | collective-permute-start | bytes 589832 | tf_op jit(solution)/shard_map/ppermute | solution.py:163
  35.8 2.8 %collective-permute-done.4.refs_6_ = bf16[6,4,4096]{2,1,0:T(4,128)(2,1)S(1)} collective-permute-done((bf16[6,4,4096]{2,1,0:T(4,128)(2,1)S(1)}, bf16[6,4,4096]{2,1,0:T(4,128)(2,1)S(1)}, u32[]{:S(2)}, u32[]{:S(2)}) %collective-permute-start.4) | collective-permute-done | bytes 196640 | tf_op jit(solution)/shard_map/ppermute | solution.py:163
  39.2 2.1 %collective-permute-done.2.refs_4_ = bf16[6,4,4096]{2,1,0:T(4,128)(2,1)S(1)} collective-permute-done((bf16[6,4,4096]{2,1,0:T(4,128)(2,1)S(1)}, bf16[6,4,4096]{2,1,0:T(4,128)(2,1)S(1)}, u32[]{:S(2)}, u32[]{:S(2)}) %collective-permute-start.2) | collective-permute-done | bytes 196640 | tf_op jit(solution)/shard_map/ppermute | solution.py:163
  41.3 8.9 %collective-permute-done.refs_1_ = bf16[6,4,4096]{2,1,0:T(4,128)(2,1)S(1)} collective-permute-done((bf16[6,4,4096]{2,1,0:T(4,128)(2,1)S(1)}, bf16[6,4,4096]{2,1,0:T(4,128)(2,1)S(1)}, u32[]{:S(2)}, u32[]{:S(2)}) %collective-permute-start) | collective-permute-done | bytes 196640 | tf_op jit(solution)/shard_map/ppermute | solution.py:163
  50.9 9.2 %shard_map.37 = f32[256,128]{1,0:T(8,128)} custom-call(bf16[6,4,4096]{2,1,0:T(4,128)(2,1)} %copy-done.1, bf16[6,4,4096]{2,1,0:T(4,128)(2,1)} %copy-done.12, bf16[6,4,4096]{2,1,0:T(4,128)(2,1)} %copy-done.1, bf16[6,4,4096]{2,1,0:T(4,128)(2,1)} %copy-done.8, bf16[6,4,4096]{2,1,0:T(4,128)(2,1)} %copy-done.7, bf16[6,4,4096]{2,1,0:T(4,128)(2,1)} %copy-done.6, ...), custom_call_target="tpu_custom_call" | custom-call | flops 293601280 | bytes 3145728 | tf_op jit(solution)/shard_map/pallas_call | solution.py:137
  61.5 9.2 %shard_map.38 = f32[256,128]{1,0:T(8,128)} custom-call(bf16[6,4,4096]{2,1,0:T(4,128)(2,1)} %copy-done.11, bf16[6,4,4096]{2,1,0:T(4,128)(2,1)} %copy-done.10, bf16[6,4,4096]{2,1,0:T(4,128)(2,1)} %copy-done.1, bf16[6,4,4096]{2,1,0:T(4,128)(2,1)} %copy-done.8, bf16[6,4,4096]{2,1,0:T(4,128)(2,1)} %copy-done.7, bf16[6,4,4096]{2,1,0:T(4,128)(2,1)} %copy-done.6, ...), custom_call_target="tpu_custom_call" | custom-call | flops 293601280 | bytes 3145728 | tf_op jit(solution)/shard_map/pallas_call | solution.py:137
  70.7 0.9 %pad_maximum_fusion.1 = f32[32,16,128]{2,1,0:T(8,128)S(1)} fusion(f32[32,8,128]{2,1,0:T(8,128)} %bitcast.83, f32[32,8,128]{2,1,0:T(8,128)S(1)} %bitcast.82), kind=kLoop, calls=%fused_computation.40 | loop fusion | flops 65536 | bytes 524288 | tf_op jit(solution)/shard_map/concatenate | solution.py:189
  72.9 0.8 %multiply_select_fusion = f32[16,1,32,128]{3,2,1,0:T(8,128)} fusion(f32[16,1,32,128]{3,2,1,0:T(8,128)S(1)} %bitcast.79, pred[16]{0:T(512)(128)(4,1)S(1)} %broadcast_in_dim.63, pred[16,128]{1,0:T(8,128)(4,1)S(1)} %broadcast_compare_fusion), kind=kLoop, calls=%fused_computation.42 | loop fusion | flops 196608 | bytes 526352 | tf_op jit(solution)/shard_map/jit(_where)/select_n | solution.py:201
  (69 shorter events, 8.5 us)
Async XLA Ops:
  0.0 2.7 %copy-start = (f32[32]{0:T(128)S(1)}, f32[32]{0:T(128)}, u32[]{:S(2)}) copy-start(f32[32]{0:T(128)} %param.4) | copy-start | bytes 388
  17.7 20.9 %copy-start.1 = (bf16[6,4,4096]{2,1,0:T(4,128)(2,1)}, bf16[6,4,4096]{2,1,0:T(4,128)(2,1)S(1)}, u32[]{:S(2)}) copy-start(bf16[6,4,4096]{2,1,0:T(4,128)(2,1)S(1)} %maximum_bitcast_fusion.refs_0_.refs_2_) | copy-start | bytes 589828
  17.7 11.3 %collective-permute-start.7 = (bf16[6,4,4096]{2,1,0:T(4,128)(2,1)S(1)}, bf16[6,4,4096]{2,1,0:T(4,128)(2,1)S(1)}, u32[]{:S(2)}, u32[]{:S(2)}) collective-permute-start(bf16[6,4,4096]{2,1,0:T(4,128)(2,1)S(1)} %maximum_bitcast_fusion.refs_0_.refs_2_), channel_id=1, source_target_pairs={{0,28},{4,24},{8,20},{12,16},{16,12},{20,8},{24,4},{28,0},{1,29},{... | collective-permute-start | bytes 589832 | tf_op jit(solution)/shard_map/ppermute | solution.py:163
  19.7 10.6 %collective-permute-start.6 = (bf16[6,4,4096]{2,1,0:T(4,128)(2,1)S(1)}, bf16[6,4,4096]{2,1,0:T(4,128)(2,1)S(1)}, u32[]{:S(2)}, u32[]{:S(2)}) collective-permute-start(bf16[6,4,4096]{2,1,0:T(4,128)(2,1)S(1)} %maximum_bitcast_fusion.refs_0_.refs_2_), channel_id=1, source_target_pairs={{0,24},{4,28},{8,16},{12,20},{16,8},{20,12},{24,0},{28,4},{1,25},{... | collective-permute-start | bytes 589832 | tf_op jit(solution)/shard_map/ppermute | solution.py:163
  20.3 14.0 %collective-permute-start.5 = (bf16[6,4,4096]{2,1,0:T(4,128)(2,1)S(1)}, bf16[6,4,4096]{2,1,0:T(4,128)(2,1)S(1)}, u32[]{:S(2)}, u32[]{:S(2)}) collective-permute-start(bf16[6,4,4096]{2,1,0:T(4,128)(2,1)S(1)} %maximum_bitcast_fusion.refs_0_.refs_2_), channel_id=1, source_target_pairs={{0,20},{4,16},{8,28},{12,24},{16,4},{20,0},{24,12},{28,8},{1,21},{... | collective-permute-start | bytes 589832 | tf_op jit(solution)/shard_map/ppermute | solution.py:163
  21.7 16.9 %collective-permute-start.4 = (bf16[6,4,4096]{2,1,0:T(4,128)(2,1)S(1)}, bf16[6,4,4096]{2,1,0:T(4,128)(2,1)S(1)}, u32[]{:S(2)}, u32[]{:S(2)}) collective-permute-start(bf16[6,4,4096]{2,1,0:T(4,128)(2,1)S(1)} %maximum_bitcast_fusion.refs_0_.refs_2_), channel_id=1, source_target_pairs={{0,16},{4,20},{8,24},{12,28},{16,0},{20,4},{24,8},{28,12},{1,17},{... | collective-permute-start | bytes 589832 | tf_op jit(solution)/shard_map/ppermute | solution.py:163
  22.2 16.4 %collective-permute-start.3 = (bf16[6,4,4096]{2,1,0:T(4,128)(2,1)S(1)}, bf16[6,4,4096]{2,1,0:T(4,128)(2,1)S(1)}, u32[]{:S(2)}, u32[]{:S(2)}) collective-permute-start(bf16[6,4,4096]{2,1,0:T(4,128)(2,1)S(1)} %maximum_bitcast_fusion.refs_0_.refs_2_), channel_id=1, source_target_pairs={{0,12},{4,8},{8,4},{12,0},{16,28},{20,24},{24,20},{28,16},{1,13},{... | collective-permute-start | bytes 589832 | tf_op jit(solution)/shard_map/ppermute | solution.py:163
  27.9 11.2 %copy-start.13 = (s32[16]{0:T(128)S(1)}, s32[16]{0:T(128)}, u32[]{:S(2)}) copy-start(s32[16]{0:T(128)} %param.5) | copy-start | bytes 196
  29.0 21.1 %copy-start.2 = (bf16[6,4,4096]{2,1,0:T(4,128)(2,1)}, bf16[6,4,4096]{2,1,0:T(4,128)(2,1)S(1)}, u32[]{:S(2)}) copy-start(bf16[6,4,4096]{2,1,0:T(4,128)(2,1)S(1)} %collective-permute-done.7.refs_9_) | copy-start | bytes 589828
  29.0 31.1 %collective-permute-start.9 = (bf16[6,4,4096]{2,1,0:T(4,128)(2,1)S(1)}, bf16[6,4,4096]{2,1,0:T(4,128)(2,1)S(1)}, u32[]{:S(2)}, u32[]{:S(2)}) collective-permute-start(bf16[6,4,4096]{2,1,0:T(4,128)(2,1)S(1)} %maximum_bitcast_fusion.refs_0_.refs_2_), channel_id=1, source_target_pairs={{0,3},{1,2},{2,1},{3,0},{4,7},{5,6},{6,5},{7,4},{8,11},{9,10},{10,... | collective-permute-start | bytes 589832 | tf_op jit(solution)/shard_map/ppermute | solution.py:163
  30.2 19.9 %copy-start.3 = (bf16[6,4,4096]{2,1,0:T(4,128)(2,1)}, bf16[6,4,4096]{2,1,0:T(4,128)(2,1)S(1)}, u32[]{:S(2)}) copy-start(bf16[6,4,4096]{2,1,0:T(4,128)(2,1)S(1)} %collective-permute-done.6.refs_8_) | copy-start | bytes 589828
  30.2 29.9 %collective-permute-start.8 = (bf16[6,4,4096]{2,1,0:T(4,128)(2,1)S(1)}, bf16[6,4,4096]{2,1,0:T(4,128)(2,1)S(1)}, u32[]{:S(2)}, u32[]{:S(2)}) collective-permute-start(bf16[6,4,4096]{2,1,0:T(4,128)(2,1)S(1)} %maximum_bitcast_fusion.refs_0_.refs_2_), channel_id=1, source_target_pairs={{0,2},{1,3},{2,0},{3,1},{4,6},{5,7},{6,4},{7,5},{8,10},{9,11},{10,... | collective-permute-start | bytes 589832 | tf_op jit(solution)/shard_map/ppermute | solution.py:163
  34.3 15.9 %copy-start.4 = (bf16[6,4,4096]{2,1,0:T(4,128)(2,1)}, bf16[6,4,4096]{2,1,0:T(4,128)(2,1)S(1)}, u32[]{:S(2)}) copy-start(bf16[6,4,4096]{2,1,0:T(4,128)(2,1)S(1)} %collective-permute-done.5.refs_7_) | copy-start | bytes 589828
  34.3 7.0 %collective-permute-start.2 = (bf16[6,4,4096]{2,1,0:T(4,128)(2,1)S(1)}, bf16[6,4,4096]{2,1,0:T(4,128)(2,1)S(1)}, u32[]{:S(2)}, u32[]{:S(2)}) collective-permute-start(bf16[6,4,4096]{2,1,0:T(4,128)(2,1)S(1)} %maximum_bitcast_fusion.refs_0_.refs_2_), channel_id=1, source_target_pairs={{0,8},{4,12},{8,0},{12,4},{16,24},{20,28},{24,16},{28,20},{1,9},{5... | collective-permute-start | bytes 589832 | tf_op jit(solution)/shard_map/ppermute | solution.py:163
  38.5 11.6 %copy-start.5 = (bf16[6,4,4096]{2,1,0:T(4,128)(2,1)}, bf16[6,4,4096]{2,1,0:T(4,128)(2,1)S(1)}, u32[]{:S(2)}) copy-start(bf16[6,4,4096]{2,1,0:T(4,128)(2,1)S(1)} %collective-permute-done.4.refs_6_) | copy-start | bytes 589828
  38.5 2.7 %collective-permute-start.1 = (bf16[6,4,4096]{2,1,0:T(4,128)(2,1)S(1)}, bf16[6,4,4096]{2,1,0:T(4,128)(2,1)S(1)}, u32[]{:S(2)}, u32[]{:S(2)}) collective-permute-start(bf16[6,4,4096]{2,1,0:T(4,128)(2,1)S(1)} %maximum_bitcast_fusion.refs_0_.refs_2_), channel_id=1, source_target_pairs={{0,4},{4,0},{8,12},{12,8},{16,20},{20,16},{24,28},{28,24},{1,5},{5... | collective-permute-start | bytes 589832 | tf_op jit(solution)/shard_map/ppermute | solution.py:163
  38.6 11.6 %copy-start.6 = (bf16[6,4,4096]{2,1,0:T(4,128)(2,1)}, bf16[6,4,4096]{2,1,0:T(4,128)(2,1)S(1)}, u32[]{:S(2)}) copy-start(bf16[6,4,4096]{2,1,0:T(4,128)(2,1)S(1)} %collective-permute-done.3.refs_5_) | copy-start | bytes 589828
  38.6 11.5 %collective-permute-start = (bf16[6,4,4096]{2,1,0:T(4,128)(2,1)S(1)}, bf16[6,4,4096]{2,1,0:T(4,128)(2,1)S(1)}, u32[]{:S(2)}, u32[]{:S(2)}) collective-permute-start(bf16[6,4,4096]{2,1,0:T(4,128)(2,1)S(1)} %maximum_bitcast_fusion.refs_0_.refs_2_), channel_id=1, source_target_pairs={{0,1},{1,0},{2,3},{3,2},{4,5},{5,4},{6,7},{7,6},{8,9},{9,8},{10,11... | collective-permute-start | bytes 589832 | tf_op jit(solution)/shard_map/ppermute | solution.py:163
  41.3 8.9 %copy-start.7 = (bf16[6,4,4096]{2,1,0:T(4,128)(2,1)}, bf16[6,4,4096]{2,1,0:T(4,128)(2,1)S(1)}, u32[]{:S(2)}) copy-start(bf16[6,4,4096]{2,1,0:T(4,128)(2,1)S(1)} %collective-permute-done.2.refs_4_) | copy-start | bytes 589828
  41.3 8.9 %copy-start.8 = (bf16[6,4,4096]{2,1,0:T(4,128)(2,1)}, bf16[6,4,4096]{2,1,0:T(4,128)(2,1)S(1)}, u32[]{:S(2)}) copy-start(bf16[6,4,4096]{2,1,0:T(4,128)(2,1)S(1)} %collective-permute-done.1.refs_3_) | copy-start | bytes 589828
  50.2 0.7 copy-start.12
  60.1 10.6 %copy-start.9 = (f32[256,128]{1,0:T(8,128)S(1)}, f32[256,128]{1,0:T(8,128)}, u32[]{:S(2)}) copy-start(f32[256,128]{1,0:T(8,128)} %shard_map.37) | copy-start | bytes 393220
  60.1 0.7 copy-start.10
  60.8 0.7 copy-start.11

commit v6 on v3

--- a/solution.py
+++ b/solution.py
@@ -83,7 +83,9 @@
     window_count, piece, width = left_refs[0].shape
     rows_left = left_f32.shape[1]
     bin_count = width // 2
-    chunk = max(128, min(512, 8192 // rows_left))
+    chunk = 512
+    while chunk > 128 and chunk * rows_left > 8192:
+        chunk //= 2
     chunks = bin_count // chunk
     group_rows = cross_ref.shape[0]
     group = group_rows // (piece * rows_left)
@@ -163,6 +165,24 @@
     return pieces, order
 
 
+def chip_gather(block, axis_name, size):
+    if size < 4 or size & (size - 1):
+        return xor_gather(block, axis_name, size)
+    chips = size // 2
+    fetched = []
+    for step in range(1, chips):
+        pairs = [(source, source ^ (2 * step)) for source in range(size)]
+        fetched.append(lax.ppermute(block, axis_name, pairs))
+    partner = [(source, source ^ 1) for source in range(size)]
+    pieces = [block, lax.ppermute(block, axis_name, partner)]
+    swapped = lax.ppermute(fetched, axis_name, partner)
+    for step in range(1, chips):
+        pieces.append(fetched[step - 1])
+        pieces.append(swapped[step - 1])
+    order = lax.axis_index(axis_name) ^ jnp.arange(size, dtype=jnp.int32)
+    return pieces, order
+
+
 def on_device(records, fir_taps, lag_limit):
     block_size = records.shape[0]
     decimated = decimate(records, fir_taps)
@@ -177,7 +197,7 @@
     cos_lag, sin_lag = angle_table(LAGS, bin_count, out_length, -LH)
     lag_table = jnp.concatenate([cos_lag.T, sin_lag.T], axis=0).astype(jnp.bfloat16)
     group_rows = sum(piece.shape[1] for piece in left_by_window)
-    piece_rows, visit_order = xor_gather(white_by_window, "row", row_size)
+    piece_rows, visit_order = chip_gather(white_by_window, "row", row_size)
     visit_count = sum(piece.shape[1] for piece in piece_rows)
     pair = pair_block(left_by_window, piece_rows, lag_table)
     pair = jnp.swapaxes(pair.reshape(visit_count, group_rows, LAGS), 0, 1)

time: 74.1 us -> 61.6 us (0.83)
  starting transfers between devices: 16.8 us -> 9.86 us
  waiting for transfers between devices: 15.9 us -> 10.1 us
    ppermute x10 -> x3, starting transfers between devices: 16.8 us -> 4.67 us  [xor_gather(): pieces.append(lax.ppermute(block, axis_name, pairs))]
    ppermute x10 -> x3, waiting for transfers between devices: 15.9 us -> 10.1 us  [xor_gather(): pieces.append(lax.ppermute(block, axis_name, pairs))]
    ppermute x0 -> x7, starting transfers between devices: none -> 5.19 us  [the longest x3 4.61 us: chip_gather(): fetched.append(lax.ppermute(block, axis_name, pairs))]
  transfers between devices with their start and end apart: 10 -> 10, of which waited for: 4 -> 1; matrix products, arithmetic and copies ran while one was open for 8% -> 10% of each run, Pallas kernels for 0% -> 0%
where the time goes in v6:
time: 61.6 us; the launch traced here: 61.5 us
  matrix products  13.9 us (23%)
  Pallas kernels  13.2 us (21%)
  waiting for transfers between devices  10.1 us (16%)
  starting transfers between devices  9.86 us (16%)
  other arithmetic  7.55 us (12%)
  local copies, waits for them, and re-layouts  6.51 us (11%)
    pallas_call x1, Pallas kernels, pair_block(): pl.pallas_call(functools.partial(cross_kernel, left_count, visit_count),...  13.2 us
    ppermute x3, waiting for transfers between devices, xor_gather(): pieces.append(lax.ppermute(block, axis_name, pairs))  10.1 us
    ppermute x3, starting transfers between devices, xor_gather(): pieces.append(lax.ppermute(block, axis_name, pairs))  4.67 us
    ppermute x3, starting transfers between devices, chip_gather(): fetched.append(lax.ppermute(block, axis_name, pairs))  4.61 us
    another operation x2, other arithmetic  4.54 us
    dot_general x1, matrix products, spectrum(): jnp.einsum('bwfq,gq->bwgf', real_t, sin_three, precision=lax.Precision.HI...  2.54 us
    dot_general x1, matrix products, spectrum(): jnp.einsum('bwfq,gq->bwgf', real_t, cos_three, precision=lax.Precision.HI...  2.27 us
    dot_general x1, matrix products, spectrum(): jnp.einsum('bwfq,gq->bwgf', imag_t, sin_three, precision=lax.Precision.HI...  2.27 us
  transfers between devices with their start and end apart: 10, of which 1 were waited for; matrix products, arithmetic and copies ran while one was open for 10% of the time, Pallas kernels for 0%

profile of v6, /device:TPU:0, one launch (start us, length us, event | category | flops | bytes accessed | tf_op | source)
XLA Modules:
  0.0 61.5 jit_solution(10479680338784134499)
XLA Ops:
  0.2 1.7 %reshape.190 = f32[4,6,32,256]{3,2,0,1:T(8,128)S(1)} reshape(f32[4,6,8192]{2,0,1:T(4,128)} %param.3) | data formatting | bytes 1572864 | tf_op jit(solution)/shard_map/reshape | solution.py:31
  2.1 0.7 %iota_compare_fusion = pred[32,288,128]{2,1,0:T(32,128)(4,1)S(1)} fusion(s32[32,128]{1,0:T(8,128)S(1)} %iota_subtract_fusion), kind=kLoop, calls=%fused_computation.2 | loop fusion | flops 1179648 | bytes 1196032 | tf_op jit(solution)/shard_map/eq | solution.py:38
  2.7 1.3 %fusion = f32[1,288,128]{2,0,1:T(1,128)S(1)} fusion(pred[32,288,128]{2,1,0:T(32,128)(4,1)S(1)} %iota_compare_fusion, f32[32]{0:T(128)S(1)} %copy-done), kind=kOutput, calls=%fused_computation.3 | convolution fusion | flops 14155776 | bytes 1327232 | tf_op jit(solution)/shard_map/k,kij->ij/dot_general | solution.py:39
  4.1 1.3 %fusion.4 = f32[4,6,32,128]{3,2,1,0:T(8,128)S(1)} fusion(f32[288,128,1,1]{1,0,3,2:T(8,128)S(1)} %bitcast.82, f32[4,6,31,32]{3,2,1,0:T(8,128)S(1)} %copy.33, f32[4,6,32,256]{3,2,0,1:T(8,128)S(1)} %reshape.190), kind=kOutput, calls=%fused_computation.14 | convolution fusion | flops 340402176 | bytes 1422336 | tf_op jit(solution)/shard_map/swbi,ij->swbj/dot_general | solution.py:40
  5.6 0.9 %convolution_negate_fusion = f32[64,4,6,64]{3,0,2,1:T(8,128)S(1)} fusion(f32[4,6,64,64]{3,2,1,0:T(8,128)S(1)} %reshape_reshape.4), kind=kOutput, calls=%fused_computation.8 | convolution fusion | flops 75653120 | bytes 786432 | tf_op jit(solution)/shard_map/bwnq,fn->bwfq/dot_general | solution.py:52
  6.5 0.9 %fusion.26 = f32[64,4,6,64]{3,0,2,1:T(8,128)S(1)} fusion(f32[4,6,64,64]{3,2,1,0:T(8,128)S(1)} %reshape_reshape.4), kind=kOutput, calls=%fused_computation.53 | convolution fusion | flops 75554816 | bytes 786432 | tf_op jit(solution)/shard_map/bwnq,fn->bwfq/dot_general | solution.py:51
  7.5 2.3 %fusion.13 = f32[32,4,6,64]{3,0,2,1:T(8,128)S(1)} fusion(f32[64,4,6,64]{3,0,2,1:T(8,128)S(1)} %fusion.26, f32[64,4,6,64]{3,0,2,1:T(8,128)S(1)} %convolution_negate_fusion, f32[64,64]{1,0:T(8,128)S(1)} %get-tuple-element.11, f32[64,64]{1,0:T(8,128)S(1)} %get-tuple-element.12), kind=kOutput, calls=%fused_computation.27 | convolution fusion | flops 38072320 | bytes 1015808 | tf_op jit(solution)/shard_map/bwfq,gq->bwgf/dot_general | solution.py:60
  9.7 2.3 %fusion.17 = f32[32,4,6,64]{3,0,2,1:T(8,128)S(1)} fusion(f32[64,4,6,64]{3,0,2,1:T(8,128)S(1)} %convolution_negate_fusion, f32[64,4,6,64]{3,0,2,1:T(8,128)S(1)} %fusion.26, f32[64,64]{1,0:T(8,128)S(1)} %get-tuple-element.11, f32[64,64]{1,0:T(8,128)S(1)} %get-tuple-element.12), kind=kOutput, calls=%fused_computation.31 | convolution fusion | flops 38072320 | bytes 1015808 | tf_op jit(solution)/shard_map/bwfq,gq->bwgf/dot_general | solution.py:57
  12.0 2.3 %fusion.3 = f32[4,6,32,64]{3,2,1,0:T(8,128)S(1)} fusion(f32[32,4,6,64]{3,0,2,1:T(8,128)S(1)} %fusion.17, f32[64,4,6,64]{3,0,2,1:T(8,128)S(1)} %fusion.26, f32[64,4,6,64]{3,0,2,1:T(8,128)S(1)} %convolution_negate_fusion, f32[64,64]{1,0:T(8,128)S(1)} %get-tuple-element.11, f32[64,64]{1,0:T(8,128)S(1)} %get-tuple-element.12), kind=kOutput, calls=%fused_computation.12 | convolution fusion | flops 38121472 | bytes 1212416 | tf_op jit(solution)/shard_map/bwfq,gq->bwgf/dot_general | solution.py:59
  14.3 2.5 %add_reduce_fusion = (f32[4,6,32]{2,1,0:T(8,128)S(1)}, f32[4,6,32,64]{3,2,1,0:T(8,128)S(1)}) fusion(f32[4,6,32,64]{3,2,1,0:T(8,128)S(1)} %fusion.3, f32[32,4,6,64]{3,0,2,1:T(8,128)S(1)} %fusion.13, f32[64,4,6,64]{3,0,2,1:T(8,128)S(1)} %convolution_negate_fusion, f32[64,64]{1,0:T(8,128)S(1)} %get-tuple-element.11, f32[64,4,6,64]{3,0,2,1:T(8,128)S(1)} %fusion.26, ...), kind=kOutput, calls=%fused_computation.39 | convolution fusion | flops 38317312 | bytes 1412096 | tf_op jit(solution)/shard_map/bwfq,gq->bwgf/dot_general | solution.py:62
  17.7 4.0 %collective-permute-start.8 = (bf16[6,4,4096]{2,1,0:T(4,128)(2,1)S(1)}, bf16[6,4,4096]{2,1,0:T(4,128)(2,1)S(1)}, u32[]{:S(2)}, u32[]{:S(2)}) collective-permute-start(bf16[6,4,4096]{2,1,0:T(4,128)(2,1)S(1)} %maximum_bitcast_fusion.refs_0_.refs_4_), channel_id=1, source_target_pairs={{0,24},{4,28},{8,16},{12,20},{16,8},{20,12},{24,0},{28,4},{1,25},{... | collective-permute-start | bytes 589832 | tf_op jit(solution)/shard_map/ppermute | solution.py:175
  21.7 0.5 collective-permute-start.6
  22.3 4.0 %collective-permute-start.2 = (bf16[6,4,4096]{2,1,0:T(4,128)(2,1)S(1)}, bf16[6,4,4096]{2,1,0:T(4,128)(2,1)S(1)}, u32[]{:S(2)}, u32[]{:S(2)}) collective-permute-start(bf16[6,4,4096]{2,1,0:T(4,128)(2,1)S(1)} %maximum_bitcast_fusion.refs_0_.refs_4_), channel_id=1, source_target_pairs={{0,3},{1,2},{2,1},{3,0},{4,7},{5,6},{6,5},{7,4},{8,11},{9,10},{10,... | collective-permute-start | bytes 589832 | tf_op jit(solution)/shard_map/ppermute | solution.py:163
  26.7 4.4 %cosine_convert_fusion = (bf16[2048,128]{1,0:T(8,128)(2,1)S(1)}, bf16[2048,128]{1,0:T(8,128)(2,1)S(1)}) fusion(s32[128]{0:T(128)S(1)} %iota_add_fusion), kind=kLoop, calls=%fused_computation.23 | loop fusion | flops 4194304 | bytes 1049088 | tf_op jit(solution)/shard_map/convert
  31.1 1.1 %pad_maximum_fusion.refs_12_ = bf16[4096,128]{1,0:T(8,128)(2,1)} fusion(bf16[2048,128]{1,0:T(8,128)(2,1)S(1)} %get-tuple-element.8, bf16[2048,128]{1,0:T(8,128)(2,1)S(1)} %get-tuple-element.7), kind=kLoop, calls=%fused_computation.21 | loop fusion | flops 2097152 | bytes 2097152 | tf_op jit(solution)/shard_map/concatenate | solution.py:198
  32.3 0.6 collective-permute-start
  32.9 0.5 collective-permute-start.7
  33.6 10.1 %collective-permute-done.1.refs_2_ = bf16[6,4,4096]{2,1,0:T(4,128)(2,1)S(1)} collective-permute-done((bf16[6,4,4096]{2,1,0:T(4,128)(2,1)S(1)}, bf16[6,4,4096]{2,1,0:T(4,128)(2,1)S(1)}, u32[]{:S(2)}, u32[]{:S(2)}) %collective-permute-start.1) | collective-permute-done | bytes 196640 | tf_op jit(solution)/shard_map/ppermute | solution.py:163
  43.8 0.6 copy-done.7
  44.6 0.7 %copy-done.11 = bf16[6,4,4096]{2,1,0:T(4,128)(2,1)} copy-done((bf16[6,4,4096]{2,1,0:T(4,128)(2,1)}, bf16[6,4,4096]{2,1,0:T(4,128)(2,1)S(1)}, u32[]{:S(2)}) %copy-start.11) | copy-done | bytes 196632
  45.3 13.2 %shard_map.37 = f32[512,128]{1,0:T(8,128)} custom-call(bf16[6,4,4096]{2,1,0:T(4,128)(2,1)} %copy-done.1, bf16[6,4,4096]{2,1,0:T(4,128)(2,1)} %copy-done.8, bf16[6,4,4096]{2,1,0:T(4,128)(2,1)} %copy-done.7, bf16[6,4,4096]{2,1,0:T(4,128)(2,1)} %copy-done.6, bf16[6,4,4096]{2,1,0:T(4,128)(2,1)} %copy-done.1, bf16[6,4,4096]{2,1,0:T(4,128)(2,1)} %copy-done.5, ...), custom_call_target="tpu_custom_call" | custom-call | flops 587202560 | bytes 3670016 | tf_op jit(solution)/shard_map/pallas_call | solution.py:137
  58.4 1.5 %gather_fusion = f32[8,16,4,128]{3,1,2,0:T(8,128)S(1)} fusion(f32[16,8,4,128]{3,0,2,1:T(8,128)} %bitcast.79, s32[1024]{0:T(1024)S(1)} %pad_clamp_fusion.1), kind=kCustom, calls=%fused_computation | custom fusion | bytes 524320 | tf_op jit(solution)/shard_map/jit(_take)/gather | solution.py:206
  60.1 0.6 gather_fusion.1
  60.6 0.8 %multiply_select_fusion = f32[16,1,32,128]{3,2,1,0:T(8,128)} fusion(f32[16,1,32,128]{3,2,1,0:T(8,128)S(1)} %bitcast.80, pred[16]{0:T(512)(128)(4,1)S(1)} %broadcast_in_dim.63, pred[16,128]{1,0:T(8,128)(4,1)S(1)} %broadcast_compare_fusion), kind=kLoop, calls=%fused_computation.41 | loop fusion | flops 196608 | bytes 526352 | tf_op jit(solution)/shard_map/jit(_where)/select_n | solution.py:214
  (65 shorter events, 2.5 us)
Async XLA Ops:
  0.0 2.7 %copy-start = (f32[32]{0:T(128)S(1)}, f32[32]{0:T(128)}, u32[]{:S(2)}) copy-start(f32[32]{0:T(128)} %param.4) | copy-start | bytes 388
  17.7 14.6 %copy-start.1 = (bf16[6,4,4096]{2,1,0:T(4,128)(2,1)}, bf16[6,4,4096]{2,1,0:T(4,128)(2,1)S(1)}, u32[]{:S(2)}) copy-start(bf16[6,4,4096]{2,1,0:T(4,128)(2,1)S(1)} %maximum_bitcast_fusion.refs_0_.refs_4_) | copy-start | bytes 589828
  17.7 14.5 %collective-permute-start.8 = (bf16[6,4,4096]{2,1,0:T(4,128)(2,1)S(1)}, bf16[6,4,4096]{2,1,0:T(4,128)(2,1)S(1)}, u32[]{:S(2)}, u32[]{:S(2)}) collective-permute-start(bf16[6,4,4096]{2,1,0:T(4,128)(2,1)S(1)} %maximum_bitcast_fusion.refs_0_.refs_4_), channel_id=1, source_target_pairs={{0,24},{4,28},{8,16},{12,20},{16,8},{20,12},{24,0},{28,4},{1,25},{... | collective-permute-start | bytes 589832 | tf_op jit(solution)/shard_map/ppermute | solution.py:175
  21.7 10.6 %collective-permute-start.6 = (bf16[6,4,4096]{2,1,0:T(4,128)(2,1)S(1)}, bf16[6,4,4096]{2,1,0:T(4,128)(2,1)S(1)}, u32[]{:S(2)}, u32[]{:S(2)}) collective-permute-start(bf16[6,4,4096]{2,1,0:T(4,128)(2,1)S(1)} %maximum_bitcast_fusion.refs_0_.refs_4_), channel_id=1, source_target_pairs={{0,16},{4,20},{8,24},{12,28},{16,0},{20,4},{24,8},{28,12},{1,17},{... | collective-permute-start | bytes 589832 | tf_op jit(solution)/shard_map/ppermute | solution.py:175
  22.2 10.7 %collective-permute-start.4 = (bf16[6,4,4096]{2,1,0:T(4,128)(2,1)S(1)}, bf16[6,4,4096]{2,1,0:T(4,128)(2,1)S(1)}, u32[]{:S(2)}, u32[]{:S(2)}) collective-permute-start(bf16[6,4,4096]{2,1,0:T(4,128)(2,1)S(1)} %maximum_bitcast_fusion.refs_0_.refs_4_), channel_id=1, source_target_pairs={{0,8},{4,12},{8,0},{12,4},{16,24},{20,28},{24,16},{28,20},{1,9},{5... | collective-permute-start | bytes 589832 | tf_op jit(solution)/shard_map/ppermute | solution.py:175
  22.3 10.6 %collective-permute-start.3 = (bf16[6,4,4096]{2,1,0:T(4,128)(2,1)S(1)}, bf16[6,4,4096]{2,1,0:T(4,128)(2,1)S(1)}, u32[]{:S(2)}, u32[]{:S(2)}) collective-permute-start(bf16[6,4,4096]{2,1,0:T(4,128)(2,1)S(1)} %maximum_bitcast_fusion.refs_0_.refs_4_), channel_id=1, source_target_pairs={{0,4},{4,0},{8,12},{12,8},{16,20},{20,16},{24,28},{28,24},{1,5},{5... | collective-permute-start | bytes 589832 | tf_op jit(solution)/shard_map/ppermute | solution.py:177
  22.3 11.1 %collective-permute-start.2 = (bf16[6,4,4096]{2,1,0:T(4,128)(2,1)S(1)}, bf16[6,4,4096]{2,1,0:T(4,128)(2,1)S(1)}, u32[]{:S(2)}, u32[]{:S(2)}) collective-permute-start(bf16[6,4,4096]{2,1,0:T(4,128)(2,1)S(1)} %maximum_bitcast_fusion.refs_0_.refs_4_), channel_id=1, source_target_pairs={{0,3},{1,2},{2,1},{3,0},{4,7},{5,6},{6,5},{7,4},{8,11},{9,10},{10,... | collective-permute-start | bytes 589832 | tf_op jit(solution)/shard_map/ppermute | solution.py:163
  31.1 2.4 %copy-start.12 = (s32[16]{0:T(128)S(1)}, s32[16]{0:T(128)}, u32[]{:S(2)}) copy-start(s32[16]{0:T(128)} %param.5) | copy-start | bytes 196
  32.2 11.6 %copy-start.2 = (bf16[6,4,4096]{2,1,0:T(4,128)(2,1)}, bf16[6,4,4096]{2,1,0:T(4,128)(2,1)S(1)}, u32[]{:S(2)}) copy-start(bf16[6,4,4096]{2,1,0:T(4,128)(2,1)S(1)} %collective-permute-done.8.refs_10_) | copy-start | bytes 589828
  32.2 11.5 %collective-permute-start.1 = (bf16[6,4,4096]{2,1,0:T(4,128)(2,1)S(1)}, bf16[6,4,4096]{2,1,0:T(4,128)(2,1)S(1)}, u32[]{:S(2)}, u32[]{:S(2)}) collective-permute-start(bf16[6,4,4096]{2,1,0:T(4,128)(2,1)S(1)} %maximum_bitcast_fusion.refs_0_.refs_4_), channel_id=1, source_target_pairs={{0,2},{1,3},{2,0},{3,1},{4,6},{5,7},{6,4},{7,5},{8,10},{9,11},{10,... | collective-permute-start | bytes 589832 | tf_op jit(solution)/shard_map/ppermute | solution.py:163
  32.3 11.5 %copy-start.3 = (bf16[6,4,4096]{2,1,0:T(4,128)(2,1)}, bf16[6,4,4096]{2,1,0:T(4,128)(2,1)S(1)}, u32[]{:S(2)}) copy-start(bf16[6,4,4096]{2,1,0:T(4,128)(2,1)S(1)} %collective-permute-done.6.refs_8_) | copy-start | bytes 589828
  32.3 11.4 %collective-permute-start = (bf16[6,4,4096]{2,1,0:T(4,128)(2,1)S(1)}, bf16[6,4,4096]{2,1,0:T(4,128)(2,1)S(1)}, u32[]{:S(2)}, u32[]{:S(2)}) collective-permute-start(bf16[6,4,4096]{2,1,0:T(4,128)(2,1)S(1)} %maximum_bitcast_fusion.refs_0_.refs_4_), channel_id=1, source_target_pairs={{0,1},{1,0},{2,3},{3,2},{4,5},{5,4},{6,7},{7,6},{8,9},{9,8},{10,11... | collective-permute-start | bytes 589832 | tf_op jit(solution)/shard_map/ppermute | solution.py:163
  32.9 10.8 %copy-start.4 = (bf16[6,4,4096]{2,1,0:T(4,128)(2,1)}, bf16[6,4,4096]{2,1,0:T(4,128)(2,1)S(1)}, u32[]{:S(2)}) copy-start(bf16[6,4,4096]{2,1,0:T(4,128)(2,1)S(1)} %collective-permute-done.4.refs_6_) | copy-start | bytes 589828
  32.9 10.8 %collective-permute-start.9 = (bf16[6,4,4096]{2,1,0:T(4,128)(2,1)S(1)}, bf16[6,4,4096]{2,1,0:T(4,128)(2,1)S(1)}, u32[]{:S(2)}, u32[]{:S(2)}) collective-permute-start(bf16[6,4,4096]{2,1,0:T(4,128)(2,1)S(1)} %collective-permute-done.8.refs_10_), channel_id=1, source_target_pairs={{0,4},{4,0},{8,12},{12,8},{16,20},{20,16},{24,28},{28,24},{1,5},{5... | collective-permute-start | bytes 589832 | tf_op jit(solution)/shard_map/ppermute | solution.py:178
  32.9 10.8 %copy-start.5 = (bf16[6,4,4096]{2,1,0:T(4,128)(2,1)}, bf16[6,4,4096]{2,1,0:T(4,128)(2,1)S(1)}, u32[]{:S(2)}) copy-start(bf16[6,4,4096]{2,1,0:T(4,128)(2,1)S(1)} %collective-permute-done.3.refs_5_) | copy-start | bytes 589828
  32.9 10.8 %collective-permute-start.7 = (bf16[6,4,4096]{2,1,0:T(4,128)(2,1)S(1)}, bf16[6,4,4096]{2,1,0:T(4,128)(2,1)S(1)}, u32[]{:S(2)}, u32[]{:S(2)}) collective-permute-start(bf16[6,4,4096]{2,1,0:T(4,128)(2,1)S(1)} %collective-permute-done.6.refs_8_), channel_id=1, source_target_pairs={{0,4},{4,0},{8,12},{12,8},{16,20},{20,16},{24,28},{28,24},{1,5},{5... | collective-permute-start | bytes 589832 | tf_op jit(solution)/shard_map/ppermute | solution.py:178
  33.4 10.3 %copy-start.6 = (bf16[6,4,4096]{2,1,0:T(4,128)(2,1)}, bf16[6,4,4096]{2,1,0:T(4,128)(2,1)S(1)}, u32[]{:S(2)}) copy-start(bf16[6,4,4096]{2,1,0:T(4,128)(2,1)S(1)} %collective-permute-done.2.refs_3_) | copy-start | bytes 589828
  33.4 10.3 %collective-permute-start.5 = (bf16[6,4,4096]{2,1,0:T(4,128)(2,1)S(1)}, bf16[6,4,4096]{2,1,0:T(4,128)(2,1)S(1)}, u32[]{:S(2)}, u32[]{:S(2)}) collective-permute-start(bf16[6,4,4096]{2,1,0:T(4,128)(2,1)S(1)} %collective-permute-done.4.refs_6_), channel_id=1, source_target_pairs={{0,4},{4,0},{8,12},{12,8},{16,20},{20,16},{24,28},{28,24},{1,5},{5... | collective-permute-start | bytes 589832 | tf_op jit(solution)/shard_map/ppermute | solution.py:178
  43.7 0.7 %copy-start.7 = (bf16[6,4,4096]{2,1,0:T(4,128)(2,1)}, bf16[6,4,4096]{2,1,0:T(4,128)(2,1)S(1)}, u32[]{:S(2)}) copy-start(bf16[6,4,4096]{2,1,0:T(4,128)(2,1)S(1)} %collective-permute-done.1.refs_2_) | copy-start | bytes 589828
  43.7 0.7 %copy-start.8 = (bf16[6,4,4096]{2,1,0:T(4,128)(2,1)}, bf16[6,4,4096]{2,1,0:T(4,128)(2,1)S(1)}, u32[]{:S(2)}) copy-start(bf16[6,4,4096]{2,1,0:T(4,128)(2,1)S(1)} %collective-permute-done.refs_1_) | copy-start | bytes 589828
  43.7 0.8 %copy-start.9 = (bf16[6,4,4096]{2,1,0:T(4,128)(2,1)}, bf16[6,4,4096]{2,1,0:T(4,128)(2,1)S(1)}, u32[]{:S(2)}) copy-start(bf16[6,4,4096]{2,1,0:T(4,128)(2,1)S(1)} %collective-permute-done.9.refs_11_) | copy-start | bytes 589828
  43.7 0.9 %copy-start.10 = (bf16[6,4,4096]{2,1,0:T(4,128)(2,1)}, bf16[6,4,4096]{2,1,0:T(4,128)(2,1)S(1)}, u32[]{:S(2)}) copy-start(bf16[6,4,4096]{2,1,0:T(4,128)(2,1)S(1)} %collective-permute-done.7.refs_9_) | copy-start | bytes 589828
  44.6 0.7 %copy-start.11 = (bf16[6,4,4096]{2,1,0:T(4,128)(2,1)}, bf16[6,4,4096]{2,1,0:T(4,128)(2,1)S(1)}, u32[]{:S(2)}) copy-start(bf16[6,4,4096]{2,1,0:T(4,128)(2,1)S(1)} %collective-permute-done.5.refs_7_) | copy-start | bytes 589828

commit v7 on v6

--- a/solution.py
+++ b/solution.py
@@ -76,10 +76,10 @@
     return jnp.concatenate([white_real, white_imag], axis=-1).astype(jnp.bfloat16)
 
 
-def cross_kernel(left_count, visit_count, *refs):
-    left_refs = refs[:left_count]
-    visit_refs = refs[left_count:left_count + visit_count]
-    table_ref, out_ref, left_f32, visit_f32, cross_ref = refs[left_count + visit_count:]
+def cross_kernel(slots, *refs):
+    piece_refs = refs[:len(slots)]
+    table_ref, out_ref, left_f32, visit_f32, cross_ref = refs[len(slots):]
+    left_refs = [ref for ref, slot in zip(piece_refs, slots) if slot[0] == 0]
     window_count, piece, width = left_refs[0].shape
     rows_left = left_f32.shape[1]
     bin_count = width // 2
@@ -89,11 +89,11 @@
     chunks = bin_count // chunk
     group_rows = cross_ref.shape[0]
     group = group_rows // (piece * rows_left)
-
-    for index, ref in enumerate(left_refs):
-        left_f32[:, index * piece:(index + 1) * piece, :] = ref[...].astype(jnp.float32)
-    for index, ref in enumerate(visit_refs):
-        visit_f32[:, index * piece:(index + 1) * piece, :] = ref[...].astype(jnp.float32)
+    visit_count = visit_f32.shape[1] // piece
+
+    for ref, (kind, index) in zip(piece_refs, slots):
+        target = left_f32 if kind == 0 else visit_f32
+        target[:, index * piece:(index + 1) * piece, :] = ref[...].astype(jnp.float32)
 
     for first in range(0, visit_count, group):
         base = first * piece
@@ -122,7 +122,7 @@
         )
 
 
-def pair_block(left_pieces, visit_pieces, lag_table):
+def pair_block(left_pieces, visit_pieces, lag_table, issue_order):
     window_count, piece, width = left_pieces[0].shape
     left_count = len(left_pieces)
     visit_count = len(visit_pieces)
@@ -135,7 +135,7 @@
     flops = visit_rows * rows_left * width * (4 * window_count + 2 * lag_count)
     vmem = pltpu.VMEM
     return pl.pallas_call(
-        functools.partial(cross_kernel, left_count, visit_count),
+        functools.partial(cross_kernel, tuple(issue_order)),
         out_shape=jax.ShapeDtypeStruct((visit_rows * rows_left, lag_count), jnp.float32),
         in_specs=[pl.BlockSpec(memory_space=vmem)] * (left_count + visit_count + 1),
         out_specs=pl.BlockSpec(memory_space=vmem),
@@ -151,7 +151,7 @@
             bytes_accessed=2 * width * (window_count * (rows_left + visit_rows) + lag_count)
             + 4 * visit_rows * rows_left * lag_count,
         ),
-    )(*left_pieces, *visit_pieces, lag_table)
+    )(*[(left_pieces, visit_pieces)[kind][index] for kind, index in issue_order], lag_table)
 
 
 def xor_gather(block, axis_name, size):
@@ -199,7 +199,14 @@
     group_rows = sum(piece.shape[1] for piece in left_by_window)
     piece_rows, visit_order = chip_gather(white_by_window, "row", row_size)
     visit_count = sum(piece.shape[1] for piece in piece_rows)
-    pair = pair_block(left_by_window, piece_rows, lag_table)
+    late_first = [(1, index) for index in range(len(piece_rows)) if index > 1 and index % 2 == 1]
+    near = [(0, 0), (1, 0), (0, 1), (1, 1)][:2 + min(1, len(left_by_window) - 1) + min(1, len(piece_rows) - 1)]
+    fetches = [(1, index) for index in range(len(piece_rows)) if index > 1 and index % 2 == 0]
+    far = [(0, index) for index in range(2, len(left_by_window))]
+    issue_order = [slot for slot in late_first + near + fetches + far[::-1]]
+    issue_order = sorted(set(issue_order), key=issue_order.index)
+    assert len(issue_order) == len(left_by_window) + len(piece_rows)
+    pair = pair_block(left_by_window, piece_rows, lag_table, issue_order)
     pair = jnp.swapaxes(pair.reshape(visit_count, group_rows, LAGS), 0, 1)
     if visit_order is not None:
         pair = pair.reshape(group_rows, row_size, block_size, LAGS)

time: 61.6 us -> 63 us (1.023)
  starting transfers between devices: 9.86 us -> 13.6 us
  waiting for transfers between devices: 10.1 us -> 7.87 us
    ppermute x3, starting transfers between devices: 4.67 us -> 9.53 us  [xor_gather(): pieces.append(lax.ppermute(block, axis_name, pairs))]
    ppermute x3, waiting for transfers between devices: 10.1 us -> 7.85 us  [xor_gather(): pieces.append(lax.ppermute(block, axis_name, pairs))]
    ppermute x3, starting transfers between devices: 4.61 us -> 3.49 us  [chip_gather(): fetched.append(lax.ppermute(block, axis_name, pairs))]
  transfers between devices with their start and end apart: 10 -> 10, of which waited for: 1 -> 2; matrix products, arithmetic and copies ran while one was open for 10% -> 9% of each run, Pallas kernels for 0% -> 0%
where the time goes in v7:
time: 63 us; the launch traced here: 62.8 us
  matrix products  13.9 us (22%)
  starting transfers between devices  13.6 us (22%)
  Pallas kernels  13.2 us (21%)
  waiting for transfers between devices  7.87 us (12%)
  other arithmetic  7.55 us (12%)
  local copies, waits for them, and re-layouts  6.44 us (10%)
    pallas_call x1, Pallas kernels, pair_block(): pl.pallas_call(functools.partial(cross_kernel, tuple(issue_order)), out_s...  13.2 us
    ppermute x3, starting transfers between devices, xor_gather(): pieces.append(lax.ppermute(block, axis_name, pairs))  9.53 us
    ppermute x3, waiting for transfers between devices, xor_gather(): pieces.append(lax.ppermute(block, axis_name, pairs))  7.85 us
    another operation x2, other arithmetic  4.54 us
    ppermute x3, starting transfers between devices, chip_gather(): fetched.append(lax.ppermute(block, axis_name, pairs))  3.49 us
    dot_general x1, matrix products, spectrum(): jnp.einsum('bwfq,gq->bwgf', real_t, sin_three, precision=lax.Precision.HI...  2.54 us
    dot_general x1, matrix products, spectrum(): jnp.einsum('bwfq,gq->bwgf', real_t, cos_three, precision=lax.Precision.HI...  2.27 us
    dot_general x1, matrix products, spectrum(): jnp.einsum('bwfq,gq->bwgf', imag_t, sin_three, precision=lax.Precision.HI...  2.27 us
  transfers between devices with their start and end apart: 10, of which 2 were waited for; matrix products, arithmetic and copies ran while one was open for 9% of the time, Pallas kernels for 0%

profile of v7, /device:TPU:0, one launch (start us, length us, event | category | flops | bytes accessed | tf_op | source)
XLA Modules:
  0.0 62.8 jit_solution(2591625245690584088)
XLA Ops:
  0.2 1.7 %reshape.190 = f32[4,6,32,256]{3,2,0,1:T(8,128)S(1)} reshape(f32[4,6,8192]{2,0,1:T(4,128)} %param.3) | data formatting | bytes 1572864 | tf_op jit(solution)/shard_map/reshape | solution.py:31
  2.1 0.7 %iota_compare_fusion = pred[32,288,128]{2,1,0:T(32,128)(4,1)S(1)} fusion(s32[32,128]{1,0:T(8,128)S(1)} %iota_subtract_fusion), kind=kLoop, calls=%fused_computation.2 | loop fusion | flops 1179648 | bytes 1196032 | tf_op jit(solution)/shard_map/eq | solution.py:38
  2.7 1.3 %fusion = f32[1,288,128]{2,0,1:T(1,128)S(1)} fusion(pred[32,288,128]{2,1,0:T(32,128)(4,1)S(1)} %iota_compare_fusion, f32[32]{0:T(128)S(1)} %copy-done), kind=kOutput, calls=%fused_computation.3 | convolution fusion | flops 14155776 | bytes 1327232 | tf_op jit(solution)/shard_map/k,kij->ij/dot_general | solution.py:39
  4.1 1.3 %fusion.4 = f32[4,6,32,128]{3,2,1,0:T(8,128)S(1)} fusion(f32[288,128,1,1]{1,0,3,2:T(8,128)S(1)} %bitcast.82, f32[4,6,31,32]{3,2,1,0:T(8,128)S(1)} %copy.33, f32[4,6,32,256]{3,2,0,1:T(8,128)S(1)} %reshape.190), kind=kOutput, calls=%fused_computation.14 | convolution fusion | flops 340402176 | bytes 1422336 | tf_op jit(solution)/shard_map/swbi,ij->swbj/dot_general | solution.py:40
  5.6 0.9 %convolution_negate_fusion = f32[64,4,6,64]{3,0,2,1:T(8,128)S(1)} fusion(f32[4,6,64,64]{3,2,1,0:T(8,128)S(1)} %reshape_reshape.4), kind=kOutput, calls=%fused_computation.8 | convolution fusion | flops 75653120 | bytes 786432 | tf_op jit(solution)/shard_map/bwnq,fn->bwfq/dot_general | solution.py:52
  6.5 0.9 %fusion.26 = f32[64,4,6,64]{3,0,2,1:T(8,128)S(1)} fusion(f32[4,6,64,64]{3,2,1,0:T(8,128)S(1)} %reshape_reshape.4), kind=kOutput, calls=%fused_computation.53 | convolution fusion | flops 75554816 | bytes 786432 | tf_op jit(solution)/shard_map/bwnq,fn->bwfq/dot_general | solution.py:51
  7.5 2.3 %fusion.13 = f32[32,4,6,64]{3,0,2,1:T(8,128)S(1)} fusion(f32[64,4,6,64]{3,0,2,1:T(8,128)S(1)} %fusion.26, f32[64,4,6,64]{3,0,2,1:T(8,128)S(1)} %convolution_negate_fusion, f32[64,64]{1,0:T(8,128)S(1)} %get-tuple-element.11, f32[64,64]{1,0:T(8,128)S(1)} %get-tuple-element.12), kind=kOutput, calls=%fused_computation.27 | convolution fusion | flops 38072320 | bytes 1015808 | tf_op jit(solution)/shard_map/bwfq,gq->bwgf/dot_general | solution.py:60
  9.7 2.3 %fusion.17 = f32[32,4,6,64]{3,0,2,1:T(8,128)S(1)} fusion(f32[64,4,6,64]{3,0,2,1:T(8,128)S(1)} %convolution_negate_fusion, f32[64,4,6,64]{3,0,2,1:T(8,128)S(1)} %fusion.26, f32[64,64]{1,0:T(8,128)S(1)} %get-tuple-element.11, f32[64,64]{1,0:T(8,128)S(1)} %get-tuple-element.12), kind=kOutput, calls=%fused_computation.31 | convolution fusion | flops 38072320 | bytes 1015808 | tf_op jit(solution)/shard_map/bwfq,gq->bwgf/dot_general | solution.py:57
  12.0 2.3 %fusion.3 = f32[4,6,32,64]{3,2,1,0:T(8,128)S(1)} fusion(f32[32,4,6,64]{3,0,2,1:T(8,128)S(1)} %fusion.17, f32[64,4,6,64]{3,0,2,1:T(8,128)S(1)} %fusion.26, f32[64,4,6,64]{3,0,2,1:T(8,128)S(1)} %convolution_negate_fusion, f32[64,64]{1,0:T(8,128)S(1)} %get-tuple-element.11, f32[64,64]{1,0:T(8,128)S(1)} %get-tuple-element.12), kind=kOutput, calls=%fused_computation.12 | convolution fusion | flops 38121472 | bytes 1212416 | tf_op jit(solution)/shard_map/bwfq,gq->bwgf/dot_general | solution.py:59
  14.3 2.5 %add_reduce_fusion = (f32[4,6,32]{2,1,0:T(8,128)S(1)}, f32[4,6,32,64]{3,2,1,0:T(8,128)S(1)}) fusion(f32[4,6,32,64]{3,2,1,0:T(8,128)S(1)} %fusion.3, f32[32,4,6,64]{3,0,2,1:T(8,128)S(1)} %fusion.13, f32[64,4,6,64]{3,0,2,1:T(8,128)S(1)} %convolution_negate_fusion, f32[64,64]{1,0:T(8,128)S(1)} %get-tuple-element.11, f32[64,4,6,64]{3,0,2,1:T(8,128)S(1)} %fusion.26, ...), kind=kOutput, calls=%fused_computation.39 | convolution fusion | flops 38317312 | bytes 1412096 | tf_op jit(solution)/shard_map/bwfq,gq->bwgf/dot_general | solution.py:62
  17.7 4.1 %collective-permute-start.9 = (bf16[6,4,4096]{2,1,0:T(4,128)(2,1)S(1)}, bf16[6,4,4096]{2,1,0:T(4,128)(2,1)S(1)}, u32[]{:S(2)}, u32[]{:S(2)}) collective-permute-start(bf16[6,4,4096]{2,1,0:T(4,128)(2,1)S(1)} %maximum_bitcast_fusion.refs_3_.refs_4_), channel_id=1, source_target_pairs={{0,2},{1,3},{2,0},{3,1},{4,6},{5,7},{6,4},{7,5},{8,10},{9,11},{10,... | collective-permute-start | bytes 589832 | tf_op jit(solution)/shard_map/ppermute | solution.py:163
  21.8 1.3 %collective-permute-start.8 = (bf16[6,4,4096]{2,1,0:T(4,128)(2,1)S(1)}, bf16[6,4,4096]{2,1,0:T(4,128)(2,1)S(1)}, u32[]{:S(2)}, u32[]{:S(2)}) collective-permute-start(bf16[6,4,4096]{2,1,0:T(4,128)(2,1)S(1)} %maximum_bitcast_fusion.refs_3_.refs_4_), channel_id=1, source_target_pairs={{0,3},{1,2},{2,1},{3,0},{4,7},{5,6},{6,5},{7,4},{8,11},{9,10},{10,... | collective-permute-start | bytes 589832 | tf_op jit(solution)/shard_map/ppermute | solution.py:163
  23.2 2.5 %collective-permute-start.4 = (bf16[6,4,4096]{2,1,0:T(4,128)(2,1)S(1)}, bf16[6,4,4096]{2,1,0:T(4,128)(2,1)S(1)}, u32[]{:S(2)}, u32[]{:S(2)}) collective-permute-start(bf16[6,4,4096]{2,1,0:T(4,128)(2,1)S(1)} %maximum_bitcast_fusion.refs_3_.refs_4_), channel_id=1, source_target_pairs={{0,24},{4,28},{8,16},{12,20},{16,8},{20,12},{24,0},{28,4},{1,25},{... | collective-permute-start | bytes 589832 | tf_op jit(solution)/shard_map/ppermute | solution.py:175
  27.0 4.4 %cosine_convert_fusion = (bf16[2048,128]{1,0:T(8,128)(2,1)S(1)}, bf16[2048,128]{1,0:T(8,128)(2,1)S(1)}) fusion(s32[128]{0:T(128)S(1)} %iota_add_fusion), kind=kLoop, calls=%fused_computation.23 | loop fusion | flops 4194304 | bytes 1049088 | tf_op jit(solution)/shard_map/convert
  31.4 1.1 %pad_maximum_fusion.refs_12_ = bf16[4096,128]{1,0:T(8,128)(2,1)} fusion(bf16[2048,128]{1,0:T(8,128)(2,1)S(1)} %get-tuple-element.8, bf16[2048,128]{1,0:T(8,128)(2,1)S(1)} %get-tuple-element.7), kind=kLoop, calls=%fused_computation.21 | loop fusion | flops 2097152 | bytes 2097152 | tf_op jit(solution)/shard_map/concatenate | solution.py:198
  32.5 3.5 %collective-permute-done.9.refs_11_ = bf16[6,4,4096]{2,1,0:T(4,128)(2,1)S(1)} collective-permute-done((bf16[6,4,4096]{2,1,0:T(4,128)(2,1)S(1)}, bf16[6,4,4096]{2,1,0:T(4,128)(2,1)S(1)}, u32[]{:S(2)}, u32[]{:S(2)}) %collective-permute-start.9) | collective-permute-done | bytes 196640 | tf_op jit(solution)/shard_map/ppermute | solution.py:163
  36.0 4.1 %collective-permute-start.6 = (bf16[6,4,4096]{2,1,0:T(4,128)(2,1)S(1)}, bf16[6,4,4096]{2,1,0:T(4,128)(2,1)S(1)}, u32[]{:S(2)}, u32[]{:S(2)}) collective-permute-start(bf16[6,4,4096]{2,1,0:T(4,128)(2,1)S(1)} %maximum_bitcast_fusion.refs_3_.refs_4_), channel_id=1, source_target_pairs={{0,1},{1,0},{2,3},{3,2},{4,5},{5,4},{6,7},{7,6},{8,9},{9,8},{10,11... | collective-permute-start | bytes 589832 | tf_op jit(solution)/shard_map/ppermute | solution.py:163
  40.8 4.4 %collective-permute-done.6.refs_5_ = bf16[6,4,4096]{2,1,0:T(4,128)(2,1)S(1)} collective-permute-done((bf16[6,4,4096]{2,1,0:T(4,128)(2,1)S(1)}, bf16[6,4,4096]{2,1,0:T(4,128)(2,1)S(1)}, u32[]{:S(2)}, u32[]{:S(2)}) %collective-permute-start.6) | collective-permute-done | bytes 196640 | tf_op jit(solution)/shard_map/ppermute | solution.py:163
  45.3 0.6 copy-done.8
  46.0 0.7 %copy-done.11 = bf16[6,4,4096]{2,1,0:T(4,128)(2,1)} copy-done((bf16[6,4,4096]{2,1,0:T(4,128)(2,1)}, bf16[6,4,4096]{2,1,0:T(4,128)(2,1)S(1)}, u32[]{:S(2)}) %copy-start.11) | copy-done | bytes 196632
  46.7 13.2 %shard_map.37 = f32[512,128]{1,0:T(8,128)} custom-call(bf16[6,4,4096]{2,1,0:T(4,128)(2,1)} %copy-done.11, bf16[6,4,4096]{2,1,0:T(4,128)(2,1)} %copy-done.10, bf16[6,4,4096]{2,1,0:T(4,128)(2,1)} %copy-done.9, bf16[6,4,4096]{2,1,0:T(4,128)(2,1)} %copy-done.1, bf16[6,4,4096]{2,1,0:T(4,128)(2,1)} %copy-done.1, bf16[6,4,4096]{2,1,0:T(4,128)(2,1)} %copy-done.8, ...), custom_call_target="tpu_custom_call" | custom-call | flops 587202560 | bytes 3670016 | tf_op jit(solution)/shard_map/pallas_call | solution.py:137
  59.8 1.5 %gather_fusion = f32[8,16,4,128]{3,1,2,0:T(8,128)S(1)} fusion(f32[16,8,4,128]{3,0,2,1:T(8,128)} %bitcast.79, s32[1024]{0:T(1024)S(1)} %pad_clamp_fusion.1), kind=kCustom, calls=%fused_computation | custom fusion | bytes 524320 | tf_op jit(solution)/shard_map/jit(_take)/gather | solution.py:213
  61.5 0.6 gather_fusion.1
  62.0 0.8 %multiply_select_fusion = f32[16,1,32,128]{3,2,1,0:T(8,128)} fusion(f32[16,1,32,128]{3,2,1,0:T(8,128)S(1)} %bitcast.80, pred[16]{0:T(512)(128)(4,1)S(1)} %broadcast_in_dim.63, pred[16,128]{1,0:T(8,128)(4,1)S(1)} %broadcast_compare_fusion), kind=kLoop, calls=%fused_computation.41 | loop fusion | flops 196608 | bytes 526352 | tf_op jit(solution)/shard_map/jit(_where)/select_n | solution.py:221
  (65 shorter events, 3.7 us)
Async XLA Ops:
  0.0 2.7 %copy-start = (f32[32]{0:T(128)S(1)}, f32[32]{0:T(128)}, u32[]{:S(2)}) copy-start(f32[32]{0:T(128)} %param.4) | copy-start | bytes 388
  17.7 18.3 %copy-start.1 = (bf16[6,4,4096]{2,1,0:T(4,128)(2,1)}, bf16[6,4,4096]{2,1,0:T(4,128)(2,1)S(1)}, u32[]{:S(2)}) copy-start(bf16[6,4,4096]{2,1,0:T(4,128)(2,1)S(1)} %maximum_bitcast_fusion.refs_3_.refs_4_) | copy-start | bytes 589828
  17.7 18.3 %collective-permute-start.9 = (bf16[6,4,4096]{2,1,0:T(4,128)(2,1)S(1)}, bf16[6,4,4096]{2,1,0:T(4,128)(2,1)S(1)}, u32[]{:S(2)}, u32[]{:S(2)}) collective-permute-start(bf16[6,4,4096]{2,1,0:T(4,128)(2,1)S(1)} %maximum_bitcast_fusion.refs_3_.refs_4_), channel_id=1, source_target_pairs={{0,2},{1,3},{2,0},{3,1},{4,6},{5,7},{6,4},{7,5},{8,10},{9,11},{10,... | collective-permute-start | bytes 589832 | tf_op jit(solution)/shard_map/ppermute | solution.py:163
  21.8 14.2 %collective-permute-start.8 = (bf16[6,4,4096]{2,1,0:T(4,128)(2,1)S(1)}, bf16[6,4,4096]{2,1,0:T(4,128)(2,1)S(1)}, u32[]{:S(2)}, u32[]{:S(2)}) collective-permute-start(bf16[6,4,4096]{2,1,0:T(4,128)(2,1)S(1)} %maximum_bitcast_fusion.refs_3_.refs_4_), channel_id=1, source_target_pairs={{0,3},{1,2},{2,1},{3,0},{4,7},{5,6},{6,5},{7,4},{8,11},{9,10},{10,... | collective-permute-start | bytes 589832 | tf_op jit(solution)/shard_map/ppermute | solution.py:163
  23.2 16.9 %collective-permute-start.4 = (bf16[6,4,4096]{2,1,0:T(4,128)(2,1)S(1)}, bf16[6,4,4096]{2,1,0:T(4,128)(2,1)S(1)}, u32[]{:S(2)}, u32[]{:S(2)}) collective-permute-start(bf16[6,4,4096]{2,1,0:T(4,128)(2,1)S(1)} %maximum_bitcast_fusion.refs_3_.refs_4_), channel_id=1, source_target_pairs={{0,24},{4,28},{8,16},{12,20},{16,8},{20,12},{24,0},{28,4},{1,25},{... | collective-permute-start | bytes 589832 | tf_op jit(solution)/shard_map/ppermute | solution.py:175
  25.6 14.5 %collective-permute-start.2 = (bf16[6,4,4096]{2,1,0:T(4,128)(2,1)S(1)}, bf16[6,4,4096]{2,1,0:T(4,128)(2,1)S(1)}, u32[]{:S(2)}, u32[]{:S(2)}) collective-permute-start(bf16[6,4,4096]{2,1,0:T(4,128)(2,1)S(1)} %maximum_bitcast_fusion.refs_3_.refs_4_), channel_id=1, source_target_pairs={{0,16},{4,20},{8,24},{12,28},{16,0},{20,4},{24,8},{28,12},{1,17},{... | collective-permute-start | bytes 589832 | tf_op jit(solution)/shard_map/ppermute | solution.py:175
  26.1 14.5 %collective-permute-start = (bf16[6,4,4096]{2,1,0:T(4,128)(2,1)S(1)}, bf16[6,4,4096]{2,1,0:T(4,128)(2,1)S(1)}, u32[]{:S(2)}, u32[]{:S(2)}) collective-permute-start(bf16[6,4,4096]{2,1,0:T(4,128)(2,1)S(1)} %maximum_bitcast_fusion.refs_3_.refs_4_), channel_id=1, source_target_pairs={{0,8},{4,12},{8,0},{12,4},{16,24},{20,28},{24,16},{28,20},{1,9},{5... | collective-permute-start | bytes 589832 | tf_op jit(solution)/shard_map/ppermute | solution.py:175
  31.4 9.3 %copy-start.12 = (s32[16]{0:T(128)S(1)}, s32[16]{0:T(128)}, u32[]{:S(2)}) copy-start(s32[16]{0:T(128)} %param.5) | copy-start | bytes 196
  36.0 9.2 %copy-start.2 = (bf16[6,4,4096]{2,1,0:T(4,128)(2,1)}, bf16[6,4,4096]{2,1,0:T(4,128)(2,1)S(1)}, u32[]{:S(2)}) copy-start(bf16[6,4,4096]{2,1,0:T(4,128)(2,1)S(1)} %collective-permute-done.9.refs_11_) | copy-start | bytes 589828
  36.0 4.8 %collective-permute-start.7 = (bf16[6,4,4096]{2,1,0:T(4,128)(2,1)S(1)}, bf16[6,4,4096]{2,1,0:T(4,128)(2,1)S(1)}, u32[]{:S(2)}, u32[]{:S(2)}) collective-permute-start(bf16[6,4,4096]{2,1,0:T(4,128)(2,1)S(1)} %maximum_bitcast_fusion.refs_3_.refs_4_), channel_id=1, source_target_pairs={{0,4},{4,0},{8,12},{12,8},{16,20},{20,16},{24,28},{28,24},{1,5},{5... | collective-permute-start | bytes 589832 | tf_op jit(solution)/shard_map/ppermute | solution.py:177
  36.0 9.2 %copy-start.3 = (bf16[6,4,4096]{2,1,0:T(4,128)(2,1)}, bf16[6,4,4096]{2,1,0:T(4,128)(2,1)S(1)}, u32[]{:S(2)}) copy-start(bf16[6,4,4096]{2,1,0:T(4,128)(2,1)S(1)} %collective-permute-done.8.refs_10_) | copy-start | bytes 589828
  36.0 9.2 %collective-permute-start.6 = (bf16[6,4,4096]{2,1,0:T(4,128)(2,1)S(1)}, bf16[6,4,4096]{2,1,0:T(4,128)(2,1)S(1)}, u32[]{:S(2)}, u32[]{:S(2)}) collective-permute-start(bf16[6,4,4096]{2,1,0:T(4,128)(2,1)S(1)} %maximum_bitcast_fusion.refs_3_.refs_4_), channel_id=1, source_target_pairs={{0,1},{1,0},{2,3},{3,2},{4,5},{5,4},{6,7},{7,6},{8,9},{9,8},{10,11... | collective-permute-start | bytes 589832 | tf_op jit(solution)/shard_map/ppermute | solution.py:163
  40.1 5.1 %copy-start.4 = (bf16[6,4,4096]{2,1,0:T(4,128)(2,1)}, bf16[6,4,4096]{2,1,0:T(4,128)(2,1)S(1)}, u32[]{:S(2)}) copy-start(bf16[6,4,4096]{2,1,0:T(4,128)(2,1)S(1)} %collective-permute-done.4.refs_9_) | copy-start | bytes 589828
  40.1 5.1 %collective-permute-start.5 = (bf16[6,4,4096]{2,1,0:T(4,128)(2,1)S(1)}, bf16[6,4,4096]{2,1,0:T(4,128)(2,1)S(1)}, u32[]{:S(2)}, u32[]{:S(2)}) collective-permute-start(bf16[6,4,4096]{2,1,0:T(4,128)(2,1)S(1)} %collective-permute-done.4.refs_9_), channel_id=1, source_target_pairs={{0,4},{4,0},{8,12},{12,8},{16,20},{20,16},{24,28},{28,24},{1,5},{5... | collective-permute-start | bytes 589832 | tf_op jit(solution)/shard_map/ppermute | solution.py:178
  40.1 5.1 %copy-start.5 = (bf16[6,4,4096]{2,1,0:T(4,128)(2,1)}, bf16[6,4,4096]{2,1,0:T(4,128)(2,1)S(1)}, u32[]{:S(2)}) copy-start(bf16[6,4,4096]{2,1,0:T(4,128)(2,1)S(1)} %collective-permute-done.2.refs_8_) | copy-start | bytes 589828
  40.1 5.1 %collective-permute-start.3 = (bf16[6,4,4096]{2,1,0:T(4,128)(2,1)S(1)}, bf16[6,4,4096]{2,1,0:T(4,128)(2,1)S(1)}, u32[]{:S(2)}, u32[]{:S(2)}) collective-permute-start(bf16[6,4,4096]{2,1,0:T(4,128)(2,1)S(1)} %collective-permute-done.2.refs_8_), channel_id=1, source_target_pairs={{0,4},{4,0},{8,12},{12,8},{16,20},{20,16},{24,28},{28,24},{1,5},{5... | collective-permute-start | bytes 589832 | tf_op jit(solution)/shard_map/ppermute | solution.py:178
  40.6 4.6 %copy-start.6 = (bf16[6,4,4096]{2,1,0:T(4,128)(2,1)}, bf16[6,4,4096]{2,1,0:T(4,128)(2,1)S(1)}, u32[]{:S(2)}) copy-start(bf16[6,4,4096]{2,1,0:T(4,128)(2,1)S(1)} %collective-permute-done.refs_7_) | copy-start | bytes 589828
  40.6 4.6 %collective-permute-start.1 = (bf16[6,4,4096]{2,1,0:T(4,128)(2,1)S(1)}, bf16[6,4,4096]{2,1,0:T(4,128)(2,1)S(1)}, u32[]{:S(2)}, u32[]{:S(2)}) collective-permute-start(bf16[6,4,4096]{2,1,0:T(4,128)(2,1)S(1)} %collective-permute-done.refs_7_), channel_id=1, source_target_pairs={{0,4},{4,0},{8,12},{12,8},{16,20},{20,16},{24,28},{28,24},{1,5},{5... | collective-permute-start | bytes 589832 | tf_op jit(solution)/shard_map/ppermute | solution.py:178
  40.8 4.5 %copy-start.7 = (bf16[6,4,4096]{2,1,0:T(4,128)(2,1)}, bf16[6,4,4096]{2,1,0:T(4,128)(2,1)S(1)}, u32[]{:S(2)}) copy-start(bf16[6,4,4096]{2,1,0:T(4,128)(2,1)S(1)} %collective-permute-done.7.refs_6_) | copy-start | bytes 589828
  45.2 0.7 %copy-start.8 = (bf16[6,4,4096]{2,1,0:T(4,128)(2,1)}, bf16[6,4,4096]{2,1,0:T(4,128)(2,1)S(1)}, u32[]{:S(2)}) copy-start(bf16[6,4,4096]{2,1,0:T(4,128)(2,1)S(1)} %collective-permute-done.6.refs_5_) | copy-start | bytes 589828
  45.2 0.7 %copy-start.9 = (bf16[6,4,4096]{2,1,0:T(4,128)(2,1)}, bf16[6,4,4096]{2,1,0:T(4,128)(2,1)S(1)}, u32[]{:S(2)}) copy-start(bf16[6,4,4096]{2,1,0:T(4,128)(2,1)S(1)} %collective-permute-done.5.refs_2_) | copy-start | bytes 589828
  45.2 0.8 %copy-start.10 = (bf16[6,4,4096]{2,1,0:T(4,128)(2,1)}, bf16[6,4,4096]{2,1,0:T(4,128)(2,1)S(1)}, u32[]{:S(2)}) copy-start(bf16[6,4,4096]{2,1,0:T(4,128)(2,1)S(1)} %collective-permute-done.3.refs_1_) | copy-start | bytes 589828
  46.0 0.7 %copy-start.11 = (bf16[6,4,4096]{2,1,0:T(4,128)(2,1)}, bf16[6,4,4096]{2,1,0:T(4,128)(2,1)S(1)}, u32[]{:S(2)}) copy-start(bf16[6,4,4096]{2,1,0:T(4,128)(2,1)S(1)} %collective-permute-done.1.refs_0_) | copy-start | bytes 589828

commit v8 on v6

--- a/solution.py
+++ b/solution.py
@@ -36,8 +36,8 @@
     in_ids = jnp.arange(in_block + tap_count, dtype=jnp.int32)[None, :, None]
     out_ids = jnp.arange(out_block, dtype=jnp.int32)[None, None, :]
     onehot = (in_ids == DECIM * out_ids + tap_count - tap_ids).astype(jnp.float32)
-    band_matrix = jnp.einsum("k,kij->ij", fir_taps, onehot, precision=lax.Precision.HIGHEST)
-    summed = jnp.einsum("swbi,ij->swbj", windows, band_matrix, precision=lax.Precision.HIGHEST)
+    band_matrix = jnp.einsum("k,kij->ij", fir_taps, onehot, precision=lax.Precision.HIGH)
+    summed = jnp.einsum("swbi,ij->swbj", windows, band_matrix, precision=lax.Precision.HIGH)
     return summed.reshape(lead_dims + (block_count * out_block,))
 
 
@@ -48,18 +48,18 @@
     lead_dims = decimated.shape[:-1]
     blocks = decimated.reshape(lead_dims + (first_len, second_len))
     cos_one, sin_one = angle_table(first_len, first_len, first_len, 0)
-    real_z = jnp.einsum("bwnq,fn->bwfq", blocks, cos_one, precision=lax.Precision.HIGHEST)
-    imag_z = -jnp.einsum("bwnq,fn->bwfq", blocks, sin_one, precision=lax.Precision.HIGHEST)
+    real_z = jnp.einsum("bwnq,fn->bwfq", blocks, cos_one, precision=lax.Precision.HIGH)
+    imag_z = -jnp.einsum("bwnq,fn->bwfq", blocks, sin_one, precision=lax.Precision.HIGH)
     cos_two, sin_two = angle_table(first_len, second_len, out_length, 0)
     real_t = real_z * cos_two + imag_z * sin_two
     imag_t = imag_z * cos_two - real_z * sin_two
     cos_three, sin_three = angle_table(second_len // 2, second_len, second_len, 0)
     real_x = jnp.einsum(
-        "bwfq,gq->bwgf", real_t, cos_three, precision=lax.Precision.HIGHEST
-    ) + jnp.einsum("bwfq,gq->bwgf", imag_t, sin_three, precision=lax.Precision.HIGHEST)
+        "bwfq,gq->bwgf", real_t, cos_three, precision=lax.Precision.HIGH
+    ) + jnp.einsum("bwfq,gq->bwgf", imag_t, sin_three, precision=lax.Precision.HIGH)
     imag_x = jnp.einsum(
-        "bwfq,gq->bwgf", imag_t, cos_three, precision=lax.Precision.HIGHEST
-    ) - jnp.einsum("bwfq,gq->bwgf", real_t, sin_three, precision=lax.Precision.HIGHEST)
+        "bwfq,gq->bwgf", imag_t, cos_three, precision=lax.Precision.HIGH
+    ) - jnp.einsum("bwfq,gq->bwgf", real_t, sin_three, precision=lax.Precision.HIGH)
     bin_count = out_length // 2
     return (real_x.reshape(lead_dims + (bin_count,)), imag_x.reshape(lead_dims + (bin_count,)))
 

time: 61.6 us -> 55.8 us (0.906)
  matrix products: 13.9 us -> 7.99 us
    dot_general x7, matrix products: 12.6 us -> 7.27 us  [the longest x1 1.31 us: spectrum(): jnp.einsum('bwfq,gq->bwgf', real_t, sin_three, precision=lax.Precision.HIGH)]
  transfers between devices with their start and end apart: 10 -> 10, of which waited for: 1 -> 2; matrix products, arithmetic and copies ran while one was open for 10% -> 11% of each run, Pallas kernels for 0% -> 0%
where the time goes in v8:
time: 55.8 us; the launch traced here: 55.6 us
  Pallas kernels  13.2 us (24%)
  waiting for transfers between devices  10 us (18%)
  starting transfers between devices  9.86 us (18%)
  matrix products  7.99 us (14%)
  other arithmetic  7.73 us (14%)
  local copies, waits for them, and re-layouts  6.48 us (12%)
    pallas_call x1, Pallas kernels, pair_block(): pl.pallas_call(functools.partial(cross_kernel, left_count, visit_count),...  13.2 us
    ppermute x3, waiting for transfers between devices, xor_gather(): pieces.append(lax.ppermute(block, axis_name, pairs))  10 us
    another operation x2, other arithmetic  4.73 us
    ppermute x3, starting transfers between devices, xor_gather(): pieces.append(lax.ppermute(block, axis_name, pairs))  4.67 us
    ppermute x3, starting transfers between devices, chip_gather(): fetched.append(lax.ppermute(block, axis_name, pairs))  4.61 us
    reshape x1, local copies, waits for them, and re-layouts, decimate(): blocks = records.reshape(lead_dims + (block_count, in_block))  1.68 us
    gather x1, local copies, waits for them, and re-layouts, on_device(): jnp.take(pair, visit_order, axis=1).reshape(group_rows, visit_count, LAGS)  1.51 us
    unnamed x27, local copies, waits for them, and re-layouts  1.51 us
  transfers between devices with their start and end apart: 10, of which 2 were waited for; matrix products, arithmetic and copies ran while one was open for 11% of the time, Pallas kernels for 0%

profile of v8, /device:TPU:0, one launch (start us, length us, event | category | flops | bytes accessed | tf_op | source)
XLA Modules:
  0.0 55.6 jit_solution(9305870597413097115)
XLA Ops:
  0.2 1.7 %reshape.190 = f32[4,6,32,256]{3,2,0,1:T(8,128)S(1)} reshape(f32[4,6,8192]{2,0,1:T(4,128)} %param.3) | data formatting | bytes 1572864 | tf_op jit(solution)/shard_map/reshape | solution.py:31
  2.1 0.7 %iota_compare_fusion = pred[32,288,128]{2,1,0:T(32,128)(4,1)S(1)} fusion(s32[32,128]{1,0:T(8,128)S(1)} %iota_subtract_fusion), kind=kLoop, calls=%fused_computation.2 | loop fusion | flops 1179648 | bytes 1196032 | tf_op jit(solution)/shard_map/eq | solution.py:38
  2.7 1.1 %fusion = f32[1,288,128]{2,0,1:T(1,128)S(1)} fusion(pred[32,288,128]{2,1,0:T(32,128)(4,1)S(1)} %iota_compare_fusion, f32[32]{0:T(128)S(1)} %copy-done), kind=kOutput, calls=%fused_computation.3 | convolution fusion | flops 7077888 | bytes 1327232 | tf_op jit(solution)/shard_map/k,kij->ij/dot_general | solution.py:39
  3.8 0.7 %fusion.4 = f32[4,6,32,128]{3,2,1,0:T(8,128)S(1)} fusion(f32[288,128,1,1]{1,0,3,2:T(8,128)S(1)} %bitcast.82, f32[4,6,31,32]{3,2,1,0:T(8,128)S(1)} %copy.33, f32[4,6,32,256]{3,2,0,1:T(8,128)S(1)} %reshape.190), kind=kOutput, calls=%fused_computation.14 | convolution fusion | flops 170532864 | bytes 1422336 | tf_op jit(solution)/shard_map/swbi,ij->swbj/dot_general | solution.py:40
  4.7 0.6 %convolution_negate_fusion = f32[64,4,6,64]{3,0,2,1:T(8,128)S(1)} fusion(f32[4,6,64,64]{3,2,1,0:T(8,128)S(1)} %reshape_reshape.4), kind=kOutput, calls=%fused_computation.8 | convolution fusion | flops 37904384 | bytes 786432 | tf_op jit(solution)/shard_map/bwnq,fn->bwfq/dot_general | solution.py:52
  5.3 0.6 %fusion.26 = f32[64,4,6,64]{3,0,2,1:T(8,128)S(1)} fusion(f32[4,6,64,64]{3,2,1,0:T(8,128)S(1)} %reshape_reshape.4), kind=kOutput, calls=%fused_computation.53 | convolution fusion | flops 37806080 | bytes 786432 | tf_op jit(solution)/shard_map/bwnq,fn->bwfq/dot_general | solution.py:51
  6.0 1.2 %fusion.13 = f32[32,4,6,64]{3,0,2,1:T(8,128)S(1)} fusion(f32[64,4,6,64]{3,0,2,1:T(8,128)S(1)} %fusion.26, f32[64,4,6,64]{3,0,2,1:T(8,128)S(1)} %convolution_negate_fusion, f32[64,64]{1,0:T(8,128)S(1)} %get-tuple-element.11, f32[64,64]{1,0:T(8,128)S(1)} %get-tuple-element.12), kind=kOutput, calls=%fused_computation.27 | convolution fusion | flops 19197952 | bytes 1015808 | tf_op jit(solution)/shard_map/bwfq,gq->bwgf/dot_general | solution.py:60
  7.2 1.2 %fusion.17 = f32[32,4,6,64]{3,0,2,1:T(8,128)S(1)} fusion(f32[64,4,6,64]{3,0,2,1:T(8,128)S(1)} %convolution_negate_fusion, f32[64,4,6,64]{3,0,2,1:T(8,128)S(1)} %fusion.26, f32[64,64]{1,0:T(8,128)S(1)} %get-tuple-element.11, f32[64,64]{1,0:T(8,128)S(1)} %get-tuple-element.12), kind=kOutput, calls=%fused_computation.31 | convolution fusion | flops 19197952 | bytes 1015808 | tf_op jit(solution)/shard_map/bwfq,gq->bwgf/dot_general | solution.py:57
  8.4 1.2 %fusion.3 = f32[4,6,32,64]{3,2,1,0:T(8,128)S(1)} fusion(f32[32,4,6,64]{3,0,2,1:T(8,128)S(1)} %fusion.17, f32[64,4,6,64]{3,0,2,1:T(8,128)S(1)} %fusion.26, f32[64,4,6,64]{3,0,2,1:T(8,128)S(1)} %convolution_negate_fusion, f32[64,64]{1,0:T(8,128)S(1)} %get-tuple-element.11, f32[64,64]{1,0:T(8,128)S(1)} %get-tuple-element.12), kind=kOutput, calls=%fused_computation.12 | convolution fusion | flops 19247104 | bytes 1212416 | tf_op jit(solution)/shard_map/bwfq,gq->bwgf/dot_general | solution.py:59
  9.6 1.3 %add_reduce_fusion = (f32[4,6,32]{2,1,0:T(8,128)S(1)}, f32[4,6,32,64]{3,2,1,0:T(8,128)S(1)}) fusion(f32[4,6,32,64]{3,2,1,0:T(8,128)S(1)} %fusion.3, f32[32,4,6,64]{3,0,2,1:T(8,128)S(1)} %fusion.13, f32[64,4,6,64]{3,0,2,1:T(8,128)S(1)} %convolution_negate_fusion, f32[64,64]{1,0:T(8,128)S(1)} %get-tuple-element.11, f32[64,4,6,64]{3,0,2,1:T(8,128)S(1)} %fusion.26, ...), kind=kOutput, calls=%fused_computation.39 | convolution fusion | flops 19442944 | bytes 1412096 | tf_op jit(solution)/shard_map/bwfq,gq->bwgf/dot_general | solution.py:62
  11.8 4.0 %collective-permute-start.8 = (bf16[6,4,4096]{2,1,0:T(4,128)(2,1)S(1)}, bf16[6,4,4096]{2,1,0:T(4,128)(2,1)S(1)}, u32[]{:S(2)}, u32[]{:S(2)}) collective-permute-start(bf16[6,4,4096]{2,1,0:T(4,128)(2,1)S(1)} %maximum_bitcast_fusion.refs_0_.refs_4_), channel_id=1, source_target_pairs={{0,24},{4,28},{8,16},{12,20},{16,8},{20,12},{24,0},{28,4},{1,25},{... | collective-permute-start | bytes 589832 | tf_op jit(solution)/shard_map/ppermute | solution.py:175
  15.8 0.5 collective-permute-start.6
  16.4 4.0 %collective-permute-start.2 = (bf16[6,4,4096]{2,1,0:T(4,128)(2,1)S(1)}, bf16[6,4,4096]{2,1,0:T(4,128)(2,1)S(1)}, u32[]{:S(2)}, u32[]{:S(2)}) collective-permute-start(bf16[6,4,4096]{2,1,0:T(4,128)(2,1)S(1)} %maximum_bitcast_fusion.refs_0_.refs_4_), channel_id=1, source_target_pairs={{0,3},{1,2},{2,1},{3,0},{4,7},{5,6},{6,5},{7,4},{8,11},{9,10},{10,... | collective-permute-start | bytes 589832 | tf_op jit(solution)/shard_map/ppermute | solution.py:163
  20.8 4.6 %cosine_convert_fusion = (bf16[2048,128]{1,0:T(8,128)(2,1)S(1)}, bf16[2048,128]{1,0:T(8,128)(2,1)S(1)}) fusion(s32[128]{0:T(128)S(1)} %iota_add_fusion), kind=kLoop, calls=%fused_computation.23 | loop fusion | flops 4194304 | bytes 1049088 | tf_op jit(solution)/shard_map/convert
  25.4 1.1 %pad_maximum_fusion.refs_12_ = bf16[4096,128]{1,0:T(8,128)(2,1)} fusion(bf16[2048,128]{1,0:T(8,128)(2,1)S(1)} %get-tuple-element.8, bf16[2048,128]{1,0:T(8,128)(2,1)S(1)} %get-tuple-element.7), kind=kLoop, calls=%fused_computation.21 | loop fusion | flops 2097152 | bytes 2097152 | tf_op jit(solution)/shard_map/concatenate | solution.py:198
  26.6 0.6 %collective-permute-start = (bf16[6,4,4096]{2,1,0:T(4,128)(2,1)S(1)}, bf16[6,4,4096]{2,1,0:T(4,128)(2,1)S(1)}, u32[]{:S(2)}, u32[]{:S(2)}) collective-permute-start(bf16[6,4,4096]{2,1,0:T(4,128)(2,1)S(1)} %maximum_bitcast_fusion.refs_0_.refs_4_), channel_id=1, source_target_pairs={{0,1},{1,0},{2,3},{3,2},{4,5},{5,4},{6,7},{7,6},{8,9},{9,8},{10,11... | collective-permute-start | bytes 589832 | tf_op jit(solution)/shard_map/ppermute | solution.py:163
  27.2 0.5 collective-permute-start.7
  27.9 10.0 %collective-permute-done.1.refs_2_ = bf16[6,4,4096]{2,1,0:T(4,128)(2,1)S(1)} collective-permute-done((bf16[6,4,4096]{2,1,0:T(4,128)(2,1)S(1)}, bf16[6,4,4096]{2,1,0:T(4,128)(2,1)S(1)}, u32[]{:S(2)}, u32[]{:S(2)}) %collective-permute-start.1) | collective-permute-done | bytes 196640 | tf_op jit(solution)/shard_map/ppermute | solution.py:163
  38.0 0.5 copy-done.7
  38.8 0.7 %copy-done.11 = bf16[6,4,4096]{2,1,0:T(4,128)(2,1)} copy-done((bf16[6,4,4096]{2,1,0:T(4,128)(2,1)}, bf16[6,4,4096]{2,1,0:T(4,128)(2,1)S(1)}, u32[]{:S(2)}) %copy-start.11) | copy-done | bytes 196632
  39.4 13.2 %shard_map.37 = f32[512,128]{1,0:T(8,128)} custom-call(bf16[6,4,4096]{2,1,0:T(4,128)(2,1)} %copy-done.1, bf16[6,4,4096]{2,1,0:T(4,128)(2,1)} %copy-done.8, bf16[6,4,4096]{2,1,0:T(4,128)(2,1)} %copy-done.7, bf16[6,4,4096]{2,1,0:T(4,128)(2,1)} %copy-done.6, bf16[6,4,4096]{2,1,0:T(4,128)(2,1)} %copy-done.1, bf16[6,4,4096]{2,1,0:T(4,128)(2,1)} %copy-done.5, ...), custom_call_target="tpu_custom_call" | custom-call | flops 587202560 | bytes 3670016 | tf_op jit(solution)/shard_map/pallas_call | solution.py:137
  52.6 1.5 %gather_fusion = f32[8,16,4,128]{3,1,2,0:T(8,128)S(1)} fusion(f32[16,8,4,128]{3,0,2,1:T(8,128)} %bitcast.79, s32[1024]{0:T(1024)S(1)} %pad_clamp_fusion.1), kind=kCustom, calls=%fused_computation | custom fusion | bytes 524320 | tf_op jit(solution)/shard_map/jit(_take)/gather | solution.py:206
  54.2 0.6 %gather_fusion.1 = f32[4,4,32,128]{3,2,1,0:T(8,128)S(1)} fusion(f32[4,4,32,128]{3,2,1,0:T(8,128)S(1)} %copy_select_fusion, s32[1024]{0:T(1024)S(1)} %pad_clamp_fusion), kind=kCustom, calls=%fused_computation.1 | custom fusion | bytes 524304 | tf_op jit(solution)/shard_map/jit(_take)/gather | solution.py:209
  54.8 0.8 %multiply_select_fusion = f32[16,1,32,128]{3,2,1,0:T(8,128)} fusion(f32[16,1,32,128]{3,2,1,0:T(8,128)S(1)} %bitcast.80, pred[16]{0:T(512)(128)(4,1)S(1)} %broadcast_in_dim.63, pred[16,128]{1,0:T(8,128)(4,1)S(1)} %broadcast_compare_fusion), kind=kLoop, calls=%fused_computation.41 | loop fusion | flops 196608 | bytes 526352 | tf_op jit(solution)/shard_map/jit(_where)/select_n | solution.py:214
  (65 shorter events, 2.5 us)
Async XLA Ops:
  0.0 2.7 %copy-start = (f32[32]{0:T(128)S(1)}, f32[32]{0:T(128)}, u32[]{:S(2)}) copy-start(f32[32]{0:T(128)} %param.4) | copy-start | bytes 388
  11.8 14.8 %copy-start.1 = (bf16[6,4,4096]{2,1,0:T(4,128)(2,1)}, bf16[6,4,4096]{2,1,0:T(4,128)(2,1)S(1)}, u32[]{:S(2)}) copy-start(bf16[6,4,4096]{2,1,0:T(4,128)(2,1)S(1)} %maximum_bitcast_fusion.refs_0_.refs_4_) | copy-start | bytes 589828
  11.8 14.7 %collective-permute-start.8 = (bf16[6,4,4096]{2,1,0:T(4,128)(2,1)S(1)}, bf16[6,4,4096]{2,1,0:T(4,128)(2,1)S(1)}, u32[]{:S(2)}, u32[]{:S(2)}) collective-permute-start(bf16[6,4,4096]{2,1,0:T(4,128)(2,1)S(1)} %maximum_bitcast_fusion.refs_0_.refs_4_), channel_id=1, source_target_pairs={{0,24},{4,28},{8,16},{12,20},{16,8},{20,12},{24,0},{28,4},{1,25},{... | collective-permute-start | bytes 589832 | tf_op jit(solution)/shard_map/ppermute | solution.py:175
  15.8 10.8 %collective-permute-start.6 = (bf16[6,4,4096]{2,1,0:T(4,128)(2,1)S(1)}, bf16[6,4,4096]{2,1,0:T(4,128)(2,1)S(1)}, u32[]{:S(2)}, u32[]{:S(2)}) collective-permute-start(bf16[6,4,4096]{2,1,0:T(4,128)(2,1)S(1)} %maximum_bitcast_fusion.refs_0_.refs_4_), channel_id=1, source_target_pairs={{0,16},{4,20},{8,24},{12,28},{16,0},{20,4},{24,8},{28,12},{1,17},{... | collective-permute-start | bytes 589832 | tf_op jit(solution)/shard_map/ppermute | solution.py:175
  16.3 10.9 %collective-permute-start.4 = (bf16[6,4,4096]{2,1,0:T(4,128)(2,1)S(1)}, bf16[6,4,4096]{2,1,0:T(4,128)(2,1)S(1)}, u32[]{:S(2)}, u32[]{:S(2)}) collective-permute-start(bf16[6,4,4096]{2,1,0:T(4,128)(2,1)S(1)} %maximum_bitcast_fusion.refs_0_.refs_4_), channel_id=1, source_target_pairs={{0,8},{4,12},{8,0},{12,4},{16,24},{20,28},{24,16},{28,20},{1,9},{5... | collective-permute-start | bytes 589832 | tf_op jit(solution)/shard_map/ppermute | solution.py:175
  16.4 10.8 %collective-permute-start.3 = (bf16[6,4,4096]{2,1,0:T(4,128)(2,1)S(1)}, bf16[6,4,4096]{2,1,0:T(4,128)(2,1)S(1)}, u32[]{:S(2)}, u32[]{:S(2)}) collective-permute-start(bf16[6,4,4096]{2,1,0:T(4,128)(2,1)S(1)} %maximum_bitcast_fusion.refs_0_.refs_4_), channel_id=1, source_target_pairs={{0,4},{4,0},{8,12},{12,8},{16,20},{20,16},{24,28},{28,24},{1,5},{5... | collective-permute-start | bytes 589832 | tf_op jit(solution)/shard_map/ppermute | solution.py:177
  16.4 11.3 %collective-permute-start.2 = (bf16[6,4,4096]{2,1,0:T(4,128)(2,1)S(1)}, bf16[6,4,4096]{2,1,0:T(4,128)(2,1)S(1)}, u32[]{:S(2)}, u32[]{:S(2)}) collective-permute-start(bf16[6,4,4096]{2,1,0:T(4,128)(2,1)S(1)} %maximum_bitcast_fusion.refs_0_.refs_4_), channel_id=1, source_target_pairs={{0,3},{1,2},{2,1},{3,0},{4,7},{5,6},{6,5},{7,4},{8,11},{9,10},{10,... | collective-permute-start | bytes 589832 | tf_op jit(solution)/shard_map/ppermute | solution.py:163
  25.4 2.4 %copy-start.12 = (s32[16]{0:T(128)S(1)}, s32[16]{0:T(128)}, u32[]{:S(2)}) copy-start(s32[16]{0:T(128)} %param.5) | copy-start | bytes 196
  26.5 11.5 %copy-start.2 = (bf16[6,4,4096]{2,1,0:T(4,128)(2,1)}, bf16[6,4,4096]{2,1,0:T(4,128)(2,1)S(1)}, u32[]{:S(2)}) copy-start(bf16[6,4,4096]{2,1,0:T(4,128)(2,1)S(1)} %collective-permute-done.8.refs_10_) | copy-start | bytes 589828
  26.5 11.4 %collective-permute-start.1 = (bf16[6,4,4096]{2,1,0:T(4,128)(2,1)S(1)}, bf16[6,4,4096]{2,1,0:T(4,128)(2,1)S(1)}, u32[]{:S(2)}, u32[]{:S(2)}) collective-permute-start(bf16[6,4,4096]{2,1,0:T(4,128)(2,1)S(1)} %maximum_bitcast_fusion.refs_0_.refs_4_), channel_id=1, source_target_pairs={{0,2},{1,3},{2,0},{3,1},{4,6},{5,7},{6,4},{7,5},{8,10},{9,11},{10,... | collective-permute-start | bytes 589832 | tf_op jit(solution)/shard_map/ppermute | solution.py:163
  26.6 11.4 %copy-start.3 = (bf16[6,4,4096]{2,1,0:T(4,128)(2,1)}, bf16[6,4,4096]{2,1,0:T(4,128)(2,1)S(1)}, u32[]{:S(2)}) copy-start(bf16[6,4,4096]{2,1,0:T(4,128)(2,1)S(1)} %collective-permute-done.6.refs_8_) | copy-start | bytes 589828
  26.6 11.3 %collective-permute-start = (bf16[6,4,4096]{2,1,0:T(4,128)(2,1)S(1)}, bf16[6,4,4096]{2,1,0:T(4,128)(2,1)S(1)}, u32[]{:S(2)}, u32[]{:S(2)}) collective-permute-start(bf16[6,4,4096]{2,1,0:T(4,128)(2,1)S(1)} %maximum_bitcast_fusion.refs_0_.refs_4_), channel_id=1, source_target_pairs={{0,1},{1,0},{2,3},{3,2},{4,5},{5,4},{6,7},{7,6},{8,9},{9,8},{10,11... | collective-permute-start | bytes 589832 | tf_op jit(solution)/shard_map/ppermute | solution.py:163
  27.2 10.8 %copy-start.4 = (bf16[6,4,4096]{2,1,0:T(4,128)(2,1)}, bf16[6,4,4096]{2,1,0:T(4,128)(2,1)S(1)}, u32[]{:S(2)}) copy-start(bf16[6,4,4096]{2,1,0:T(4,128)(2,1)S(1)} %collective-permute-done.4.refs_6_) | copy-start | bytes 589828
  27.2 10.7 %collective-permute-start.9 = (bf16[6,4,4096]{2,1,0:T(4,128)(2,1)S(1)}, bf16[6,4,4096]{2,1,0:T(4,128)(2,1)S(1)}, u32[]{:S(2)}, u32[]{:S(2)}) collective-permute-start(bf16[6,4,4096]{2,1,0:T(4,128)(2,1)S(1)} %collective-permute-done.8.refs_10_), channel_id=1, source_target_pairs={{0,4},{4,0},{8,12},{12,8},{16,20},{20,16},{24,28},{28,24},{1,5},{5... | collective-permute-start | bytes 589832 | tf_op jit(solution)/shard_map/ppermute | solution.py:178
  27.2 10.8 %copy-start.5 = (bf16[6,4,4096]{2,1,0:T(4,128)(2,1)}, bf16[6,4,4096]{2,1,0:T(4,128)(2,1)S(1)}, u32[]{:S(2)}) copy-start(bf16[6,4,4096]{2,1,0:T(4,128)(2,1)S(1)} %collective-permute-done.3.refs_5_) | copy-start | bytes 589828
  27.2 10.7 %collective-permute-start.7 = (bf16[6,4,4096]{2,1,0:T(4,128)(2,1)S(1)}, bf16[6,4,4096]{2,1,0:T(4,128)(2,1)S(1)}, u32[]{:S(2)}, u32[]{:S(2)}) collective-permute-start(bf16[6,4,4096]{2,1,0:T(4,128)(2,1)S(1)} %collective-permute-done.6.refs_8_), channel_id=1, source_target_pairs={{0,4},{4,0},{8,12},{12,8},{16,20},{20,16},{24,28},{28,24},{1,5},{5... | collective-permute-start | bytes 589832 | tf_op jit(solution)/shard_map/ppermute | solution.py:178
  27.7 10.3 %copy-start.6 = (bf16[6,4,4096]{2,1,0:T(4,128)(2,1)}, bf16[6,4,4096]{2,1,0:T(4,128)(2,1)S(1)}, u32[]{:S(2)}) copy-start(bf16[6,4,4096]{2,1,0:T(4,128)(2,1)S(1)} %collective-permute-done.2.refs_3_) | copy-start | bytes 589828
  27.7 10.2 %collective-permute-start.5 = (bf16[6,4,4096]{2,1,0:T(4,128)(2,1)S(1)}, bf16[6,4,4096]{2,1,0:T(4,128)(2,1)S(1)}, u32[]{:S(2)}, u32[]{:S(2)}) collective-permute-start(bf16[6,4,4096]{2,1,0:T(4,128)(2,1)S(1)} %collective-permute-done.4.refs_6_), channel_id=1, source_target_pairs={{0,4},{4,0},{8,12},{12,8},{16,20},{20,16},{24,28},{28,24},{1,5},{5... | collective-permute-start | bytes 589832 | tf_op jit(solution)/shard_map/ppermute | solution.py:178
  37.8 0.7 %copy-start.7 = (bf16[6,4,4096]{2,1,0:T(4,128)(2,1)}, bf16[6,4,4096]{2,1,0:T(4,128)(2,1)S(1)}, u32[]{:S(2)}) copy-start(bf16[6,4,4096]{2,1,0:T(4,128)(2,1)S(1)} %collective-permute-done.1.refs_2_) | copy-start | bytes 589828
  37.9 0.7 %copy-start.8 = (bf16[6,4,4096]{2,1,0:T(4,128)(2,1)}, bf16[6,4,4096]{2,1,0:T(4,128)(2,1)S(1)}, u32[]{:S(2)}) copy-start(bf16[6,4,4096]{2,1,0:T(4,128)(2,1)S(1)} %collective-permute-done.refs_1_) | copy-start | bytes 589828
  37.9 0.8 %copy-start.9 = (bf16[6,4,4096]{2,1,0:T(4,128)(2,1)}, bf16[6,4,4096]{2,1,0:T(4,128)(2,1)S(1)}, u32[]{:S(2)}) copy-start(bf16[6,4,4096]{2,1,0:T(4,128)(2,1)S(1)} %collective-permute-done.9.refs_11_) | copy-start | bytes 589828
  37.9 0.8 %copy-start.10 = (bf16[6,4,4096]{2,1,0:T(4,128)(2,1)}, bf16[6,4,4096]{2,1,0:T(4,128)(2,1)S(1)}, u32[]{:S(2)}) copy-start(bf16[6,4,4096]{2,1,0:T(4,128)(2,1)S(1)} %collective-permute-done.7.refs_9_) | copy-start | bytes 589828
  38.8 0.7 %copy-start.11 = (bf16[6,4,4096]{2,1,0:T(4,128)(2,1)}, bf16[6,4,4096]{2,1,0:T(4,128)(2,1)S(1)}, u32[]{:S(2)}) copy-start(bf16[6,4,4096]{2,1,0:T(4,128)(2,1)S(1)} %collective-permute-done.5.refs_7_) | copy-start | bytes 589828

commit v9 on v8

--- a/solution.py
+++ b/solution.py
@@ -165,6 +165,22 @@
     return pieces, order
 
 
+def line_gather(block, axis_name, size):
+    if size != 4:
+        return xor_gather(block, axis_name, size)
+    outer = lax.ppermute(block, axis_name, [(0, 1), (1, 0), (2, 3), (3, 2)])
+    middle = lax.ppermute(block, axis_name, [(1, 2), (2, 1)])
+    outward = lax.ppermute(middle, axis_name, [(1, 0), (2, 3)])
+    inward = lax.ppermute(outer, axis_name, [(1, 2), (2, 1)])
+    last = lax.ppermute(inward, axis_name, [(1, 0), (2, 3)])
+    me = lax.axis_index(axis_name)
+    is_end = (me == 0) | (me == size - 1)
+    third = jnp.where(is_end, outward, middle)
+    fourth = jnp.where(is_end, last, inward)
+    table = jnp.array([[0, 1, 2, 3], [1, 0, 2, 3], [3, 2, 0, 1], [3, 2, 1, 0]], jnp.int32)
+    return [block, outer, third, fourth], table[me]
+
+
 def chip_gather(block, axis_name, size):
     if size < 4 or size & (size - 1):
         return xor_gather(block, axis_name, size)
@@ -193,7 +209,7 @@
     white_by_window = jnp.moveaxis(white, 1, 0)
     col_size = lax.axis_size("col")
     row_size = lax.axis_size("row")
-    left_by_window, left_order = xor_gather(white_by_window, "col", col_size)
+    left_by_window, left_order = line_gather(white_by_window, "col", col_size)
     cos_lag, sin_lag = angle_table(LAGS, bin_count, out_length, -LH)
     lag_table = jnp.concatenate([cos_lag.T, sin_lag.T], axis=0).astype(jnp.bfloat16)
     group_rows = sum(piece.shape[1] for piece in left_by_window)

time: 55.8 us -> 62.7 us (1.12)
  starting transfers between devices: 9.86 us -> 14.2 us
  waiting for transfers between devices: 10 us -> 11.8 us
  other arithmetic: 7.73 us -> 8.99 us
  local copies, waits for them, and re-layouts: 6.48 us -> 5.84 us
    ppermute x3 -> x5, starting transfers between devices: 4.67 us -> 8.94 us  [the longest x1 4.85 us: line_gather(): outer = lax.ppermute(block, axis_name, [(0, 1), (1, 0), (2, 3), (3, 2)])]
    ppermute x3 -> x5, waiting for transfers between devices: 10 us -> 11.8 us  [the longest x1 7.02 us: line_gather(): last = lax.ppermute(inward, axis_name, [(1, 0), (2, 3)])]
    select_n x0 -> x2, other arithmetic: none -> 1.42 us  [the longest x1 0.71 us: line_gather(): third = jnp.where(is_end, outward, middle)]
    unnamed x27 -> x25, local copies, waits for them, and re-layouts: 1.51 us -> 0.88 us
  transfers between devices with their start and end apart: 10 -> 12, of which waited for: 2 -> 2; matrix products, arithmetic and copies ran while one was open for 11% -> 12% of each run, Pallas kernels for 0% -> 0%
where the time goes in v9:
time: 62.7 us; the launch traced here: 62.4 us
  starting transfers between devices  14.2 us (23%)
  Pallas kernels  13.2 us (21%)
  waiting for transfers between devices  11.8 us (19%)
  other arithmetic  8.99 us (14%)
  matrix products  7.99 us (13%)
  local copies, waits for them, and re-layouts  5.84 us (9%)
    pallas_call x1, Pallas kernels, pair_block(): pl.pallas_call(functools.partial(cross_kernel, left_count, visit_count),...  13.2 us
    ppermute x1, waiting for transfers between devices, line_gather(): last = lax.ppermute(inward, axis_name, [(1, 0), (2, 3)])  7.02 us
    ppermute x1, starting transfers between devices, line_gather(): outer = lax.ppermute(block, axis_name, [(0, 1), (1, 0), (2, 3), (3, 2)])  4.85 us
    ppermute x1, waiting for transfers between devices, line_gather(): outward = lax.ppermute(middle, axis_name, [(1, 0), (2, 3)])  4.78 us
    ppermute x3, starting transfers between devices, chip_gather(): fetched.append(lax.ppermute(block, axis_name, pairs))  4.61 us
    another operation x2, other arithmetic  4.54 us
    reshape x1, local copies, waits for them, and re-layouts, decimate(): blocks = records.reshape(lead_dims + (block_count, in_block))  1.68 us
    gather x1, local copies, waits for them, and re-layouts, on_device(): jnp.take(pair, visit_order, axis=1).reshape(group_rows, visit_count, LAGS)  1.51 us
  transfers between devices with their start and end apart: 12, of which 2 were waited for; matrix products, arithmetic and copies ran while one was open for 12% of the time, Pallas kernels for 0%

profile of v9, /device:TPU:0, one launch (start us, length us, event | category | flops | bytes accessed | tf_op | source)
XLA Modules:
  0.0 62.4 jit_solution(1259109378460237618)
XLA Ops:
  0.2 1.7 %reshape.203 = f32[4,6,32,256]{3,2,0,1:T(8,128)S(1)} reshape(f32[4,6,8192]{2,0,1:T(4,128)} %param.4) | data formatting | bytes 1572864 | tf_op jit(solution)/shard_map/reshape | solution.py:31
  2.1 0.7 %iota_compare_fusion = pred[32,288,128]{2,1,0:T(32,128)(4,1)S(1)} fusion(s32[32,128]{1,0:T(8,128)S(1)} %iota_subtract_fusion), kind=kLoop, calls=%fused_computation.2 | loop fusion | flops 1179648 | bytes 1196032 | tf_op jit(solution)/shard_map/eq | solution.py:38
  2.7 1.1 %fusion = f32[1,288,128]{2,0,1:T(1,128)S(1)} fusion(pred[32,288,128]{2,1,0:T(32,128)(4,1)S(1)} %iota_compare_fusion, f32[32]{0:T(128)S(1)} %copy-done), kind=kOutput, calls=%fused_computation.3 | convolution fusion | flops 7077888 | bytes 1327232 | tf_op jit(solution)/shard_map/k,kij->ij/dot_general | solution.py:39
  3.8 0.7 %fusion.4 = f32[4,6,32,128]{3,2,1,0:T(8,128)S(1)} fusion(f32[288,128,1,1]{1,0,3,2:T(8,128)S(1)} %bitcast.98, f32[4,6,31,32]{3,2,1,0:T(8,128)S(1)} %copy.34, f32[4,6,32,256]{3,2,0,1:T(8,128)S(1)} %reshape.203), kind=kOutput, calls=%fused_computation.14 | convolution fusion | flops 170532864 | bytes 1422336 | tf_op jit(solution)/shard_map/swbi,ij->swbj/dot_general | solution.py:40
  4.7 0.6 convolution_negate_fusion
  6.0 1.2 %fusion.13 = f32[32,4,6,64]{3,0,2,1:T(8,128)S(1)} fusion(f32[64,4,6,64]{3,0,2,1:T(8,128)S(1)} %fusion.26, f32[64,4,6,64]{3,0,2,1:T(8,128)S(1)} %convolution_negate_fusion, f32[64,64]{1,0:T(8,128)S(1)} %get-tuple-element.11, f32[64,64]{1,0:T(8,128)S(1)} %get-tuple-element.12), kind=kOutput, calls=%fused_computation.27 | convolution fusion | flops 19197952 | bytes 1015808 | tf_op jit(solution)/shard_map/bwfq,gq->bwgf/dot_general | solution.py:60
  7.2 1.2 %fusion.17 = f32[32,4,6,64]{3,0,2,1:T(8,128)S(1)} fusion(f32[64,4,6,64]{3,0,2,1:T(8,128)S(1)} %convolution_negate_fusion, f32[64,4,6,64]{3,0,2,1:T(8,128)S(1)} %fusion.26, f32[64,64]{1,0:T(8,128)S(1)} %get-tuple-element.11, f32[64,64]{1,0:T(8,128)S(1)} %get-tuple-element.12), kind=kOutput, calls=%fused_computation.31 | convolution fusion | flops 19197952 | bytes 1015808 | tf_op jit(solution)/shard_map/bwfq,gq->bwgf/dot_general | solution.py:57
  8.4 1.2 %fusion.3 = f32[4,6,32,64]{3,2,1,0:T(8,128)S(1)} fusion(f32[32,4,6,64]{3,0,2,1:T(8,128)S(1)} %fusion.17, f32[64,4,6,64]{3,0,2,1:T(8,128)S(1)} %fusion.26, f32[64,4,6,64]{3,0,2,1:T(8,128)S(1)} %convolution_negate_fusion, f32[64,64]{1,0:T(8,128)S(1)} %get-tuple-element.11, f32[64,64]{1,0:T(8,128)S(1)} %get-tuple-element.12), kind=kOutput, calls=%fused_computation.12 | convolution fusion | flops 19247104 | bytes 1212416 | tf_op jit(solution)/shard_map/bwfq,gq->bwgf/dot_general | solution.py:59
  9.6 1.3 %add_reduce_fusion = (f32[4,6,32]{2,1,0:T(8,128)S(1)}, f32[4,6,32,64]{3,2,1,0:T(8,128)S(1)}) fusion(f32[4,6,32,64]{3,2,1,0:T(8,128)S(1)} %fusion.3, f32[32,4,6,64]{3,0,2,1:T(8,128)S(1)} %fusion.13, f32[64,4,6,64]{3,0,2,1:T(8,128)S(1)} %convolution_negate_fusion, f32[64,64]{1,0:T(8,128)S(1)} %get-tuple-element.11, f32[64,4,6,64]{3,0,2,1:T(8,128)S(1)} %fusion.26, ...), kind=kOutput, calls=%fused_computation.39 | convolution fusion | flops 19442944 | bytes 1412096 | tf_op jit(solution)/shard_map/bwfq,gq->bwgf/dot_general | solution.py:62
  11.8 4.0 %collective-permute-start.10 = (bf16[6,4,4096]{2,1,0:T(4,128)(2,1)S(1)}, bf16[6,4,4096]{2,1,0:T(4,128)(2,1)S(1)}, u32[]{:S(2)}, u32[]{:S(2)}) collective-permute-start(bf16[6,4,4096]{2,1,0:T(4,128)(2,1)S(1)} %maximum_bitcast_fusion.refs_0_.refs_4_), channel_id=1, source_target_pairs={{0,24},{4,28},{8,16},{12,20},{16,8},{20,12},{24,0},{28,4},{1,25},{... | collective-permute-start | bytes 589832 | tf_op jit(solution)/shard_map/ppermute | solution.py:191
  16.4 0.7 %collective-permute-start.1 = (bf16[6,4,4096]{2,1,0:T(4,128)(2,1)S(1)}, bf16[6,4,4096]{2,1,0:T(4,128)(2,1)S(1)}, u32[]{:S(2)}, u32[]{:S(2)}) collective-permute-start(bf16[6,4,4096]{2,1,0:T(4,128)(2,1)S(1)} %maximum_bitcast_fusion.refs_0_.refs_4_), channel_id=1, source_target_pairs={{1,2},{2,1},{5,6},{6,5},{9,10},{10,9},{13,14},{14,13},{17,18},{18,... | collective-permute-start | bytes 589832 | tf_op jit(solution)/shard_map/ppermute | solution.py:172
  17.1 4.9 %collective-permute-start = (bf16[6,4,4096]{2,1,0:T(4,128)(2,1)S(1)}, bf16[6,4,4096]{2,1,0:T(4,128)(2,1)S(1)}, u32[]{:S(2)}, u32[]{:S(2)}) collective-permute-start(bf16[6,4,4096]{2,1,0:T(4,128)(2,1)S(1)} %maximum_bitcast_fusion.refs_0_.refs_4_), channel_id=1, source_target_pairs={{0,1},{1,0},{2,3},{3,2},{4,5},{5,4},{6,7},{7,6},{8,9},{9,8},{10,11... | collective-permute-start | bytes 589832 | tf_op jit(solution)/shard_map/ppermute | solution.py:171
  22.4 4.4 %cosine_convert_fusion = (bf16[2048,128]{1,0:T(8,128)(2,1)S(1)}, bf16[2048,128]{1,0:T(8,128)(2,1)S(1)}) fusion(s32[128]{0:T(128)S(1)} %iota_add_fusion), kind=kLoop, calls=%fused_computation.23 | loop fusion | flops 4194304 | bytes 1049088 | tf_op jit(solution)/shard_map/convert
  26.8 1.1 %pad_maximum_fusion.refs_12_ = bf16[4096,128]{1,0:T(8,128)(2,1)} fusion(bf16[2048,128]{1,0:T(8,128)(2,1)S(1)} %get-tuple-element.8, bf16[2048,128]{1,0:T(8,128)(2,1)S(1)} %get-tuple-element.7), kind=kLoop, calls=%fused_computation.21 | loop fusion | flops 2097152 | bytes 2097152 | tf_op jit(solution)/shard_map/concatenate | solution.py:214
  27.9 1.3 %collective-permute-start.2 = (bf16[6,4,4096]{2,1,0:T(4,128)(2,1)S(1)}, bf16[6,4,4096]{2,1,0:T(4,128)(2,1)S(1)}, u32[]{:S(2)}, u32[]{:S(2)}) collective-permute-start(bf16[6,4,4096]{2,1,0:T(4,128)(2,1)S(1)} %collective-permute-done.1), channel_id=1, source_target_pairs={{1,0},{2,3},{5,4},{6,7},{9,8},{10,11},{13,12},{14,15},{17,16},{18,... | collective-permute-start | bytes 589832 | tf_op jit(solution)/shard_map/ppermute | solution.py:173
  29.2 0.7 %collective-permute-start.3 = (bf16[6,4,4096]{2,1,0:T(4,128)(2,1)S(1)}, bf16[6,4,4096]{2,1,0:T(4,128)(2,1)S(1)}, u32[]{:S(2)}, u32[]{:S(2)}) collective-permute-start(bf16[6,4,4096]{2,1,0:T(4,128)(2,1)S(1)} %collective-permute-done.refs_1_), channel_id=1, source_target_pairs={{1,2},{2,1},{5,6},{6,5},{9,10},{10,9},{13,14},{14,13},{17,18},{18,... | collective-permute-start | bytes 589832 | tf_op jit(solution)/shard_map/ppermute | solution.py:174
  30.7 4.8 %collective-permute-done.2 = bf16[6,4,4096]{2,1,0:T(4,128)(2,1)S(1)} collective-permute-done((bf16[6,4,4096]{2,1,0:T(4,128)(2,1)S(1)}, bf16[6,4,4096]{2,1,0:T(4,128)(2,1)S(1)}, u32[]{:S(2)}, u32[]{:S(2)}) %collective-permute-start.2) | collective-permute-done | bytes 196640 | tf_op jit(solution)/shard_map/ppermute | solution.py:173
  35.4 1.5 %collective-permute-start.4 = (bf16[6,4,4096]{2,1,0:T(4,128)(2,1)S(1)}, bf16[6,4,4096]{2,1,0:T(4,128)(2,1)S(1)}, u32[]{:S(2)}, u32[]{:S(2)}) collective-permute-start(bf16[6,4,4096]{2,1,0:T(4,128)(2,1)S(1)} %collective-permute-done.3), channel_id=1, source_target_pairs={{1,0},{2,3},{5,4},{6,7},{9,8},{10,11},{13,12},{14,15},{17,16},{18,... | collective-permute-start | bytes 589832 | tf_op jit(solution)/shard_map/ppermute | solution.py:175
  36.9 0.7 %broadcast_select_fusion.1 = bf16[3,8,4096]{2,1,0:T(8,128)(2,1)} fusion(bf16[3,8,4096]{2,1,0:T(8,128)(2,1)S(1)} %bitcast.95, bf16[3,8,4096]{2,1,0:T(8,128)(2,1)S(1)} %bitcast.94, pred[]{:T(512)S(6)} %or.3), kind=kLoop, calls=%fused_computation.44 | loop fusion | flops 98304 | bytes 589825 | tf_op jit(solution)/shard_map/jit(_where)/select_n | solution.py:178
  37.6 7.0 %collective-permute-done.4 = bf16[6,4,4096]{2,1,0:T(4,128)(2,1)S(1)} collective-permute-done((bf16[6,4,4096]{2,1,0:T(4,128)(2,1)S(1)}, bf16[6,4,4096]{2,1,0:T(4,128)(2,1)S(1)}, u32[]{:S(2)}, u32[]{:S(2)}) %collective-permute-start.4) | collective-permute-done | bytes 196640 | tf_op jit(solution)/shard_map/ppermute | solution.py:175
  44.6 0.7 %broadcast_select_fusion = bf16[3,8,4096]{2,1,0:T(8,128)(2,1)} fusion(bf16[3,8,4096]{2,1,0:T(8,128)(2,1)S(1)} %bitcast.97, bf16[3,8,4096]{2,1,0:T(8,128)(2,1)S(1)} %bitcast.96, pred[]{:T(512)S(6)} %or.3), kind=kLoop, calls=%fused_computation.43 | loop fusion | flops 98304 | bytes 589825 | tf_op jit(solution)/shard_map/jit(_where)/select_n | solution.py:179
  46.3 13.2 %shard_map.46 = f32[512,128]{1,0:T(8,128)} custom-call(bf16[6,4,4096]{2,1,0:T(4,128)(2,1)} %copy-done.1, bf16[6,4,4096]{2,1,0:T(4,128)(2,1)} %copy-done.5, bf16[6,4,4096]{2,1,0:T(4,128)(2,1)} %bitcast.92, bf16[6,4,4096]{2,1,0:T(4,128)(2,1)} %bitcast.93, bf16[6,4,4096]{2,1,0:T(4,128)(2,1)} %copy-done.1, bf16[6,4,4096]{2,1,0:T(4,128)(2,1)} %copy-done.6, ...), custom_call_target="tpu_custom_call" | custom-call | flops 587202560 | bytes 3670016 | tf_op jit(solution)/shard_map/pallas_call | solution.py:137
  59.4 1.5 %gather_fusion = f32[8,16,4,128]{3,1,2,0:T(8,128)S(1)} fusion(f32[16,8,4,128]{3,0,2,1:T(8,128)} %bitcast.89, s32[1024]{0:T(1024)S(1)} %pad_clamp_fusion.1), kind=kCustom, calls=%fused_computation | custom fusion | bytes 524320 | tf_op jit(solution)/shard_map/jit(_take)/gather | solution.py:222
  61.6 0.8 %multiply_select_fusion = f32[16,1,32,128]{3,2,1,0:T(8,128)} fusion(f32[16,1,32,128]{3,2,1,0:T(8,128)S(1)} %bitcast.90, pred[16]{0:T(512)(128)(4,1)S(1)} %broadcast_in_dim.63, pred[16,128]{1,0:T(8,128)(4,1)S(1)} %broadcast_compare_fusion), kind=kLoop, calls=%fused_computation.41 | loop fusion | flops 196608 | bytes 526352 | tf_op jit(solution)/shard_map/jit(_where)/select_n | solution.py:230
  (69 shorter events, 5.2 us)
Async XLA Ops:
  0.0 2.7 %copy-start = (f32[32]{0:T(128)S(1)}, f32[32]{0:T(128)}, u32[]{:S(2)}) copy-start(f32[32]{0:T(128)} %param.5) | copy-start | bytes 388
  11.0 11.0 %copy-start.11 = (s32[4,4]{1,0:T(4,128)S(1)}, s32[4,4]{1,0:T(4,128)}, u32[]{:S(2)}) copy-start(s32[4,4]{1,0:T(4,128)} %constant.110.clone) | copy-start | bytes 196
  11.8 18.1 %copy-start.1 = (bf16[6,4,4096]{2,1,0:T(4,128)(2,1)}, bf16[6,4,4096]{2,1,0:T(4,128)(2,1)S(1)}, u32[]{:S(2)}) copy-start(bf16[6,4,4096]{2,1,0:T(4,128)(2,1)S(1)} %maximum_bitcast_fusion.refs_0_.refs_4_) | copy-start | bytes 589828
  11.8 18.1 %collective-permute-start.10 = (bf16[6,4,4096]{2,1,0:T(4,128)(2,1)S(1)}, bf16[6,4,4096]{2,1,0:T(4,128)(2,1)S(1)}, u32[]{:S(2)}, u32[]{:S(2)}) collective-permute-start(bf16[6,4,4096]{2,1,0:T(4,128)(2,1)S(1)} %maximum_bitcast_fusion.refs_0_.refs_4_), channel_id=1, source_target_pairs={{0,24},{4,28},{8,16},{12,20},{16,8},{20,12},{24,0},{28,4},{1,25},{... | collective-permute-start | bytes 589832 | tf_op jit(solution)/shard_map/ppermute | solution.py:191
  15.8 14.3 %collective-permute-start.8 = (bf16[6,4,4096]{2,1,0:T(4,128)(2,1)S(1)}, bf16[6,4,4096]{2,1,0:T(4,128)(2,1)S(1)}, u32[]{:S(2)}, u32[]{:S(2)}) collective-permute-start(bf16[6,4,4096]{2,1,0:T(4,128)(2,1)S(1)} %maximum_bitcast_fusion.refs_0_.refs_4_), channel_id=1, source_target_pairs={{0,16},{4,20},{8,24},{12,28},{16,0},{20,4},{24,8},{28,12},{1,17},{... | collective-permute-start | bytes 589832 | tf_op jit(solution)/shard_map/ppermute | solution.py:191
  16.3 14.3 %collective-permute-start.6 = (bf16[6,4,4096]{2,1,0:T(4,128)(2,1)S(1)}, bf16[6,4,4096]{2,1,0:T(4,128)(2,1)S(1)}, u32[]{:S(2)}, u32[]{:S(2)}) collective-permute-start(bf16[6,4,4096]{2,1,0:T(4,128)(2,1)S(1)} %maximum_bitcast_fusion.refs_0_.refs_4_), channel_id=1, source_target_pairs={{0,8},{4,12},{8,0},{12,4},{16,24},{20,28},{24,16},{28,20},{1,9},{5... | collective-permute-start | bytes 589832 | tf_op jit(solution)/shard_map/ppermute | solution.py:191
  16.4 11.4 %collective-permute-start.1 = (bf16[6,4,4096]{2,1,0:T(4,128)(2,1)S(1)}, bf16[6,4,4096]{2,1,0:T(4,128)(2,1)S(1)}, u32[]{:S(2)}, u32[]{:S(2)}) collective-permute-start(bf16[6,4,4096]{2,1,0:T(4,128)(2,1)S(1)} %maximum_bitcast_fusion.refs_0_.refs_4_), channel_id=1, source_target_pairs={{1,2},{2,1},{5,6},{6,5},{9,10},{10,9},{13,14},{14,13},{17,18},{18,... | collective-permute-start | bytes 589832 | tf_op jit(solution)/shard_map/ppermute | solution.py:172
  17.1 12.1 %collective-permute-start = (bf16[6,4,4096]{2,1,0:T(4,128)(2,1)S(1)}, bf16[6,4,4096]{2,1,0:T(4,128)(2,1)S(1)}, u32[]{:S(2)}, u32[]{:S(2)}) collective-permute-start(bf16[6,4,4096]{2,1,0:T(4,128)(2,1)S(1)} %maximum_bitcast_fusion.refs_0_.refs_4_), channel_id=1, source_target_pairs={{0,1},{1,0},{2,3},{3,2},{4,5},{5,4},{6,7},{7,6},{8,9},{9,8},{10,11... | collective-permute-start | bytes 589832 | tf_op jit(solution)/shard_map/ppermute | solution.py:171
  26.8 3.1 %copy-start.10 = (s32[16]{0:T(128)S(1)}, s32[16]{0:T(128)}, u32[]{:S(2)}) copy-start(s32[16]{0:T(128)} %param.6) | copy-start | bytes 196
  27.9 7.6 %collective-permute-start.2 = (bf16[6,4,4096]{2,1,0:T(4,128)(2,1)S(1)}, bf16[6,4,4096]{2,1,0:T(4,128)(2,1)S(1)}, u32[]{:S(2)}, u32[]{:S(2)}) collective-permute-start(bf16[6,4,4096]{2,1,0:T(4,128)(2,1)S(1)} %collective-permute-done.1), channel_id=1, source_target_pairs={{1,0},{2,3},{5,4},{6,7},{9,8},{10,11},{13,12},{14,15},{17,16},{18,... | collective-permute-start | bytes 589832 | tf_op jit(solution)/shard_map/ppermute | solution.py:173
  29.2 16.2 %copy-start.5 = (bf16[6,4,4096]{2,1,0:T(4,128)(2,1)}, bf16[6,4,4096]{2,1,0:T(4,128)(2,1)S(1)}, u32[]{:S(2)}) copy-start(bf16[6,4,4096]{2,1,0:T(4,128)(2,1)S(1)} %collective-permute-done.refs_1_) | copy-start | bytes 589828
  29.2 6.2 %collective-permute-start.3 = (bf16[6,4,4096]{2,1,0:T(4,128)(2,1)S(1)}, bf16[6,4,4096]{2,1,0:T(4,128)(2,1)S(1)}, u32[]{:S(2)}, u32[]{:S(2)}) collective-permute-start(bf16[6,4,4096]{2,1,0:T(4,128)(2,1)S(1)} %collective-permute-done.refs_1_), channel_id=1, source_target_pairs={{1,2},{2,1},{5,6},{6,5},{9,10},{10,9},{13,14},{14,13},{17,18},{18,... | collective-permute-start | bytes 589832 | tf_op jit(solution)/shard_map/ppermute | solution.py:174
  30.0 15.5 %copy-start.2 = (bf16[6,4,4096]{2,1,0:T(4,128)(2,1)}, bf16[6,4,4096]{2,1,0:T(4,128)(2,1)S(1)}, u32[]{:S(2)}) copy-start(bf16[6,4,4096]{2,1,0:T(4,128)(2,1)S(1)} %collective-permute-done.10.refs_10_) | copy-start | bytes 589828
  30.0 15.4 %collective-permute-start.5 = (bf16[6,4,4096]{2,1,0:T(4,128)(2,1)S(1)}, bf16[6,4,4096]{2,1,0:T(4,128)(2,1)S(1)}, u32[]{:S(2)}, u32[]{:S(2)}) collective-permute-start(bf16[6,4,4096]{2,1,0:T(4,128)(2,1)S(1)} %maximum_bitcast_fusion.refs_0_.refs_4_), channel_id=1, source_target_pairs={{0,4},{4,0},{8,12},{12,8},{16,20},{20,16},{24,28},{28,24},{1,5},{5... | collective-permute-start | bytes 589832 | tf_op jit(solution)/shard_map/ppermute | solution.py:193
  30.1 15.4 %copy-start.3 = (bf16[6,4,4096]{2,1,0:T(4,128)(2,1)}, bf16[6,4,4096]{2,1,0:T(4,128)(2,1)S(1)}, u32[]{:S(2)}) copy-start(bf16[6,4,4096]{2,1,0:T(4,128)(2,1)S(1)} %collective-permute-done.8.refs_8_) | copy-start | bytes 589828
  30.1 15.3 %collective-permute-start.11 = (bf16[6,4,4096]{2,1,0:T(4,128)(2,1)S(1)}, bf16[6,4,4096]{2,1,0:T(4,128)(2,1)S(1)}, u32[]{:S(2)}, u32[]{:S(2)}) collective-permute-start(bf16[6,4,4096]{2,1,0:T(4,128)(2,1)S(1)} %collective-permute-done.10.refs_10_), channel_id=1, source_target_pairs={{0,4},{4,0},{8,12},{12,8},{16,20},{20,16},{24,28},{28,24},{1,5},{5... | collective-permute-start | bytes 589832 | tf_op jit(solution)/shard_map/ppermute | solution.py:194
  30.6 14.9 %copy-start.4 = (bf16[6,4,4096]{2,1,0:T(4,128)(2,1)}, bf16[6,4,4096]{2,1,0:T(4,128)(2,1)S(1)}, u32[]{:S(2)}) copy-start(bf16[6,4,4096]{2,1,0:T(4,128)(2,1)S(1)} %collective-permute-done.6.refs_6_) | copy-start | bytes 589828
  30.6 14.8 %collective-permute-start.9 = (bf16[6,4,4096]{2,1,0:T(4,128)(2,1)S(1)}, bf16[6,4,4096]{2,1,0:T(4,128)(2,1)S(1)}, u32[]{:S(2)}, u32[]{:S(2)}) collective-permute-start(bf16[6,4,4096]{2,1,0:T(4,128)(2,1)S(1)} %collective-permute-done.8.refs_8_), channel_id=1, source_target_pairs={{0,4},{4,0},{8,12},{12,8},{16,20},{20,16},{24,28},{28,24},{1,5},{5... | collective-permute-start | bytes 589832 | tf_op jit(solution)/shard_map/ppermute | solution.py:194
  35.4 10.0 %collective-permute-start.7 = (bf16[6,4,4096]{2,1,0:T(4,128)(2,1)S(1)}, bf16[6,4,4096]{2,1,0:T(4,128)(2,1)S(1)}, u32[]{:S(2)}, u32[]{:S(2)}) collective-permute-start(bf16[6,4,4096]{2,1,0:T(4,128)(2,1)S(1)} %collective-permute-done.6.refs_6_), channel_id=1, source_target_pairs={{0,4},{4,0},{8,12},{12,8},{16,20},{20,16},{24,28},{28,24},{1,5},{5... | collective-permute-start | bytes 589832 | tf_op jit(solution)/shard_map/ppermute | solution.py:194
  35.4 9.2 %collective-permute-start.4 = (bf16[6,4,4096]{2,1,0:T(4,128)(2,1)S(1)}, bf16[6,4,4096]{2,1,0:T(4,128)(2,1)S(1)}, u32[]{:S(2)}, u32[]{:S(2)}) collective-permute-start(bf16[6,4,4096]{2,1,0:T(4,128)(2,1)S(1)} %collective-permute-done.3), channel_id=1, source_target_pairs={{1,0},{2,3},{5,4},{6,7},{9,8},{10,11},{13,12},{14,15},{17,16},{18,... | collective-permute-start | bytes 589832 | tf_op jit(solution)/shard_map/ppermute | solution.py:175
  45.4 0.7 %copy-start.6 = (bf16[6,4,4096]{2,1,0:T(4,128)(2,1)}, bf16[6,4,4096]{2,1,0:T(4,128)(2,1)S(1)}, u32[]{:S(2)}) copy-start(bf16[6,4,4096]{2,1,0:T(4,128)(2,1)S(1)} %collective-permute-done.5.refs_5_) | copy-start | bytes 589828
  45.4 0.7 %copy-start.7 = (bf16[6,4,4096]{2,1,0:T(4,128)(2,1)}, bf16[6,4,4096]{2,1,0:T(4,128)(2,1)S(1)}, u32[]{:S(2)}) copy-start(bf16[6,4,4096]{2,1,0:T(4,128)(2,1)S(1)} %collective-permute-done.11.refs_11_) | copy-start | bytes 589828
  45.4 0.8 %copy-start.8 = (bf16[6,4,4096]{2,1,0:T(4,128)(2,1)}, bf16[6,4,4096]{2,1,0:T(4,128)(2,1)S(1)}, u32[]{:S(2)}) copy-start(bf16[6,4,4096]{2,1,0:T(4,128)(2,1)S(1)} %collective-permute-done.9.refs_9_) | copy-start | bytes 589828
  45.4 0.9 %copy-start.9 = (bf16[6,4,4096]{2,1,0:T(4,128)(2,1)}, bf16[6,4,4096]{2,1,0:T(4,128)(2,1)S(1)}, u32[]{:S(2)}) copy-start(bf16[6,4,4096]{2,1,0:T(4,128)(2,1)S(1)} %collective-permute-done.7.refs_7_) | copy-start | bytes 589828

commit v10 on v8

--- a/solution.py
+++ b/solution.py
@@ -175,10 +175,11 @@
         fetched.append(lax.ppermute(block, axis_name, pairs))
     partner = [(source, source ^ 1) for source in range(size)]
     pieces = [block, lax.ppermute(block, axis_name, partner)]
-    swapped = lax.ppermute(fetched, axis_name, partner)
+    piece = block.shape[1]
+    swapped = lax.ppermute(jnp.concatenate(fetched, axis=1), axis_name, partner)
     for step in range(1, chips):
         pieces.append(fetched[step - 1])
-        pieces.append(swapped[step - 1])
+        pieces.append(swapped[:, (step - 1) * piece:step * piece, :])
     order = lax.axis_index(axis_name) ^ jnp.arange(size, dtype=jnp.int32)
     return pieces, order
 

time: 55.8 us -> 54.3 us (0.973)
  waiting for transfers between devices: 10 us -> 8.41 us
    ppermute x3, waiting for transfers between devices: 10 us -> 7.53 us  [xor_gather(): pieces.append(lax.ppermute(block, axis_name, pairs))]
    unnamed x27 -> x13, local copies, waits for them, and re-layouts: 1.51 us -> 0.05 us
    slice x0 -> x1, local copies, waits for them, and re-layouts: none -> 0.99 us  [chip_gather(): pieces.append(swapped[:, (step - 1) * piece:step * piece, :])]
    ppermute x3 -> x1, waiting for transfers between devices: 0.01 us -> 0.87 us  [chip_gather(): swapped = lax.ppermute(jnp.concatenate(fetched, axis=1), axis_name, partner)]
    ppermute x3, starting transfers between devices: 4.67 us -> 5.49 us  [xor_gather(): pieces.append(lax.ppermute(block, axis_name, pairs))]
  transfers between devices with their start and end apart: 10 -> 8, of which waited for: 2 -> 2; matrix products, arithmetic and copies ran while one was open for 11% -> 14% of each run, Pallas kernels for 0% -> 0%
where the time goes in v10:
time: 54.3 us; the launch traced here: 54.1 us
  Pallas kernels  13.2 us (24%)
  starting transfers between devices  10.2 us (19%)
  waiting for transfers between devices  8.41 us (15%)
  other arithmetic  8.06 us (15%)
  matrix products  7.99 us (15%)
  local copies, waits for them, and re-layouts  6.01 us (11%)
    pallas_call x1, Pallas kernels, pair_block(): pl.pallas_call(functools.partial(cross_kernel, left_count, visit_count),...  13.2 us
    ppermute x3, waiting for transfers between devices, xor_gather(): pieces.append(lax.ppermute(block, axis_name, pairs))  7.53 us
    ppermute x3, starting transfers between devices, xor_gather(): pieces.append(lax.ppermute(block, axis_name, pairs))  5.49 us
    another operation x2, other arithmetic  4.73 us
    ppermute x3, starting transfers between devices, chip_gather(): fetched.append(lax.ppermute(block, axis_name, pairs))  4.61 us
    reshape x1, local copies, waits for them, and re-layouts, decimate(): blocks = records.reshape(lead_dims + (block_count, in_block))  1.68 us
    gather x1, local copies, waits for them, and re-layouts, on_device(): jnp.take(pair, visit_order, axis=1).reshape(group_rows, visit_count, LAGS)  1.51 us
    dot_general x1, matrix products, spectrum(): jnp.einsum('bwfq,gq->bwgf', real_t, sin_three, precision=lax.Precision.HIGH)  1.31 us
  transfers between devices with their start and end apart: 8, of which 2 were waited for; matrix products, arithmetic and copies ran while one was open for 14% of the time, Pallas kernels for 0%

profile of v10, /device:TPU:0, one launch (start us, length us, event | category | flops | bytes accessed | tf_op | source)
XLA Modules:
  0.0 54.1 jit_solution(8634069567461826403)
XLA Ops:
  0.2 1.7 %reshape.190 = f32[4,6,32,256]{3,2,0,1:T(8,128)S(1)} reshape(f32[4,6,8192]{2,0,1:T(4,128)} %param.3) | data formatting | bytes 1572864 | tf_op jit(solution)/shard_map/reshape | solution.py:31
  2.1 0.7 %iota_compare_fusion = pred[32,288,128]{2,1,0:T(32,128)(4,1)S(1)} fusion(s32[32,128]{1,0:T(8,128)S(1)} %iota_subtract_fusion), kind=kLoop, calls=%fused_computation.2 | loop fusion | flops 1179648 | bytes 1196032 | tf_op jit(solution)/shard_map/eq | solution.py:38
  2.7 1.1 %fusion = f32[1,288,128]{2,0,1:T(1,128)S(1)} fusion(pred[32,288,128]{2,1,0:T(32,128)(4,1)S(1)} %iota_compare_fusion, f32[32]{0:T(128)S(1)} %copy-done), kind=kOutput, calls=%fused_computation.3 | convolution fusion | flops 7077888 | bytes 1327232 | tf_op jit(solution)/shard_map/k,kij->ij/dot_general | solution.py:39
  3.8 0.7 %fusion.4 = f32[4,6,32,128]{3,2,1,0:T(8,128)S(1)} fusion(f32[288,128,1,1]{1,0,3,2:T(8,128)S(1)} %bitcast.82, f32[4,6,31,32]{3,2,1,0:T(8,128)S(1)} %copy.33, f32[4,6,32,256]{3,2,0,1:T(8,128)S(1)} %reshape.190), kind=kOutput, calls=%fused_computation.14 | convolution fusion | flops 170532864 | bytes 1422336 | tf_op jit(solution)/shard_map/swbi,ij->swbj/dot_general | solution.py:40
  4.7 0.6 %convolution_negate_fusion = f32[64,4,6,64]{3,0,2,1:T(8,128)S(1)} fusion(f32[4,6,64,64]{3,2,1,0:T(8,128)S(1)} %reshape_reshape.4), kind=kOutput, calls=%fused_computation.8 | convolution fusion | flops 37904384 | bytes 786432 | tf_op jit(solution)/shard_map/bwnq,fn->bwfq/dot_general | solution.py:52
  5.3 0.6 %fusion.26 = f32[64,4,6,64]{3,0,2,1:T(8,128)S(1)} fusion(f32[4,6,64,64]{3,2,1,0:T(8,128)S(1)} %reshape_reshape.4), kind=kOutput, calls=%fused_computation.54 | convolution fusion | flops 37806080 | bytes 786432 | tf_op jit(solution)/shard_map/bwnq,fn->bwfq/dot_general | solution.py:51
  6.0 1.2 %fusion.13 = f32[32,4,6,64]{3,0,2,1:T(8,128)S(1)} fusion(f32[64,4,6,64]{3,0,2,1:T(8,128)S(1)} %fusion.26, f32[64,4,6,64]{3,0,2,1:T(8,128)S(1)} %convolution_negate_fusion, f32[64,64]{1,0:T(8,128)S(1)} %get-tuple-element.14, f32[64,64]{1,0:T(8,128)S(1)} %get-tuple-element.15), kind=kOutput, calls=%fused_computation.28 | convolution fusion | flops 19197952 | bytes 1015808 | tf_op jit(solution)/shard_map/bwfq,gq->bwgf/dot_general | solution.py:60
  7.2 1.2 %fusion.17 = f32[32,4,6,64]{3,0,2,1:T(8,128)S(1)} fusion(f32[64,4,6,64]{3,0,2,1:T(8,128)S(1)} %convolution_negate_fusion, f32[64,4,6,64]{3,0,2,1:T(8,128)S(1)} %fusion.26, f32[64,64]{1,0:T(8,128)S(1)} %get-tuple-element.14, f32[64,64]{1,0:T(8,128)S(1)} %get-tuple-element.15), kind=kOutput, calls=%fused_computation.32 | convolution fusion | flops 19197952 | bytes 1015808 | tf_op jit(solution)/shard_map/bwfq,gq->bwgf/dot_general | solution.py:57
  8.4 1.2 %fusion.3 = f32[4,6,32,64]{3,2,1,0:T(8,128)S(1)} fusion(f32[32,4,6,64]{3,0,2,1:T(8,128)S(1)} %fusion.17, f32[64,4,6,64]{3,0,2,1:T(8,128)S(1)} %fusion.26, f32[64,4,6,64]{3,0,2,1:T(8,128)S(1)} %convolution_negate_fusion, f32[64,64]{1,0:T(8,128)S(1)} %get-tuple-element.14, f32[64,64]{1,0:T(8,128)S(1)} %get-tuple-element.15), kind=kOutput, calls=%fused_computation.12 | convolution fusion | flops 19247104 | bytes 1212416 | tf_op jit(solution)/shard_map/bwfq,gq->bwgf/dot_general | solution.py:59
  9.6 1.3 %add_reduce_fusion = (f32[4,6,32]{2,1,0:T(8,128)S(1)}, f32[4,6,32,64]{3,2,1,0:T(8,128)S(1)}) fusion(f32[4,6,32,64]{3,2,1,0:T(8,128)S(1)} %fusion.3, f32[32,4,6,64]{3,0,2,1:T(8,128)S(1)} %fusion.13, f32[64,4,6,64]{3,0,2,1:T(8,128)S(1)} %convolution_negate_fusion, f32[64,64]{1,0:T(8,128)S(1)} %get-tuple-element.14, f32[64,4,6,64]{3,0,2,1:T(8,128)S(1)} %fusion.26, ...), kind=kOutput, calls=%fused_computation.40 | convolution fusion | flops 19442944 | bytes 1412096 | tf_op jit(solution)/shard_map/bwfq,gq->bwgf/dot_general | solution.py:62
  11.8 4.0 %collective-permute-start.6 = (bf16[6,4,4096]{2,1,0:T(4,128)(2,1)S(1)}, bf16[6,4,4096]{2,1,0:T(4,128)(2,1)S(1)}, u32[]{:S(2)}, u32[]{:S(2)}) collective-permute-start(bf16[6,4,4096]{2,1,0:T(4,128)(2,1)S(1)} %maximum_bitcast_fusion.refs_0_.refs_4_), channel_id=1, source_target_pairs={{0,24},{4,28},{8,16},{12,20},{16,8},{20,12},{24,0},{28,4},{1,25},{... | collective-permute-start | bytes 589832 | tf_op jit(solution)/shard_map/ppermute | solution.py:175
  15.8 0.5 collective-permute-start.5
  16.4 4.0 %collective-permute-start.2 = (bf16[6,4,4096]{2,1,0:T(4,128)(2,1)S(1)}, bf16[6,4,4096]{2,1,0:T(4,128)(2,1)}, u32[]{:S(2)}, u32[]{:S(2)}) collective-permute-start(bf16[6,4,4096]{2,1,0:T(4,128)(2,1)S(1)} %maximum_bitcast_fusion.refs_0_.refs_4_), channel_id=1, source_target_pairs={{0,3},{1,2},{2,1},{3,0},{4,7},{5,6},{6,5},{7,4},{8,11},{9,10},{10,... | collective-permute-start | bytes 589832 | tf_op jit(solution)/shard_map/ppermute | solution.py:163
  20.5 4.6 %cosine_convert_fusion = (bf16[2048,128]{1,0:T(8,128)(2,1)S(1)}, bf16[2048,128]{1,0:T(8,128)(2,1)S(1)}) fusion(s32[128]{0:T(128)S(1)} %iota_add_fusion), kind=kLoop, calls=%fused_computation.23 | loop fusion | flops 4194304 | bytes 1049088 | tf_op jit(solution)/shard_map/convert
  25.3 1.4 %collective-permute-start = (bf16[6,4,4096]{2,1,0:T(4,128)(2,1)S(1)}, bf16[6,4,4096]{2,1,0:T(4,128)(2,1)}, u32[]{:S(2)}, u32[]{:S(2)}) collective-permute-start(bf16[6,4,4096]{2,1,0:T(4,128)(2,1)S(1)} %maximum_bitcast_fusion.refs_0_.refs_4_), channel_id=1, source_target_pairs={{0,1},{1,0},{2,3},{3,2},{4,5},{5,4},{6,7},{7,6},{8,9},{9,8},{10,11... | collective-permute-start | bytes 589832 | tf_op jit(solution)/shard_map/ppermute | solution.py:163
  26.7 0.3 pad_maximum_fusion.1
  27.5 1.0 %pad_maximum_fusion.refs_12_ = bf16[4096,128]{1,0:T(8,128)(2,1)} fusion(bf16[2048,128]{1,0:T(8,128)(2,1)S(1)} %get-tuple-element.11, bf16[2048,128]{1,0:T(8,128)(2,1)S(1)} %get-tuple-element.10), kind=kLoop, calls=%fused_computation.21 | loop fusion | flops 2097152 | bytes 2097152 | tf_op jit(solution)/shard_map/concatenate | solution.py:199
  28.5 0.9 %collective-permute-done.7 = bf16[6,12,4096]{2,1,0:T(8,128)(2,1)S(1)} collective-permute-done((bf16[6,12,4096]{2,1,0:T(8,128)(2,1)S(1)}, bf16[6,12,4096]{2,1,0:T(8,128)(2,1)S(1)}, u32[]{:S(2)}, u32[]{:S(2)}) %collective-permute-start.7) | collective-permute-done | bytes 589856 | tf_op jit(solution)/shard_map/ppermute | solution.py:179
  29.4 1.0 %fusion.88 = (bf16[6,4,4096]{2,1,0:T(4,128)(2,1)}, bf16[6,4,4096]{2,1,0:T(4,128)(2,1)}, bf16[6,4,4096]{2,1,0:T(4,128)(2,1)}) fusion(bf16[6,12,4096]{2,1,0:T(8,128)(2,1)S(1)} %collective-permute-done.7), kind=kLoop, calls=%fused_computation.127 | loop fusion | bytes 1179648 | tf_op jit(solution)/shard_map/slice | solution.py:182
  30.4 7.5 %collective-permute-done.1.refs_2_ = bf16[6,4,4096]{2,1,0:T(4,128)(2,1)} collective-permute-done((bf16[6,4,4096]{2,1,0:T(4,128)(2,1)S(1)}, bf16[6,4,4096]{2,1,0:T(4,128)(2,1)}, u32[]{:S(2)}, u32[]{:S(2)}) %collective-permute-start.1) | collective-permute-done | bytes 196640 | tf_op jit(solution)/shard_map/ppermute | solution.py:163
  37.9 13.2 %shard_map.37 = f32[512,128]{1,0:T(8,128)} custom-call(bf16[6,4,4096]{2,1,0:T(4,128)(2,1)} %copy-done.1, bf16[6,4,4096]{2,1,0:T(4,128)(2,1)} %collective-permute-done.refs_1_, bf16[6,4,4096]{2,1,0:T(4,128)(2,1)} %collective-permute-done.1.refs_2_, bf16[6,4,4096]{2,1,0:T(4,128)(2,1)} %collective-permute-done.2.refs_3_, bf16[6,4,4096]{2,1,0:T(4,128)(2,1)} %copy-done.1, ...), custom_call_target="tpu_custom_call" | custom-call | flops 587202560 | bytes 3670016 | tf_op jit(solution)/shard_map/pallas_call | solution.py:137
  51.1 1.5 %gather_fusion = f32[8,16,4,128]{3,1,2,0:T(8,128)S(1)} fusion(f32[16,8,4,128]{3,0,2,1:T(8,128)} %bitcast.79, s32[1024]{0:T(1024)S(1)} %pad_clamp_fusion.1), kind=kCustom, calls=%fused_computation | custom fusion | bytes 524320 | tf_op jit(solution)/shard_map/jit(_take)/gather | solution.py:207
  52.7 0.6 %gather_fusion.1 = f32[4,4,32,128]{3,2,1,0:T(8,128)S(1)} fusion(f32[4,4,32,128]{3,2,1,0:T(8,128)S(1)} %copy_select_fusion, s32[1024]{0:T(1024)S(1)} %pad_clamp_fusion), kind=kCustom, calls=%fused_computation.1 | custom fusion | bytes 524304 | tf_op jit(solution)/shard_map/jit(_take)/gather | solution.py:210
  53.3 0.8 %multiply_select_fusion = f32[16,1,32,128]{3,2,1,0:T(8,128)} fusion(f32[16,1,32,128]{3,2,1,0:T(8,128)S(1)} %bitcast.80, pred[16]{0:T(512)(128)(4,1)S(1)} %broadcast_in_dim.63, pred[16,128]{1,0:T(8,128)(4,1)S(1)} %broadcast_compare_fusion), kind=kLoop, calls=%fused_computation.42 | loop fusion | flops 196608 | bytes 526352 | tf_op jit(solution)/shard_map/jit(_where)/select_n | solution.py:215
  (49 shorter events, 2.2 us)
Async XLA Ops:
  0.0 2.7 %copy-start = (f32[32]{0:T(128)S(1)}, f32[32]{0:T(128)}, u32[]{:S(2)}) copy-start(f32[32]{0:T(128)} %param.4) | copy-start | bytes 388
  11.4 13.7 %copy-start.5 = (s32[16]{0:T(128)S(1)}, s32[16]{0:T(128)}, u32[]{:S(2)}) copy-start(s32[16]{0:T(128)} %param.5) | copy-start | bytes 196
  11.8 15.2 %copy-start.1 = (bf16[6,4,4096]{2,1,0:T(4,128)(2,1)}, bf16[6,4,4096]{2,1,0:T(4,128)(2,1)S(1)}, u32[]{:S(2)}) copy-start(bf16[6,4,4096]{2,1,0:T(4,128)(2,1)S(1)} %maximum_bitcast_fusion.refs_0_.refs_4_) | copy-start | bytes 589828
  11.8 13.3 %collective-permute-start.6 = (bf16[6,4,4096]{2,1,0:T(4,128)(2,1)S(1)}, bf16[6,4,4096]{2,1,0:T(4,128)(2,1)S(1)}, u32[]{:S(2)}, u32[]{:S(2)}) collective-permute-start(bf16[6,4,4096]{2,1,0:T(4,128)(2,1)S(1)} %maximum_bitcast_fusion.refs_0_.refs_4_), channel_id=1, source_target_pairs={{0,24},{4,28},{8,16},{12,20},{16,8},{20,12},{24,0},{28,4},{1,25},{... | collective-permute-start | bytes 589832 | tf_op jit(solution)/shard_map/ppermute | solution.py:175
  15.8 9.5 %collective-permute-start.5 = (bf16[6,4,4096]{2,1,0:T(4,128)(2,1)S(1)}, bf16[6,4,4096]{2,1,0:T(4,128)(2,1)S(1)}, u32[]{:S(2)}, u32[]{:S(2)}) collective-permute-start(bf16[6,4,4096]{2,1,0:T(4,128)(2,1)S(1)} %maximum_bitcast_fusion.refs_0_.refs_4_), channel_id=1, source_target_pairs={{0,16},{4,20},{8,24},{12,28},{16,0},{20,4},{24,8},{28,12},{1,17},{... | collective-permute-start | bytes 589832 | tf_op jit(solution)/shard_map/ppermute | solution.py:175
  16.3 10.4 %collective-permute-start.4 = (bf16[6,4,4096]{2,1,0:T(4,128)(2,1)S(1)}, bf16[6,4,4096]{2,1,0:T(4,128)(2,1)S(1)}, u32[]{:S(2)}, u32[]{:S(2)}) collective-permute-start(bf16[6,4,4096]{2,1,0:T(4,128)(2,1)S(1)} %maximum_bitcast_fusion.refs_0_.refs_4_), channel_id=1, source_target_pairs={{0,8},{4,12},{8,0},{12,4},{16,24},{20,28},{24,16},{28,20},{1,9},{5... | collective-permute-start | bytes 589832 | tf_op jit(solution)/shard_map/ppermute | solution.py:175
  16.4 13.9 %collective-permute-start.3 = (bf16[6,4,4096]{2,1,0:T(4,128)(2,1)S(1)}, bf16[6,4,4096]{2,1,0:T(4,128)(2,1)}, u32[]{:S(2)}, u32[]{:S(2)}) collective-permute-start(bf16[6,4,4096]{2,1,0:T(4,128)(2,1)S(1)} %maximum_bitcast_fusion.refs_0_.refs_4_), channel_id=1, source_target_pairs={{0,4},{4,0},{8,12},{12,8},{16,20},{20,16},{24,28},{28,24},{1,5},{5... | collective-permute-start | bytes 589832 | tf_op jit(solution)/shard_map/ppermute | solution.py:177
  16.4 13.9 %collective-permute-start.2 = (bf16[6,4,4096]{2,1,0:T(4,128)(2,1)S(1)}, bf16[6,4,4096]{2,1,0:T(4,128)(2,1)}, u32[]{:S(2)}, u32[]{:S(2)}) collective-permute-start(bf16[6,4,4096]{2,1,0:T(4,128)(2,1)S(1)} %maximum_bitcast_fusion.refs_0_.refs_4_), channel_id=1, source_target_pairs={{0,3},{1,2},{2,1},{3,0},{4,7},{5,6},{6,5},{7,4},{8,11},{9,10},{10,... | collective-permute-start | bytes 589832 | tf_op jit(solution)/shard_map/ppermute | solution.py:163
  25.2 3.4 %copy-start.2 = (bf16[6,4,4096]{2,1,0:T(4,128)(2,1)}, bf16[6,4,4096]{2,1,0:T(4,128)(2,1)S(1)}, u32[]{:S(2)}) copy-start(bf16[6,4,4096]{2,1,0:T(4,128)(2,1)S(1)} %collective-permute-done.6.refs_10_) | copy-start | bytes 589828
  25.2 12.8 %collective-permute-start.1 = (bf16[6,4,4096]{2,1,0:T(4,128)(2,1)S(1)}, bf16[6,4,4096]{2,1,0:T(4,128)(2,1)}, u32[]{:S(2)}, u32[]{:S(2)}) collective-permute-start(bf16[6,4,4096]{2,1,0:T(4,128)(2,1)S(1)} %maximum_bitcast_fusion.refs_0_.refs_4_), channel_id=1, source_target_pairs={{0,2},{1,3},{2,0},{3,1},{4,6},{5,7},{6,4},{7,5},{8,10},{9,11},{10,... | collective-permute-start | bytes 589832 | tf_op jit(solution)/shard_map/ppermute | solution.py:163
  25.3 3.3 %copy-start.3 = (bf16[6,4,4096]{2,1,0:T(4,128)(2,1)}, bf16[6,4,4096]{2,1,0:T(4,128)(2,1)S(1)}, u32[]{:S(2)}) copy-start(bf16[6,4,4096]{2,1,0:T(4,128)(2,1)S(1)} %collective-permute-done.5.refs_8_) | copy-start | bytes 589828
  25.3 12.7 %collective-permute-start = (bf16[6,4,4096]{2,1,0:T(4,128)(2,1)S(1)}, bf16[6,4,4096]{2,1,0:T(4,128)(2,1)}, u32[]{:S(2)}, u32[]{:S(2)}) collective-permute-start(bf16[6,4,4096]{2,1,0:T(4,128)(2,1)S(1)} %maximum_bitcast_fusion.refs_0_.refs_4_), channel_id=1, source_target_pairs={{0,1},{1,0},{2,3},{3,2},{4,5},{5,4},{6,7},{7,6},{8,9},{9,8},{10,11... | collective-permute-start | bytes 589832 | tf_op jit(solution)/shard_map/ppermute | solution.py:163
  26.7 1.8 %copy-start.4 = (bf16[6,4,4096]{2,1,0:T(4,128)(2,1)}, bf16[6,4,4096]{2,1,0:T(4,128)(2,1)S(1)}, u32[]{:S(2)}) copy-start(bf16[6,4,4096]{2,1,0:T(4,128)(2,1)S(1)} %collective-permute-done.4.refs_6_) | copy-start | bytes 589828
  27.0 2.4 %collective-permute-start.7 = (bf16[6,12,4096]{2,1,0:T(8,128)(2,1)S(1)}, bf16[6,12,4096]{2,1,0:T(8,128)(2,1)S(1)}, u32[]{:S(2)}, u32[]{:S(2)}) collective-permute-start(bf16[6,12,4096]{2,1,0:T(8,128)(2,1)S(1)} %pad_maximum_fusion.1), channel_id=1, source_target_pairs={{0,4},{4,0},{8,12},{12,8},{16,20},{20,16},{24,28},{28,24},{1,5},{5... | collective-permute-start | bytes 1769480 | tf_op jit(solution)/shard_map/ppermute | solution.py:179

commit v11 on v7

--- a/solution.py
+++ b/solution.py
@@ -36,8 +36,8 @@
     in_ids = jnp.arange(in_block + tap_count, dtype=jnp.int32)[None, :, None]
     out_ids = jnp.arange(out_block, dtype=jnp.int32)[None, None, :]
     onehot = (in_ids == DECIM * out_ids + tap_count - tap_ids).astype(jnp.float32)
-    band_matrix = jnp.einsum("k,kij->ij", fir_taps, onehot, precision=lax.Precision.HIGHEST)
-    summed = jnp.einsum("swbi,ij->swbj", windows, band_matrix, precision=lax.Precision.HIGHEST)
+    band_matrix = jnp.einsum("k,kij->ij", fir_taps, onehot, precision=lax.Precision.HIGH)
+    summed = jnp.einsum("swbi,ij->swbj", windows, band_matrix, precision=lax.Precision.HIGH)
     return summed.reshape(lead_dims + (block_count * out_block,))
 
 
@@ -48,18 +48,18 @@
     lead_dims = decimated.shape[:-1]
     blocks = decimated.reshape(lead_dims + (first_len, second_len))
     cos_one, sin_one = angle_table(first_len, first_len, first_len, 0)
-    real_z = jnp.einsum("bwnq,fn->bwfq", blocks, cos_one, precision=lax.Precision.HIGHEST)
-    imag_z = -jnp.einsum("bwnq,fn->bwfq", blocks, sin_one, precision=lax.Precision.HIGHEST)
+    real_z = jnp.einsum("bwnq,fn->bwfq", blocks, cos_one, precision=lax.Precision.HIGH)
+    imag_z = -jnp.einsum("bwnq,fn->bwfq", blocks, sin_one, precision=lax.Precision.HIGH)
     cos_two, sin_two = angle_table(first_len, second_len, out_length, 0)
     real_t = real_z * cos_two + imag_z * sin_two
     imag_t = imag_z * cos_two - real_z * sin_two
     cos_three, sin_three = angle_table(second_len // 2, second_len, second_len, 0)
     real_x = jnp.einsum(
-        "bwfq,gq->bwgf", real_t, cos_three, precision=lax.Precision.HIGHEST
-    ) + jnp.einsum("bwfq,gq->bwgf", imag_t, sin_three, precision=lax.Precision.HIGHEST)
+        "bwfq,gq->bwgf", real_t, cos_three, precision=lax.Precision.HIGH
+    ) + jnp.einsum("bwfq,gq->bwgf", imag_t, sin_three, precision=lax.Precision.HIGH)
     imag_x = jnp.einsum(
-        "bwfq,gq->bwgf", imag_t, cos_three, precision=lax.Precision.HIGHEST
-    ) - jnp.einsum("bwfq,gq->bwgf", real_t, sin_three, precision=lax.Precision.HIGHEST)
+        "bwfq,gq->bwgf", imag_t, cos_three, precision=lax.Precision.HIGH
+    ) - jnp.einsum("bwfq,gq->bwgf", real_t, sin_three, precision=lax.Precision.HIGH)
     bin_count = out_length // 2
     return (real_x.reshape(lead_dims + (bin_count,)), imag_x.reshape(lead_dims + (bin_count,)))
 
@@ -175,10 +175,11 @@
         fetched.append(lax.ppermute(block, axis_name, pairs))
     partner = [(source, source ^ 1) for source in range(size)]
     pieces = [block, lax.ppermute(block, axis_name, partner)]
-    swapped = lax.ppermute(fetched, axis_name, partner)
+    piece = block.shape[1]
+    swapped = lax.ppermute(jnp.concatenate(fetched, axis=1), axis_name, partner)
     for step in range(1, chips):
         pieces.append(fetched[step - 1])
-        pieces.append(swapped[step - 1])
+        pieces.append(swapped[:, (step - 1) * piece:step * piece, :])
     order = lax.axis_index(axis_name) ^ jnp.arange(size, dtype=jnp.int32)
     return pieces, order
 

time: 63 us -> 51.6 us (0.82)
  matrix products: 13.9 us -> 7.99 us
  starting transfers between devices: 13.6 us -> 9.51 us
  waiting for transfers between devices: 7.87 us -> 6.35 us
    ppermute x3, waiting for transfers between devices: 7.85 us -> 2.47 us  [xor_gather(): pieces.append(lax.ppermute(block, axis_name, pairs))]
    dot_general x7, matrix products: 12.6 us -> 7.27 us  [the longest x1 1.31 us: spectrum(): jnp.einsum('bwfq,gq->bwgf', real_t, sin_three, precision=lax.Precision.HIGH)]
    ppermute x3, starting transfers between devices: 9.53 us -> 5.94 us  [xor_gather(): pieces.append(lax.ppermute(block, axis_name, pairs))]
    ppermute x3, waiting for transfers between devices: 0.01 us -> 3.01 us  [chip_gather(): fetched.append(lax.ppermute(block, axis_name, pairs))]
    unnamed x27 -> x13, local copies, waits for them, and re-layouts: 1.48 us -> 0.05 us
    slice x0 -> x1, local copies, waits for them, and re-layouts: none -> 1.02 us  [chip_gather(): pieces.append(swapped[:, (step - 1) * piece:step * piece, :])]
    ppermute x3 -> x1, waiting for transfers between devices: 0.01 us -> 0.87 us  [chip_gather(): swapped = lax.ppermute(jnp.concatenate(fetched, axis=1), axis_name, partner)]
  transfers between devices with their start and end apart: 10 -> 8, of which waited for: 2 -> 4; matrix products, arithmetic and copies ran while one was open for 9% -> 14% of each run, Pallas kernels for 0% -> 0%
where the time goes in v11:
time: 51.6 us; the launch traced here: 51.4 us
  Pallas kernels  13.2 us (26%)
  starting transfers between devices  9.51 us (18%)
  other arithmetic  8.06 us (16%)
  matrix products  7.99 us (15%)
  waiting for transfers between devices  6.35 us (12%)
  local copies, waits for them, and re-layouts  6.04 us (12%)
    pallas_call x1, Pallas kernels, pair_block(): pl.pallas_call(functools.partial(cross_kernel, tuple(issue_order)), out_s...  13.2 us
    ppermute x3, starting transfers between devices, xor_gather(): pieces.append(lax.ppermute(block, axis_name, pairs))  5.94 us
    another operation x2, other arithmetic  4.73 us
    ppermute x3, starting transfers between devices, chip_gather(): fetched.append(lax.ppermute(block, axis_name, pairs))  3.49 us
    ppermute x3, waiting for transfers between devices, chip_gather(): fetched.append(lax.ppermute(block, axis_name, pairs))  3.01 us
    ppermute x3, waiting for transfers between devices, xor_gather(): pieces.append(lax.ppermute(block, axis_name, pairs))  2.47 us
    reshape x1, local copies, waits for them, and re-layouts, decimate(): blocks = records.reshape(lead_dims + (block_count, in_block))  1.68 us
    gather x1, local copies, waits for them, and re-layouts, on_device(): jnp.take(pair, visit_order, axis=1).reshape(group_rows, visit_count, LAGS)  1.51 us
  transfers between devices with their start and end apart: 8, of which 4 were waited for; matrix products, arithmetic and copies ran while one was open for 14% of the time, Pallas kernels for 0%

profile of v11, /device:TPU:0, one launch (start us, length us, event | category | flops | bytes accessed | tf_op | source)
XLA Modules:
  0.0 51.4 jit_solution(8725229517875601886)
XLA Ops:
  0.2 1.7 %reshape.190 = f32[4,6,32,256]{3,2,0,1:T(8,128)S(1)} reshape(f32[4,6,8192]{2,0,1:T(4,128)} %param.3) | data formatting | bytes 1572864 | tf_op jit(solution)/shard_map/reshape | solution.py:31
  2.1 0.7 %iota_compare_fusion = pred[32,288,128]{2,1,0:T(32,128)(4,1)S(1)} fusion(s32[32,128]{1,0:T(8,128)S(1)} %iota_subtract_fusion), kind=kLoop, calls=%fused_computation.2 | loop fusion | flops 1179648 | bytes 1196032 | tf_op jit(solution)/shard_map/eq | solution.py:38
  2.7 1.1 %fusion = f32[1,288,128]{2,0,1:T(1,128)S(1)} fusion(pred[32,288,128]{2,1,0:T(32,128)(4,1)S(1)} %iota_compare_fusion, f32[32]{0:T(128)S(1)} %copy-done), kind=kOutput, calls=%fused_computation.3 | convolution fusion | flops 7077888 | bytes 1327232 | tf_op jit(solution)/shard_map/k,kij->ij/dot_general | solution.py:39
  3.8 0.7 %fusion.4 = f32[4,6,32,128]{3,2,1,0:T(8,128)S(1)} fusion(f32[288,128,1,1]{1,0,3,2:T(8,128)S(1)} %bitcast.82, f32[4,6,31,32]{3,2,1,0:T(8,128)S(1)} %copy.33, f32[4,6,32,256]{3,2,0,1:T(8,128)S(1)} %reshape.190), kind=kOutput, calls=%fused_computation.14 | convolution fusion | flops 170532864 | bytes 1422336 | tf_op jit(solution)/shard_map/swbi,ij->swbj/dot_general | solution.py:40
  4.7 0.6 %convolution_negate_fusion = f32[64,4,6,64]{3,0,2,1:T(8,128)S(1)} fusion(f32[4,6,64,64]{3,2,1,0:T(8,128)S(1)} %reshape_reshape.4), kind=kOutput, calls=%fused_computation.8 | convolution fusion | flops 37904384 | bytes 786432 | tf_op jit(solution)/shard_map/bwnq,fn->bwfq/dot_general | solution.py:52
  5.3 0.6 %fusion.26 = f32[64,4,6,64]{3,0,2,1:T(8,128)S(1)} fusion(f32[4,6,64,64]{3,2,1,0:T(8,128)S(1)} %reshape_reshape.4), kind=kOutput, calls=%fused_computation.54 | convolution fusion | flops 37806080 | bytes 786432 | tf_op jit(solution)/shard_map/bwnq,fn->bwfq/dot_general | solution.py:51
  6.0 1.2 %fusion.13 = f32[32,4,6,64]{3,0,2,1:T(8,128)S(1)} fusion(f32[64,4,6,64]{3,0,2,1:T(8,128)S(1)} %fusion.26, f32[64,4,6,64]{3,0,2,1:T(8,128)S(1)} %convolution_negate_fusion, f32[64,64]{1,0:T(8,128)S(1)} %get-tuple-element.14, f32[64,64]{1,0:T(8,128)S(1)} %get-tuple-element.15), kind=kOutput, calls=%fused_computation.28 | convolution fusion | flops 19197952 | bytes 1015808 | tf_op jit(solution)/shard_map/bwfq,gq->bwgf/dot_general | solution.py:60
  7.2 1.2 %fusion.17 = f32[32,4,6,64]{3,0,2,1:T(8,128)S(1)} fusion(f32[64,4,6,64]{3,0,2,1:T(8,128)S(1)} %convolution_negate_fusion, f32[64,4,6,64]{3,0,2,1:T(8,128)S(1)} %fusion.26, f32[64,64]{1,0:T(8,128)S(1)} %get-tuple-element.14, f32[64,64]{1,0:T(8,128)S(1)} %get-tuple-element.15), kind=kOutput, calls=%fused_computation.32 | convolution fusion | flops 19197952 | bytes 1015808 | tf_op jit(solution)/shard_map/bwfq,gq->bwgf/dot_general | solution.py:57
  8.4 1.2 %fusion.3 = f32[4,6,32,64]{3,2,1,0:T(8,128)S(1)} fusion(f32[32,4,6,64]{3,0,2,1:T(8,128)S(1)} %fusion.17, f32[64,4,6,64]{3,0,2,1:T(8,128)S(1)} %fusion.26, f32[64,4,6,64]{3,0,2,1:T(8,128)S(1)} %convolution_negate_fusion, f32[64,64]{1,0:T(8,128)S(1)} %get-tuple-element.14, f32[64,64]{1,0:T(8,128)S(1)} %get-tuple-element.15), kind=kOutput, calls=%fused_computation.12 | convolution fusion | flops 19247104 | bytes 1212416 | tf_op jit(solution)/shard_map/bwfq,gq->bwgf/dot_general | solution.py:59
  9.6 1.3 %add_reduce_fusion = (f32[4,6,32]{2,1,0:T(8,128)S(1)}, f32[4,6,32,64]{3,2,1,0:T(8,128)S(1)}) fusion(f32[4,6,32,64]{3,2,1,0:T(8,128)S(1)} %fusion.3, f32[32,4,6,64]{3,0,2,1:T(8,128)S(1)} %fusion.13, f32[64,4,6,64]{3,0,2,1:T(8,128)S(1)} %convolution_negate_fusion, f32[64,64]{1,0:T(8,128)S(1)} %get-tuple-element.14, f32[64,4,6,64]{3,0,2,1:T(8,128)S(1)} %fusion.26, ...), kind=kOutput, calls=%fused_computation.40 | convolution fusion | flops 19442944 | bytes 1412096 | tf_op jit(solution)/shard_map/bwfq,gq->bwgf/dot_general | solution.py:62
  11.8 4.1 %collective-permute-start.7 = (bf16[6,4,4096]{2,1,0:T(4,128)(2,1)S(1)}, bf16[6,4,4096]{2,1,0:T(4,128)(2,1)}, u32[]{:S(2)}, u32[]{:S(2)}) collective-permute-start(bf16[6,4,4096]{2,1,0:T(4,128)(2,1)S(1)} %maximum_bitcast_fusion.refs_3_.refs_4_), channel_id=1, source_target_pairs={{0,2},{1,3},{2,0},{3,1},{4,6},{5,7},{6,4},{7,5},{8,10},{9,11},{10,... | collective-permute-start | bytes 589832 | tf_op jit(solution)/shard_map/ppermute | solution.py:163
  15.9 1.4 %collective-permute-start.6 = (bf16[6,4,4096]{2,1,0:T(4,128)(2,1)S(1)}, bf16[6,4,4096]{2,1,0:T(4,128)(2,1)}, u32[]{:S(2)}, u32[]{:S(2)}) collective-permute-start(bf16[6,4,4096]{2,1,0:T(4,128)(2,1)S(1)} %maximum_bitcast_fusion.refs_3_.refs_4_), channel_id=1, source_target_pairs={{0,3},{1,2},{2,1},{3,0},{4,7},{5,6},{6,5},{7,4},{8,11},{9,10},{10,... | collective-permute-start | bytes 589832 | tf_op jit(solution)/shard_map/ppermute | solution.py:163
  17.3 2.4 %collective-permute-start.2 = (bf16[6,4,4096]{2,1,0:T(4,128)(2,1)S(1)}, bf16[6,4,4096]{2,1,0:T(4,128)(2,1)S(1)}, u32[]{:S(2)}, u32[]{:S(2)}) collective-permute-start(bf16[6,4,4096]{2,1,0:T(4,128)(2,1)S(1)} %maximum_bitcast_fusion.refs_3_.refs_4_), channel_id=1, source_target_pairs={{0,24},{4,28},{8,16},{12,20},{16,8},{20,12},{24,0},{28,4},{1,25},{... | collective-permute-start | bytes 589832 | tf_op jit(solution)/shard_map/ppermute | solution.py:175
  20.9 4.6 %cosine_convert_fusion = (bf16[2048,128]{1,0:T(8,128)(2,1)S(1)}, bf16[2048,128]{1,0:T(8,128)(2,1)S(1)}) fusion(s32[128]{0:T(128)S(1)} %iota_add_fusion), kind=kLoop, calls=%fused_computation.23 | loop fusion | flops 4194304 | bytes 1049088 | tf_op jit(solution)/shard_map/convert
  25.5 0.5 %collective-permute-done.2.refs_9_ = bf16[6,4,4096]{2,1,0:T(4,128)(2,1)S(1)} collective-permute-done((bf16[6,4,4096]{2,1,0:T(4,128)(2,1)S(1)}, bf16[6,4,4096]{2,1,0:T(4,128)(2,1)S(1)}, u32[]{:S(2)}, u32[]{:S(2)}) %collective-permute-start.2) | collective-permute-done | bytes 196640 | tf_op jit(solution)/shard_map/ppermute | solution.py:175
  26.0 2.5 %collective-permute-done.1.refs_8_ = bf16[6,4,4096]{2,1,0:T(4,128)(2,1)S(1)} collective-permute-done((bf16[6,4,4096]{2,1,0:T(4,128)(2,1)S(1)}, bf16[6,4,4096]{2,1,0:T(4,128)(2,1)S(1)}, u32[]{:S(2)}, u32[]{:S(2)}) %collective-permute-start.1) | collective-permute-done | bytes 196640 | tf_op jit(solution)/shard_map/ppermute | solution.py:175
  29.8 1.0 %pad_maximum_fusion.refs_12_ = bf16[4096,128]{1,0:T(8,128)(2,1)} fusion(bf16[2048,128]{1,0:T(8,128)(2,1)S(1)} %get-tuple-element.11, bf16[2048,128]{1,0:T(8,128)(2,1)S(1)} %get-tuple-element.10), kind=kLoop, calls=%fused_computation.21 | loop fusion | flops 2097152 | bytes 2097152 | tf_op jit(solution)/shard_map/concatenate | solution.py:199
  30.8 0.9 %collective-permute-done.3 = bf16[6,12,4096]{2,1,0:T(8,128)(2,1)S(1)} collective-permute-done((bf16[6,12,4096]{2,1,0:T(8,128)(2,1)S(1)}, bf16[6,12,4096]{2,1,0:T(8,128)(2,1)S(1)}, u32[]{:S(2)}, u32[]{:S(2)}) %collective-permute-start.3) | collective-permute-done | bytes 589856 | tf_op jit(solution)/shard_map/ppermute | solution.py:179
  31.7 1.0 %fusion.88 = (bf16[6,4,4096]{2,1,0:T(4,128)(2,1)}, bf16[6,4,4096]{2,1,0:T(4,128)(2,1)}, bf16[6,4,4096]{2,1,0:T(4,128)(2,1)}) fusion(bf16[6,12,4096]{2,1,0:T(8,128)(2,1)S(1)} %collective-permute-done.3), kind=kLoop, calls=%fused_computation.127 | loop fusion | bytes 1179648 | tf_op jit(solution)/shard_map/slice | solution.py:182
  32.7 2.5 %collective-permute-done.4.refs_5_ = bf16[6,4,4096]{2,1,0:T(4,128)(2,1)} collective-permute-done((bf16[6,4,4096]{2,1,0:T(4,128)(2,1)S(1)}, bf16[6,4,4096]{2,1,0:T(4,128)(2,1)}, u32[]{:S(2)}, u32[]{:S(2)}) %collective-permute-start.4) | collective-permute-done | bytes 196640 | tf_op jit(solution)/shard_map/ppermute | solution.py:163
  35.2 13.2 %shard_map.37 = f32[512,128]{1,0:T(8,128)} custom-call(bf16[6,4,4096]{2,1,0:T(4,128)(2,1)} %get-tuple-element.7.refs_0_, bf16[6,4,4096]{2,1,0:T(4,128)(2,1)} %get-tuple-element.6.refs_1_, bf16[6,4,4096]{2,1,0:T(4,128)(2,1)} %get-tuple-element.5.refs_2_, bf16[6,4,4096]{2,1,0:T(4,128)(2,1)} %copy-done.1, bf16[6,4,4096]{2,1,0:T(4,128)(2,1)} %copy-done.1, ...), custom_call_target="tpu_custom_call" | custom-call | flops 587202560 | bytes 3670016 | tf_op jit(solution)/shard_map/pallas_call | solution.py:137
  48.4 1.5 %gather_fusion = f32[8,16,4,128]{3,1,2,0:T(8,128)S(1)} fusion(f32[16,8,4,128]{3,0,2,1:T(8,128)} %bitcast.79, s32[1024]{0:T(1024)S(1)} %pad_clamp_fusion.1), kind=kCustom, calls=%fused_computation | custom fusion | bytes 524320 | tf_op jit(solution)/shard_map/jit(_take)/gather | solution.py:214
  50.0 0.6 %gather_fusion.1 = f32[4,4,32,128]{3,2,1,0:T(8,128)S(1)} fusion(f32[4,4,32,128]{3,2,1,0:T(8,128)S(1)} %copy_select_fusion, s32[1024]{0:T(1024)S(1)} %pad_clamp_fusion), kind=kCustom, calls=%fused_computation.1 | custom fusion | bytes 524304 | tf_op jit(solution)/shard_map/jit(_take)/gather | solution.py:217
  50.6 0.8 %multiply_select_fusion = f32[16,1,32,128]{3,2,1,0:T(8,128)} fusion(f32[16,1,32,128]{3,2,1,0:T(8,128)S(1)} %bitcast.80, pred[16]{0:T(512)(128)(4,1)S(1)} %broadcast_in_dim.63, pred[16,128]{1,0:T(8,128)(4,1)S(1)} %broadcast_compare_fusion), kind=kLoop, calls=%fused_computation.42 | loop fusion | flops 196608 | bytes 526352 | tf_op jit(solution)/shard_map/jit(_where)/select_n | solution.py:222
  (49 shorter events, 3.9 us)
Async XLA Ops:
  0.0 2.7 %copy-start = (f32[32]{0:T(128)S(1)}, f32[32]{0:T(128)}, u32[]{:S(2)}) copy-start(f32[32]{0:T(128)} %param.4) | copy-start | bytes 388
  11.4 14.1 %copy-start.5 = (s32[16]{0:T(128)S(1)}, s32[16]{0:T(128)}, u32[]{:S(2)}) copy-start(s32[16]{0:T(128)} %param.5) | copy-start | bytes 196
  11.8 17.5 %copy-start.1 = (bf16[6,4,4096]{2,1,0:T(4,128)(2,1)}, bf16[6,4,4096]{2,1,0:T(4,128)(2,1)S(1)}, u32[]{:S(2)}) copy-start(bf16[6,4,4096]{2,1,0:T(4,128)(2,1)S(1)} %maximum_bitcast_fusion.refs_3_.refs_4_) | copy-start | bytes 589828
  11.8 20.9 %collective-permute-start.7 = (bf16[6,4,4096]{2,1,0:T(4,128)(2,1)S(1)}, bf16[6,4,4096]{2,1,0:T(4,128)(2,1)}, u32[]{:S(2)}, u32[]{:S(2)}) collective-permute-start(bf16[6,4,4096]{2,1,0:T(4,128)(2,1)S(1)} %maximum_bitcast_fusion.refs_3_.refs_4_), channel_id=1, source_target_pairs={{0,2},{1,3},{2,0},{3,1},{4,6},{5,7},{6,4},{7,5},{8,10},{9,11},{10,... | collective-permute-start | bytes 589832 | tf_op jit(solution)/shard_map/ppermute | solution.py:163
  15.9 16.8 %collective-permute-start.6 = (bf16[6,4,4096]{2,1,0:T(4,128)(2,1)S(1)}, bf16[6,4,4096]{2,1,0:T(4,128)(2,1)}, u32[]{:S(2)}, u32[]{:S(2)}) collective-permute-start(bf16[6,4,4096]{2,1,0:T(4,128)(2,1)S(1)} %maximum_bitcast_fusion.refs_3_.refs_4_), channel_id=1, source_target_pairs={{0,3},{1,2},{2,1},{3,0},{4,7},{5,6},{6,5},{7,4},{8,11},{9,10},{10,... | collective-permute-start | bytes 589832 | tf_op jit(solution)/shard_map/ppermute | solution.py:163
  17.3 8.7 %collective-permute-start.2 = (bf16[6,4,4096]{2,1,0:T(4,128)(2,1)S(1)}, bf16[6,4,4096]{2,1,0:T(4,128)(2,1)S(1)}, u32[]{:S(2)}, u32[]{:S(2)}) collective-permute-start(bf16[6,4,4096]{2,1,0:T(4,128)(2,1)S(1)} %maximum_bitcast_fusion.refs_3_.refs_4_), channel_id=1, source_target_pairs={{0,24},{4,28},{8,16},{12,20},{16,8},{20,12},{24,0},{28,4},{1,25},{... | collective-permute-start | bytes 589832 | tf_op jit(solution)/shard_map/ppermute | solution.py:175
  19.7 8.8 %collective-permute-start.1 = (bf16[6,4,4096]{2,1,0:T(4,128)(2,1)S(1)}, bf16[6,4,4096]{2,1,0:T(4,128)(2,1)S(1)}, u32[]{:S(2)}, u32[]{:S(2)}) collective-permute-start(bf16[6,4,4096]{2,1,0:T(4,128)(2,1)S(1)} %maximum_bitcast_fusion.refs_3_.refs_4_), channel_id=1, source_target_pairs={{0,16},{4,20},{8,24},{12,28},{16,0},{20,4},{24,8},{28,12},{1,17},{... | collective-permute-start | bytes 589832 | tf_op jit(solution)/shard_map/ppermute | solution.py:175
  20.2 8.8 %collective-permute-start = (bf16[6,4,4096]{2,1,0:T(4,128)(2,1)S(1)}, bf16[6,4,4096]{2,1,0:T(4,128)(2,1)S(1)}, u32[]{:S(2)}, u32[]{:S(2)}) collective-permute-start(bf16[6,4,4096]{2,1,0:T(4,128)(2,1)S(1)} %maximum_bitcast_fusion.refs_3_.refs_4_), channel_id=1, source_target_pairs={{0,8},{4,12},{8,0},{12,4},{16,24},{20,28},{24,16},{28,20},{1,9},{5... | collective-permute-start | bytes 589832 | tf_op jit(solution)/shard_map/ppermute | solution.py:175
  26.0 4.8 %copy-start.2 = (bf16[6,4,4096]{2,1,0:T(4,128)(2,1)}, bf16[6,4,4096]{2,1,0:T(4,128)(2,1)S(1)}, u32[]{:S(2)}) copy-start(bf16[6,4,4096]{2,1,0:T(4,128)(2,1)S(1)} %collective-permute-done.2.refs_9_) | copy-start | bytes 589828
  26.0 6.7 %collective-permute-start.5 = (bf16[6,4,4096]{2,1,0:T(4,128)(2,1)S(1)}, bf16[6,4,4096]{2,1,0:T(4,128)(2,1)}, u32[]{:S(2)}, u32[]{:S(2)}) collective-permute-start(bf16[6,4,4096]{2,1,0:T(4,128)(2,1)S(1)} %maximum_bitcast_fusion.refs_3_.refs_4_), channel_id=1, source_target_pairs={{0,4},{4,0},{8,12},{12,8},{16,20},{20,16},{24,28},{28,24},{1,5},{5... | collective-permute-start | bytes 589832 | tf_op jit(solution)/shard_map/ppermute | solution.py:177
  28.5 2.3 %copy-start.3 = (bf16[6,4,4096]{2,1,0:T(4,128)(2,1)}, bf16[6,4,4096]{2,1,0:T(4,128)(2,1)S(1)}, u32[]{:S(2)}) copy-start(bf16[6,4,4096]{2,1,0:T(4,128)(2,1)S(1)} %collective-permute-done.1.refs_8_) | copy-start | bytes 589828
  28.5 6.7 %collective-permute-start.4 = (bf16[6,4,4096]{2,1,0:T(4,128)(2,1)S(1)}, bf16[6,4,4096]{2,1,0:T(4,128)(2,1)}, u32[]{:S(2)}, u32[]{:S(2)}) collective-permute-start(bf16[6,4,4096]{2,1,0:T(4,128)(2,1)S(1)} %maximum_bitcast_fusion.refs_3_.refs_4_), channel_id=1, source_target_pairs={{0,1},{1,0},{2,3},{3,2},{4,5},{5,4},{6,7},{7,6},{8,9},{9,8},{10,11... | collective-permute-start | bytes 589832 | tf_op jit(solution)/shard_map/ppermute | solution.py:163
  29.0 1.8 %copy-start.4 = (bf16[6,4,4096]{2,1,0:T(4,128)(2,1)}, bf16[6,4,4096]{2,1,0:T(4,128)(2,1)S(1)}, u32[]{:S(2)}) copy-start(bf16[6,4,4096]{2,1,0:T(4,128)(2,1)S(1)} %collective-permute-done.refs_7_) | copy-start | bytes 589828
  29.4 2.4 %collective-permute-start.3 = (bf16[6,12,4096]{2,1,0:T(8,128)(2,1)S(1)}, bf16[6,12,4096]{2,1,0:T(8,128)(2,1)S(1)}, u32[]{:S(2)}, u32[]{:S(2)}) collective-permute-start(bf16[6,12,4096]{2,1,0:T(8,128)(2,1)S(1)} %pad_maximum_fusion.1), channel_id=1, source_target_pairs={{0,4},{4,0},{8,12},{12,8},{16,20},{20,16},{24,28},{28,24},{1,5},{5... | collective-permute-start | bytes 1769480 | tf_op jit(solution)/shard_map/ppermute | solution.py:179

commit v12 on v11

--- a/solution.py
+++ b/solution.py
@@ -208,13 +208,15 @@
     issue_order = sorted(set(issue_order), key=issue_order.index)
     assert len(issue_order) == len(left_by_window) + len(piece_rows)
     pair = pair_block(left_by_window, piece_rows, lag_table, issue_order)
-    pair = jnp.swapaxes(pair.reshape(visit_count, group_rows, LAGS), 0, 1)
+    piece = block_size
+    left_pos = jnp.arange(group_rows, dtype=jnp.int32)
+    visit_pos = jnp.arange(visit_count, dtype=jnp.int32)
+    if left_order is not None:
+        left_pos = left_order[left_pos // piece] * piece + left_pos % piece
     if visit_order is not None:
-        pair = pair.reshape(group_rows, row_size, block_size, LAGS)
-        pair = jnp.take(pair, visit_order, axis=1).reshape(group_rows, visit_count, LAGS)
-    if left_order is not None:
-        pair = pair.reshape(col_size, block_size, visit_count, LAGS)
-        pair = jnp.take(pair, left_order, axis=0).reshape(group_rows, visit_count, LAGS)
+        visit_pos = visit_order[visit_pos // piece] * piece + visit_pos % piece
+    source_row = visit_pos[None, :] * group_rows + left_pos[:, None]
+    pair = jnp.take(pair, source_row.reshape(-1), axis=0).reshape(group_rows, visit_count, LAGS)
     norm_scale = 1.0 / math.sqrt(white.shape[1] * bin_count)
     pair = pair * norm_scale
     lag_offset = jnp.abs(jnp.arange(LAGS, dtype=jnp.int32) - LH)

time: 51.6 us -> 51.8 us (level)
  local copies, waits for them, and re-layouts: 6.04 us -> 7.72 us
  waiting for transfers between devices: 6.35 us -> 4.71 us
    ppermute x3, waiting for transfers between devices: 3.01 us -> 1.36 us  [chip_gather(): fetched.append(lax.ppermute(block, axis_name, pairs))]
    gather x2 -> x3, local copies, waits for them, and re-layouts: 2.08 us -> 3.33 us  [the longest x1 1.98 us: on_device(): jnp.take(pair, source_row.reshape(-1), axis=0)]
    unnamed x13 -> x21, local copies, waits for them, and re-layouts: 0.05 us -> 0.74 us
  transfers between devices with their start and end apart: 8 -> 8, of which waited for: 4 -> 3; matrix products, arithmetic and copies ran while one was open for 14% -> 17% of each run, Pallas kernels for 0% -> 0%
where the time goes in v12:
time: 51.8 us; the launch traced here: 51.6 us
  Pallas kernels  13.2 us (25%)
  starting transfers between devices  9.57 us (18%)
  other arithmetic  8.18 us (16%)
  matrix products  7.97 us (15%)
  local copies, waits for them, and re-layouts  7.72 us (15%)
  waiting for transfers between devices  4.71 us (9%)
    pallas_call x1, Pallas kernels, pair_block(): pl.pallas_call(functools.partial(cross_kernel, tuple(issue_order)), out_s...  13.2 us
    ppermute x3, starting transfers between devices, xor_gather(): pieces.append(lax.ppermute(block, axis_name, pairs))  5.94 us
    another operation x2, other arithmetic  4.73 us
    ppermute x3, starting transfers between devices, chip_gather(): fetched.append(lax.ppermute(block, axis_name, pairs))  3.49 us
    ppermute x3, waiting for transfers between devices, xor_gather(): pieces.append(lax.ppermute(block, axis_name, pairs))  2.25 us
    gather x1, local copies, waits for them, and re-layouts, on_device(): jnp.take(pair, source_row.reshape(-1), axis=0)  1.98 us
    reshape x1, local copies, waits for them, and re-layouts, decimate(): blocks = records.reshape(lead_dims + (block_count, in_block))  1.68 us
    ppermute x3, waiting for transfers between devices, chip_gather(): fetched.append(lax.ppermute(block, axis_name, pairs))  1.36 us
  transfers between devices with their start and end apart: 8, of which 3 were waited for; matrix products, arithmetic and copies ran while one was open for 17% of the time, Pallas kernels for 0%

profile of v12, /device:TPU:0, one launch (start us, length us, event | category | flops | bytes accessed | tf_op | source)
XLA Modules:
  0.0 51.6 jit_solution(15938753144690479394)
XLA Ops:
  0.2 1.7 %reshape.296 = f32[4,6,32,256]{3,2,0,1:T(8,128)S(1)} reshape(f32[4,6,8192]{2,0,1:T(4,128)} %param.3) | data formatting | bytes 1572864 | tf_op jit(solution)/shard_map/reshape | solution.py:31
  2.1 0.7 %iota_compare_fusion = pred[32,288,128]{2,1,0:T(32,128)(4,1)S(1)} fusion(s32[32,128]{1,0:T(8,128)S(1)} %iota_subtract_fusion), kind=kLoop, calls=%fused_computation.3 | loop fusion | flops 1179648 | bytes 1196032 | tf_op jit(solution)/shard_map/eq | solution.py:38
  2.7 1.1 %fusion = f32[1,288,128]{2,0,1:T(1,128)S(1)} fusion(pred[32,288,128]{2,1,0:T(32,128)(4,1)S(1)} %iota_compare_fusion, f32[32]{0:T(128)S(1)} %copy-done), kind=kOutput, calls=%fused_computation.4 | convolution fusion | flops 7077888 | bytes 1327232 | tf_op jit(solution)/shard_map/k,kij->ij/dot_general | solution.py:39
  3.8 0.7 %fusion.4 = f32[4,6,32,128]{3,2,1,0:T(8,128)S(1)} fusion(f32[288,128,1,1]{1,0,3,2:T(8,128)S(1)} %bitcast.74, f32[4,6,31,32]{3,2,1,0:T(8,128)S(1)} %copy.27, f32[4,6,32,256]{3,2,0,1:T(8,128)S(1)} %reshape.296), kind=kOutput, calls=%fused_computation.15 | convolution fusion | flops 170532864 | bytes 1422336 | tf_op jit(solution)/shard_map/swbi,ij->swbj/dot_general | solution.py:40
  4.7 0.6 %convolution_negate_fusion = f32[64,4,6,64]{3,0,2,1:T(8,128)S(1)} fusion(f32[4,6,64,64]{3,2,1,0:T(8,128)S(1)} %reshape_reshape.3), kind=kOutput, calls=%fused_computation.9 | convolution fusion | flops 37904384 | bytes 786432 | tf_op jit(solution)/shard_map/bwnq,fn->bwfq/dot_general | solution.py:52
  5.9 1.2 %fusion.13 = f32[32,4,6,64]{3,0,2,1:T(8,128)S(1)} fusion(f32[64,4,6,64]{3,0,2,1:T(8,128)S(1)} %fusion.26, f32[64,4,6,64]{3,0,2,1:T(8,128)S(1)} %convolution_negate_fusion, f32[64,64]{1,0:T(8,128)S(1)} %get-tuple-element.14, f32[64,64]{1,0:T(8,128)S(1)} %get-tuple-element.15), kind=kOutput, calls=%fused_computation.29 | convolution fusion | flops 19197952 | bytes 1015808 | tf_op jit(solution)/shard_map/bwfq,gq->bwgf/dot_general | solution.py:60
  7.2 1.2 %fusion.17 = f32[32,4,6,64]{3,0,2,1:T(8,128)S(1)} fusion(f32[64,4,6,64]{3,0,2,1:T(8,128)S(1)} %convolution_negate_fusion, f32[64,4,6,64]{3,0,2,1:T(8,128)S(1)} %fusion.26, f32[64,64]{1,0:T(8,128)S(1)} %get-tuple-element.14, f32[64,64]{1,0:T(8,128)S(1)} %get-tuple-element.15), kind=kOutput, calls=%fused_computation.33 | convolution fusion | flops 19197952 | bytes 1015808 | tf_op jit(solution)/shard_map/bwfq,gq->bwgf/dot_general | solution.py:57
  8.4 1.2 %fusion.3 = f32[4,6,32,64]{3,2,1,0:T(8,128)S(1)} fusion(f32[32,4,6,64]{3,0,2,1:T(8,128)S(1)} %fusion.17, f32[64,4,6,64]{3,0,2,1:T(8,128)S(1)} %fusion.26, f32[64,4,6,64]{3,0,2,1:T(8,128)S(1)} %convolution_negate_fusion, f32[64,64]{1,0:T(8,128)S(1)} %get-tuple-element.14, f32[64,64]{1,0:T(8,128)S(1)} %get-tuple-element.15), kind=kOutput, calls=%fused_computation.13 | convolution fusion | flops 19247104 | bytes 1212416 | tf_op jit(solution)/shard_map/bwfq,gq->bwgf/dot_general | solution.py:59
  9.6 1.3 %add_reduce_fusion = (f32[4,6,32]{2,1,0:T(8,128)S(1)}, f32[4,6,32,64]{3,2,1,0:T(8,128)S(1)}) fusion(f32[4,6,32,64]{3,2,1,0:T(8,128)S(1)} %fusion.3, f32[32,4,6,64]{3,0,2,1:T(8,128)S(1)} %fusion.13, f32[64,4,6,64]{3,0,2,1:T(8,128)S(1)} %convolution_negate_fusion, f32[64,64]{1,0:T(8,128)S(1)} %get-tuple-element.14, f32[64,4,6,64]{3,0,2,1:T(8,128)S(1)} %fusion.26, ...), kind=kOutput, calls=%fused_computation.41 | convolution fusion | flops 19442944 | bytes 1412096 | tf_op jit(solution)/shard_map/bwfq,gq->bwgf/dot_general | solution.py:62
  11.8 4.1 %collective-permute-start.7 = (bf16[6,4,4096]{2,1,0:T(4,128)(2,1)S(1)}, bf16[6,4,4096]{2,1,0:T(4,128)(2,1)S(1)}, u32[]{:S(2)}, u32[]{:S(2)}) collective-permute-start(bf16[6,4,4096]{2,1,0:T(4,128)(2,1)S(1)} %maximum_bitcast_fusion.refs_3_.refs_4_), channel_id=1, source_target_pairs={{0,2},{1,3},{2,0},{3,1},{4,6},{5,7},{6,4},{7,5},{8,10},{9,11},{10,... | collective-permute-start | bytes 589832 | tf_op jit(solution)/shard_map/ppermute | solution.py:163
  15.9 1.3 %collective-permute-start.6 = (bf16[6,4,4096]{2,1,0:T(4,128)(2,1)S(1)}, bf16[6,4,4096]{2,1,0:T(4,128)(2,1)S(1)}, u32[]{:S(2)}, u32[]{:S(2)}) collective-permute-start(bf16[6,4,4096]{2,1,0:T(4,128)(2,1)S(1)} %maximum_bitcast_fusion.refs_3_.refs_4_), channel_id=1, source_target_pairs={{0,3},{1,2},{2,1},{3,0},{4,7},{5,6},{6,5},{7,4},{8,11},{9,10},{10,... | collective-permute-start | bytes 589832 | tf_op jit(solution)/shard_map/ppermute | solution.py:163
  17.3 2.4 %collective-permute-start.2 = (bf16[6,4,4096]{2,1,0:T(4,128)(2,1)S(1)}, bf16[6,4,4096]{2,1,0:T(4,128)(2,1)S(1)}, u32[]{:S(2)}, u32[]{:S(2)}) collective-permute-start(bf16[6,4,4096]{2,1,0:T(4,128)(2,1)S(1)} %maximum_bitcast_fusion.refs_3_.refs_4_), channel_id=1, source_target_pairs={{0,24},{4,28},{8,16},{12,20},{16,8},{20,12},{24,0},{28,4},{1,25},{... | collective-permute-start | bytes 589832 | tf_op jit(solution)/shard_map/ppermute | solution.py:175
  20.8 0.7 %gather_fusion = s32[32]{0:T(128)S(1)} fusion(s32[8]{0:T(128)S(1)} %iota_xor_fusion.1, s32[1024]{0:T(1024)S(1)} %pad_clamp_fusion.2), kind=kCustom, calls=%fused_computation | custom fusion | bytes 384 | tf_op jit(solution)/shard_map/gather | solution.py:217
  21.5 0.7 %gather_fusion.1 = s32[16]{0:T(128)S(1)} fusion(s32[4]{0:T(128)S(1)} %iota_xor_fusion, s32[1024]{0:T(1024)S(1)} %pad_clamp_fusion.1), kind=kCustom, calls=%fused_computation.1 | custom fusion | bytes 192 | tf_op jit(solution)/shard_map/gather | solution.py:215
  22.4 4.6 %cosine_convert_fusion = (bf16[2048,128]{1,0:T(8,128)(2,1)S(1)}, bf16[2048,128]{1,0:T(8,128)(2,1)S(1)}) fusion(s32[128]{0:T(128)S(1)} %iota_add_fusion), kind=kLoop, calls=%fused_computation.24 | loop fusion | flops 4194304 | bytes 1049088 | tf_op jit(solution)/shard_map/convert
  27.1 1.4 %collective-permute-done.1.refs_8_ = bf16[6,4,4096]{2,1,0:T(4,128)(2,1)S(1)} collective-permute-done((bf16[6,4,4096]{2,1,0:T(4,128)(2,1)S(1)}, bf16[6,4,4096]{2,1,0:T(4,128)(2,1)S(1)}, u32[]{:S(2)}, u32[]{:S(2)}) %collective-permute-start.1) | collective-permute-done | bytes 196640 | tf_op jit(solution)/shard_map/ppermute | solution.py:175
  29.5 1.1 %pad_maximum_fusion.refs_12_ = bf16[4096,128]{1,0:T(8,128)(2,1)} fusion(bf16[2048,128]{1,0:T(8,128)(2,1)S(1)} %get-tuple-element.11, bf16[2048,128]{1,0:T(8,128)(2,1)S(1)} %get-tuple-element.10), kind=kLoop, calls=%fused_computation.22 | loop fusion | flops 2097152 | bytes 2097152 | tf_op jit(solution)/shard_map/concatenate | solution.py:199
  30.6 1.1 %collective-permute-done.3 = bf16[6,12,4096]{2,1,0:T(8,128)(2,1)S(1)} collective-permute-done((bf16[6,12,4096]{2,1,0:T(8,128)(2,1)S(1)}, bf16[6,12,4096]{2,1,0:T(8,128)(2,1)S(1)}, u32[]{:S(2)}, u32[]{:S(2)}) %collective-permute-start.3) | collective-permute-done | bytes 589856 | tf_op jit(solution)/shard_map/ppermute | solution.py:179
  31.7 1.0 %fusion.91 = (bf16[6,4,4096]{2,1,0:T(4,128)(2,1)}, bf16[6,4,4096]{2,1,0:T(4,128)(2,1)}, bf16[6,4,4096]{2,1,0:T(4,128)(2,1)}) fusion(bf16[6,12,4096]{2,1,0:T(8,128)(2,1)S(1)} %collective-permute-done.3), kind=kLoop, calls=%fused_computation.143 | loop fusion | bytes 1179648 | tf_op jit(solution)/shard_map/slice | solution.py:182
  32.7 2.2 %collective-permute-done.4.refs_5_ = bf16[6,4,4096]{2,1,0:T(4,128)(2,1)S(1)} collective-permute-done((bf16[6,4,4096]{2,1,0:T(4,128)(2,1)S(1)}, bf16[6,4,4096]{2,1,0:T(4,128)(2,1)S(1)}, u32[]{:S(2)}, u32[]{:S(2)}) %collective-permute-start.4) | collective-permute-done | bytes 196640 | tf_op jit(solution)/shard_map/ppermute | solution.py:163
  35.0 0.7 %copy-done.8 = bf16[6,4,4096]{2,1,0:T(4,128)(2,1)} copy-done((bf16[6,4,4096]{2,1,0:T(4,128)(2,1)}, bf16[6,4,4096]{2,1,0:T(4,128)(2,1)S(1)}, u32[]{:S(2)}) %copy-start.8) | copy-done | bytes 196632
  35.6 13.2 %shard_map.37 = f32[512,128]{1,0:T(8,128)} custom-call(bf16[6,4,4096]{2,1,0:T(4,128)(2,1)} %get-tuple-element.7.refs_0_, bf16[6,4,4096]{2,1,0:T(4,128)(2,1)} %get-tuple-element.6.refs_1_, bf16[6,4,4096]{2,1,0:T(4,128)(2,1)} %get-tuple-element.5.refs_2_, bf16[6,4,4096]{2,1,0:T(4,128)(2,1)} %copy-done.1, bf16[6,4,4096]{2,1,0:T(4,128)(2,1)} %copy-done.1, ...), custom_call_target="tpu_custom_call" | custom-call | flops 587202560 | bytes 3670016 | tf_op jit(solution)/shard_map/pallas_call | solution.py:137
  48.8 2.0 %gather_fusion.2 = f32[512,128]{1,0:T(8,128)S(1)} fusion(f32[512,128]{1,0:T(8,128)} %shard_map.37, s32[1024]{0:T(1024)S(1)} %pad_clamp_fusion), kind=kCustom, calls=%fused_computation.2 | custom fusion | bytes 526336 | tf_op jit(solution)/shard_map/jit(_take)/gather | solution.py:219
  50.8 0.8 %multiply_select_fusion = f32[16,1,32,128]{3,2,1,0:T(8,128)} fusion(f32[16,1,32,128]{3,2,1,0:T(8,128)S(1)} %bitcast.72, pred[16,32]{1,0:T(8,128)(4,1)S(1)} %compare_and_fusion, pred[16,128]{1,0:T(8,128)(4,1)S(1)} %broadcast_compare_fusion), kind=kLoop, calls=%fused_computation.42 | loop fusion | flops 196608 | bytes 526848 | tf_op jit(solution)/shard_map/jit(_where)/select_n | solution.py:224
  (60 shorter events, 4.4 us)
Async XLA Ops:
  0.0 2.7 %copy-start = (f32[32]{0:T(128)S(1)}, f32[32]{0:T(128)}, u32[]{:S(2)}) copy-start(f32[32]{0:T(128)} %param.4) | copy-start | bytes 388
  11.8 17.5 %copy-start.1 = (bf16[6,4,4096]{2,1,0:T(4,128)(2,1)}, bf16[6,4,4096]{2,1,0:T(4,128)(2,1)S(1)}, u32[]{:S(2)}) copy-start(bf16[6,4,4096]{2,1,0:T(4,128)(2,1)S(1)} %maximum_bitcast_fusion.refs_3_.refs_4_) | copy-start | bytes 589828
  11.8 20.9 %collective-permute-start.7 = (bf16[6,4,4096]{2,1,0:T(4,128)(2,1)S(1)}, bf16[6,4,4096]{2,1,0:T(4,128)(2,1)S(1)}, u32[]{:S(2)}, u32[]{:S(2)}) collective-permute-start(bf16[6,4,4096]{2,1,0:T(4,128)(2,1)S(1)} %maximum_bitcast_fusion.refs_3_.refs_4_), channel_id=1, source_target_pairs={{0,2},{1,3},{2,0},{3,1},{4,6},{5,7},{6,4},{7,5},{8,10},{9,11},{10,... | collective-permute-start | bytes 589832 | tf_op jit(solution)/shard_map/ppermute | solution.py:163
  15.9 16.8 %collective-permute-start.6 = (bf16[6,4,4096]{2,1,0:T(4,128)(2,1)S(1)}, bf16[6,4,4096]{2,1,0:T(4,128)(2,1)S(1)}, u32[]{:S(2)}, u32[]{:S(2)}) collective-permute-start(bf16[6,4,4096]{2,1,0:T(4,128)(2,1)S(1)} %maximum_bitcast_fusion.refs_3_.refs_4_), channel_id=1, source_target_pairs={{0,3},{1,2},{2,1},{3,0},{4,7},{5,6},{6,5},{7,4},{8,11},{9,10},{10,... | collective-permute-start | bytes 589832 | tf_op jit(solution)/shard_map/ppermute | solution.py:163
  17.3 9.8 %collective-permute-start.2 = (bf16[6,4,4096]{2,1,0:T(4,128)(2,1)S(1)}, bf16[6,4,4096]{2,1,0:T(4,128)(2,1)S(1)}, u32[]{:S(2)}, u32[]{:S(2)}) collective-permute-start(bf16[6,4,4096]{2,1,0:T(4,128)(2,1)S(1)} %maximum_bitcast_fusion.refs_3_.refs_4_), channel_id=1, source_target_pairs={{0,24},{4,28},{8,16},{12,20},{16,8},{20,12},{24,0},{28,4},{1,25},{... | collective-permute-start | bytes 589832 | tf_op jit(solution)/shard_map/ppermute | solution.py:175
  19.7 8.8 %collective-permute-start.1 = (bf16[6,4,4096]{2,1,0:T(4,128)(2,1)S(1)}, bf16[6,4,4096]{2,1,0:T(4,128)(2,1)S(1)}, u32[]{:S(2)}, u32[]{:S(2)}) collective-permute-start(bf16[6,4,4096]{2,1,0:T(4,128)(2,1)S(1)} %maximum_bitcast_fusion.refs_3_.refs_4_), channel_id=1, source_target_pairs={{0,16},{4,20},{8,24},{12,28},{16,0},{20,4},{24,8},{28,12},{1,17},{... | collective-permute-start | bytes 589832 | tf_op jit(solution)/shard_map/ppermute | solution.py:175
  20.2 8.8 %collective-permute-start = (bf16[6,4,4096]{2,1,0:T(4,128)(2,1)S(1)}, bf16[6,4,4096]{2,1,0:T(4,128)(2,1)S(1)}, u32[]{:S(2)}, u32[]{:S(2)}) collective-permute-start(bf16[6,4,4096]{2,1,0:T(4,128)(2,1)S(1)} %maximum_bitcast_fusion.refs_3_.refs_4_), channel_id=1, source_target_pairs={{0,8},{4,12},{8,0},{12,4},{16,24},{20,28},{24,16},{28,20},{1,9},{5... | collective-permute-start | bytes 589832 | tf_op jit(solution)/shard_map/ppermute | solution.py:175
  22.4 7.0 %copy-start.9 = (s32[16]{0:T(128)S(1)}, s32[16]{0:T(128)}, u32[]{:S(2)}) copy-start(s32[16]{0:T(128)} %param.5) | copy-start | bytes 196
  27.0 3.5 %copy-start.2 = (bf16[6,4,4096]{2,1,0:T(4,128)(2,1)}, bf16[6,4,4096]{2,1,0:T(4,128)(2,1)S(1)}, u32[]{:S(2)}) copy-start(bf16[6,4,4096]{2,1,0:T(4,128)(2,1)S(1)} %collective-permute-done.2.refs_9_) | copy-start | bytes 589828
  27.0 5.7 %collective-permute-start.5 = (bf16[6,4,4096]{2,1,0:T(4,128)(2,1)S(1)}, bf16[6,4,4096]{2,1,0:T(4,128)(2,1)S(1)}, u32[]{:S(2)}, u32[]{:S(2)}) collective-permute-start(bf16[6,4,4096]{2,1,0:T(4,128)(2,1)S(1)} %maximum_bitcast_fusion.refs_3_.refs_4_), channel_id=1, source_target_pairs={{0,4},{4,0},{8,12},{12,8},{16,20},{20,16},{24,28},{28,24},{1,5},{5... | collective-permute-start | bytes 589832 | tf_op jit(solution)/shard_map/ppermute | solution.py:177
  28.5 2.1 %copy-start.3 = (bf16[6,4,4096]{2,1,0:T(4,128)(2,1)}, bf16[6,4,4096]{2,1,0:T(4,128)(2,1)S(1)}, u32[]{:S(2)}) copy-start(bf16[6,4,4096]{2,1,0:T(4,128)(2,1)S(1)} %collective-permute-done.1.refs_8_) | copy-start | bytes 589828
  28.5 6.5 %collective-permute-start.4 = (bf16[6,4,4096]{2,1,0:T(4,128)(2,1)S(1)}, bf16[6,4,4096]{2,1,0:T(4,128)(2,1)S(1)}, u32[]{:S(2)}, u32[]{:S(2)}) collective-permute-start(bf16[6,4,4096]{2,1,0:T(4,128)(2,1)S(1)} %maximum_bitcast_fusion.refs_3_.refs_4_), channel_id=1, source_target_pairs={{0,1},{1,0},{2,3},{3,2},{4,5},{5,4},{6,7},{7,6},{8,9},{9,8},{10,11... | collective-permute-start | bytes 589832 | tf_op jit(solution)/shard_map/ppermute | solution.py:163
  29.0 1.6 %copy-start.4 = (bf16[6,4,4096]{2,1,0:T(4,128)(2,1)}, bf16[6,4,4096]{2,1,0:T(4,128)(2,1)S(1)}, u32[]{:S(2)}) copy-start(bf16[6,4,4096]{2,1,0:T(4,128)(2,1)S(1)} %collective-permute-done.refs_7_) | copy-start | bytes 589828
  29.3 2.4 %collective-permute-start.3 = (bf16[6,12,4096]{2,1,0:T(8,128)(2,1)S(1)}, bf16[6,12,4096]{2,1,0:T(8,128)(2,1)S(1)}, u32[]{:S(2)}, u32[]{:S(2)}) collective-permute-start(bf16[6,12,4096]{2,1,0:T(8,128)(2,1)S(1)} %pad_maximum_fusion.1), channel_id=1, source_target_pairs={{0,4},{4,0},{8,12},{12,8},{16,20},{20,16},{24,28},{28,24},{1,5},{5... | collective-permute-start | bytes 1769480 | tf_op jit(solution)/shard_map/ppermute | solution.py:179
  32.7 2.3 %copy-start.5 = (bf16[6,4,4096]{2,1,0:T(4,128)(2,1)}, bf16[6,4,4096]{2,1,0:T(4,128)(2,1)S(1)}, u32[]{:S(2)}) copy-start(bf16[6,4,4096]{2,1,0:T(4,128)(2,1)S(1)} %collective-permute-done.7.refs_11_) | copy-start | bytes 589828
  32.7 2.3 %copy-start.6 = (bf16[6,4,4096]{2,1,0:T(4,128)(2,1)}, bf16[6,4,4096]{2,1,0:T(4,128)(2,1)S(1)}, u32[]{:S(2)}) copy-start(bf16[6,4,4096]{2,1,0:T(4,128)(2,1)S(1)} %collective-permute-done.6.refs_10_) | copy-start | bytes 589828
  32.7 2.3 %copy-start.7 = (bf16[6,4,4096]{2,1,0:T(4,128)(2,1)}, bf16[6,4,4096]{2,1,0:T(4,128)(2,1)S(1)}, u32[]{:S(2)}) copy-start(bf16[6,4,4096]{2,1,0:T(4,128)(2,1)S(1)} %collective-permute-done.5.refs_6_) | copy-start | bytes 589828
  34.9 0.7 %copy-start.8 = (bf16[6,4,4096]{2,1,0:T(4,128)(2,1)}, bf16[6,4,4096]{2,1,0:T(4,128)(2,1)S(1)}, u32[]{:S(2)}) copy-start(bf16[6,4,4096]{2,1,0:T(4,128)(2,1)S(1)} %collective-permute-done.4.refs_5_) | copy-start | bytes 589828

commit v13 on v12

--- a/solution.py
+++ b/solution.py
@@ -78,7 +78,7 @@
 
 def cross_kernel(slots, *refs):
     piece_refs = refs[:len(slots)]
-    table_ref, out_ref, left_f32, visit_f32, cross_ref = refs[len(slots):]
+    left_perm, visit_perm, table_ref, out_ref, left_f32, visit_f32, cross_ref = refs[len(slots):]
     left_refs = [ref for ref, slot in zip(piece_refs, slots) if slot[0] == 0]
     window_count, piece, width = left_refs[0].shape
     rows_left = left_f32.shape[1]
@@ -94,6 +94,11 @@
     for ref, (kind, index) in zip(piece_refs, slots):
         target = left_f32 if kind == 0 else visit_f32
         target[:, index * piece:(index + 1) * piece, :] = ref[...].astype(jnp.float32)
+    for window in range(window_count):
+        for perm_ref, target in ((left_perm, left_f32), (visit_perm, visit_f32)):
+            target[window] = jnp.dot(
+                perm_ref[...], target[window].astype(jnp.bfloat16), preferred_element_type=jnp.float32
+            )
 
     for first in range(0, visit_count, group):
         base = first * piece
@@ -122,7 +127,7 @@
         )
 
 
-def pair_block(left_pieces, visit_pieces, lag_table, issue_order):
+def pair_block(left_pieces, visit_pieces, left_perm, visit_perm, lag_table, issue_order):
     window_count, piece, width = left_pieces[0].shape
     left_count = len(left_pieces)
     visit_count = len(visit_pieces)
@@ -137,7 +142,7 @@
     return pl.pallas_call(
         functools.partial(cross_kernel, tuple(issue_order)),
         out_shape=jax.ShapeDtypeStruct((visit_rows * rows_left, lag_count), jnp.float32),
-        in_specs=[pl.BlockSpec(memory_space=vmem)] * (left_count + visit_count + 1),
+        in_specs=[pl.BlockSpec(memory_space=vmem)] * (left_count + visit_count + 3),
         out_specs=pl.BlockSpec(memory_space=vmem),
         scratch_shapes=[
             vmem((window_count, rows_left, width), jnp.float32),
@@ -151,7 +156,7 @@
             bytes_accessed=2 * width * (window_count * (rows_left + visit_rows) + lag_count)
             + 4 * visit_rows * rows_left * lag_count,
         ),
-    )(*[(left_pieces, visit_pieces)[kind][index] for kind, index in issue_order], lag_table)
+    )(*[(left_pieces, visit_pieces)[kind][index] for kind, index in issue_order], left_perm, visit_perm, lag_table)
 
 
 def xor_gather(block, axis_name, size):
@@ -207,7 +212,6 @@
     issue_order = [slot for slot in late_first + near + fetches + far[::-1]]
     issue_order = sorted(set(issue_order), key=issue_order.index)
     assert len(issue_order) == len(left_by_window) + len(piece_rows)
-    pair = pair_block(left_by_window, piece_rows, lag_table, issue_order)
     piece = block_size
     left_pos = jnp.arange(group_rows, dtype=jnp.int32)
     visit_pos = jnp.arange(visit_count, dtype=jnp.int32)
@@ -215,8 +219,10 @@
         left_pos = left_order[left_pos // piece] * piece + left_pos % piece
     if visit_order is not None:
         visit_pos = visit_order[visit_pos // piece] * piece + visit_pos % piece
-    source_row = visit_pos[None, :] * group_rows + left_pos[:, None]
-    pair = jnp.take(pair, source_row.reshape(-1), axis=0).reshape(group_rows, visit_count, LAGS)
+    left_perm = (jnp.arange(group_rows)[None, :] == left_pos[:, None]).astype(jnp.bfloat16)
+    visit_perm = (jnp.arange(visit_count)[None, :] == visit_pos[:, None]).astype(jnp.bfloat16)
+    pair = pair_block(left_by_window, piece_rows, left_perm, visit_perm, lag_table, issue_order)
+    pair = jnp.swapaxes(pair.reshape(visit_count, group_rows, LAGS), 0, 1)
     norm_scale = 1.0 / math.sqrt(white.shape[1] * bin_count)
     pair = pair * norm_scale
     lag_offset = jnp.abs(jnp.arange(LAGS, dtype=jnp.int32) - LH)

time: 51.8 us -> 51.8 us (level)
  local copies, waits for them, and re-layouts: 7.72 us -> 5.66 us
  other arithmetic: 8.18 us -> 10.1 us
  Pallas kernels: 13.2 us -> 13.9 us
    gather x1 -> x0, local copies, waits for them, and re-layouts: 1.98 us -> none  [on_device(): jnp.take(pair, source_row.reshape(-1), axis=0)]
    convert_element_type x0 -> x2, other arithmetic: none -> 1.33 us  [the longest x1 0.67 us: on_device(): (jnp.arange(visit_count)[None, :] == visit_pos[:, None]).astype(jnp.bfloa...]
    mul x1, other arithmetic: 0.01 us -> 0.97 us  [on_device(): pair = pair * norm_scale]
    select_n x2 -> x0, other arithmetic: 0.85 us -> none  [the longest x1 0.84 us: on_device(): tile_stack = jnp.where(keep_mask[:, None, :], pair, 0.0)]
    broadcast_in_dim x0 -> x1, other arithmetic: none -> 0.81 us  [on_device(): return tile_stack[:, None]]
    ppermute x3, waiting for transfers between devices: 1.36 us -> 0.56 us  [chip_gather(): fetched.append(lax.ppermute(block, axis_name, pairs))]
    pallas_call x1, Pallas kernels: 13.2 us -> 13.9 us  [pair_block(): pl.pallas_call(functools.partial(cross_kernel, tuple(issue_order)), out_s...]
  transfers between devices with their start and end apart: 8 -> 8, of which waited for: 3 -> 3; matrix products, arithmetic and copies ran while one was open for 17% -> 19% of each run, Pallas kernels for 0% -> 0%
where the time goes in v13:
time: 51.8 us; the launch traced here: 51.6 us
  Pallas kernels  13.9 us (27%)
  other arithmetic  10.1 us (19%)
  starting transfers between devices  9.51 us (18%)
  matrix products  7.97 us (15%)
  local copies, waits for them, and re-layouts  5.66 us (11%)
  waiting for transfers between devices  4.21 us (8%)
    pallas_call x1, Pallas kernels, pair_block(): pl.pallas_call(functools.partial(cross_kernel, tuple(issue_order)), out_s...  13.9 us
    ppermute x3, starting transfers between devices, xor_gather(): pieces.append(lax.ppermute(block, axis_name, pairs))  5.94 us
    another operation x2, other arithmetic  4.53 us
    ppermute x3, starting transfers between devices, chip_gather(): fetched.append(lax.ppermute(block, axis_name, pairs))  3.49 us
    ppermute x3, waiting for transfers between devices, xor_gather(): pieces.append(lax.ppermute(block, axis_name, pairs))  2.53 us
    reshape x1, local copies, waits for them, and re-layouts, decimate(): blocks = records.reshape(lead_dims + (block_count, in_block))  1.68 us
    dot_general x1, matrix products, spectrum(): jnp.einsum('bwfq,gq->bwgf', real_t, sin_three, precision=lax.Precision.HIGH)  1.31 us
    dot_general x1, matrix products, spectrum(): jnp.einsum('bwfq,gq->bwgf', imag_t, sin_three, precision=lax.Precision.HIGH)  1.24 us
  transfers between devices with their start and end apart: 8, of which 3 were waited for; matrix products, arithmetic and copies ran while one was open for 19% of the time, Pallas kernels for 0%

profile of v13, /device:TPU:0, one launch (start us, length us, event | category | flops | bytes accessed | tf_op | source)
XLA Modules:
  0.0 51.6 jit_solution(13244118180401119206)
XLA Ops:
  0.2 1.7 %reshape.236 = f32[4,6,32,256]{3,2,0,1:T(8,128)S(1)} reshape(f32[4,6,8192]{2,0,1:T(4,128)} %param.3) | data formatting | bytes 1572864 | tf_op jit(solution)/shard_map/reshape | solution.py:31
  2.1 0.7 %iota_compare_fusion = pred[32,288,128]{2,1,0:T(32,128)(4,1)S(1)} fusion(s32[32,128]{1,0:T(8,128)S(1)} %iota_subtract_fusion), kind=kLoop, calls=%fused_computation.2 | loop fusion | flops 1179648 | bytes 1196032 | tf_op jit(solution)/shard_map/eq | solution.py:38
  2.7 1.1 %fusion = f32[1,288,128]{2,0,1:T(1,128)S(1)} fusion(pred[32,288,128]{2,1,0:T(32,128)(4,1)S(1)} %iota_compare_fusion, f32[32]{0:T(128)S(1)} %copy-done), kind=kOutput, calls=%fused_computation.3 | convolution fusion | flops 7077888 | bytes 1327232 | tf_op jit(solution)/shard_map/k,kij->ij/dot_general | solution.py:39
  3.8 0.7 %fusion.4 = f32[4,6,32,128]{3,2,1,0:T(8,128)S(1)} fusion(f32[288,128,1,1]{1,0,3,2:T(8,128)S(1)} %bitcast.74, f32[4,6,31,32]{3,2,1,0:T(8,128)S(1)} %copy.30, f32[4,6,32,256]{3,2,0,1:T(8,128)S(1)} %reshape.236), kind=kOutput, calls=%fused_computation.14 | convolution fusion | flops 170532864 | bytes 1422336 | tf_op jit(solution)/shard_map/swbi,ij->swbj/dot_general | solution.py:40
  5.9 1.2 %fusion.13 = f32[32,4,6,64]{3,0,2,1:T(8,128)S(1)} fusion(f32[64,4,6,64]{3,0,2,1:T(8,128)S(1)} %fusion.27, f32[64,4,6,64]{3,0,2,1:T(8,128)S(1)} %convolution_negate_fusion, f32[64,64]{1,0:T(8,128)S(1)} %get-tuple-element.14, f32[64,64]{1,0:T(8,128)S(1)} %get-tuple-element.15), kind=kOutput, calls=%fused_computation.28 | convolution fusion | flops 19197952 | bytes 1015808 | tf_op jit(solution)/shard_map/bwfq,gq->bwgf/dot_general | solution.py:60
  7.2 1.2 %fusion.17 = f32[32,4,6,64]{3,0,2,1:T(8,128)S(1)} fusion(f32[64,4,6,64]{3,0,2,1:T(8,128)S(1)} %convolution_negate_fusion, f32[64,4,6,64]{3,0,2,1:T(8,128)S(1)} %fusion.27, f32[64,64]{1,0:T(8,128)S(1)} %get-tuple-element.14, f32[64,64]{1,0:T(8,128)S(1)} %get-tuple-element.15), kind=kOutput, calls=%fused_computation.32 | convolution fusion | flops 19197952 | bytes 1015808 | tf_op jit(solution)/shard_map/bwfq,gq->bwgf/dot_general | solution.py:57
  8.4 1.2 %fusion.3 = f32[4,6,32,64]{3,2,1,0:T(8,128)S(1)} fusion(f32[32,4,6,64]{3,0,2,1:T(8,128)S(1)} %fusion.17, f32[64,4,6,64]{3,0,2,1:T(8,128)S(1)} %fusion.27, f32[64,4,6,64]{3,0,2,1:T(8,128)S(1)} %convolution_negate_fusion, f32[64,64]{1,0:T(8,128)S(1)} %get-tuple-element.14, f32[64,64]{1,0:T(8,128)S(1)} %get-tuple-element.15), kind=kOutput, calls=%fused_computation.12 | convolution fusion | flops 19247104 | bytes 1212416 | tf_op jit(solution)/shard_map/bwfq,gq->bwgf/dot_general | solution.py:59
  9.6 1.3 %add_reduce_fusion = (f32[4,6,32]{2,1,0:T(8,128)S(1)}, f32[4,6,32,64]{3,2,1,0:T(8,128)S(1)}) fusion(f32[4,6,32,64]{3,2,1,0:T(8,128)S(1)} %fusion.3, f32[32,4,6,64]{3,0,2,1:T(8,128)S(1)} %fusion.13, f32[64,4,6,64]{3,0,2,1:T(8,128)S(1)} %convolution_negate_fusion, f32[64,64]{1,0:T(8,128)S(1)} %get-tuple-element.14, f32[64,4,6,64]{3,0,2,1:T(8,128)S(1)} %fusion.27, ...), kind=kOutput, calls=%fused_computation.40 | convolution fusion | flops 19442944 | bytes 1412096 | tf_op jit(solution)/shard_map/bwfq,gq->bwgf/dot_general | solution.py:62
  11.8 4.1 %collective-permute-start.7 = (bf16[6,4,4096]{2,1,0:T(4,128)(2,1)S(1)}, bf16[6,4,4096]{2,1,0:T(4,128)(2,1)S(1)}, u32[]{:S(2)}, u32[]{:S(2)}) collective-permute-start(bf16[6,4,4096]{2,1,0:T(4,128)(2,1)S(1)} %maximum_bitcast_fusion.refs_3_.refs_4_), channel_id=1, source_target_pairs={{0,2},{1,3},{2,0},{3,1},{4,6},{5,7},{6,4},{7,5},{8,10},{9,11},{10,... | collective-permute-start | bytes 589832 | tf_op jit(solution)/shard_map/ppermute | solution.py:168
  15.9 1.3 %collective-permute-start.6 = (bf16[6,4,4096]{2,1,0:T(4,128)(2,1)S(1)}, bf16[6,4,4096]{2,1,0:T(4,128)(2,1)S(1)}, u32[]{:S(2)}, u32[]{:S(2)}) collective-permute-start(bf16[6,4,4096]{2,1,0:T(4,128)(2,1)S(1)} %maximum_bitcast_fusion.refs_3_.refs_4_), channel_id=1, source_target_pairs={{0,3},{1,2},{2,1},{3,0},{4,7},{5,6},{6,5},{7,4},{8,11},{9,10},{10,... | collective-permute-start | bytes 589832 | tf_op jit(solution)/shard_map/ppermute | solution.py:168
  17.3 2.4 %collective-permute-start.2 = (bf16[6,4,4096]{2,1,0:T(4,128)(2,1)S(1)}, bf16[6,4,4096]{2,1,0:T(4,128)(2,1)S(1)}, u32[]{:S(2)}, u32[]{:S(2)}) collective-permute-start(bf16[6,4,4096]{2,1,0:T(4,128)(2,1)S(1)} %maximum_bitcast_fusion.refs_3_.refs_4_), channel_id=1, source_target_pairs={{0,24},{4,28},{8,16},{12,20},{16,8},{20,12},{24,0},{28,4},{1,25},{... | collective-permute-start | bytes 589832 | tf_op jit(solution)/shard_map/ppermute | solution.py:180
  20.8 0.7 %gather_fusion = s32[16]{0:T(128)S(1)} fusion(s32[4]{0:T(128)S(1)} %iota_xor_fusion.1, s32[1024]{0:T(1024)S(1)} %pad_clamp_fusion.1), kind=kCustom, calls=%fused_computation | custom fusion | bytes 192 | tf_op jit(solution)/shard_map/gather | solution.py:219
  21.5 0.7 %gather_fusion.1 = s32[32]{0:T(128)S(1)} fusion(s32[8]{0:T(128)S(1)} %iota_xor_fusion, s32[1024]{0:T(1024)S(1)} %pad_clamp_fusion), kind=kCustom, calls=%fused_computation.1 | custom fusion | bytes 384 | tf_op jit(solution)/shard_map/gather | solution.py:221
  22.2 0.7 %fusion.52.refs_13_ = bf16[32,32]{1,0:T(8,128)(2,1)} fusion(s32[32]{0:T(128)S(1)} %fusion.61), kind=kLoop, calls=%fused_computation.85 | loop fusion | flops 2048 | bytes 2176 | tf_op jit(solution)/shard_map/convert_element_type | solution.py:223
  22.9 4.4 %cosine_convert_fusion = (bf16[2048,128]{1,0:T(8,128)(2,1)S(1)}, bf16[2048,128]{1,0:T(8,128)(2,1)S(1)}) fusion(s32[128]{0:T(128)S(1)} %iota_add_fusion), kind=kLoop, calls=%fused_computation.23 | loop fusion | flops 4194304 | bytes 1049088 | tf_op jit(solution)/shard_map/convert
  27.2 0.7 %fusion.59.refs_12_ = bf16[16,16]{1,0:T(8,128)(2,1)} fusion(s32[16]{0:T(128)S(1)} %fusion.60), kind=kLoop, calls=%fused_computation.89 | loop fusion | flops 512 | bytes 576 | tf_op jit(solution)/shard_map/convert_element_type | solution.py:222
  29.5 1.1 %pad_maximum_fusion.refs_14_ = bf16[4096,128]{1,0:T(8,128)(2,1)} fusion(bf16[2048,128]{1,0:T(8,128)(2,1)S(1)} %get-tuple-element.11, bf16[2048,128]{1,0:T(8,128)(2,1)S(1)} %get-tuple-element.10), kind=kLoop, calls=%fused_computation.21 | loop fusion | flops 2097152 | bytes 2097152 | tf_op jit(solution)/shard_map/concatenate | solution.py:204
  30.5 1.1 %collective-permute-done.3 = bf16[6,12,4096]{2,1,0:T(8,128)(2,1)S(1)} collective-permute-done((bf16[6,12,4096]{2,1,0:T(8,128)(2,1)S(1)}, bf16[6,12,4096]{2,1,0:T(8,128)(2,1)S(1)}, u32[]{:S(2)}, u32[]{:S(2)}) %collective-permute-start.3) | collective-permute-done | bytes 589856 | tf_op jit(solution)/shard_map/ppermute | solution.py:184
  31.7 1.0 %fusion.93 = (bf16[6,4,4096]{2,1,0:T(4,128)(2,1)}, bf16[6,4,4096]{2,1,0:T(4,128)(2,1)}, bf16[6,4,4096]{2,1,0:T(4,128)(2,1)}) fusion(bf16[6,12,4096]{2,1,0:T(8,128)(2,1)S(1)} %collective-permute-done.3), kind=kLoop, calls=%fused_computation.142 | loop fusion | bytes 1179648 | tf_op jit(solution)/shard_map/slice | solution.py:187
  32.7 2.5 %collective-permute-done.4.refs_5_ = bf16[6,4,4096]{2,1,0:T(4,128)(2,1)S(1)} collective-permute-done((bf16[6,4,4096]{2,1,0:T(4,128)(2,1)S(1)}, bf16[6,4,4096]{2,1,0:T(4,128)(2,1)S(1)}, u32[]{:S(2)}, u32[]{:S(2)}) %collective-permute-start.4) | collective-permute-done | bytes 196640 | tf_op jit(solution)/shard_map/ppermute | solution.py:168
  35.2 0.7 %copy-done.8 = bf16[6,4,4096]{2,1,0:T(4,128)(2,1)} copy-done((bf16[6,4,4096]{2,1,0:T(4,128)(2,1)}, bf16[6,4,4096]{2,1,0:T(4,128)(2,1)S(1)}, u32[]{:S(2)}) %copy-start.8) | copy-done | bytes 196632
  35.9 13.9 %shard_map.37 = f32[512,128]{1,0:T(8,128)} custom-call(bf16[6,4,4096]{2,1,0:T(4,128)(2,1)} %get-tuple-element.7.refs_0_, bf16[6,4,4096]{2,1,0:T(4,128)(2,1)} %get-tuple-element.6.refs_1_, bf16[6,4,4096]{2,1,0:T(4,128)(2,1)} %get-tuple-element.5.refs_2_, bf16[6,4,4096]{2,1,0:T(4,128)(2,1)} %copy-done.1, bf16[6,4,4096]{2,1,0:T(4,128)(2,1)} %copy-done.1, ...), custom_call_target="tpu_custom_call" | custom-call | flops 587202560 | bytes 3670016 | tf_op jit(solution)/shard_map/pallas_call | solution.py:142
  49.8 1.0 %broadcast_multiply_fusion = f32[512,128]{1,0:T(8,128)S(1)} fusion(f32[512,128]{1,0:T(8,128)} %shard_map.37), kind=kLoop, calls=%fused_computation.44 | loop fusion | flops 65536 | bytes 524288 | tf_op jit(solution)/shard_map/mul | solution.py:227
  50.8 0.8 %fusion.21 = f32[16,1,32,128]{3,2,1,0:T(8,128)} fusion(f32[32,16,128]{2,1,0:T(8,128)S(1)} %bitcast.73, pred[16,128]{1,0:T(8,128)(4,1)S(1)} %broadcast_compare_fusion), kind=kLoop, calls=%fused_computation.42 | loop fusion | flops 65536 | bytes 526336 | tf_op jit(solution)/shard_map/broadcast_in_dim | solution.py:231
  (57 shorter events, 5.2 us)
Async XLA Ops:
  0.0 2.7 %copy-start = (f32[32]{0:T(128)S(1)}, f32[32]{0:T(128)}, u32[]{:S(2)}) copy-start(f32[32]{0:T(128)} %param.4) | copy-start | bytes 388
  11.8 17.5 %copy-start.1 = (bf16[6,4,4096]{2,1,0:T(4,128)(2,1)}, bf16[6,4,4096]{2,1,0:T(4,128)(2,1)S(1)}, u32[]{:S(2)}) copy-start(bf16[6,4,4096]{2,1,0:T(4,128)(2,1)S(1)} %maximum_bitcast_fusion.refs_3_.refs_4_) | copy-start | bytes 589828
  11.8 20.9 %collective-permute-start.7 = (bf16[6,4,4096]{2,1,0:T(4,128)(2,1)S(1)}, bf16[6,4,4096]{2,1,0:T(4,128)(2,1)S(1)}, u32[]{:S(2)}, u32[]{:S(2)}) collective-permute-start(bf16[6,4,4096]{2,1,0:T(4,128)(2,1)S(1)} %maximum_bitcast_fusion.refs_3_.refs_4_), channel_id=1, source_target_pairs={{0,2},{1,3},{2,0},{3,1},{4,6},{5,7},{6,4},{7,5},{8,10},{9,11},{10,... | collective-permute-start | bytes 589832 | tf_op jit(solution)/shard_map/ppermute | solution.py:168
  15.9 16.8 %collective-permute-start.6 = (bf16[6,4,4096]{2,1,0:T(4,128)(2,1)S(1)}, bf16[6,4,4096]{2,1,0:T(4,128)(2,1)S(1)}, u32[]{:S(2)}, u32[]{:S(2)}) collective-permute-start(bf16[6,4,4096]{2,1,0:T(4,128)(2,1)S(1)} %maximum_bitcast_fusion.refs_3_.refs_4_), channel_id=1, source_target_pairs={{0,3},{1,2},{2,1},{3,0},{4,7},{5,6},{6,5},{7,4},{8,11},{9,10},{10,... | collective-permute-start | bytes 589832 | tf_op jit(solution)/shard_map/ppermute | solution.py:168
  17.3 10.7 %collective-permute-start.2 = (bf16[6,4,4096]{2,1,0:T(4,128)(2,1)S(1)}, bf16[6,4,4096]{2,1,0:T(4,128)(2,1)S(1)}, u32[]{:S(2)}, u32[]{:S(2)}) collective-permute-start(bf16[6,4,4096]{2,1,0:T(4,128)(2,1)S(1)} %maximum_bitcast_fusion.refs_3_.refs_4_), channel_id=1, source_target_pairs={{0,24},{4,28},{8,16},{12,20},{16,8},{20,12},{24,0},{28,4},{1,25},{... | collective-permute-start | bytes 589832 | tf_op jit(solution)/shard_map/ppermute | solution.py:180
  19.7 8.8 %collective-permute-start.1 = (bf16[6,4,4096]{2,1,0:T(4,128)(2,1)S(1)}, bf16[6,4,4096]{2,1,0:T(4,128)(2,1)S(1)}, u32[]{:S(2)}, u32[]{:S(2)}) collective-permute-start(bf16[6,4,4096]{2,1,0:T(4,128)(2,1)S(1)} %maximum_bitcast_fusion.refs_3_.refs_4_), channel_id=1, source_target_pairs={{0,16},{4,20},{8,24},{12,28},{16,0},{20,4},{24,8},{28,12},{1,17},{... | collective-permute-start | bytes 589832 | tf_op jit(solution)/shard_map/ppermute | solution.py:180
  20.2 8.8 %collective-permute-start = (bf16[6,4,4096]{2,1,0:T(4,128)(2,1)S(1)}, bf16[6,4,4096]{2,1,0:T(4,128)(2,1)S(1)}, u32[]{:S(2)}, u32[]{:S(2)}) collective-permute-start(bf16[6,4,4096]{2,1,0:T(4,128)(2,1)S(1)} %maximum_bitcast_fusion.refs_3_.refs_4_), channel_id=1, source_target_pairs={{0,8},{4,12},{8,0},{12,4},{16,24},{20,28},{24,16},{28,20},{1,9},{5... | collective-permute-start | bytes 589832 | tf_op jit(solution)/shard_map/ppermute | solution.py:180
  22.9 6.5 %copy-start.9 = (s32[16]{0:T(128)S(1)}, s32[16]{0:T(128)}, u32[]{:S(2)}) copy-start(s32[16]{0:T(128)} %param.5) | copy-start | bytes 196
  27.9 2.6 %copy-start.2 = (bf16[6,4,4096]{2,1,0:T(4,128)(2,1)}, bf16[6,4,4096]{2,1,0:T(4,128)(2,1)S(1)}, u32[]{:S(2)}) copy-start(bf16[6,4,4096]{2,1,0:T(4,128)(2,1)S(1)} %collective-permute-done.2.refs_9_) | copy-start | bytes 589828
  27.9 4.8 %collective-permute-start.5 = (bf16[6,4,4096]{2,1,0:T(4,128)(2,1)S(1)}, bf16[6,4,4096]{2,1,0:T(4,128)(2,1)S(1)}, u32[]{:S(2)}, u32[]{:S(2)}) collective-permute-start(bf16[6,4,4096]{2,1,0:T(4,128)(2,1)S(1)} %maximum_bitcast_fusion.refs_3_.refs_4_), channel_id=1, source_target_pairs={{0,4},{4,0},{8,12},{12,8},{16,20},{20,16},{24,28},{28,24},{1,5},{5... | collective-permute-start | bytes 589832 | tf_op jit(solution)/shard_map/ppermute | solution.py:182
  28.5 2.1 %copy-start.3 = (bf16[6,4,4096]{2,1,0:T(4,128)(2,1)}, bf16[6,4,4096]{2,1,0:T(4,128)(2,1)S(1)}, u32[]{:S(2)}) copy-start(bf16[6,4,4096]{2,1,0:T(4,128)(2,1)S(1)} %collective-permute-done.1.refs_8_) | copy-start | bytes 589828
  28.5 6.8 %collective-permute-start.4 = (bf16[6,4,4096]{2,1,0:T(4,128)(2,1)S(1)}, bf16[6,4,4096]{2,1,0:T(4,128)(2,1)S(1)}, u32[]{:S(2)}, u32[]{:S(2)}) collective-permute-start(bf16[6,4,4096]{2,1,0:T(4,128)(2,1)S(1)} %maximum_bitcast_fusion.refs_3_.refs_4_), channel_id=1, source_target_pairs={{0,1},{1,0},{2,3},{3,2},{4,5},{5,4},{6,7},{7,6},{8,9},{9,8},{10,11... | collective-permute-start | bytes 589832 | tf_op jit(solution)/shard_map/ppermute | solution.py:168
  29.0 1.6 %copy-start.4 = (bf16[6,4,4096]{2,1,0:T(4,128)(2,1)}, bf16[6,4,4096]{2,1,0:T(4,128)(2,1)S(1)}, u32[]{:S(2)}) copy-start(bf16[6,4,4096]{2,1,0:T(4,128)(2,1)S(1)} %collective-permute-done.refs_7_) | copy-start | bytes 589828
  29.3 2.4 %collective-permute-start.3 = (bf16[6,12,4096]{2,1,0:T(8,128)(2,1)S(1)}, bf16[6,12,4096]{2,1,0:T(8,128)(2,1)S(1)}, u32[]{:S(2)}, u32[]{:S(2)}) collective-permute-start(bf16[6,12,4096]{2,1,0:T(8,128)(2,1)S(1)} %pad_maximum_fusion.1), channel_id=1, source_target_pairs={{0,4},{4,0},{8,12},{12,8},{16,20},{20,16},{24,28},{28,24},{1,5},{5... | collective-permute-start | bytes 1769480 | tf_op jit(solution)/shard_map/ppermute | solution.py:184
  32.7 2.6 %copy-start.5 = (bf16[6,4,4096]{2,1,0:T(4,128)(2,1)}, bf16[6,4,4096]{2,1,0:T(4,128)(2,1)S(1)}, u32[]{:S(2)}) copy-start(bf16[6,4,4096]{2,1,0:T(4,128)(2,1)S(1)} %collective-permute-done.7.refs_11_) | copy-start | bytes 589828
  32.7 2.6 %copy-start.6 = (bf16[6,4,4096]{2,1,0:T(4,128)(2,1)}, bf16[6,4,4096]{2,1,0:T(4,128)(2,1)S(1)}, u32[]{:S(2)}) copy-start(bf16[6,4,4096]{2,1,0:T(4,128)(2,1)S(1)} %collective-permute-done.6.refs_10_) | copy-start | bytes 589828
  32.7 2.5 %copy-start.7 = (bf16[6,4,4096]{2,1,0:T(4,128)(2,1)}, bf16[6,4,4096]{2,1,0:T(4,128)(2,1)S(1)}, u32[]{:S(2)}) copy-start(bf16[6,4,4096]{2,1,0:T(4,128)(2,1)S(1)} %collective-permute-done.5.refs_6_) | copy-start | bytes 589828
  35.2 0.7 %copy-start.8 = (bf16[6,4,4096]{2,1,0:T(4,128)(2,1)}, bf16[6,4,4096]{2,1,0:T(4,128)(2,1)S(1)}, u32[]{:S(2)}) copy-start(bf16[6,4,4096]{2,1,0:T(4,128)(2,1)S(1)} %collective-permute-done.4.refs_5_) | copy-start | bytes 589828

commit v14 on v13

--- a/solution.py
+++ b/solution.py
@@ -2,6 +2,7 @@
 import math
 
 import jax
+import numpy as np
 import jax.numpy as jnp
 from jax import lax
 from jax.experimental import pallas as pl
@@ -32,11 +33,12 @@
     tails = blocks[:, :, :-1, in_block - tap_count :]
     tails = jnp.concatenate([jnp.zeros(lead_dims + (1, tap_count), records.dtype), tails], axis=2)
     windows = jnp.concatenate([tails, blocks], axis=3)
-    tap_ids = jnp.arange(tap_count, dtype=jnp.int32)[:, None, None]
-    in_ids = jnp.arange(in_block + tap_count, dtype=jnp.int32)[None, :, None]
-    out_ids = jnp.arange(out_block, dtype=jnp.int32)[None, None, :]
-    onehot = (in_ids == DECIM * out_ids + tap_count - tap_ids).astype(jnp.float32)
-    band_matrix = jnp.einsum("k,kij->ij", fir_taps, onehot, precision=lax.Precision.HIGH)
+    in_ids = np.arange(in_block + tap_count)[:, None]
+    out_ids = np.arange(out_block)[None, :]
+    tap_index = DECIM * out_ids + tap_count - in_ids
+    inside = (tap_index >= 0) & (tap_index < tap_count)
+    padded_taps = jnp.concatenate([fir_taps, jnp.zeros((1,), fir_taps.dtype)])
+    band_matrix = padded_taps[np.where(inside, tap_index, tap_count).astype(np.int32)]
     summed = jnp.einsum("swbi,ij->swbj", windows, band_matrix, precision=lax.Precision.HIGH)
     return summed.reshape(lead_dims + (block_count * out_block,))
 
@@ -78,7 +80,7 @@
 
 def cross_kernel(slots, *refs):
     piece_refs = refs[:len(slots)]
-    left_perm, visit_perm, table_ref, out_ref, left_f32, visit_f32, cross_ref = refs[len(slots):]
+    left_perm, visit_perm, limit_ref, table_ref, out_ref, left_f32, visit_f32, cross_ref = refs[len(slots):]
     left_refs = [ref for ref, slot in zip(piece_refs, slots) if slot[0] == 0]
     window_count, piece, width = left_refs[0].shape
     rows_left = left_f32.shape[1]
@@ -90,6 +92,7 @@
     group_rows = cross_ref.shape[0]
     group = group_rows // (piece * rows_left)
     visit_count = visit_f32.shape[1] // piece
+    scale = 1.0 / math.sqrt(window_count * bin_count)
 
     for ref, (kind, index) in zip(piece_refs, slots):
         target = left_f32 if kind == 0 else visit_f32
@@ -122,12 +125,14 @@
             return carry
 
         lax.fori_loop(0, group * piece * chunks, one_chunk, 0)
-        out_ref[base * rows_left:base * rows_left + group_rows, :] = jnp.dot(
-            cross_ref[...], table_ref[...], preferred_element_type=jnp.float32
-        )
-
-
-def pair_block(left_pieces, visit_pieces, left_perm, visit_perm, lag_table, issue_order):
+        rows = pl.ds(base * rows_left, group_rows)
+        block = jnp.dot(cross_ref[...], table_ref[...], preferred_element_type=jnp.float32) * scale
+        lag = lax.broadcasted_iota(jnp.int32, block.shape, 1)
+        keep = jnp.abs(lag - block.shape[1] // 2) <= limit_ref[rows, :]
+        out_ref[rows, :] = jnp.where(keep, block, 0.0)
+
+
+def pair_block(left_pieces, visit_pieces, left_perm, visit_perm, limit, lag_table, issue_order):
     window_count, piece, width = left_pieces[0].shape
     left_count = len(left_pieces)
     visit_count = len(visit_pieces)
@@ -142,7 +147,7 @@
     return pl.pallas_call(
         functools.partial(cross_kernel, tuple(issue_order)),
         out_shape=jax.ShapeDtypeStruct((visit_rows * rows_left, lag_count), jnp.float32),
-        in_specs=[pl.BlockSpec(memory_space=vmem)] * (left_count + visit_count + 3),
+        in_specs=[pl.BlockSpec(memory_space=vmem)] * (left_count + visit_count + 4),
         out_specs=pl.BlockSpec(memory_space=vmem),
         scratch_shapes=[
             vmem((window_count, rows_left, width), jnp.float32),
@@ -156,7 +161,7 @@
             bytes_accessed=2 * width * (window_count * (rows_left + visit_rows) + lag_count)
             + 4 * visit_rows * rows_left * lag_count,
         ),
-    )(*[(left_pieces, visit_pieces)[kind][index] for kind, index in issue_order], left_perm, visit_perm, lag_table)
+    )(*[(left_pieces, visit_pieces)[kind][index] for kind, index in issue_order], left_perm, visit_perm, limit, lag_table)
 
 
 def xor_gather(block, axis_name, size):
@@ -221,14 +226,10 @@
         visit_pos = visit_order[visit_pos // piece] * piece + visit_pos % piece
     left_perm = (jnp.arange(group_rows)[None, :] == left_pos[:, None]).astype(jnp.bfloat16)
     visit_perm = (jnp.arange(visit_count)[None, :] == visit_pos[:, None]).astype(jnp.bfloat16)
-    pair = pair_block(left_by_window, piece_rows, left_perm, visit_perm, lag_table, issue_order)
+    limit = jnp.tile(lag_limit, visit_count)[:, None]
+    pair = pair_block(left_by_window, piece_rows, left_perm, visit_perm, limit, lag_table, issue_order)
     pair = jnp.swapaxes(pair.reshape(visit_count, group_rows, LAGS), 0, 1)
-    norm_scale = 1.0 / math.sqrt(white.shape[1] * bin_count)
-    pair = pair * norm_scale
-    lag_offset = jnp.abs(jnp.arange(LAGS, dtype=jnp.int32) - LH)
-    keep_mask = lag_offset[None, :] <= lag_limit[:, None]
-    tile_stack = jnp.where(keep_mask[:, None, :], pair, 0.0)
-    return tile_stack[:, None]
+    return pair[:, None]
 
 
 def solution(mesh):

time: 51.8 us -> 87.5 us (1.69)
  matrix products: 7.97 us -> 27.3 us
  waiting for transfers between devices: 4.21 us -> 14.7 us
  local copies, waits for them, and re-layouts: 5.66 us -> 13 us
  other arithmetic: 10.1 us -> 7.76 us
    dot_general x1, matrix products: 0.71 us -> 21.2 us  [decimate(): jnp.einsum('swbi,ij->swbj', windows, band_matrix, precision=lax.Precision...]
    ppermute x3, waiting for transfers between devices: 2.53 us -> 14.4 us  [xor_gather(): pieces.append(lax.ppermute(block, axis_name, pairs))]
    gather x0 -> x2, local copies, waits for them, and re-layouts: none -> 3.9 us  [decimate(): padded_taps[np.where(inside, tap_index, tap_count).astype(np.int32)]]
    reshape x0 -> x1, local copies, waits for them, and re-layouts: none -> 1.74 us  [on_device(): pair = jnp.swapaxes(pair.reshape(visit_count, group_rows, LAGS), 0, 1)]
    ppermute x3, starting transfers between devices: 5.94 us -> 4.79 us  [xor_gather(): pieces.append(lax.ppermute(block, axis_name, pairs))]
    ppermute x3, starting transfers between devices: 3.49 us -> 4.55 us  [chip_gather(): fetched.append(lax.ppermute(block, axis_name, pairs))]
    dot_general x1 -> x0, matrix products: 1.06 us -> none  [decimate(): jnp.einsum('k,kij->ij', fir_taps, onehot, precision=lax.Precision.HIGH)]
    mul x1 -> x0, other arithmetic: 0.97 us -> none  [on_device(): pair = pair * norm_scale]
  transfers between devices with their start and end apart: 8 -> 8, of which waited for: 3 -> 3; matrix products, arithmetic and copies ran while one was open for 19% -> 12% of each run, Pallas kernels for 0% -> 0%
where the time goes in v14:
time: 87.5 us; the launch traced here: 86.9 us
  matrix products  27.3 us (31%)
  waiting for transfers between devices  14.7 us (17%)
  Pallas kernels  13.9 us (16%)
  local copies, waits for them, and re-layouts  13 us (15%)
  starting transfers between devices  9.63 us (11%)
  other arithmetic  7.76 us (9%)
    dot_general x1, matrix products, decimate(): jnp.einsum('swbi,ij->swbj', windows, band_matrix, precision=lax.Precision...  21.2 us
    ppermute x3, waiting for transfers between devices, xor_gather(): pieces.append(lax.ppermute(block, axis_name, pairs))  14.4 us
    pallas_call x1, Pallas kernels, pair_block(): pl.pallas_call(functools.partial(cross_kernel, tuple(issue_order)), out_s...  13.9 us
    ppermute x3, starting transfers between devices, xor_gather(): pieces.append(lax.ppermute(block, axis_name, pairs))  4.79 us
    another operation x2, other arithmetic  4.73 us
    ppermute x3, starting transfers between devices, chip_gather(): fetched.append(lax.ppermute(block, axis_name, pairs))  4.55 us
    gather x2, local copies, waits for them, and re-layouts, decimate(): padded_taps[np.where(inside, tap_index, tap_count).astype(np.int32)]  3.9 us
  transfers between devices with their start and end apart: 8, of which 3 were waited for; matrix products, arithmetic and copies ran while one was open for 12% of the time, Pallas kernels for 0%

profile of v14, /device:TPU:0, one launch (start us, length us, event | category | flops | bytes accessed | tf_op | source)
XLA Modules:
  0.0 86.9 jit_solution(4561018203117811407)
XLA Ops:
  0.0 2.1 %fusion.155 = (f32[1]{0:T(128)}, f32[1]{0:T(128)}, f32[1]{0:T(128)}, f32[1]{0:T(128)}, f32[1]{0:T(128)}, /*index=5*/f32[1]{0:T(128)}, f32[1]{0:T(128)}, f32[1]{0...) fusion(f32[32]{0:T(128)} %param.6), kind=kLoop, calls=%fused_computation.199 | loop fusion | bytes 152 | tf_op jit(solution)/shard_map/gather | solution.py:41
  2.1 1.8 %fusion.156 = (f32[1]{0:T(128)}, f32[1]{0:T(128)}, f32[1]{0:T(128)}, f32[1]{0:T(128)}, f32[1]{0:T(128)}, /*index=5*/f32[1]{0:T(128)}, f32[1]{0:T(128)}, f32[1]{0...) fusion(f32[32]{0:T(128)} %param.6), kind=kLoop, calls=%fused_computation.200 | loop fusion | bytes 104 | tf_op jit(solution)/shard_map/gather | solution.py:41
  3.9 1.7 %reshape.180 = f32[4,6,32,256]{3,2,0,1:T(8,128)S(1)} reshape(f32[4,6,8192]{2,0,1:T(4,128)} %param.5) | data formatting | bytes 1572864 | tf_op jit(solution)/shard_map/reshape | solution.py:32
  6.9 21.2 %fusion.2 = f32[4,6,32,128]{3,2,1,0:T(8,128)S(1)} fusion(f32[4,6,31,32]{3,2,1,0:T(8,128)S(1)} %copy.28, pred[288,128]{1,0:T(32,128)(4,1)S(1)} %copy-done.9, pred[288,128]{1,0:T(32,128)(4,1)S(1)} %copy-done.10, pred[288,128]{1,0:T(32,128)(4,1)S(1)} %copy-done.11, pred[288,128]{1,0:T(32,128)(4,1)S(1)} %copy-done.12, pred[288,128]{1,0:T(32,128)(4,1)S(1)} %copy-done.13, ...), kind=kOutput, calls=%fused_computation.11 | convolution fusion | flops 171712512 | bytes 2454656 | tf_op jit(solution)/shard_map/swbi,ij->swbj/dot_general | solution.py:42
  29.6 1.2 %fusion.11 = f32[32,4,6,64]{3,0,2,1:T(8,128)S(1)} fusion(f32[64,4,6,64]{3,0,2,1:T(8,128)S(1)} %fusion.90, f32[64,4,6,64]{3,0,2,1:T(8,128)S(1)} %convolution_negate_fusion, f32[64,64]{1,0:T(8,128)S(1)} %get-tuple-element.46, f32[64,64]{1,0:T(8,128)S(1)} %get-tuple-element.47), kind=kOutput, calls=%fused_computation.25 | convolution fusion | flops 19197952 | bytes 1015808 | tf_op jit(solution)/shard_map/bwfq,gq->bwgf/dot_general | solution.py:62
  30.9 1.2 %fusion.15 = f32[32,4,6,64]{3,0,2,1:T(8,128)S(1)} fusion(f32[64,4,6,64]{3,0,2,1:T(8,128)S(1)} %convolution_negate_fusion, f32[64,4,6,64]{3,0,2,1:T(8,128)S(1)} %fusion.90, f32[64,64]{1,0:T(8,128)S(1)} %get-tuple-element.46, f32[64,64]{1,0:T(8,128)S(1)} %get-tuple-element.47), kind=kOutput, calls=%fused_computation.29 | convolution fusion | flops 19197952 | bytes 1015808 | tf_op jit(solution)/shard_map/bwfq,gq->bwgf/dot_general | solution.py:59
  32.1 1.2 %fusion.1 = f32[4,6,32,64]{3,2,1,0:T(8,128)S(1)} fusion(f32[32,4,6,64]{3,0,2,1:T(8,128)S(1)} %fusion.15, f32[64,4,6,64]{3,0,2,1:T(8,128)S(1)} %fusion.90, f32[64,4,6,64]{3,0,2,1:T(8,128)S(1)} %convolution_negate_fusion, f32[64,64]{1,0:T(8,128)S(1)} %get-tuple-element.46, f32[64,64]{1,0:T(8,128)S(1)} %get-tuple-element.47), kind=kOutput, calls=%fused_computation.9 | convolution fusion | flops 19247104 | bytes 1212416 | tf_op jit(solution)/shard_map/bwfq,gq->bwgf/dot_general | solution.py:61
  33.3 1.3 %add_reduce_fusion = (f32[4,6,32]{2,1,0:T(8,128)S(1)}, f32[4,6,32,64]{3,2,1,0:T(8,128)S(1)}) fusion(f32[4,6,32,64]{3,2,1,0:T(8,128)S(1)} %fusion.1, f32[32,4,6,64]{3,0,2,1:T(8,128)S(1)} %fusion.11, f32[64,4,6,64]{3,0,2,1:T(8,128)S(1)} %convolution_negate_fusion, f32[64,64]{1,0:T(8,128)S(1)} %get-tuple-element.46, f32[64,4,6,64]{3,0,2,1:T(8,128)S(1)} %fusion.90, ...), kind=kOutput, calls=%fused_computation.37 | convolution fusion | flops 19442944 | bytes 1412096 | tf_op jit(solution)/shard_map/bwfq,gq->bwgf/dot_general | solution.py:64
  35.5 3.0 %collective-permute-start = (bf16[6,4,4096]{2,1,0:T(4,128)(2,1)S(1)}, bf16[6,4,4096]{2,1,0:T(4,128)(2,1)S(1)}, u32[]{:S(2)}, u32[]{:S(2)}) collective-permute-start(bf16[6,4,4096]{2,1,0:T(4,128)(2,1)S(1)} %maximum_bitcast_fusion.refs_3_.refs_4_), channel_id=1, source_target_pairs={{0,8},{4,12},{8,0},{12,4},{16,24},{20,28},{24,16},{28,20},{1,9},{5... | collective-permute-start | bytes 589832 | tf_op jit(solution)/shard_map/ppermute | solution.py:185
  38.5 1.5 %collective-permute-start.1 = (bf16[6,4,4096]{2,1,0:T(4,128)(2,1)S(1)}, bf16[6,4,4096]{2,1,0:T(4,128)(2,1)S(1)}, u32[]{:S(2)}, u32[]{:S(2)}) collective-permute-start(bf16[6,4,4096]{2,1,0:T(4,128)(2,1)S(1)} %maximum_bitcast_fusion.refs_3_.refs_4_), channel_id=1, source_target_pairs={{0,16},{4,20},{8,24},{12,28},{16,0},{20,4},{24,8},{28,12},{1,17},{... | collective-permute-start | bytes 589832 | tf_op jit(solution)/shard_map/ppermute | solution.py:185
  40.0 2.0 %collective-permute-start.4 = (bf16[6,4,4096]{2,1,0:T(4,128)(2,1)S(1)}, bf16[6,4,4096]{2,1,0:T(4,128)(2,1)S(1)}, u32[]{:S(2)}, u32[]{:S(2)}) collective-permute-start(bf16[6,4,4096]{2,1,0:T(4,128)(2,1)S(1)} %maximum_bitcast_fusion.refs_3_.refs_4_), channel_id=1, source_target_pairs={{0,1},{1,0},{2,3},{3,2},{4,5},{5,4},{6,7},{7,6},{8,9},{9,8},{10,11... | collective-permute-start | bytes 589832 | tf_op jit(solution)/shard_map/ppermute | solution.py:173
  42.1 4.6 %cosine_convert_fusion = (bf16[2048,128]{1,0:T(8,128)(2,1)S(1)}, bf16[2048,128]{1,0:T(8,128)(2,1)S(1)}) fusion(s32[128]{0:T(128)S(1)} %iota_add_fusion), kind=kLoop, calls=%fused_computation.20 | loop fusion | flops 4194304 | bytes 1049088 | tf_op jit(solution)/shard_map/convert
  46.7 0.7 gather_fusion.1
  47.4 0.7 fusion.115.refs_13_
  48.1 0.9 broadcast_in_dim_tile.4.refs_14_
  49.0 0.7 gather_fusion
  49.7 2.5 %collective-permute-start.6 = (bf16[6,4,4096]{2,1,0:T(4,128)(2,1)S(1)}, bf16[6,4,4096]{2,1,0:T(4,128)(2,1)S(1)}, u32[]{:S(2)}, u32[]{:S(2)}) collective-permute-start(bf16[6,4,4096]{2,1,0:T(4,128)(2,1)S(1)} %maximum_bitcast_fusion.refs_3_.refs_4_), channel_id=1, source_target_pairs={{0,3},{1,2},{2,1},{3,0},{4,7},{5,6},{6,5},{7,4},{8,11},{9,10},{10,... | collective-permute-start | bytes 589832 | tf_op jit(solution)/shard_map/ppermute | solution.py:173
  53.1 0.7 fusion.122.refs_12_
  53.7 1.1 %pad_maximum_fusion.refs_15_ = bf16[4096,128]{1,0:T(8,128)(2,1)} fusion(bf16[2048,128]{1,0:T(8,128)(2,1)S(1)} %get-tuple-element.11, bf16[2048,128]{1,0:T(8,128)(2,1)S(1)} %get-tuple-element.10), kind=kLoop, calls=%fused_computation.18 | loop fusion | flops 2097152 | bytes 2097152 | tf_op jit(solution)/shard_map/concatenate | solution.py:209
  55.1 1.0 %fusion.154 = (bf16[6,4,4096]{2,1,0:T(4,128)(2,1)}, bf16[6,4,4096]{2,1,0:T(4,128)(2,1)}, bf16[6,4,4096]{2,1,0:T(4,128)(2,1)}) fusion(bf16[6,12,4096]{2,1,0:T(8,128)(2,1)S(1)} %collective-permute-done.3), kind=kLoop, calls=%fused_computation.198 | loop fusion | bytes 1179648 | tf_op jit(solution)/shard_map/slice | solution.py:192
  56.1 3.2 %collective-permute-done.6.refs_10_ = bf16[6,4,4096]{2,1,0:T(4,128)(2,1)S(1)} collective-permute-done((bf16[6,4,4096]{2,1,0:T(4,128)(2,1)S(1)}, bf16[6,4,4096]{2,1,0:T(4,128)(2,1)S(1)}, u32[]{:S(2)}, u32[]{:S(2)}) %collective-permute-start.6) | collective-permute-done | bytes 196640 | tf_op jit(solution)/shard_map/ppermute | solution.py:173
  59.3 11.2 %collective-permute-done.7.refs_11_ = bf16[6,4,4096]{2,1,0:T(4,128)(2,1)S(1)} collective-permute-done((bf16[6,4,4096]{2,1,0:T(4,128)(2,1)S(1)}, bf16[6,4,4096]{2,1,0:T(4,128)(2,1)S(1)}, u32[]{:S(2)}, u32[]{:S(2)}) %collective-permute-start.7) | collective-permute-done | bytes 196640 | tf_op jit(solution)/shard_map/ppermute | solution.py:173
  71.2 13.9 %shard_map.55 = f32[512,128]{1,0:T(8,128)} custom-call(bf16[6,4,4096]{2,1,0:T(4,128)(2,1)} %get-tuple-element.7.refs_0_, bf16[6,4,4096]{2,1,0:T(4,128)(2,1)} %get-tuple-element.6.refs_1_, bf16[6,4,4096]{2,1,0:T(4,128)(2,1)} %get-tuple-element.5.refs_2_, bf16[6,4,4096]{2,1,0:T(4,128)(2,1)} %copy-done, bf16[6,4,4096]{2,1,0:T(4,128)(2,1)} %copy-done, ...), custom_call_target="tpu_custom_call" | custom-call | flops 587202560 | bytes 3670016 | tf_op jit(solution)/shard_map/pallas_call | solution.py:147
  85.1 1.7 %copy.27 = f32[32,16,128]{2,0,1:T(8,128)} copy(f32[32,16,128]{2,1,0:T(8,128)} %bitcast.101) | data formatting | bytes 524288 | tf_op jit(solution)/shard_map/reshape | solution.py:231
  (116 shorter events, 5.3 us)
Async XLA Ops:
  5.9 0.9 %copy-start.33 = (pred[288,128]{1,0:T(32,128)(4,1)S(1)}, pred[288,128]{1,0:T(32,128)(4,1)}, u32[]{:S(2)}) copy-start(pred[288,128]{1,0:T(32,128)(4,1)} %constant.197) | copy-start | bytes 110596
  5.9 0.9 %copy-start.34 = (pred[288,128]{1,0:T(32,128)(4,1)S(1)}, pred[288,128]{1,0:T(32,128)(4,1)}, u32[]{:S(2)}) copy-start(pred[288,128]{1,0:T(32,128)(4,1)} %constant.198) | copy-start | bytes 110596
  5.9 0.9 %copy-start.35 = (pred[288,128]{1,0:T(32,128)(4,1)S(1)}, pred[288,128]{1,0:T(32,128)(4,1)}, u32[]{:S(2)}) copy-start(pred[288,128]{1,0:T(32,128)(4,1)} %constant.199) | copy-start | bytes 110596
  5.9 1.0 %copy-start.36 = (pred[288,128]{1,0:T(32,128)(4,1)S(1)}, pred[288,128]{1,0:T(32,128)(4,1)}, u32[]{:S(2)}) copy-start(pred[288,128]{1,0:T(32,128)(4,1)} %constant.200) | copy-start | bytes 110596
  5.9 1.0 %copy-start.37 = (pred[288,128]{1,0:T(32,128)(4,1)S(1)}, pred[288,128]{1,0:T(32,128)(4,1)}, u32[]{:S(2)}) copy-start(pred[288,128]{1,0:T(32,128)(4,1)} %constant.201) | copy-start | bytes 110596
  6.0 1.0 %copy-start.38 = (pred[288,128]{1,0:T(32,128)(4,1)S(1)}, pred[288,128]{1,0:T(32,128)(4,1)}, u32[]{:S(2)}) copy-start(pred[288,128]{1,0:T(32,128)(4,1)} %constant.202) | copy-start | bytes 110596
  6.0 1.0 %copy-start.39 = (pred[288,128]{1,0:T(32,128)(4,1)S(1)}, pred[288,128]{1,0:T(32,128)(4,1)}, u32[]{:S(2)}) copy-start(pred[288,128]{1,0:T(32,128)(4,1)} %constant.203) | copy-start | bytes 110596
  6.0 1.0 %copy-start.40 = (pred[288,128]{1,0:T(32,128)(4,1)S(1)}, pred[288,128]{1,0:T(32,128)(4,1)}, u32[]{:S(2)}) copy-start(pred[288,128]{1,0:T(32,128)(4,1)} %constant.204) | copy-start | bytes 110596
  35.4 12.7 %copy-start.8 = (s32[16]{0:T(128)S(1)}, s32[16]{0:T(128)}, u32[]{:S(2)}) copy-start(s32[16]{0:T(128)} %param.7) | copy-start | bytes 196
  35.5 16.7 %copy-start = (bf16[6,4,4096]{2,1,0:T(4,128)(2,1)}, bf16[6,4,4096]{2,1,0:T(4,128)(2,1)S(1)}, u32[]{:S(2)}) copy-start(bf16[6,4,4096]{2,1,0:T(4,128)(2,1)S(1)} %maximum_bitcast_fusion.refs_3_.refs_4_) | copy-start | bytes 589828
  35.5 14.1 %collective-permute-start = (bf16[6,4,4096]{2,1,0:T(4,128)(2,1)S(1)}, bf16[6,4,4096]{2,1,0:T(4,128)(2,1)S(1)}, u32[]{:S(2)}, u32[]{:S(2)}) collective-permute-start(bf16[6,4,4096]{2,1,0:T(4,128)(2,1)S(1)} %maximum_bitcast_fusion.refs_3_.refs_4_), channel_id=1, source_target_pairs={{0,8},{4,12},{8,0},{12,4},{16,24},{20,28},{24,16},{28,20},{1,9},{5... | collective-permute-start | bytes 589832 | tf_op jit(solution)/shard_map/ppermute | solution.py:185
  38.5 13.7 %collective-permute-start.1 = (bf16[6,4,4096]{2,1,0:T(4,128)(2,1)S(1)}, bf16[6,4,4096]{2,1,0:T(4,128)(2,1)S(1)}, u32[]{:S(2)}, u32[]{:S(2)}) collective-permute-start(bf16[6,4,4096]{2,1,0:T(4,128)(2,1)S(1)} %maximum_bitcast_fusion.refs_3_.refs_4_), channel_id=1, source_target_pairs={{0,16},{4,20},{8,24},{12,28},{16,0},{20,4},{24,8},{28,12},{1,17},{... | collective-permute-start | bytes 589832 | tf_op jit(solution)/shard_map/ppermute | solution.py:185
  40.0 12.4 %collective-permute-start.2 = (bf16[6,4,4096]{2,1,0:T(4,128)(2,1)S(1)}, bf16[6,4,4096]{2,1,0:T(4,128)(2,1)S(1)}, u32[]{:S(2)}, u32[]{:S(2)}) collective-permute-start(bf16[6,4,4096]{2,1,0:T(4,128)(2,1)S(1)} %maximum_bitcast_fusion.refs_3_.refs_4_), channel_id=1, source_target_pairs={{0,24},{4,28},{8,16},{12,20},{16,8},{20,12},{24,0},{28,4},{1,25},{... | collective-permute-start | bytes 589832 | tf_op jit(solution)/shard_map/ppermute | solution.py:185
  40.0 16.1 %collective-permute-start.4 = (bf16[6,4,4096]{2,1,0:T(4,128)(2,1)S(1)}, bf16[6,4,4096]{2,1,0:T(4,128)(2,1)S(1)}, u32[]{:S(2)}, u32[]{:S(2)}) collective-permute-start(bf16[6,4,4096]{2,1,0:T(4,128)(2,1)S(1)} %maximum_bitcast_fusion.refs_3_.refs_4_), channel_id=1, source_target_pairs={{0,1},{1,0},{2,3},{3,2},{4,5},{5,4},{6,7},{7,6},{8,9},{9,8},{10,11... | collective-permute-start | bytes 589832 | tf_op jit(solution)/shard_map/ppermute | solution.py:173
  42.1 14.0 %collective-permute-start.5 = (bf16[6,4,4096]{2,1,0:T(4,128)(2,1)S(1)}, bf16[6,4,4096]{2,1,0:T(4,128)(2,1)S(1)}, u32[]{:S(2)}, u32[]{:S(2)}) collective-permute-start(bf16[6,4,4096]{2,1,0:T(4,128)(2,1)S(1)} %maximum_bitcast_fusion.refs_3_.refs_4_), channel_id=1, source_target_pairs={{0,4},{4,0},{8,12},{12,8},{16,20},{20,16},{24,28},{28,24},{1,5},{5... | collective-permute-start | bytes 589832 | tf_op jit(solution)/shard_map/ppermute | solution.py:187
  49.7 5.1 %copy-start.1 = (bf16[6,4,4096]{2,1,0:T(4,128)(2,1)}, bf16[6,4,4096]{2,1,0:T(4,128)(2,1)S(1)}, u32[]{:S(2)}) copy-start(bf16[6,4,4096]{2,1,0:T(4,128)(2,1)S(1)} %collective-permute-done.refs_7_) | copy-start | bytes 589828
  49.7 9.7 %collective-permute-start.6 = (bf16[6,4,4096]{2,1,0:T(4,128)(2,1)S(1)}, bf16[6,4,4096]{2,1,0:T(4,128)(2,1)S(1)}, u32[]{:S(2)}, u32[]{:S(2)}) collective-permute-start(bf16[6,4,4096]{2,1,0:T(4,128)(2,1)S(1)} %maximum_bitcast_fusion.refs_3_.refs_4_), channel_id=1, source_target_pairs={{0,3},{1,2},{2,1},{3,0},{4,7},{5,6},{6,5},{7,4},{8,11},{9,10},{10,... | collective-permute-start | bytes 589832 | tf_op jit(solution)/shard_map/ppermute | solution.py:173
  52.2 2.6 %copy-start.2 = (bf16[6,4,4096]{2,1,0:T(4,128)(2,1)}, bf16[6,4,4096]{2,1,0:T(4,128)(2,1)S(1)}, u32[]{:S(2)}) copy-start(bf16[6,4,4096]{2,1,0:T(4,128)(2,1)S(1)} %collective-permute-done.1.refs_8_) | copy-start | bytes 589828
  52.2 18.3 %collective-permute-start.7 = (bf16[6,4,4096]{2,1,0:T(4,128)(2,1)S(1)}, bf16[6,4,4096]{2,1,0:T(4,128)(2,1)S(1)}, u32[]{:S(2)}, u32[]{:S(2)}) collective-permute-start(bf16[6,4,4096]{2,1,0:T(4,128)(2,1)S(1)} %maximum_bitcast_fusion.refs_3_.refs_4_), channel_id=1, source_target_pairs={{0,2},{1,3},{2,0},{3,1},{4,6},{5,7},{6,4},{7,5},{8,10},{9,11},{10,... | collective-permute-start | bytes 589832 | tf_op jit(solution)/shard_map/ppermute | solution.py:173
  52.4 2.4 %copy-start.3 = (bf16[6,4,4096]{2,1,0:T(4,128)(2,1)}, bf16[6,4,4096]{2,1,0:T(4,128)(2,1)S(1)}, u32[]{:S(2)}) copy-start(bf16[6,4,4096]{2,1,0:T(4,128)(2,1)S(1)} %collective-permute-done.2.refs_9_) | copy-start | bytes 589828
  52.8 2.4 %collective-permute-start.3 = (bf16[6,12,4096]{2,1,0:T(8,128)(2,1)S(1)}, bf16[6,12,4096]{2,1,0:T(8,128)(2,1)S(1)}, u32[]{:S(2)}, u32[]{:S(2)}) collective-permute-start(bf16[6,12,4096]{2,1,0:T(8,128)(2,1)S(1)} %pad_maximum_fusion.1), channel_id=1, source_target_pairs={{0,4},{4,0},{8,12},{12,8},{16,20},{20,16},{24,28},{28,24},{1,5},{5... | collective-permute-start | bytes 1769480 | tf_op jit(solution)/shard_map/ppermute | solution.py:189
  56.1 14.4 %copy-start.4 = (bf16[6,4,4096]{2,1,0:T(4,128)(2,1)}, bf16[6,4,4096]{2,1,0:T(4,128)(2,1)S(1)}, u32[]{:S(2)}) copy-start(bf16[6,4,4096]{2,1,0:T(4,128)(2,1)S(1)} %collective-permute-done.4.refs_5_) | copy-start | bytes 589828
  56.1 14.4 %copy-start.5 = (bf16[6,4,4096]{2,1,0:T(4,128)(2,1)}, bf16[6,4,4096]{2,1,0:T(4,128)(2,1)S(1)}, u32[]{:S(2)}) copy-start(bf16[6,4,4096]{2,1,0:T(4,128)(2,1)S(1)} %collective-permute-done.5.refs_6_) | copy-start | bytes 589828
  59.3 11.2 %copy-start.6 = (bf16[6,4,4096]{2,1,0:T(4,128)(2,1)}, bf16[6,4,4096]{2,1,0:T(4,128)(2,1)S(1)}, u32[]{:S(2)}) copy-start(bf16[6,4,4096]{2,1,0:T(4,128)(2,1)S(1)} %collective-permute-done.6.refs_10_) | copy-start | bytes 589828
  (25 other events, 21.2 us)

commit v15 on v14

--- a/solution.py
+++ b/solution.py
@@ -2,7 +2,6 @@
 import math
 
 import jax
-import numpy as np
 import jax.numpy as jnp
 from jax import lax
 from jax.experimental import pallas as pl
@@ -33,12 +32,11 @@
     tails = blocks[:, :, :-1, in_block - tap_count :]
     tails = jnp.concatenate([jnp.zeros(lead_dims + (1, tap_count), records.dtype), tails], axis=2)
     windows = jnp.concatenate([tails, blocks], axis=3)
-    in_ids = np.arange(in_block + tap_count)[:, None]
-    out_ids = np.arange(out_block)[None, :]
-    tap_index = DECIM * out_ids + tap_count - in_ids
-    inside = (tap_index >= 0) & (tap_index < tap_count)
-    padded_taps = jnp.concatenate([fir_taps, jnp.zeros((1,), fir_taps.dtype)])
-    band_matrix = padded_taps[np.where(inside, tap_index, tap_count).astype(np.int32)]
+    tap_ids = jnp.arange(tap_count, dtype=jnp.int32)[:, None, None]
+    in_ids = jnp.arange(in_block + tap_count, dtype=jnp.int32)[None, :, None]
+    out_ids = jnp.arange(out_block, dtype=jnp.int32)[None, None, :]
+    onehot = (in_ids == DECIM * out_ids + tap_count - tap_ids).astype(jnp.float32)
+    band_matrix = jnp.einsum("k,kij->ij", fir_taps, onehot, precision=lax.Precision.HIGH)
     summed = jnp.einsum("swbi,ij->swbj", windows, band_matrix, precision=lax.Precision.HIGH)
     return summed.reshape(lead_dims + (block_count * out_block,))
 

time: 87.5 us -> 63.4 us (0.72)
  matrix products: 27.3 us -> 7.97 us
  local copies, waits for them, and re-layouts: 13 us -> 8.3 us
    dot_general x1, matrix products: 21.2 us -> 0.71 us  [decimate(): jnp.einsum('swbi,ij->swbj', windows, band_matrix, precision=lax.Precision...]
    gather x2 -> x0, local copies, waits for them, and re-layouts: 3.9 us -> none  [decimate(): padded_taps[np.where(inside, tap_index, tap_count).astype(np.int32)]]
    dot_general x0 -> x1, matrix products: none -> 1.06 us  [decimate(): jnp.einsum('k,kij->ij', fir_taps, onehot, precision=lax.Precision.HIGH)]
  transfers between devices with their start and end apart: 8 -> 8, of which waited for: 3 -> 3; matrix products, arithmetic and copies ran while one was open for 12% -> 17% of each run, Pallas kernels for 0% -> 0%
where the time goes in v15:
time: 63.4 us; the launch traced here: 63.2 us
  waiting for transfers between devices  14.7 us (23%)
  Pallas kernels  14 us (22%)
  starting transfers between devices  9.63 us (15%)
  other arithmetic  8.43 us (13%)
  local copies, waits for them, and re-layouts  8.3 us (13%)
  matrix products  7.97 us (13%)
    ppermute x3, waiting for transfers between devices, xor_gather(): pieces.append(lax.ppermute(block, axis_name, pairs))  14.3 us
    pallas_call x1, Pallas kernels, pair_block(): pl.pallas_call(functools.partial(cross_kernel, tuple(issue_order)), out_s...  14 us
    ppermute x3, starting transfers between devices, xor_gather(): pieces.append(lax.ppermute(block, axis_name, pairs))  4.79 us
    another operation x2, other arithmetic  4.73 us
    ppermute x3, starting transfers between devices, chip_gather(): fetched.append(lax.ppermute(block, axis_name, pairs))  4.54 us
    reshape x1, local copies, waits for them, and re-layouts, on_device(): pair = jnp.swapaxes(pair.reshape(visit_count, group_rows, LAGS), 0, 1)  1.74 us
    reshape x1, local copies, waits for them, and re-layouts, decimate(): blocks = records.reshape(lead_dims + (block_count, in_block))  1.68 us
    dot_general x1, matrix products, spectrum(): jnp.einsum('bwfq,gq->bwgf', real_t, sin_three, precision=lax.Precision.HIGH)  1.31 us
  transfers between devices with their start and end apart: 8, of which 3 were waited for; matrix products, arithmetic and copies ran while one was open for 17% of the time, Pallas kernels for 0%

profile of v15, /device:TPU:0, one launch (start us, length us, event | category | flops | bytes accessed | tf_op | source)
XLA Modules:
  0.0 63.2 jit_solution(162881830924851114)
XLA Ops:
  0.0 1.7 %reshape.209 = f32[4,6,32,256]{3,2,0,1:T(8,128)S(1)} reshape(f32[4,6,8192]{2,0,1:T(4,128)} %param.3) | data formatting | bytes 1572864 | tf_op jit(solution)/shard_map/reshape | solution.py:31
  1.9 0.7 %iota_compare_fusion = pred[32,288,128]{2,1,0:T(32,128)(4,1)S(1)} fusion(s32[32,128]{1,0:T(8,128)S(1)} %iota_subtract_fusion), kind=kLoop, calls=%fused_computation.2 | loop fusion | flops 1179648 | bytes 1196032 | tf_op jit(solution)/shard_map/eq | solution.py:38
  2.6 1.1 %fusion = f32[1,288,128]{2,0,1:T(1,128)S(1)} fusion(pred[32,288,128]{2,1,0:T(32,128)(4,1)S(1)} %iota_compare_fusion, f32[32]{0:T(128)S(1)} %copy-done), kind=kOutput, calls=%fused_computation.3 | convolution fusion | flops 7077888 | bytes 1327232 | tf_op jit(solution)/shard_map/k,kij->ij/dot_general | solution.py:39
  3.6 0.7 %fusion.4 = f32[4,6,32,128]{3,2,1,0:T(8,128)S(1)} fusion(f32[288,128,1,1]{1,0,3,2:T(8,128)S(1)} %bitcast.75, f32[4,6,31,32]{3,2,1,0:T(8,128)S(1)} %copy.30, f32[4,6,32,256]{3,2,0,1:T(8,128)S(1)} %reshape.209), kind=kOutput, calls=%fused_computation.14 | convolution fusion | flops 170532864 | bytes 1422336 | tf_op jit(solution)/shard_map/swbi,ij->swbj/dot_general | solution.py:40
  6.0 1.2 %fusion.17 = f32[32,4,6,64]{3,0,2,1:T(8,128)S(1)} fusion(f32[64,4,6,64]{3,0,2,1:T(8,128)S(1)} %convolution_negate_fusion, f32[64,4,6,64]{3,0,2,1:T(8,128)S(1)} %fusion.26, f32[64,64]{1,0:T(8,128)S(1)} %get-tuple-element.14, f32[64,64]{1,0:T(8,128)S(1)} %get-tuple-element.15), kind=kOutput, calls=%fused_computation.32 | convolution fusion | flops 19197952 | bytes 1015808 | tf_op jit(solution)/shard_map/bwfq,gq->bwgf/dot_general | solution.py:57
  7.2 1.2 %fusion.13 = f32[32,4,6,64]{3,0,2,1:T(8,128)S(1)} fusion(f32[64,4,6,64]{3,0,2,1:T(8,128)S(1)} %fusion.26, f32[64,4,6,64]{3,0,2,1:T(8,128)S(1)} %convolution_negate_fusion, f32[64,64]{1,0:T(8,128)S(1)} %get-tuple-element.14, f32[64,64]{1,0:T(8,128)S(1)} %get-tuple-element.15), kind=kOutput, calls=%fused_computation.28 | convolution fusion | flops 19197952 | bytes 1015808 | tf_op jit(solution)/shard_map/bwfq,gq->bwgf/dot_general | solution.py:60
  8.4 1.2 %fusion.3 = f32[4,6,32,64]{3,2,1,0:T(8,128)S(1)} fusion(f32[32,4,6,64]{3,0,2,1:T(8,128)S(1)} %fusion.17, f32[64,4,6,64]{3,0,2,1:T(8,128)S(1)} %fusion.26, f32[64,4,6,64]{3,0,2,1:T(8,128)S(1)} %convolution_negate_fusion, f32[64,64]{1,0:T(8,128)S(1)} %get-tuple-element.14, f32[64,64]{1,0:T(8,128)S(1)} %get-tuple-element.15), kind=kOutput, calls=%fused_computation.12 | convolution fusion | flops 19247104 | bytes 1212416 | tf_op jit(solution)/shard_map/bwfq,gq->bwgf/dot_general | solution.py:59
  9.6 1.3 %add_reduce_fusion = (f32[4,6,32]{2,1,0:T(8,128)S(1)}, f32[4,6,32,64]{3,2,1,0:T(8,128)S(1)}) fusion(f32[4,6,32,64]{3,2,1,0:T(8,128)S(1)} %fusion.3, f32[32,4,6,64]{3,0,2,1:T(8,128)S(1)} %fusion.13, f32[64,4,6,64]{3,0,2,1:T(8,128)S(1)} %convolution_negate_fusion, f32[64,64]{1,0:T(8,128)S(1)} %get-tuple-element.14, f32[64,4,6,64]{3,0,2,1:T(8,128)S(1)} %fusion.26, ...), kind=kOutput, calls=%fused_computation.40 | convolution fusion | flops 19442944 | bytes 1412096 | tf_op jit(solution)/shard_map/bwfq,gq->bwgf/dot_general | solution.py:62
  11.8 3.0 %collective-permute-start = (bf16[6,4,4096]{2,1,0:T(4,128)(2,1)S(1)}, bf16[6,4,4096]{2,1,0:T(4,128)(2,1)S(1)}, u32[]{:S(2)}, u32[]{:S(2)}) collective-permute-start(bf16[6,4,4096]{2,1,0:T(4,128)(2,1)S(1)} %maximum_bitcast_fusion.refs_3_.refs_4_), channel_id=1, source_target_pairs={{0,8},{4,12},{8,0},{12,4},{16,24},{20,28},{24,16},{28,20},{1,9},{5... | collective-permute-start | bytes 589832 | tf_op jit(solution)/shard_map/ppermute | solution.py:183
  14.8 1.5 %collective-permute-start.1 = (bf16[6,4,4096]{2,1,0:T(4,128)(2,1)S(1)}, bf16[6,4,4096]{2,1,0:T(4,128)(2,1)S(1)}, u32[]{:S(2)}, u32[]{:S(2)}) collective-permute-start(bf16[6,4,4096]{2,1,0:T(4,128)(2,1)S(1)} %maximum_bitcast_fusion.refs_3_.refs_4_), channel_id=1, source_target_pairs={{0,16},{4,20},{8,24},{12,28},{16,0},{20,4},{24,8},{28,12},{1,17},{... | collective-permute-start | bytes 589832 | tf_op jit(solution)/shard_map/ppermute | solution.py:183
  16.4 2.0 %collective-permute-start.4 = (bf16[6,4,4096]{2,1,0:T(4,128)(2,1)S(1)}, bf16[6,4,4096]{2,1,0:T(4,128)(2,1)S(1)}, u32[]{:S(2)}, u32[]{:S(2)}) collective-permute-start(bf16[6,4,4096]{2,1,0:T(4,128)(2,1)S(1)} %maximum_bitcast_fusion.refs_3_.refs_4_), channel_id=1, source_target_pairs={{0,1},{1,0},{2,3},{3,2},{4,5},{5,4},{6,7},{7,6},{8,9},{9,8},{10,11... | collective-permute-start | bytes 589832 | tf_op jit(solution)/shard_map/ppermute | solution.py:171
  18.4 4.6 %cosine_convert_fusion = (bf16[2048,128]{1,0:T(8,128)(2,1)S(1)}, bf16[2048,128]{1,0:T(8,128)(2,1)S(1)}) fusion(s32[128]{0:T(128)S(1)} %iota_add_fusion), kind=kLoop, calls=%fused_computation.23 | loop fusion | flops 4194304 | bytes 1049088 | tf_op jit(solution)/shard_map/convert
  23.0 0.7 %gather_fusion.1 = s32[32]{0:T(128)S(1)} fusion(s32[8]{0:T(128)S(1)} %iota_xor_fusion, s32[1024]{0:T(1024)S(1)} %pad_clamp_fusion), kind=kCustom, calls=%fused_computation.1 | custom fusion | bytes 384 | tf_op jit(solution)/shard_map/gather | solution.py:224
  23.7 0.7 %fusion.51.refs_13_ = bf16[32,32]{1,0:T(8,128)(2,1)} fusion(s32[32]{0:T(128)S(1)} %fusion.60), kind=kLoop, calls=%fused_computation.83 | loop fusion | flops 2048 | bytes 2176 | tf_op jit(solution)/shard_map/convert_element_type | solution.py:226
  24.4 0.9 %broadcast_in_dim_tile.4.refs_14_ = s32[512,1]{1,0:T(8,128)} reshape(s32[32,16]{1,0:T(8,128)S(1)} %tile.2) | data formatting | bytes 4096 | tf_op jit(solution)/shard_map/broadcast_in_dim;tile | solution.py:227
  26.0 2.5 %collective-permute-start.6 = (bf16[6,4,4096]{2,1,0:T(4,128)(2,1)S(1)}, bf16[6,4,4096]{2,1,0:T(4,128)(2,1)S(1)}, u32[]{:S(2)}, u32[]{:S(2)}) collective-permute-start(bf16[6,4,4096]{2,1,0:T(4,128)(2,1)S(1)} %maximum_bitcast_fusion.refs_3_.refs_4_), channel_id=1, source_target_pairs={{0,3},{1,2},{2,1},{3,0},{4,7},{5,6},{6,5},{7,4},{8,11},{9,10},{10,... | collective-permute-start | bytes 589832 | tf_op jit(solution)/shard_map/ppermute | solution.py:171
  29.4 0.7 %fusion.58.refs_12_ = bf16[16,16]{1,0:T(8,128)(2,1)} fusion(s32[16]{0:T(128)S(1)} %fusion.59), kind=kLoop, calls=%fused_computation.87 | loop fusion | flops 512 | bytes 576 | tf_op jit(solution)/shard_map/convert_element_type | solution.py:225
  30.1 1.1 %pad_maximum_fusion.refs_15_ = bf16[4096,128]{1,0:T(8,128)(2,1)} fusion(bf16[2048,128]{1,0:T(8,128)(2,1)S(1)} %get-tuple-element.11, bf16[2048,128]{1,0:T(8,128)(2,1)S(1)} %get-tuple-element.10), kind=kLoop, calls=%fused_computation.21 | loop fusion | flops 2097152 | bytes 2097152 | tf_op jit(solution)/shard_map/concatenate | solution.py:207
  31.4 1.0 %fusion.91 = (bf16[6,4,4096]{2,1,0:T(4,128)(2,1)}, bf16[6,4,4096]{2,1,0:T(4,128)(2,1)}, bf16[6,4,4096]{2,1,0:T(4,128)(2,1)}) fusion(bf16[6,12,4096]{2,1,0:T(8,128)(2,1)S(1)} %collective-permute-done.3), kind=kLoop, calls=%fused_computation.138 | loop fusion | bytes 1179648 | tf_op jit(solution)/shard_map/slice | solution.py:190
  32.5 3.1 %collective-permute-done.6.refs_10_ = bf16[6,4,4096]{2,1,0:T(4,128)(2,1)S(1)} collective-permute-done((bf16[6,4,4096]{2,1,0:T(4,128)(2,1)S(1)}, bf16[6,4,4096]{2,1,0:T(4,128)(2,1)S(1)}, u32[]{:S(2)}, u32[]{:S(2)}) %collective-permute-start.6) | collective-permute-done | bytes 196640 | tf_op jit(solution)/shard_map/ppermute | solution.py:171
  35.7 11.2 %collective-permute-done.7.refs_11_ = bf16[6,4,4096]{2,1,0:T(4,128)(2,1)S(1)} collective-permute-done((bf16[6,4,4096]{2,1,0:T(4,128)(2,1)S(1)}, bf16[6,4,4096]{2,1,0:T(4,128)(2,1)S(1)}, u32[]{:S(2)}, u32[]{:S(2)}) %collective-permute-start.7) | collective-permute-done | bytes 196640 | tf_op jit(solution)/shard_map/ppermute | solution.py:171
  46.9 0.7 %copy-done.8 = bf16[6,4,4096]{2,1,0:T(4,128)(2,1)} copy-done((bf16[6,4,4096]{2,1,0:T(4,128)(2,1)}, bf16[6,4,4096]{2,1,0:T(4,128)(2,1)S(1)}, u32[]{:S(2)}) %copy-start.8) | copy-done | bytes 196632
  47.5 14.0 %shard_map.37 = f32[512,128]{1,0:T(8,128)} custom-call(bf16[6,4,4096]{2,1,0:T(4,128)(2,1)} %get-tuple-element.7.refs_0_, bf16[6,4,4096]{2,1,0:T(4,128)(2,1)} %get-tuple-element.6.refs_1_, bf16[6,4,4096]{2,1,0:T(4,128)(2,1)} %get-tuple-element.5.refs_2_, bf16[6,4,4096]{2,1,0:T(4,128)(2,1)} %copy-done.1, bf16[6,4,4096]{2,1,0:T(4,128)(2,1)} %copy-done.1, ...), custom_call_target="tpu_custom_call" | custom-call | flops 587202560 | bytes 3670016 | tf_op jit(solution)/shard_map/pallas_call | solution.py:145
  61.5 1.7 %copy.29 = f32[32,16,128]{2,0,1:T(8,128)} copy(f32[32,16,128]{2,1,0:T(8,128)} %bitcast.74) | data formatting | bytes 524288 | tf_op jit(solution)/shard_map/reshape | solution.py:229
  (56 shorter events, 4.5 us)
Async XLA Ops:
  0.0 2.6 %copy-start = (f32[32]{0:T(128)S(1)}, f32[32]{0:T(128)}, u32[]{:S(2)}) copy-start(f32[32]{0:T(128)} %param.4) | copy-start | bytes 388
  11.6 12.8 %copy-start.9 = (s32[16]{0:T(128)S(1)}, s32[16]{0:T(128)}, u32[]{:S(2)}) copy-start(s32[16]{0:T(128)} %param.5) | copy-start | bytes 196
  11.8 16.7 %copy-start.1 = (bf16[6,4,4096]{2,1,0:T(4,128)(2,1)}, bf16[6,4,4096]{2,1,0:T(4,128)(2,1)S(1)}, u32[]{:S(2)}) copy-start(bf16[6,4,4096]{2,1,0:T(4,128)(2,1)S(1)} %maximum_bitcast_fusion.refs_3_.refs_4_) | copy-start | bytes 589828
  11.8 14.1 %collective-permute-start = (bf16[6,4,4096]{2,1,0:T(4,128)(2,1)S(1)}, bf16[6,4,4096]{2,1,0:T(4,128)(2,1)S(1)}, u32[]{:S(2)}, u32[]{:S(2)}) collective-permute-start(bf16[6,4,4096]{2,1,0:T(4,128)(2,1)S(1)} %maximum_bitcast_fusion.refs_3_.refs_4_), channel_id=1, source_target_pairs={{0,8},{4,12},{8,0},{12,4},{16,24},{20,28},{24,16},{28,20},{1,9},{5... | collective-permute-start | bytes 589832 | tf_op jit(solution)/shard_map/ppermute | solution.py:183
  14.8 13.7 %collective-permute-start.1 = (bf16[6,4,4096]{2,1,0:T(4,128)(2,1)S(1)}, bf16[6,4,4096]{2,1,0:T(4,128)(2,1)S(1)}, u32[]{:S(2)}, u32[]{:S(2)}) collective-permute-start(bf16[6,4,4096]{2,1,0:T(4,128)(2,1)S(1)} %maximum_bitcast_fusion.refs_3_.refs_4_), channel_id=1, source_target_pairs={{0,16},{4,20},{8,24},{12,28},{16,0},{20,4},{24,8},{28,12},{1,17},{... | collective-permute-start | bytes 589832 | tf_op jit(solution)/shard_map/ppermute | solution.py:183
  16.3 12.4 %collective-permute-start.2 = (bf16[6,4,4096]{2,1,0:T(4,128)(2,1)S(1)}, bf16[6,4,4096]{2,1,0:T(4,128)(2,1)S(1)}, u32[]{:S(2)}, u32[]{:S(2)}) collective-permute-start(bf16[6,4,4096]{2,1,0:T(4,128)(2,1)S(1)} %maximum_bitcast_fusion.refs_3_.refs_4_), channel_id=1, source_target_pairs={{0,24},{4,28},{8,16},{12,20},{16,8},{20,12},{24,0},{28,4},{1,25},{... | collective-permute-start | bytes 589832 | tf_op jit(solution)/shard_map/ppermute | solution.py:183
  16.4 16.1 %collective-permute-start.4 = (bf16[6,4,4096]{2,1,0:T(4,128)(2,1)S(1)}, bf16[6,4,4096]{2,1,0:T(4,128)(2,1)S(1)}, u32[]{:S(2)}, u32[]{:S(2)}) collective-permute-start(bf16[6,4,4096]{2,1,0:T(4,128)(2,1)S(1)} %maximum_bitcast_fusion.refs_3_.refs_4_), channel_id=1, source_target_pairs={{0,1},{1,0},{2,3},{3,2},{4,5},{5,4},{6,7},{7,6},{8,9},{9,8},{10,11... | collective-permute-start | bytes 589832 | tf_op jit(solution)/shard_map/ppermute | solution.py:171
  18.4 14.1 %collective-permute-start.5 = (bf16[6,4,4096]{2,1,0:T(4,128)(2,1)S(1)}, bf16[6,4,4096]{2,1,0:T(4,128)(2,1)S(1)}, u32[]{:S(2)}, u32[]{:S(2)}) collective-permute-start(bf16[6,4,4096]{2,1,0:T(4,128)(2,1)S(1)} %maximum_bitcast_fusion.refs_3_.refs_4_), channel_id=1, source_target_pairs={{0,4},{4,0},{8,12},{12,8},{16,20},{20,16},{24,28},{28,24},{1,5},{5... | collective-permute-start | bytes 589832 | tf_op jit(solution)/shard_map/ppermute | solution.py:185
  26.0 5.1 %copy-start.2 = (bf16[6,4,4096]{2,1,0:T(4,128)(2,1)}, bf16[6,4,4096]{2,1,0:T(4,128)(2,1)S(1)}, u32[]{:S(2)}) copy-start(bf16[6,4,4096]{2,1,0:T(4,128)(2,1)S(1)} %collective-permute-done.refs_7_) | copy-start | bytes 589828
  26.0 9.7 %collective-permute-start.6 = (bf16[6,4,4096]{2,1,0:T(4,128)(2,1)S(1)}, bf16[6,4,4096]{2,1,0:T(4,128)(2,1)S(1)}, u32[]{:S(2)}, u32[]{:S(2)}) collective-permute-start(bf16[6,4,4096]{2,1,0:T(4,128)(2,1)S(1)} %maximum_bitcast_fusion.refs_3_.refs_4_), channel_id=1, source_target_pairs={{0,3},{1,2},{2,1},{3,0},{4,7},{5,6},{6,5},{7,4},{8,11},{9,10},{10,... | collective-permute-start | bytes 589832 | tf_op jit(solution)/shard_map/ppermute | solution.py:171
  28.5 2.6 %copy-start.3 = (bf16[6,4,4096]{2,1,0:T(4,128)(2,1)}, bf16[6,4,4096]{2,1,0:T(4,128)(2,1)S(1)}, u32[]{:S(2)}) copy-start(bf16[6,4,4096]{2,1,0:T(4,128)(2,1)S(1)} %collective-permute-done.1.refs_8_) | copy-start | bytes 589828
  28.5 18.3 %collective-permute-start.7 = (bf16[6,4,4096]{2,1,0:T(4,128)(2,1)S(1)}, bf16[6,4,4096]{2,1,0:T(4,128)(2,1)S(1)}, u32[]{:S(2)}, u32[]{:S(2)}) collective-permute-start(bf16[6,4,4096]{2,1,0:T(4,128)(2,1)S(1)} %maximum_bitcast_fusion.refs_3_.refs_4_), channel_id=1, source_target_pairs={{0,2},{1,3},{2,0},{3,1},{4,6},{5,7},{6,4},{7,5},{8,10},{9,11},{10,... | collective-permute-start | bytes 589832 | tf_op jit(solution)/shard_map/ppermute | solution.py:171
  28.8 2.4 %copy-start.4 = (bf16[6,4,4096]{2,1,0:T(4,128)(2,1)}, bf16[6,4,4096]{2,1,0:T(4,128)(2,1)S(1)}, u32[]{:S(2)}) copy-start(bf16[6,4,4096]{2,1,0:T(4,128)(2,1)S(1)} %collective-permute-done.2.refs_9_) | copy-start | bytes 589828
  29.1 2.4 %collective-permute-start.3 = (bf16[6,12,4096]{2,1,0:T(8,128)(2,1)S(1)}, bf16[6,12,4096]{2,1,0:T(8,128)(2,1)S(1)}, u32[]{:S(2)}, u32[]{:S(2)}) collective-permute-start(bf16[6,12,4096]{2,1,0:T(8,128)(2,1)S(1)} %pad_maximum_fusion.1), channel_id=1, source_target_pairs={{0,4},{4,0},{8,12},{12,8},{16,20},{20,16},{24,28},{28,24},{1,5},{5... | collective-permute-start | bytes 1769480 | tf_op jit(solution)/shard_map/ppermute | solution.py:187
  32.5 14.4 %copy-start.5 = (bf16[6,4,4096]{2,1,0:T(4,128)(2,1)}, bf16[6,4,4096]{2,1,0:T(4,128)(2,1)S(1)}, u32[]{:S(2)}) copy-start(bf16[6,4,4096]{2,1,0:T(4,128)(2,1)S(1)} %collective-permute-done.4.refs_5_) | copy-start | bytes 589828
  32.5 14.4 %copy-start.6 = (bf16[6,4,4096]{2,1,0:T(4,128)(2,1)}, bf16[6,4,4096]{2,1,0:T(4,128)(2,1)S(1)}, u32[]{:S(2)}) copy-start(bf16[6,4,4096]{2,1,0:T(4,128)(2,1)S(1)} %collective-permute-done.5.refs_6_) | copy-start | bytes 589828
  35.7 11.2 %copy-start.7 = (bf16[6,4,4096]{2,1,0:T(4,128)(2,1)}, bf16[6,4,4096]{2,1,0:T(4,128)(2,1)S(1)}, u32[]{:S(2)}) copy-start(bf16[6,4,4096]{2,1,0:T(4,128)(2,1)S(1)} %collective-permute-done.6.refs_10_) | copy-start | bytes 589828
  46.9 0.7 %copy-start.8 = (bf16[6,4,4096]{2,1,0:T(4,128)(2,1)}, bf16[6,4,4096]{2,1,0:T(4,128)(2,1)S(1)}, u32[]{:S(2)}) copy-start(bf16[6,4,4096]{2,1,0:T(4,128)(2,1)S(1)} %collective-permute-done.7.refs_11_) | copy-start | bytes 589828

commit v16 on v13

--- a/solution.py
+++ b/solution.py
@@ -209,7 +209,7 @@
     near = [(0, 0), (1, 0), (0, 1), (1, 1)][:2 + min(1, len(left_by_window) - 1) + min(1, len(piece_rows) - 1)]
     fetches = [(1, index) for index in range(len(piece_rows)) if index > 1 and index % 2 == 0]
     far = [(0, index) for index in range(2, len(left_by_window))]
-    issue_order = [slot for slot in late_first + near + fetches + far[::-1]]
+    issue_order = [slot for slot in late_first + near[:2] + near[3:] + fetches[:1] + near[2:3] + fetches[1:] + far[::-1]]
     issue_order = sorted(set(issue_order), key=issue_order.index)
     assert len(issue_order) == len(left_by_window) + len(piece_rows)
     piece = block_size

time: 51.8 us -> 50.3 us (0.971)
  waiting for transfers between devices: 4.21 us -> 2.59 us
    ppermute x3, waiting for transfers between devices: 2.53 us -> 1.39 us  [xor_gather(): pieces.append(lax.ppermute(block, axis_name, pairs))]
  transfers between devices with their start and end apart: 8 -> 8, of which waited for: 3 -> 4; matrix products, arithmetic and copies ran while one was open for 19% -> 19% of each run, Pallas kernels for 0% -> 0%
where the time goes in v16:
time: 50.3 us; the launch traced here: 50.1 us
  Pallas kernels  13.9 us (28%)
  other arithmetic  10.1 us (20%)
  starting transfers between devices  9.66 us (19%)
  matrix products  7.97 us (16%)
  local copies, waits for them, and re-layouts  5.71 us (11%)
  waiting for transfers between devices  2.59 us (5%)
    pallas_call x1, Pallas kernels, pair_block(): pl.pallas_call(functools.partial(cross_kernel, tuple(issue_order)), out_s...  13.9 us
    ppermute x3, starting transfers between devices, xor_gather(): pieces.append(lax.ppermute(block, axis_name, pairs))  5.69 us
    another operation x2, other arithmetic  4.53 us
    ppermute x3, starting transfers between devices, chip_gather(): fetched.append(lax.ppermute(block, axis_name, pairs))  3.49 us
    reshape x1, local copies, waits for them, and re-layouts, decimate(): blocks = records.reshape(lead_dims + (block_count, in_block))  1.68 us
    ppermute x3, waiting for transfers between devices, xor_gather(): pieces.append(lax.ppermute(block, axis_name, pairs))  1.39 us
    dot_general x1, matrix products, spectrum(): jnp.einsum('bwfq,gq->bwgf', real_t, sin_three, precision=lax.Precision.HIGH)  1.31 us
    dot_general x1, matrix products, spectrum(): jnp.einsum('bwfq,gq->bwgf', imag_t, sin_three, precision=lax.Precision.HIGH)  1.24 us
  transfers between devices with their start and end apart: 8, of which 4 were waited for; matrix products, arithmetic and copies ran while one was open for 19% of the time, Pallas kernels for 0%

profile of v16, /device:TPU:0, one launch (start us, length us, event | category | flops | bytes accessed | tf_op | source)
XLA Modules:
  0.0 50.1 jit_solution(16632707292127914787)
XLA Ops:
  0.2 1.7 %reshape.236 = f32[4,6,32,256]{3,2,0,1:T(8,128)S(1)} reshape(f32[4,6,8192]{2,0,1:T(4,128)} %param.3) | data formatting | bytes 1572864 | tf_op jit(solution)/shard_map/reshape | solution.py:31
  2.1 0.7 %iota_compare_fusion = pred[32,288,128]{2,1,0:T(32,128)(4,1)S(1)} fusion(s32[32,128]{1,0:T(8,128)S(1)} %iota_subtract_fusion), kind=kLoop, calls=%fused_computation.2 | loop fusion | flops 1179648 | bytes 1196032 | tf_op jit(solution)/shard_map/eq | solution.py:38
  2.7 1.1 %fusion = f32[1,288,128]{2,0,1:T(1,128)S(1)} fusion(pred[32,288,128]{2,1,0:T(32,128)(4,1)S(1)} %iota_compare_fusion, f32[32]{0:T(128)S(1)} %copy-done), kind=kOutput, calls=%fused_computation.3 | convolution fusion | flops 7077888 | bytes 1327232 | tf_op jit(solution)/shard_map/k,kij->ij/dot_general | solution.py:39
  3.8 0.7 %fusion.4 = f32[4,6,32,128]{3,2,1,0:T(8,128)S(1)} fusion(f32[288,128,1,1]{1,0,3,2:T(8,128)S(1)} %bitcast.74, f32[4,6,31,32]{3,2,1,0:T(8,128)S(1)} %copy.30, f32[4,6,32,256]{3,2,0,1:T(8,128)S(1)} %reshape.236), kind=kOutput, calls=%fused_computation.14 | convolution fusion | flops 170532864 | bytes 1422336 | tf_op jit(solution)/shard_map/swbi,ij->swbj/dot_general | solution.py:40
  5.9 1.2 %fusion.13 = f32[32,4,6,64]{3,0,2,1:T(8,128)S(1)} fusion(f32[64,4,6,64]{3,0,2,1:T(8,128)S(1)} %fusion.27, f32[64,4,6,64]{3,0,2,1:T(8,128)S(1)} %convolution_negate_fusion, f32[64,64]{1,0:T(8,128)S(1)} %get-tuple-element.14, f32[64,64]{1,0:T(8,128)S(1)} %get-tuple-element.15), kind=kOutput, calls=%fused_computation.28 | convolution fusion | flops 19197952 | bytes 1015808 | tf_op jit(solution)/shard_map/bwfq,gq->bwgf/dot_general | solution.py:60
  7.2 1.2 %fusion.17 = f32[32,4,6,64]{3,0,2,1:T(8,128)S(1)} fusion(f32[64,4,6,64]{3,0,2,1:T(8,128)S(1)} %convolution_negate_fusion, f32[64,4,6,64]{3,0,2,1:T(8,128)S(1)} %fusion.27, f32[64,64]{1,0:T(8,128)S(1)} %get-tuple-element.14, f32[64,64]{1,0:T(8,128)S(1)} %get-tuple-element.15), kind=kOutput, calls=%fused_computation.32 | convolution fusion | flops 19197952 | bytes 1015808 | tf_op jit(solution)/shard_map/bwfq,gq->bwgf/dot_general | solution.py:57
  8.4 1.2 %fusion.3 = f32[4,6,32,64]{3,2,1,0:T(8,128)S(1)} fusion(f32[32,4,6,64]{3,0,2,1:T(8,128)S(1)} %fusion.17, f32[64,4,6,64]{3,0,2,1:T(8,128)S(1)} %fusion.27, f32[64,4,6,64]{3,0,2,1:T(8,128)S(1)} %convolution_negate_fusion, f32[64,64]{1,0:T(8,128)S(1)} %get-tuple-element.14, f32[64,64]{1,0:T(8,128)S(1)} %get-tuple-element.15), kind=kOutput, calls=%fused_computation.12 | convolution fusion | flops 19247104 | bytes 1212416 | tf_op jit(solution)/shard_map/bwfq,gq->bwgf/dot_general | solution.py:59
  9.6 1.3 %add_reduce_fusion = (f32[4,6,32]{2,1,0:T(8,128)S(1)}, f32[4,6,32,64]{3,2,1,0:T(8,128)S(1)}) fusion(f32[4,6,32,64]{3,2,1,0:T(8,128)S(1)} %fusion.3, f32[32,4,6,64]{3,0,2,1:T(8,128)S(1)} %fusion.13, f32[64,4,6,64]{3,0,2,1:T(8,128)S(1)} %convolution_negate_fusion, f32[64,64]{1,0:T(8,128)S(1)} %get-tuple-element.14, f32[64,4,6,64]{3,0,2,1:T(8,128)S(1)} %fusion.27, ...), kind=kOutput, calls=%fused_computation.40 | convolution fusion | flops 19442944 | bytes 1412096 | tf_op jit(solution)/shard_map/bwfq,gq->bwgf/dot_general | solution.py:62
  11.8 4.1 %collective-permute-start.7 = (bf16[6,4,4096]{2,1,0:T(4,128)(2,1)S(1)}, bf16[6,4,4096]{2,1,0:T(4,128)(2,1)S(1)}, u32[]{:S(2)}, u32[]{:S(2)}) collective-permute-start(bf16[6,4,4096]{2,1,0:T(4,128)(2,1)S(1)} %maximum_bitcast_fusion.refs_3_.refs_4_), channel_id=1, source_target_pairs={{0,2},{1,3},{2,0},{3,1},{4,6},{5,7},{6,4},{7,5},{8,10},{9,11},{10,... | collective-permute-start | bytes 589832 | tf_op jit(solution)/shard_map/ppermute | solution.py:168
  15.9 1.3 %collective-permute-start.6 = (bf16[6,4,4096]{2,1,0:T(4,128)(2,1)S(1)}, bf16[6,4,4096]{2,1,0:T(4,128)(2,1)S(1)}, u32[]{:S(2)}, u32[]{:S(2)}) collective-permute-start(bf16[6,4,4096]{2,1,0:T(4,128)(2,1)S(1)} %maximum_bitcast_fusion.refs_3_.refs_4_), channel_id=1, source_target_pairs={{0,3},{1,2},{2,1},{3,0},{4,7},{5,6},{6,5},{7,4},{8,11},{9,10},{10,... | collective-permute-start | bytes 589832 | tf_op jit(solution)/shard_map/ppermute | solution.py:168
  17.3 2.4 %collective-permute-start.2 = (bf16[6,4,4096]{2,1,0:T(4,128)(2,1)S(1)}, bf16[6,4,4096]{2,1,0:T(4,128)(2,1)S(1)}, u32[]{:S(2)}, u32[]{:S(2)}) collective-permute-start(bf16[6,4,4096]{2,1,0:T(4,128)(2,1)S(1)} %maximum_bitcast_fusion.refs_3_.refs_4_), channel_id=1, source_target_pairs={{0,24},{4,28},{8,16},{12,20},{16,8},{20,12},{24,0},{28,4},{1,25},{... | collective-permute-start | bytes 589832 | tf_op jit(solution)/shard_map/ppermute | solution.py:180
  20.8 0.7 %gather_fusion = s32[16]{0:T(128)S(1)} fusion(s32[4]{0:T(128)S(1)} %iota_xor_fusion.1, s32[1024]{0:T(1024)S(1)} %pad_clamp_fusion.1), kind=kCustom, calls=%fused_computation | custom fusion | bytes 192 | tf_op jit(solution)/shard_map/gather | solution.py:219
  21.5 0.7 %gather_fusion.1 = s32[32]{0:T(128)S(1)} fusion(s32[8]{0:T(128)S(1)} %iota_xor_fusion, s32[1024]{0:T(1024)S(1)} %pad_clamp_fusion), kind=kCustom, calls=%fused_computation.1 | custom fusion | bytes 384 | tf_op jit(solution)/shard_map/gather | solution.py:221
  22.2 0.7 %fusion.52.refs_13_ = bf16[32,32]{1,0:T(8,128)(2,1)} fusion(s32[32]{0:T(128)S(1)} %fusion.61), kind=kLoop, calls=%fused_computation.85 | loop fusion | flops 2048 | bytes 2176 | tf_op jit(solution)/shard_map/convert_element_type | solution.py:223
  22.9 4.4 %cosine_convert_fusion = (bf16[2048,128]{1,0:T(8,128)(2,1)S(1)}, bf16[2048,128]{1,0:T(8,128)(2,1)S(1)}) fusion(s32[128]{0:T(128)S(1)} %iota_add_fusion), kind=kLoop, calls=%fused_computation.23 | loop fusion | flops 4194304 | bytes 1049088 | tf_op jit(solution)/shard_map/convert
  27.2 0.7 %fusion.59.refs_12_ = bf16[16,16]{1,0:T(8,128)(2,1)} fusion(s32[16]{0:T(128)S(1)} %fusion.60), kind=kLoop, calls=%fused_computation.89 | loop fusion | flops 512 | bytes 576 | tf_op jit(solution)/shard_map/convert_element_type | solution.py:222
  29.5 1.1 %pad_maximum_fusion.refs_14_ = bf16[4096,128]{1,0:T(8,128)(2,1)} fusion(bf16[2048,128]{1,0:T(8,128)(2,1)S(1)} %get-tuple-element.11, bf16[2048,128]{1,0:T(8,128)(2,1)S(1)} %get-tuple-element.10), kind=kLoop, calls=%fused_computation.21 | loop fusion | flops 2097152 | bytes 2097152 | tf_op jit(solution)/shard_map/concatenate | solution.py:204
  30.5 0.8 %collective-permute-done.3 = bf16[6,12,4096]{2,1,0:T(8,128)(2,1)S(1)} collective-permute-done((bf16[6,12,4096]{2,1,0:T(8,128)(2,1)S(1)}, bf16[6,12,4096]{2,1,0:T(8,128)(2,1)S(1)}, u32[]{:S(2)}, u32[]{:S(2)}) %collective-permute-start.3) | collective-permute-done | bytes 589856 | tf_op jit(solution)/shard_map/ppermute | solution.py:184
  31.3 1.0 %fusion.93 = (bf16[6,4,4096]{2,1,0:T(4,128)(2,1)}, bf16[6,4,4096]{2,1,0:T(4,128)(2,1)}, bf16[6,4,4096]{2,1,0:T(4,128)(2,1)}) fusion(bf16[6,12,4096]{2,1,0:T(8,128)(2,1)S(1)} %collective-permute-done.3), kind=kLoop, calls=%fused_computation.142 | loop fusion | bytes 1179648 | tf_op jit(solution)/shard_map/slice | solution.py:187
  32.3 1.4 %collective-permute-done.5.refs_7_ = bf16[6,4,4096]{2,1,0:T(4,128)(2,1)S(1)} collective-permute-done((bf16[6,4,4096]{2,1,0:T(4,128)(2,1)S(1)}, bf16[6,4,4096]{2,1,0:T(4,128)(2,1)S(1)}, u32[]{:S(2)}, u32[]{:S(2)}) %collective-permute-start.5) | collective-permute-done | bytes 196640 | tf_op jit(solution)/shard_map/ppermute | solution.py:168
  33.7 0.6 %copy-done.7 = bf16[6,4,4096]{2,1,0:T(4,128)(2,1)} copy-done((bf16[6,4,4096]{2,1,0:T(4,128)(2,1)}, bf16[6,4,4096]{2,1,0:T(4,128)(2,1)S(1)}, u32[]{:S(2)}) %copy-start.7) | copy-done | bytes 196632
  34.5 13.9 %shard_map.37 = f32[512,128]{1,0:T(8,128)} custom-call(bf16[6,4,4096]{2,1,0:T(4,128)(2,1)} %get-tuple-element.7.refs_0_, bf16[6,4,4096]{2,1,0:T(4,128)(2,1)} %get-tuple-element.6.refs_1_, bf16[6,4,4096]{2,1,0:T(4,128)(2,1)} %get-tuple-element.5.refs_2_, bf16[6,4,4096]{2,1,0:T(4,128)(2,1)} %copy-done.1, bf16[6,4,4096]{2,1,0:T(4,128)(2,1)} %copy-done.1, ...), custom_call_target="tpu_custom_call" | custom-call | flops 587202560 | bytes 3670016 | tf_op jit(solution)/shard_map/pallas_call | solution.py:142
  48.4 1.0 %broadcast_multiply_fusion = f32[512,128]{1,0:T(8,128)S(1)} fusion(f32[512,128]{1,0:T(8,128)} %shard_map.37), kind=kLoop, calls=%fused_computation.44 | loop fusion | flops 65536 | bytes 524288 | tf_op jit(solution)/shard_map/mul | solution.py:227
  49.3 0.8 %fusion.21 = f32[16,1,32,128]{3,2,1,0:T(8,128)} fusion(f32[32,16,128]{2,1,0:T(8,128)S(1)} %bitcast.73, pred[16,128]{1,0:T(8,128)(4,1)S(1)} %broadcast_compare_fusion), kind=kLoop, calls=%fused_computation.42 | loop fusion | flops 65536 | bytes 526336 | tf_op jit(solution)/shard_map/broadcast_in_dim | solution.py:231
  (57 shorter events, 5.3 us)
Async XLA Ops:
  0.0 2.7 %copy-start = (f32[32]{0:T(128)S(1)}, f32[32]{0:T(128)}, u32[]{:S(2)}) copy-start(f32[32]{0:T(128)} %param.4) | copy-start | bytes 388
  11.8 17.1 %copy-start.1 = (bf16[6,4,4096]{2,1,0:T(4,128)(2,1)}, bf16[6,4,4096]{2,1,0:T(4,128)(2,1)S(1)}, u32[]{:S(2)}) copy-start(bf16[6,4,4096]{2,1,0:T(4,128)(2,1)S(1)} %maximum_bitcast_fusion.refs_3_.refs_4_) | copy-start | bytes 589828
  11.8 20.5 %collective-permute-start.7 = (bf16[6,4,4096]{2,1,0:T(4,128)(2,1)S(1)}, bf16[6,4,4096]{2,1,0:T(4,128)(2,1)S(1)}, u32[]{:S(2)}, u32[]{:S(2)}) collective-permute-start(bf16[6,4,4096]{2,1,0:T(4,128)(2,1)S(1)} %maximum_bitcast_fusion.refs_3_.refs_4_), channel_id=1, source_target_pairs={{0,2},{1,3},{2,0},{3,1},{4,6},{5,7},{6,4},{7,5},{8,10},{9,11},{10,... | collective-permute-start | bytes 589832 | tf_op jit(solution)/shard_map/ppermute | solution.py:168
  15.9 16.4 %collective-permute-start.6 = (bf16[6,4,4096]{2,1,0:T(4,128)(2,1)S(1)}, bf16[6,4,4096]{2,1,0:T(4,128)(2,1)S(1)}, u32[]{:S(2)}, u32[]{:S(2)}) collective-permute-start(bf16[6,4,4096]{2,1,0:T(4,128)(2,1)S(1)} %maximum_bitcast_fusion.refs_3_.refs_4_), channel_id=1, source_target_pairs={{0,3},{1,2},{2,1},{3,0},{4,7},{5,6},{6,5},{7,4},{8,11},{9,10},{10,... | collective-permute-start | bytes 589832 | tf_op jit(solution)/shard_map/ppermute | solution.py:168
  17.3 10.7 %collective-permute-start.2 = (bf16[6,4,4096]{2,1,0:T(4,128)(2,1)S(1)}, bf16[6,4,4096]{2,1,0:T(4,128)(2,1)S(1)}, u32[]{:S(2)}, u32[]{:S(2)}) collective-permute-start(bf16[6,4,4096]{2,1,0:T(4,128)(2,1)S(1)} %maximum_bitcast_fusion.refs_3_.refs_4_), channel_id=1, source_target_pairs={{0,24},{4,28},{8,16},{12,20},{16,8},{20,12},{24,0},{28,4},{1,25},{... | collective-permute-start | bytes 589832 | tf_op jit(solution)/shard_map/ppermute | solution.py:180
  19.7 8.8 %collective-permute-start.1 = (bf16[6,4,4096]{2,1,0:T(4,128)(2,1)S(1)}, bf16[6,4,4096]{2,1,0:T(4,128)(2,1)S(1)}, u32[]{:S(2)}, u32[]{:S(2)}) collective-permute-start(bf16[6,4,4096]{2,1,0:T(4,128)(2,1)S(1)} %maximum_bitcast_fusion.refs_3_.refs_4_), channel_id=1, source_target_pairs={{0,16},{4,20},{8,24},{12,28},{16,0},{20,4},{24,8},{28,12},{1,17},{... | collective-permute-start | bytes 589832 | tf_op jit(solution)/shard_map/ppermute | solution.py:180
  20.2 8.4 %collective-permute-start = (bf16[6,4,4096]{2,1,0:T(4,128)(2,1)S(1)}, bf16[6,4,4096]{2,1,0:T(4,128)(2,1)S(1)}, u32[]{:S(2)}, u32[]{:S(2)}) collective-permute-start(bf16[6,4,4096]{2,1,0:T(4,128)(2,1)S(1)} %maximum_bitcast_fusion.refs_3_.refs_4_), channel_id=1, source_target_pairs={{0,8},{4,12},{8,0},{12,4},{16,24},{20,28},{24,16},{28,20},{1,9},{5... | collective-permute-start | bytes 589832 | tf_op jit(solution)/shard_map/ppermute | solution.py:180
  22.9 6.5 %copy-start.9 = (s32[16]{0:T(128)S(1)}, s32[16]{0:T(128)}, u32[]{:S(2)}) copy-start(s32[16]{0:T(128)} %param.5) | copy-start | bytes 196
  27.9 2.6 %copy-start.2 = (bf16[6,4,4096]{2,1,0:T(4,128)(2,1)}, bf16[6,4,4096]{2,1,0:T(4,128)(2,1)S(1)}, u32[]{:S(2)}) copy-start(bf16[6,4,4096]{2,1,0:T(4,128)(2,1)S(1)} %collective-permute-done.2.refs_9_) | copy-start | bytes 589828
  27.9 5.8 %collective-permute-start.5 = (bf16[6,4,4096]{2,1,0:T(4,128)(2,1)S(1)}, bf16[6,4,4096]{2,1,0:T(4,128)(2,1)S(1)}, u32[]{:S(2)}, u32[]{:S(2)}) collective-permute-start(bf16[6,4,4096]{2,1,0:T(4,128)(2,1)S(1)} %maximum_bitcast_fusion.refs_3_.refs_4_), channel_id=1, source_target_pairs={{0,1},{1,0},{2,3},{3,2},{4,5},{5,4},{6,7},{7,6},{8,9},{9,8},{10,11... | collective-permute-start | bytes 589832 | tf_op jit(solution)/shard_map/ppermute | solution.py:168
  28.5 2.1 %copy-start.3 = (bf16[6,4,4096]{2,1,0:T(4,128)(2,1)}, bf16[6,4,4096]{2,1,0:T(4,128)(2,1)S(1)}, u32[]{:S(2)}) copy-start(bf16[6,4,4096]{2,1,0:T(4,128)(2,1)S(1)} %collective-permute-done.1.refs_8_) | copy-start | bytes 589828
  28.5 5.3 %collective-permute-start.4 = (bf16[6,4,4096]{2,1,0:T(4,128)(2,1)S(1)}, bf16[6,4,4096]{2,1,0:T(4,128)(2,1)S(1)}, u32[]{:S(2)}, u32[]{:S(2)}) collective-permute-start(bf16[6,4,4096]{2,1,0:T(4,128)(2,1)S(1)} %maximum_bitcast_fusion.refs_3_.refs_4_), channel_id=1, source_target_pairs={{0,4},{4,0},{8,12},{12,8},{16,20},{20,16},{24,28},{28,24},{1,5},{5... | collective-permute-start | bytes 589832 | tf_op jit(solution)/shard_map/ppermute | solution.py:182
  28.6 2.0 %copy-start.4 = (bf16[6,4,4096]{2,1,0:T(4,128)(2,1)}, bf16[6,4,4096]{2,1,0:T(4,128)(2,1)S(1)}, u32[]{:S(2)}) copy-start(bf16[6,4,4096]{2,1,0:T(4,128)(2,1)S(1)} %collective-permute-done.refs_6_) | copy-start | bytes 589828
  28.9 2.4 %collective-permute-start.3 = (bf16[6,12,4096]{2,1,0:T(8,128)(2,1)S(1)}, bf16[6,12,4096]{2,1,0:T(8,128)(2,1)S(1)}, u32[]{:S(2)}, u32[]{:S(2)}) collective-permute-start(bf16[6,12,4096]{2,1,0:T(8,128)(2,1)S(1)} %pad_maximum_fusion.1), channel_id=1, source_target_pairs={{0,4},{4,0},{8,12},{12,8},{16,20},{20,16},{24,28},{28,24},{1,5},{5... | collective-permute-start | bytes 1769480 | tf_op jit(solution)/shard_map/ppermute | solution.py:184
  32.3 1.4 %copy-start.5 = (bf16[6,4,4096]{2,1,0:T(4,128)(2,1)}, bf16[6,4,4096]{2,1,0:T(4,128)(2,1)S(1)}, u32[]{:S(2)}) copy-start(bf16[6,4,4096]{2,1,0:T(4,128)(2,1)S(1)} %collective-permute-done.7.refs_11_) | copy-start | bytes 589828
  32.3 1.4 %copy-start.6 = (bf16[6,4,4096]{2,1,0:T(4,128)(2,1)}, bf16[6,4,4096]{2,1,0:T(4,128)(2,1)S(1)}, u32[]{:S(2)}) copy-start(bf16[6,4,4096]{2,1,0:T(4,128)(2,1)S(1)} %collective-permute-done.6.refs_10_) | copy-start | bytes 589828
  33.7 0.7 %copy-start.7 = (bf16[6,4,4096]{2,1,0:T(4,128)(2,1)}, bf16[6,4,4096]{2,1,0:T(4,128)(2,1)S(1)}, u32[]{:S(2)}) copy-start(bf16[6,4,4096]{2,1,0:T(4,128)(2,1)S(1)} %collective-permute-done.5.refs_7_) | copy-start | bytes 589828
  33.7 0.8 %copy-start.8 = (bf16[6,4,4096]{2,1,0:T(4,128)(2,1)}, bf16[6,4,4096]{2,1,0:T(4,128)(2,1)S(1)}, u32[]{:S(2)}) copy-start(bf16[6,4,4096]{2,1,0:T(4,128)(2,1)S(1)} %collective-permute-done.4.refs_5_) | copy-start | bytes 589828

commit v17 on v16

--- a/solution.py
+++ b/solution.py
@@ -83,7 +83,7 @@
     window_count, piece, width = left_refs[0].shape
     rows_left = left_f32.shape[1]
     bin_count = width // 2
-    chunk = 512
+    chunk = 256
     while chunk > 128 and chunk * rows_left > 8192:
         chunk //= 2
     chunks = bin_count // chunk
@@ -104,24 +104,27 @@
         base = first * piece
 
         def one_chunk(step, carry):
-            local = step // chunks
-            partner = base + local
+            local = (step // chunks) * 2
             off = pl.multiple_of((step % chunks) * chunk, chunk)
-            acc_re = jnp.zeros((rows_left, chunk), jnp.float32)
-            acc_im = jnp.zeros((rows_left, chunk), jnp.float32)
+            sums = [jnp.zeros((rows_left, chunk), jnp.float32) for _ in range(4)]
             for window in range(window_count):
                 left_c = left_f32[window, :, pl.ds(off, chunk)]
                 left_d = left_f32[window, :, pl.ds(off + bin_count, chunk)]
-                vis_c = visit_f32[window, pl.ds(partner, 1), pl.ds(off, chunk)]
-                vis_d = visit_f32[window, pl.ds(partner, 1), pl.ds(off + bin_count, chunk)]
-                acc_re = acc_re + (left_c * vis_c + left_d * vis_d)
-                acc_im = acc_im + (left_c * vis_d - left_d * vis_c)
-            row = pl.multiple_of(local * rows_left, rows_left)
-            cross_ref[pl.ds(row, rows_left), pl.ds(off, chunk)] = acc_re.astype(jnp.bfloat16)
-            cross_ref[pl.ds(row, rows_left), pl.ds(off + bin_count, chunk)] = acc_im.astype(jnp.bfloat16)
+                for pick in range(2):
+                    partner = base + local + pick
+                    vis_c = visit_f32[window, pl.ds(partner, 1), pl.ds(off, chunk)]
+                    vis_d = visit_f32[window, pl.ds(partner, 1), pl.ds(off + bin_count, chunk)]
+                    sums[2 * pick] = sums[2 * pick] + (left_c * vis_c + left_d * vis_d)
+                    sums[2 * pick + 1] = sums[2 * pick + 1] + (left_c * vis_d - left_d * vis_c)
+            for pick in range(2):
+                row = pl.multiple_of((local + pick) * rows_left, rows_left)
+                cross_ref[pl.ds(row, rows_left), pl.ds(off, chunk)] = sums[2 * pick].astype(jnp.bfloat16)
+                cross_ref[pl.ds(row, rows_left), pl.ds(off + bin_count, chunk)] = sums[2 * pick + 1].astype(
+                    jnp.bfloat16
+                )
             return carry
 
-        lax.fori_loop(0, group * piece * chunks, one_chunk, 0)
+        lax.fori_loop(0, group * piece // 2 * chunks, one_chunk, 0)
         out_ref[base * rows_left:base * rows_left + group_rows, :] = jnp.dot(
             cross_ref[...], table_ref[...], preferred_element_type=jnp.float32
         )

time: 50.3 us -> 50.7 us (level)
  no operation moved by 1% of the time
where the time goes in v17:
time: 50.7 us; the launch traced here: 50.6 us
  Pallas kernels  14.3 us (28%)
  other arithmetic  10.1 us (20%)
  starting transfers between devices  9.66 us (19%)
  matrix products  7.97 us (16%)
  local copies, waits for them, and re-layouts  5.71 us (11%)
  waiting for transfers between devices  2.59 us (5%)
    pallas_call x1, Pallas kernels, pair_block(): pl.pallas_call(functools.partial(cross_kernel, tuple(issue_order)), out_s...  14.3 us
    ppermute x3, starting transfers between devices, xor_gather(): pieces.append(lax.ppermute(block, axis_name, pairs))  5.69 us
    another operation x2, other arithmetic  4.53 us
    ppermute x3, starting transfers between devices, chip_gather(): fetched.append(lax.ppermute(block, axis_name, pairs))  3.49 us
    reshape x1, local copies, waits for them, and re-layouts, decimate(): blocks = records.reshape(lead_dims + (block_count, in_block))  1.68 us
    ppermute x3, waiting for transfers between devices, xor_gather(): pieces.append(lax.ppermute(block, axis_name, pairs))  1.39 us
    dot_general x1, matrix products, spectrum(): jnp.einsum('bwfq,gq->bwgf', real_t, sin_three, precision=lax.Precision.HIGH)  1.31 us
    dot_general x1, matrix products, spectrum(): jnp.einsum('bwfq,gq->bwgf', imag_t, sin_three, precision=lax.Precision.HIGH)  1.24 us
  transfers between devices with their start and end apart: 8, of which 4 were waited for; matrix products, arithmetic and copies ran while one was open for 19% of the time, Pallas kernels for 0%

profile of v17, /device:TPU:0, one launch (start us, length us, event | category | flops | bytes accessed | tf_op | source)
XLA Modules:
  0.0 50.6 jit_solution(12177930666232870249)
XLA Ops:
  0.2 1.7 %reshape.236 = f32[4,6,32,256]{3,2,0,1:T(8,128)S(1)} reshape(f32[4,6,8192]{2,0,1:T(4,128)} %param.3) | data formatting | bytes 1572864 | tf_op jit(solution)/shard_map/reshape | solution.py:31
  2.1 0.7 %iota_compare_fusion = pred[32,288,128]{2,1,0:T(32,128)(4,1)S(1)} fusion(s32[32,128]{1,0:T(8,128)S(1)} %iota_subtract_fusion), kind=kLoop, calls=%fused_computation.2 | loop fusion | flops 1179648 | bytes 1196032 | tf_op jit(solution)/shard_map/eq | solution.py:38
  2.7 1.1 %fusion = f32[1,288,128]{2,0,1:T(1,128)S(1)} fusion(pred[32,288,128]{2,1,0:T(32,128)(4,1)S(1)} %iota_compare_fusion, f32[32]{0:T(128)S(1)} %copy-done), kind=kOutput, calls=%fused_computation.3 | convolution fusion | flops 7077888 | bytes 1327232 | tf_op jit(solution)/shard_map/k,kij->ij/dot_general | solution.py:39
  3.8 0.7 %fusion.4 = f32[4,6,32,128]{3,2,1,0:T(8,128)S(1)} fusion(f32[288,128,1,1]{1,0,3,2:T(8,128)S(1)} %bitcast.74, f32[4,6,31,32]{3,2,1,0:T(8,128)S(1)} %copy.30, f32[4,6,32,256]{3,2,0,1:T(8,128)S(1)} %reshape.236), kind=kOutput, calls=%fused_computation.14 | convolution fusion | flops 170532864 | bytes 1422336 | tf_op jit(solution)/shard_map/swbi,ij->swbj/dot_general | solution.py:40
  5.9 1.2 %fusion.13 = f32[32,4,6,64]{3,0,2,1:T(8,128)S(1)} fusion(f32[64,4,6,64]{3,0,2,1:T(8,128)S(1)} %fusion.27, f32[64,4,6,64]{3,0,2,1:T(8,128)S(1)} %convolution_negate_fusion, f32[64,64]{1,0:T(8,128)S(1)} %get-tuple-element.14, f32[64,64]{1,0:T(8,128)S(1)} %get-tuple-element.15), kind=kOutput, calls=%fused_computation.28 | convolution fusion | flops 19197952 | bytes 1015808 | tf_op jit(solution)/shard_map/bwfq,gq->bwgf/dot_general | solution.py:60
  7.2 1.2 %fusion.17 = f32[32,4,6,64]{3,0,2,1:T(8,128)S(1)} fusion(f32[64,4,6,64]{3,0,2,1:T(8,128)S(1)} %convolution_negate_fusion, f32[64,4,6,64]{3,0,2,1:T(8,128)S(1)} %fusion.27, f32[64,64]{1,0:T(8,128)S(1)} %get-tuple-element.14, f32[64,64]{1,0:T(8,128)S(1)} %get-tuple-element.15), kind=kOutput, calls=%fused_computation.32 | convolution fusion | flops 19197952 | bytes 1015808 | tf_op jit(solution)/shard_map/bwfq,gq->bwgf/dot_general | solution.py:57
  8.4 1.2 %fusion.3 = f32[4,6,32,64]{3,2,1,0:T(8,128)S(1)} fusion(f32[32,4,6,64]{3,0,2,1:T(8,128)S(1)} %fusion.17, f32[64,4,6,64]{3,0,2,1:T(8,128)S(1)} %fusion.27, f32[64,4,6,64]{3,0,2,1:T(8,128)S(1)} %convolution_negate_fusion, f32[64,64]{1,0:T(8,128)S(1)} %get-tuple-element.14, f32[64,64]{1,0:T(8,128)S(1)} %get-tuple-element.15), kind=kOutput, calls=%fused_computation.12 | convolution fusion | flops 19247104 | bytes 1212416 | tf_op jit(solution)/shard_map/bwfq,gq->bwgf/dot_general | solution.py:59
  9.6 1.3 %add_reduce_fusion = (f32[4,6,32]{2,1,0:T(8,128)S(1)}, f32[4,6,32,64]{3,2,1,0:T(8,128)S(1)}) fusion(f32[4,6,32,64]{3,2,1,0:T(8,128)S(1)} %fusion.3, f32[32,4,6,64]{3,0,2,1:T(8,128)S(1)} %fusion.13, f32[64,4,6,64]{3,0,2,1:T(8,128)S(1)} %convolution_negate_fusion, f32[64,64]{1,0:T(8,128)S(1)} %get-tuple-element.14, f32[64,4,6,64]{3,0,2,1:T(8,128)S(1)} %fusion.27, ...), kind=kOutput, calls=%fused_computation.40 | convolution fusion | flops 19442944 | bytes 1412096 | tf_op jit(solution)/shard_map/bwfq,gq->bwgf/dot_general | solution.py:62
  11.8 4.1 %collective-permute-start.7 = (bf16[6,4,4096]{2,1,0:T(4,128)(2,1)S(1)}, bf16[6,4,4096]{2,1,0:T(4,128)(2,1)S(1)}, u32[]{:S(2)}, u32[]{:S(2)}) collective-permute-start(bf16[6,4,4096]{2,1,0:T(4,128)(2,1)S(1)} %maximum_bitcast_fusion.refs_3_.refs_4_), channel_id=1, source_target_pairs={{0,2},{1,3},{2,0},{3,1},{4,6},{5,7},{6,4},{7,5},{8,10},{9,11},{10,... | collective-permute-start | bytes 589832 | tf_op jit(solution)/shard_map/ppermute | solution.py:171
  15.9 1.3 %collective-permute-start.6 = (bf16[6,4,4096]{2,1,0:T(4,128)(2,1)S(1)}, bf16[6,4,4096]{2,1,0:T(4,128)(2,1)S(1)}, u32[]{:S(2)}, u32[]{:S(2)}) collective-permute-start(bf16[6,4,4096]{2,1,0:T(4,128)(2,1)S(1)} %maximum_bitcast_fusion.refs_3_.refs_4_), channel_id=1, source_target_pairs={{0,3},{1,2},{2,1},{3,0},{4,7},{5,6},{6,5},{7,4},{8,11},{9,10},{10,... | collective-permute-start | bytes 589832 | tf_op jit(solution)/shard_map/ppermute | solution.py:171
  17.3 2.4 %collective-permute-start.2 = (bf16[6,4,4096]{2,1,0:T(4,128)(2,1)S(1)}, bf16[6,4,4096]{2,1,0:T(4,128)(2,1)S(1)}, u32[]{:S(2)}, u32[]{:S(2)}) collective-permute-start(bf16[6,4,4096]{2,1,0:T(4,128)(2,1)S(1)} %maximum_bitcast_fusion.refs_3_.refs_4_), channel_id=1, source_target_pairs={{0,24},{4,28},{8,16},{12,20},{16,8},{20,12},{24,0},{28,4},{1,25},{... | collective-permute-start | bytes 589832 | tf_op jit(solution)/shard_map/ppermute | solution.py:183
  20.8 0.7 %gather_fusion = s32[16]{0:T(128)S(1)} fusion(s32[4]{0:T(128)S(1)} %iota_xor_fusion.1, s32[1024]{0:T(1024)S(1)} %pad_clamp_fusion.1), kind=kCustom, calls=%fused_computation | custom fusion | bytes 192 | tf_op jit(solution)/shard_map/gather | solution.py:222
  21.5 0.7 %gather_fusion.1 = s32[32]{0:T(128)S(1)} fusion(s32[8]{0:T(128)S(1)} %iota_xor_fusion, s32[1024]{0:T(1024)S(1)} %pad_clamp_fusion), kind=kCustom, calls=%fused_computation.1 | custom fusion | bytes 384 | tf_op jit(solution)/shard_map/gather | solution.py:224
  22.2 0.7 %fusion.52.refs_13_ = bf16[32,32]{1,0:T(8,128)(2,1)} fusion(s32[32]{0:T(128)S(1)} %fusion.61), kind=kLoop, calls=%fused_computation.85 | loop fusion | flops 2048 | bytes 2176 | tf_op jit(solution)/shard_map/convert_element_type | solution.py:226
  22.9 4.4 %cosine_convert_fusion = (bf16[2048,128]{1,0:T(8,128)(2,1)S(1)}, bf16[2048,128]{1,0:T(8,128)(2,1)S(1)}) fusion(s32[128]{0:T(128)S(1)} %iota_add_fusion), kind=kLoop, calls=%fused_computation.23 | loop fusion | flops 4194304 | bytes 1049088 | tf_op jit(solution)/shard_map/convert
  27.2 0.7 %fusion.59.refs_12_ = bf16[16,16]{1,0:T(8,128)(2,1)} fusion(s32[16]{0:T(128)S(1)} %fusion.60), kind=kLoop, calls=%fused_computation.89 | loop fusion | flops 512 | bytes 576 | tf_op jit(solution)/shard_map/convert_element_type | solution.py:225
  29.5 1.1 %pad_maximum_fusion.refs_14_ = bf16[4096,128]{1,0:T(8,128)(2,1)} fusion(bf16[2048,128]{1,0:T(8,128)(2,1)S(1)} %get-tuple-element.11, bf16[2048,128]{1,0:T(8,128)(2,1)S(1)} %get-tuple-element.10), kind=kLoop, calls=%fused_computation.21 | loop fusion | flops 2097152 | bytes 2097152 | tf_op jit(solution)/shard_map/concatenate | solution.py:207
  30.5 0.8 %collective-permute-done.3 = bf16[6,12,4096]{2,1,0:T(8,128)(2,1)S(1)} collective-permute-done((bf16[6,12,4096]{2,1,0:T(8,128)(2,1)S(1)}, bf16[6,12,4096]{2,1,0:T(8,128)(2,1)S(1)}, u32[]{:S(2)}, u32[]{:S(2)}) %collective-permute-start.3) | collective-permute-done | bytes 589856 | tf_op jit(solution)/shard_map/ppermute | solution.py:187
  31.3 1.0 %fusion.93 = (bf16[6,4,4096]{2,1,0:T(4,128)(2,1)}, bf16[6,4,4096]{2,1,0:T(4,128)(2,1)}, bf16[6,4,4096]{2,1,0:T(4,128)(2,1)}) fusion(bf16[6,12,4096]{2,1,0:T(8,128)(2,1)S(1)} %collective-permute-done.3), kind=kLoop, calls=%fused_computation.142 | loop fusion | bytes 1179648 | tf_op jit(solution)/shard_map/slice | solution.py:190
  32.3 1.4 %collective-permute-done.5.refs_7_ = bf16[6,4,4096]{2,1,0:T(4,128)(2,1)S(1)} collective-permute-done((bf16[6,4,4096]{2,1,0:T(4,128)(2,1)S(1)}, bf16[6,4,4096]{2,1,0:T(4,128)(2,1)S(1)}, u32[]{:S(2)}, u32[]{:S(2)}) %collective-permute-start.5) | collective-permute-done | bytes 196640 | tf_op jit(solution)/shard_map/ppermute | solution.py:171
  33.7 0.6 %copy-done.7 = bf16[6,4,4096]{2,1,0:T(4,128)(2,1)} copy-done((bf16[6,4,4096]{2,1,0:T(4,128)(2,1)}, bf16[6,4,4096]{2,1,0:T(4,128)(2,1)S(1)}, u32[]{:S(2)}) %copy-start.7) | copy-done | bytes 196632
  34.5 14.3 %shard_map.37 = f32[512,128]{1,0:T(8,128)} custom-call(bf16[6,4,4096]{2,1,0:T(4,128)(2,1)} %get-tuple-element.7.refs_0_, bf16[6,4,4096]{2,1,0:T(4,128)(2,1)} %get-tuple-element.6.refs_1_, bf16[6,4,4096]{2,1,0:T(4,128)(2,1)} %get-tuple-element.5.refs_2_, bf16[6,4,4096]{2,1,0:T(4,128)(2,1)} %copy-done.1, bf16[6,4,4096]{2,1,0:T(4,128)(2,1)} %copy-done.1, ...), custom_call_target="tpu_custom_call" | custom-call | flops 587202560 | bytes 3670016 | tf_op jit(solution)/shard_map/pallas_call | solution.py:145
  48.8 1.0 %broadcast_multiply_fusion = f32[512,128]{1,0:T(8,128)S(1)} fusion(f32[512,128]{1,0:T(8,128)} %shard_map.37), kind=kLoop, calls=%fused_computation.44 | loop fusion | flops 65536 | bytes 524288 | tf_op jit(solution)/shard_map/mul | solution.py:230
  49.8 0.8 %fusion.21 = f32[16,1,32,128]{3,2,1,0:T(8,128)} fusion(f32[32,16,128]{2,1,0:T(8,128)S(1)} %bitcast.73, pred[16,128]{1,0:T(8,128)(4,1)S(1)} %broadcast_compare_fusion), kind=kLoop, calls=%fused_computation.42 | loop fusion | flops 65536 | bytes 526336 | tf_op jit(solution)/shard_map/broadcast_in_dim | solution.py:234
  (57 shorter events, 5.3 us)
Async XLA Ops:
  0.0 2.7 %copy-start = (f32[32]{0:T(128)S(1)}, f32[32]{0:T(128)}, u32[]{:S(2)}) copy-start(f32[32]{0:T(128)} %param.4) | copy-start | bytes 388
  11.8 17.1 %copy-start.1 = (bf16[6,4,4096]{2,1,0:T(4,128)(2,1)}, bf16[6,4,4096]{2,1,0:T(4,128)(2,1)S(1)}, u32[]{:S(2)}) copy-start(bf16[6,4,4096]{2,1,0:T(4,128)(2,1)S(1)} %maximum_bitcast_fusion.refs_3_.refs_4_) | copy-start | bytes 589828
  11.8 20.5 %collective-permute-start.7 = (bf16[6,4,4096]{2,1,0:T(4,128)(2,1)S(1)}, bf16[6,4,4096]{2,1,0:T(4,128)(2,1)S(1)}, u32[]{:S(2)}, u32[]{:S(2)}) collective-permute-start(bf16[6,4,4096]{2,1,0:T(4,128)(2,1)S(1)} %maximum_bitcast_fusion.refs_3_.refs_4_), channel_id=1, source_target_pairs={{0,2},{1,3},{2,0},{3,1},{4,6},{5,7},{6,4},{7,5},{8,10},{9,11},{10,... | collective-permute-start | bytes 589832 | tf_op jit(solution)/shard_map/ppermute | solution.py:171
  15.9 16.4 %collective-permute-start.6 = (bf16[6,4,4096]{2,1,0:T(4,128)(2,1)S(1)}, bf16[6,4,4096]{2,1,0:T(4,128)(2,1)S(1)}, u32[]{:S(2)}, u32[]{:S(2)}) collective-permute-start(bf16[6,4,4096]{2,1,0:T(4,128)(2,1)S(1)} %maximum_bitcast_fusion.refs_3_.refs_4_), channel_id=1, source_target_pairs={{0,3},{1,2},{2,1},{3,0},{4,7},{5,6},{6,5},{7,4},{8,11},{9,10},{10,... | collective-permute-start | bytes 589832 | tf_op jit(solution)/shard_map/ppermute | solution.py:171
  17.3 10.7 %collective-permute-start.2 = (bf16[6,4,4096]{2,1,0:T(4,128)(2,1)S(1)}, bf16[6,4,4096]{2,1,0:T(4,128)(2,1)S(1)}, u32[]{:S(2)}, u32[]{:S(2)}) collective-permute-start(bf16[6,4,4096]{2,1,0:T(4,128)(2,1)S(1)} %maximum_bitcast_fusion.refs_3_.refs_4_), channel_id=1, source_target_pairs={{0,24},{4,28},{8,16},{12,20},{16,8},{20,12},{24,0},{28,4},{1,25},{... | collective-permute-start | bytes 589832 | tf_op jit(solution)/shard_map/ppermute | solution.py:183
  19.7 8.8 %collective-permute-start.1 = (bf16[6,4,4096]{2,1,0:T(4,128)(2,1)S(1)}, bf16[6,4,4096]{2,1,0:T(4,128)(2,1)S(1)}, u32[]{:S(2)}, u32[]{:S(2)}) collective-permute-start(bf16[6,4,4096]{2,1,0:T(4,128)(2,1)S(1)} %maximum_bitcast_fusion.refs_3_.refs_4_), channel_id=1, source_target_pairs={{0,16},{4,20},{8,24},{12,28},{16,0},{20,4},{24,8},{28,12},{1,17},{... | collective-permute-start | bytes 589832 | tf_op jit(solution)/shard_map/ppermute | solution.py:183
  20.2 8.4 %collective-permute-start = (bf16[6,4,4096]{2,1,0:T(4,128)(2,1)S(1)}, bf16[6,4,4096]{2,1,0:T(4,128)(2,1)S(1)}, u32[]{:S(2)}, u32[]{:S(2)}) collective-permute-start(bf16[6,4,4096]{2,1,0:T(4,128)(2,1)S(1)} %maximum_bitcast_fusion.refs_3_.refs_4_), channel_id=1, source_target_pairs={{0,8},{4,12},{8,0},{12,4},{16,24},{20,28},{24,16},{28,20},{1,9},{5... | collective-permute-start | bytes 589832 | tf_op jit(solution)/shard_map/ppermute | solution.py:183
  22.9 6.5 %copy-start.9 = (s32[16]{0:T(128)S(1)}, s32[16]{0:T(128)}, u32[]{:S(2)}) copy-start(s32[16]{0:T(128)} %param.5) | copy-start | bytes 196
  27.9 2.6 %copy-start.2 = (bf16[6,4,4096]{2,1,0:T(4,128)(2,1)}, bf16[6,4,4096]{2,1,0:T(4,128)(2,1)S(1)}, u32[]{:S(2)}) copy-start(bf16[6,4,4096]{2,1,0:T(4,128)(2,1)S(1)} %collective-permute-done.2.refs_9_) | copy-start | bytes 589828
  27.9 5.8 %collective-permute-start.5 = (bf16[6,4,4096]{2,1,0:T(4,128)(2,1)S(1)}, bf16[6,4,4096]{2,1,0:T(4,128)(2,1)S(1)}, u32[]{:S(2)}, u32[]{:S(2)}) collective-permute-start(bf16[6,4,4096]{2,1,0:T(4,128)(2,1)S(1)} %maximum_bitcast_fusion.refs_3_.refs_4_), channel_id=1, source_target_pairs={{0,1},{1,0},{2,3},{3,2},{4,5},{5,4},{6,7},{7,6},{8,9},{9,8},{10,11... | collective-permute-start | bytes 589832 | tf_op jit(solution)/shard_map/ppermute | solution.py:171
  28.5 2.1 %copy-start.3 = (bf16[6,4,4096]{2,1,0:T(4,128)(2,1)}, bf16[6,4,4096]{2,1,0:T(4,128)(2,1)S(1)}, u32[]{:S(2)}) copy-start(bf16[6,4,4096]{2,1,0:T(4,128)(2,1)S(1)} %collective-permute-done.1.refs_8_) | copy-start | bytes 589828
  28.5 5.3 %collective-permute-start.4 = (bf16[6,4,4096]{2,1,0:T(4,128)(2,1)S(1)}, bf16[6,4,4096]{2,1,0:T(4,128)(2,1)S(1)}, u32[]{:S(2)}, u32[]{:S(2)}) collective-permute-start(bf16[6,4,4096]{2,1,0:T(4,128)(2,1)S(1)} %maximum_bitcast_fusion.refs_3_.refs_4_), channel_id=1, source_target_pairs={{0,4},{4,0},{8,12},{12,8},{16,20},{20,16},{24,28},{28,24},{1,5},{5... | collective-permute-start | bytes 589832 | tf_op jit(solution)/shard_map/ppermute | solution.py:185
  28.6 2.0 %copy-start.4 = (bf16[6,4,4096]{2,1,0:T(4,128)(2,1)}, bf16[6,4,4096]{2,1,0:T(4,128)(2,1)S(1)}, u32[]{:S(2)}) copy-start(bf16[6,4,4096]{2,1,0:T(4,128)(2,1)S(1)} %collective-permute-done.refs_6_) | copy-start | bytes 589828
  28.9 2.4 %collective-permute-start.3 = (bf16[6,12,4096]{2,1,0:T(8,128)(2,1)S(1)}, bf16[6,12,4096]{2,1,0:T(8,128)(2,1)S(1)}, u32[]{:S(2)}, u32[]{:S(2)}) collective-permute-start(bf16[6,12,4096]{2,1,0:T(8,128)(2,1)S(1)} %pad_maximum_fusion.1), channel_id=1, source_target_pairs={{0,4},{4,0},{8,12},{12,8},{16,20},{20,16},{24,28},{28,24},{1,5},{5... | collective-permute-start | bytes 1769480 | tf_op jit(solution)/shard_map/ppermute | solution.py:187
  32.3 1.4 %copy-start.5 = (bf16[6,4,4096]{2,1,0:T(4,128)(2,1)}, bf16[6,4,4096]{2,1,0:T(4,128)(2,1)S(1)}, u32[]{:S(2)}) copy-start(bf16[6,4,4096]{2,1,0:T(4,128)(2,1)S(1)} %collective-permute-done.7.refs_11_) | copy-start | bytes 589828
  32.3 1.4 %copy-start.6 = (bf16[6,4,4096]{2,1,0:T(4,128)(2,1)}, bf16[6,4,4096]{2,1,0:T(4,128)(2,1)S(1)}, u32[]{:S(2)}) copy-start(bf16[6,4,4096]{2,1,0:T(4,128)(2,1)S(1)} %collective-permute-done.6.refs_10_) | copy-start | bytes 589828
  33.7 0.7 %copy-start.7 = (bf16[6,4,4096]{2,1,0:T(4,128)(2,1)}, bf16[6,4,4096]{2,1,0:T(4,128)(2,1)S(1)}, u32[]{:S(2)}) copy-start(bf16[6,4,4096]{2,1,0:T(4,128)(2,1)S(1)} %collective-permute-done.5.refs_7_) | copy-start | bytes 589828
  33.7 0.8 %copy-start.8 = (bf16[6,4,4096]{2,1,0:T(4,128)(2,1)}, bf16[6,4,4096]{2,1,0:T(4,128)(2,1)S(1)}, u32[]{:S(2)}) copy-start(bf16[6,4,4096]{2,1,0:T(4,128)(2,1)S(1)} %collective-permute-done.4.refs_5_) | copy-start | bytes 589828

commit v18 on v16

--- a/solution.py
+++ b/solution.py
@@ -78,7 +78,9 @@
 
 def cross_kernel(slots, *refs):
     piece_refs = refs[:len(slots)]
-    left_perm, visit_perm, table_ref, out_ref, left_f32, visit_f32, cross_ref = refs[len(slots):]
+    left_perm, visit_perm, table_ref, out_ref, left_f32, visit_f32, left_diff, visit_mix, cross_ref = refs[
+        len(slots):
+    ]
     left_refs = [ref for ref, slot in zip(piece_refs, slots) if slot[0] == 0]
     window_count, piece, width = left_refs[0].shape
     rows_left = left_f32.shape[1]
@@ -99,6 +101,11 @@
             target[window] = jnp.dot(
                 perm_ref[...], target[window].astype(jnp.bfloat16), preferred_element_type=jnp.float32
             )
+        left_diff[window] = left_f32[window, :, :bin_count] - left_f32[window, :, bin_count:]
+        vis_c = visit_f32[window, :, :bin_count]
+        vis_d = visit_f32[window, :, bin_count:]
+        visit_mix[window, :, :bin_count] = vis_c + vis_d
+        visit_mix[window, :, bin_count:] = vis_d - vis_c
 
     for first in range(0, visit_count, group):
         base = first * piece
@@ -112,10 +119,13 @@
             for window in range(window_count):
                 left_c = left_f32[window, :, pl.ds(off, chunk)]
                 left_d = left_f32[window, :, pl.ds(off + bin_count, chunk)]
+                left_cd = left_diff[window, :, pl.ds(off, chunk)]
                 vis_c = visit_f32[window, pl.ds(partner, 1), pl.ds(off, chunk)]
-                vis_d = visit_f32[window, pl.ds(partner, 1), pl.ds(off + bin_count, chunk)]
-                acc_re = acc_re + (left_c * vis_c + left_d * vis_d)
-                acc_im = acc_im + (left_c * vis_d - left_d * vis_c)
+                vis_sum = visit_mix[window, pl.ds(partner, 1), pl.ds(off, chunk)]
+                vis_diff = visit_mix[window, pl.ds(partner, 1), pl.ds(off + bin_count, chunk)]
+                shared = vis_c * left_cd
+                acc_re = acc_re + (shared + left_d * vis_sum)
+                acc_im = acc_im + (shared + left_c * vis_diff)
             row = pl.multiple_of(local * rows_left, rows_left)
             cross_ref[pl.ds(row, rows_left), pl.ds(off, chunk)] = acc_re.astype(jnp.bfloat16)
             cross_ref[pl.ds(row, rows_left), pl.ds(off + bin_count, chunk)] = acc_im.astype(jnp.bfloat16)
@@ -146,6 +156,8 @@
         out_specs=pl.BlockSpec(memory_space=vmem),
         scratch_shapes=[
             vmem((window_count, rows_left, width), jnp.float32),
+            vmem((window_count, visit_rows, width), jnp.float32),
+            vmem((window_count, rows_left, width // 2), jnp.float32),
             vmem((window_count, visit_rows, width), jnp.float32),
             vmem((group * piece * rows_left, width), jnp.bfloat16),
         ],

time: 50.3 us -> 52 us (1.034)
  Pallas kernels: 13.9 us -> 15.5 us
    pallas_call x1, Pallas kernels: 13.9 us -> 15.5 us  [pair_block(): pl.pallas_call(functools.partial(cross_kernel, tuple(issue_order)), out_s...]
  transfers between devices with their start and end apart: 8 -> 8, of which waited for: 4 -> 4; matrix products, arithmetic and copies ran while one was open for 19% -> 18% of each run, Pallas kernels for 0% -> 0%
where the time goes in v18:
time: 52 us; the launch traced here: 51.8 us
  Pallas kernels  15.5 us (30%)
  other arithmetic  10.1 us (19%)
  starting transfers between devices  9.66 us (19%)
  matrix products  7.97 us (15%)
  local copies, waits for them, and re-layouts  5.71 us (11%)
  waiting for transfers between devices  2.59 us (5%)
    pallas_call x1, Pallas kernels, pair_block(): pl.pallas_call(functools.partial(cross_kernel, tuple(issue_order)), out_s...  15.5 us
    ppermute x3, starting transfers between devices, xor_gather(): pieces.append(lax.ppermute(block, axis_name, pairs))  5.69 us
    another operation x2, other arithmetic  4.53 us
    ppermute x3, starting transfers between devices, chip_gather(): fetched.append(lax.ppermute(block, axis_name, pairs))  3.49 us
    reshape x1, local copies, waits for them, and re-layouts, decimate(): blocks = records.reshape(lead_dims + (block_count, in_block))  1.68 us
    ppermute x3, waiting for transfers between devices, xor_gather(): pieces.append(lax.ppermute(block, axis_name, pairs))  1.39 us
    dot_general x1, matrix products, spectrum(): jnp.einsum('bwfq,gq->bwgf', real_t, sin_three, precision=lax.Precision.HIGH)  1.31 us
    dot_general x1, matrix products, spectrum(): jnp.einsum('bwfq,gq->bwgf', imag_t, sin_three, precision=lax.Precision.HIGH)  1.24 us
  transfers between devices with their start and end apart: 8, of which 4 were waited for; matrix products, arithmetic and copies ran while one was open for 18% of the time, Pallas kernels for 0%

profile of v18, /device:TPU:0, one launch (start us, length us, event | category | flops | bytes accessed | tf_op | source)
XLA Modules:
  0.0 51.8 jit_solution(15309410419604168190)
XLA Ops:
  0.2 1.7 %reshape.236 = f32[4,6,32,256]{3,2,0,1:T(8,128)S(1)} reshape(f32[4,6,8192]{2,0,1:T(4,128)} %param.3) | data formatting | bytes 1572864 | tf_op jit(solution)/shard_map/reshape | solution.py:31
  2.1 0.7 %iota_compare_fusion = pred[32,288,128]{2,1,0:T(32,128)(4,1)S(1)} fusion(s32[32,128]{1,0:T(8,128)S(1)} %iota_subtract_fusion), kind=kLoop, calls=%fused_computation.2 | loop fusion | flops 1179648 | bytes 1196032 | tf_op jit(solution)/shard_map/eq | solution.py:38
  2.7 1.1 %fusion = f32[1,288,128]{2,0,1:T(1,128)S(1)} fusion(pred[32,288,128]{2,1,0:T(32,128)(4,1)S(1)} %iota_compare_fusion, f32[32]{0:T(128)S(1)} %copy-done), kind=kOutput, calls=%fused_computation.3 | convolution fusion | flops 7077888 | bytes 1327232 | tf_op jit(solution)/shard_map/k,kij->ij/dot_general | solution.py:39
  3.8 0.7 %fusion.4 = f32[4,6,32,128]{3,2,1,0:T(8,128)S(1)} fusion(f32[288,128,1,1]{1,0,3,2:T(8,128)S(1)} %bitcast.74, f32[4,6,31,32]{3,2,1,0:T(8,128)S(1)} %copy.30, f32[4,6,32,256]{3,2,0,1:T(8,128)S(1)} %reshape.236), kind=kOutput, calls=%fused_computation.14 | convolution fusion | flops 170532864 | bytes 1422336 | tf_op jit(solution)/shard_map/swbi,ij->swbj/dot_general | solution.py:40
  5.9 1.2 %fusion.13 = f32[32,4,6,64]{3,0,2,1:T(8,128)S(1)} fusion(f32[64,4,6,64]{3,0,2,1:T(8,128)S(1)} %fusion.27, f32[64,4,6,64]{3,0,2,1:T(8,128)S(1)} %convolution_negate_fusion, f32[64,64]{1,0:T(8,128)S(1)} %get-tuple-element.14, f32[64,64]{1,0:T(8,128)S(1)} %get-tuple-element.15), kind=kOutput, calls=%fused_computation.28 | convolution fusion | flops 19197952 | bytes 1015808 | tf_op jit(solution)/shard_map/bwfq,gq->bwgf/dot_general | solution.py:60
  7.2 1.2 %fusion.17 = f32[32,4,6,64]{3,0,2,1:T(8,128)S(1)} fusion(f32[64,4,6,64]{3,0,2,1:T(8,128)S(1)} %convolution_negate_fusion, f32[64,4,6,64]{3,0,2,1:T(8,128)S(1)} %fusion.27, f32[64,64]{1,0:T(8,128)S(1)} %get-tuple-element.14, f32[64,64]{1,0:T(8,128)S(1)} %get-tuple-element.15), kind=kOutput, calls=%fused_computation.32 | convolution fusion | flops 19197952 | bytes 1015808 | tf_op jit(solution)/shard_map/bwfq,gq->bwgf/dot_general | solution.py:57
  8.4 1.2 %fusion.3 = f32[4,6,32,64]{3,2,1,0:T(8,128)S(1)} fusion(f32[32,4,6,64]{3,0,2,1:T(8,128)S(1)} %fusion.17, f32[64,4,6,64]{3,0,2,1:T(8,128)S(1)} %fusion.27, f32[64,4,6,64]{3,0,2,1:T(8,128)S(1)} %convolution_negate_fusion, f32[64,64]{1,0:T(8,128)S(1)} %get-tuple-element.14, f32[64,64]{1,0:T(8,128)S(1)} %get-tuple-element.15), kind=kOutput, calls=%fused_computation.12 | convolution fusion | flops 19247104 | bytes 1212416 | tf_op jit(solution)/shard_map/bwfq,gq->bwgf/dot_general | solution.py:59
  9.6 1.3 %add_reduce_fusion = (f32[4,6,32]{2,1,0:T(8,128)S(1)}, f32[4,6,32,64]{3,2,1,0:T(8,128)S(1)}) fusion(f32[4,6,32,64]{3,2,1,0:T(8,128)S(1)} %fusion.3, f32[32,4,6,64]{3,0,2,1:T(8,128)S(1)} %fusion.13, f32[64,4,6,64]{3,0,2,1:T(8,128)S(1)} %convolution_negate_fusion, f32[64,64]{1,0:T(8,128)S(1)} %get-tuple-element.14, f32[64,4,6,64]{3,0,2,1:T(8,128)S(1)} %fusion.27, ...), kind=kOutput, calls=%fused_computation.40 | convolution fusion | flops 19442944 | bytes 1412096 | tf_op jit(solution)/shard_map/bwfq,gq->bwgf/dot_general | solution.py:62
  11.8 4.1 %collective-permute-start.7 = (bf16[6,4,4096]{2,1,0:T(4,128)(2,1)S(1)}, bf16[6,4,4096]{2,1,0:T(4,128)(2,1)S(1)}, u32[]{:S(2)}, u32[]{:S(2)}) collective-permute-start(bf16[6,4,4096]{2,1,0:T(4,128)(2,1)S(1)} %maximum_bitcast_fusion.refs_3_.refs_4_), channel_id=1, source_target_pairs={{0,2},{1,3},{2,0},{3,1},{4,6},{5,7},{6,4},{7,5},{8,10},{9,11},{10,... | collective-permute-start | bytes 589832 | tf_op jit(solution)/shard_map/ppermute | solution.py:180
  15.9 1.3 %collective-permute-start.6 = (bf16[6,4,4096]{2,1,0:T(4,128)(2,1)S(1)}, bf16[6,4,4096]{2,1,0:T(4,128)(2,1)S(1)}, u32[]{:S(2)}, u32[]{:S(2)}) collective-permute-start(bf16[6,4,4096]{2,1,0:T(4,128)(2,1)S(1)} %maximum_bitcast_fusion.refs_3_.refs_4_), channel_id=1, source_target_pairs={{0,3},{1,2},{2,1},{3,0},{4,7},{5,6},{6,5},{7,4},{8,11},{9,10},{10,... | collective-permute-start | bytes 589832 | tf_op jit(solution)/shard_map/ppermute | solution.py:180
  17.3 2.4 %collective-permute-start.2 = (bf16[6,4,4096]{2,1,0:T(4,128)(2,1)S(1)}, bf16[6,4,4096]{2,1,0:T(4,128)(2,1)S(1)}, u32[]{:S(2)}, u32[]{:S(2)}) collective-permute-start(bf16[6,4,4096]{2,1,0:T(4,128)(2,1)S(1)} %maximum_bitcast_fusion.refs_3_.refs_4_), channel_id=1, source_target_pairs={{0,24},{4,28},{8,16},{12,20},{16,8},{20,12},{24,0},{28,4},{1,25},{... | collective-permute-start | bytes 589832 | tf_op jit(solution)/shard_map/ppermute | solution.py:192
  20.8 0.7 %gather_fusion = s32[16]{0:T(128)S(1)} fusion(s32[4]{0:T(128)S(1)} %iota_xor_fusion.1, s32[1024]{0:T(1024)S(1)} %pad_clamp_fusion.1), kind=kCustom, calls=%fused_computation | custom fusion | bytes 192 | tf_op jit(solution)/shard_map/gather | solution.py:231
  21.5 0.7 %gather_fusion.1 = s32[32]{0:T(128)S(1)} fusion(s32[8]{0:T(128)S(1)} %iota_xor_fusion, s32[1024]{0:T(1024)S(1)} %pad_clamp_fusion), kind=kCustom, calls=%fused_computation.1 | custom fusion | bytes 384 | tf_op jit(solution)/shard_map/gather | solution.py:233
  22.2 0.7 %fusion.52.refs_13_ = bf16[32,32]{1,0:T(8,128)(2,1)} fusion(s32[32]{0:T(128)S(1)} %fusion.61), kind=kLoop, calls=%fused_computation.85 | loop fusion | flops 2048 | bytes 2176 | tf_op jit(solution)/shard_map/convert_element_type | solution.py:235
  22.9 4.4 %cosine_convert_fusion = (bf16[2048,128]{1,0:T(8,128)(2,1)S(1)}, bf16[2048,128]{1,0:T(8,128)(2,1)S(1)}) fusion(s32[128]{0:T(128)S(1)} %iota_add_fusion), kind=kLoop, calls=%fused_computation.23 | loop fusion | flops 4194304 | bytes 1049088 | tf_op jit(solution)/shard_map/convert
  27.2 0.7 %fusion.59.refs_12_ = bf16[16,16]{1,0:T(8,128)(2,1)} fusion(s32[16]{0:T(128)S(1)} %fusion.60), kind=kLoop, calls=%fused_computation.89 | loop fusion | flops 512 | bytes 576 | tf_op jit(solution)/shard_map/convert_element_type | solution.py:234
  29.5 1.1 %pad_maximum_fusion.refs_14_ = bf16[4096,128]{1,0:T(8,128)(2,1)} fusion(bf16[2048,128]{1,0:T(8,128)(2,1)S(1)} %get-tuple-element.11, bf16[2048,128]{1,0:T(8,128)(2,1)S(1)} %get-tuple-element.10), kind=kLoop, calls=%fused_computation.21 | loop fusion | flops 2097152 | bytes 2097152 | tf_op jit(solution)/shard_map/concatenate | solution.py:216
  30.5 0.8 %collective-permute-done.3 = bf16[6,12,4096]{2,1,0:T(8,128)(2,1)S(1)} collective-permute-done((bf16[6,12,4096]{2,1,0:T(8,128)(2,1)S(1)}, bf16[6,12,4096]{2,1,0:T(8,128)(2,1)S(1)}, u32[]{:S(2)}, u32[]{:S(2)}) %collective-permute-start.3) | collective-permute-done | bytes 589856 | tf_op jit(solution)/shard_map/ppermute | solution.py:196
  31.3 1.0 %fusion.93 = (bf16[6,4,4096]{2,1,0:T(4,128)(2,1)}, bf16[6,4,4096]{2,1,0:T(4,128)(2,1)}, bf16[6,4,4096]{2,1,0:T(4,128)(2,1)}) fusion(bf16[6,12,4096]{2,1,0:T(8,128)(2,1)S(1)} %collective-permute-done.3), kind=kLoop, calls=%fused_computation.142 | loop fusion | bytes 1179648 | tf_op jit(solution)/shard_map/slice | solution.py:199
  32.3 1.4 %collective-permute-done.5.refs_7_ = bf16[6,4,4096]{2,1,0:T(4,128)(2,1)S(1)} collective-permute-done((bf16[6,4,4096]{2,1,0:T(4,128)(2,1)S(1)}, bf16[6,4,4096]{2,1,0:T(4,128)(2,1)S(1)}, u32[]{:S(2)}, u32[]{:S(2)}) %collective-permute-start.5) | collective-permute-done | bytes 196640 | tf_op jit(solution)/shard_map/ppermute | solution.py:180
  33.7 0.6 %copy-done.7 = bf16[6,4,4096]{2,1,0:T(4,128)(2,1)} copy-done((bf16[6,4,4096]{2,1,0:T(4,128)(2,1)}, bf16[6,4,4096]{2,1,0:T(4,128)(2,1)S(1)}, u32[]{:S(2)}) %copy-start.7) | copy-done | bytes 196632
  34.5 15.5 %shard_map.37 = f32[512,128]{1,0:T(8,128)} custom-call(bf16[6,4,4096]{2,1,0:T(4,128)(2,1)} %get-tuple-element.7.refs_0_, bf16[6,4,4096]{2,1,0:T(4,128)(2,1)} %get-tuple-element.6.refs_1_, bf16[6,4,4096]{2,1,0:T(4,128)(2,1)} %get-tuple-element.5.refs_2_, bf16[6,4,4096]{2,1,0:T(4,128)(2,1)} %copy-done.1, bf16[6,4,4096]{2,1,0:T(4,128)(2,1)} %copy-done.1, ...), custom_call_target="tpu_custom_call" | custom-call | flops 587202560 | bytes 3670016 | tf_op jit(solution)/shard_map/pallas_call | solution.py:152
  50.0 1.0 %broadcast_multiply_fusion = f32[512,128]{1,0:T(8,128)S(1)} fusion(f32[512,128]{1,0:T(8,128)} %shard_map.37), kind=kLoop, calls=%fused_computation.44 | loop fusion | flops 65536 | bytes 524288 | tf_op jit(solution)/shard_map/mul | solution.py:239
  51.0 0.8 %fusion.21 = f32[16,1,32,128]{3,2,1,0:T(8,128)} fusion(f32[32,16,128]{2,1,0:T(8,128)S(1)} %bitcast.73, pred[16,128]{1,0:T(8,128)(4,1)S(1)} %broadcast_compare_fusion), kind=kLoop, calls=%fused_computation.42 | loop fusion | flops 65536 | bytes 526336 | tf_op jit(solution)/shard_map/broadcast_in_dim | solution.py:243
  (57 shorter events, 5.3 us)
Async XLA Ops:
  0.0 2.7 %copy-start = (f32[32]{0:T(128)S(1)}, f32[32]{0:T(128)}, u32[]{:S(2)}) copy-start(f32[32]{0:T(128)} %param.4) | copy-start | bytes 388
  11.8 17.1 %copy-start.1 = (bf16[6,4,4096]{2,1,0:T(4,128)(2,1)}, bf16[6,4,4096]{2,1,0:T(4,128)(2,1)S(1)}, u32[]{:S(2)}) copy-start(bf16[6,4,4096]{2,1,0:T(4,128)(2,1)S(1)} %maximum_bitcast_fusion.refs_3_.refs_4_) | copy-start | bytes 589828
  11.8 20.5 %collective-permute-start.7 = (bf16[6,4,4096]{2,1,0:T(4,128)(2,1)S(1)}, bf16[6,4,4096]{2,1,0:T(4,128)(2,1)S(1)}, u32[]{:S(2)}, u32[]{:S(2)}) collective-permute-start(bf16[6,4,4096]{2,1,0:T(4,128)(2,1)S(1)} %maximum_bitcast_fusion.refs_3_.refs_4_), channel_id=1, source_target_pairs={{0,2},{1,3},{2,0},{3,1},{4,6},{5,7},{6,4},{7,5},{8,10},{9,11},{10,... | collective-permute-start | bytes 589832 | tf_op jit(solution)/shard_map/ppermute | solution.py:180
  15.9 16.4 %collective-permute-start.6 = (bf16[6,4,4096]{2,1,0:T(4,128)(2,1)S(1)}, bf16[6,4,4096]{2,1,0:T(4,128)(2,1)S(1)}, u32[]{:S(2)}, u32[]{:S(2)}) collective-permute-start(bf16[6,4,4096]{2,1,0:T(4,128)(2,1)S(1)} %maximum_bitcast_fusion.refs_3_.refs_4_), channel_id=1, source_target_pairs={{0,3},{1,2},{2,1},{3,0},{4,7},{5,6},{6,5},{7,4},{8,11},{9,10},{10,... | collective-permute-start | bytes 589832 | tf_op jit(solution)/shard_map/ppermute | solution.py:180
  17.3 10.7 %collective-permute-start.2 = (bf16[6,4,4096]{2,1,0:T(4,128)(2,1)S(1)}, bf16[6,4,4096]{2,1,0:T(4,128)(2,1)S(1)}, u32[]{:S(2)}, u32[]{:S(2)}) collective-permute-start(bf16[6,4,4096]{2,1,0:T(4,128)(2,1)S(1)} %maximum_bitcast_fusion.refs_3_.refs_4_), channel_id=1, source_target_pairs={{0,24},{4,28},{8,16},{12,20},{16,8},{20,12},{24,0},{28,4},{1,25},{... | collective-permute-start | bytes 589832 | tf_op jit(solution)/shard_map/ppermute | solution.py:192
  19.7 8.8 %collective-permute-start.1 = (bf16[6,4,4096]{2,1,0:T(4,128)(2,1)S(1)}, bf16[6,4,4096]{2,1,0:T(4,128)(2,1)S(1)}, u32[]{:S(2)}, u32[]{:S(2)}) collective-permute-start(bf16[6,4,4096]{2,1,0:T(4,128)(2,1)S(1)} %maximum_bitcast_fusion.refs_3_.refs_4_), channel_id=1, source_target_pairs={{0,16},{4,20},{8,24},{12,28},{16,0},{20,4},{24,8},{28,12},{1,17},{... | collective-permute-start | bytes 589832 | tf_op jit(solution)/shard_map/ppermute | solution.py:192
  20.2 8.4 %collective-permute-start = (bf16[6,4,4096]{2,1,0:T(4,128)(2,1)S(1)}, bf16[6,4,4096]{2,1,0:T(4,128)(2,1)S(1)}, u32[]{:S(2)}, u32[]{:S(2)}) collective-permute-start(bf16[6,4,4096]{2,1,0:T(4,128)(2,1)S(1)} %maximum_bitcast_fusion.refs_3_.refs_4_), channel_id=1, source_target_pairs={{0,8},{4,12},{8,0},{12,4},{16,24},{20,28},{24,16},{28,20},{1,9},{5... | collective-permute-start | bytes 589832 | tf_op jit(solution)/shard_map/ppermute | solution.py:192
  22.9 6.5 %copy-start.9 = (s32[16]{0:T(128)S(1)}, s32[16]{0:T(128)}, u32[]{:S(2)}) copy-start(s32[16]{0:T(128)} %param.5) | copy-start | bytes 196
  27.9 2.6 %copy-start.2 = (bf16[6,4,4096]{2,1,0:T(4,128)(2,1)}, bf16[6,4,4096]{2,1,0:T(4,128)(2,1)S(1)}, u32[]{:S(2)}) copy-start(bf16[6,4,4096]{2,1,0:T(4,128)(2,1)S(1)} %collective-permute-done.2.refs_9_) | copy-start | bytes 589828
  27.9 5.8 %collective-permute-start.5 = (bf16[6,4,4096]{2,1,0:T(4,128)(2,1)S(1)}, bf16[6,4,4096]{2,1,0:T(4,128)(2,1)S(1)}, u32[]{:S(2)}, u32[]{:S(2)}) collective-permute-start(bf16[6,4,4096]{2,1,0:T(4,128)(2,1)S(1)} %maximum_bitcast_fusion.refs_3_.refs_4_), channel_id=1, source_target_pairs={{0,1},{1,0},{2,3},{3,2},{4,5},{5,4},{6,7},{7,6},{8,9},{9,8},{10,11... | collective-permute-start | bytes 589832 | tf_op jit(solution)/shard_map/ppermute | solution.py:180
  28.5 2.1 %copy-start.3 = (bf16[6,4,4096]{2,1,0:T(4,128)(2,1)}, bf16[6,4,4096]{2,1,0:T(4,128)(2,1)S(1)}, u32[]{:S(2)}) copy-start(bf16[6,4,4096]{2,1,0:T(4,128)(2,1)S(1)} %collective-permute-done.1.refs_8_) | copy-start | bytes 589828
  28.5 5.3 %collective-permute-start.4 = (bf16[6,4,4096]{2,1,0:T(4,128)(2,1)S(1)}, bf16[6,4,4096]{2,1,0:T(4,128)(2,1)S(1)}, u32[]{:S(2)}, u32[]{:S(2)}) collective-permute-start(bf16[6,4,4096]{2,1,0:T(4,128)(2,1)S(1)} %maximum_bitcast_fusion.refs_3_.refs_4_), channel_id=1, source_target_pairs={{0,4},{4,0},{8,12},{12,8},{16,20},{20,16},{24,28},{28,24},{1,5},{5... | collective-permute-start | bytes 589832 | tf_op jit(solution)/shard_map/ppermute | solution.py:194
  28.6 2.0 %copy-start.4 = (bf16[6,4,4096]{2,1,0:T(4,128)(2,1)}, bf16[6,4,4096]{2,1,0:T(4,128)(2,1)S(1)}, u32[]{:S(2)}) copy-start(bf16[6,4,4096]{2,1,0:T(4,128)(2,1)S(1)} %collective-permute-done.refs_6_) | copy-start | bytes 589828
  28.9 2.4 %collective-permute-start.3 = (bf16[6,12,4096]{2,1,0:T(8,128)(2,1)S(1)}, bf16[6,12,4096]{2,1,0:T(8,128)(2,1)S(1)}, u32[]{:S(2)}, u32[]{:S(2)}) collective-permute-start(bf16[6,12,4096]{2,1,0:T(8,128)(2,1)S(1)} %pad_maximum_fusion.1), channel_id=1, source_target_pairs={{0,4},{4,0},{8,12},{12,8},{16,20},{20,16},{24,28},{28,24},{1,5},{5... | collective-permute-start | bytes 1769480 | tf_op jit(solution)/shard_map/ppermute | solution.py:196
  32.3 1.4 %copy-start.5 = (bf16[6,4,4096]{2,1,0:T(4,128)(2,1)}, bf16[6,4,4096]{2,1,0:T(4,128)(2,1)S(1)}, u32[]{:S(2)}) copy-start(bf16[6,4,4096]{2,1,0:T(4,128)(2,1)S(1)} %collective-permute-done.7.refs_11_) | copy-start | bytes 589828
  32.3 1.4 %copy-start.6 = (bf16[6,4,4096]{2,1,0:T(4,128)(2,1)}, bf16[6,4,4096]{2,1,0:T(4,128)(2,1)S(1)}, u32[]{:S(2)}) copy-start(bf16[6,4,4096]{2,1,0:T(4,128)(2,1)S(1)} %collective-permute-done.6.refs_10_) | copy-start | bytes 589828
  33.7 0.7 %copy-start.7 = (bf16[6,4,4096]{2,1,0:T(4,128)(2,1)}, bf16[6,4,4096]{2,1,0:T(4,128)(2,1)S(1)}, u32[]{:S(2)}) copy-start(bf16[6,4,4096]{2,1,0:T(4,128)(2,1)S(1)} %collective-permute-done.5.refs_7_) | copy-start | bytes 589828
  33.7 0.8 %copy-start.8 = (bf16[6,4,4096]{2,1,0:T(4,128)(2,1)}, bf16[6,4,4096]{2,1,0:T(4,128)(2,1)S(1)}, u32[]{:S(2)}) copy-start(bf16[6,4,4096]{2,1,0:T(4,128)(2,1)S(1)} %collective-permute-done.4.refs_5_) | copy-start | bytes 589828

commit v19 on v16

--- a/solution.py
+++ b/solution.py
@@ -31,13 +31,14 @@
     blocks = records.reshape(lead_dims + (block_count, in_block))
     tails = blocks[:, :, :-1, in_block - tap_count :]
     tails = jnp.concatenate([jnp.zeros(lead_dims + (1, tap_count), records.dtype), tails], axis=2)
-    windows = jnp.concatenate([tails, blocks], axis=3)
     tap_ids = jnp.arange(tap_count, dtype=jnp.int32)[:, None, None]
     in_ids = jnp.arange(in_block + tap_count, dtype=jnp.int32)[None, :, None]
     out_ids = jnp.arange(out_block, dtype=jnp.int32)[None, None, :]
     onehot = (in_ids == DECIM * out_ids + tap_count - tap_ids).astype(jnp.float32)
     band_matrix = jnp.einsum("k,kij->ij", fir_taps, onehot, precision=lax.Precision.HIGH)
-    summed = jnp.einsum("swbi,ij->swbj", windows, band_matrix, precision=lax.Precision.HIGH)
+    summed = jnp.einsum(
+        "swbi,ij->swbj", blocks, band_matrix[tap_count:], precision=lax.Precision.HIGH
+    ) + jnp.einsum("swbi,ij->swbj", tails, band_matrix[:tap_count], precision=lax.Precision.HIGH)
     return summed.reshape(lead_dims + (block_count * out_block,))
 
 

time: 50.3 us -> 50.3 us (level)
  no operation moved by 1% of the time
where the time goes in v19:
time: 50.3 us; the launch traced here: 50.1 us
  Pallas kernels  13.9 us (28%)
  other arithmetic  10.1 us (20%)
  starting transfers between devices  9.66 us (19%)
  matrix products  8.14 us (16%)
  local copies, waits for them, and re-layouts  5.51 us (11%)
  waiting for transfers between devices  2.59 us (5%)
    pallas_call x1, Pallas kernels, pair_block(): pl.pallas_call(functools.partial(cross_kernel, tuple(issue_order)), out_s...  13.9 us
    ppermute x3, starting transfers between devices, xor_gather(): pieces.append(lax.ppermute(block, axis_name, pairs))  5.69 us
    another operation x2, other arithmetic  4.53 us
    ppermute x3, starting transfers between devices, chip_gather(): fetched.append(lax.ppermute(block, axis_name, pairs))  3.49 us
    reshape x1, local copies, waits for them, and re-layouts, decimate(): blocks = records.reshape(lead_dims + (block_count, in_block))  1.68 us
    ppermute x3, waiting for transfers between devices, xor_gather(): pieces.append(lax.ppermute(block, axis_name, pairs))  1.39 us
    dot_general x1, matrix products, spectrum(): jnp.einsum('bwfq,gq->bwgf', real_t, sin_three, precision=lax.Precision.HIGH)  1.31 us
    dot_general x1, matrix products, spectrum(): jnp.einsum('bwfq,gq->bwgf', imag_t, sin_three, precision=lax.Precision.HIGH)  1.24 us
  transfers between devices with their start and end apart: 8, of which 4 were waited for; matrix products, arithmetic and copies ran while one was open for 19% of the time, Pallas kernels for 0%

profile of v19, /device:TPU:0, one launch (start us, length us, event | category | flops | bytes accessed | tf_op | source)
XLA Modules:
  0.0 50.1 jit_solution(1711426490493333341)
XLA Ops:
  0.2 1.7 %reshape.236 = f32[4,6,32,256]{3,2,0,1:T(8,128)S(1)} reshape(f32[4,6,8192]{2,0,1:T(4,128)} %param.3) | data formatting | bytes 1572864 | tf_op jit(solution)/shard_map/reshape | solution.py:31
  1.8 0.7 %iota_compare_fusion = pred[32,288,128]{2,1,0:T(32,128)(4,1)S(1)} fusion(s32[32,128]{1,0:T(8,128)S(1)} %iota_subtract_fusion), kind=kLoop, calls=%fused_computation.2 | loop fusion | flops 1179648 | bytes 1196032 | tf_op jit(solution)/shard_map/eq | solution.py:37
  2.5 1.1 %fusion = f32[1,288,128]{2,0,1:T(1,128)S(1)} fusion(pred[32,288,128]{2,1,0:T(32,128)(4,1)S(1)} %iota_compare_fusion, f32[32]{0:T(128)S(1)} %copy-done), kind=kOutput, calls=%fused_computation.3 | convolution fusion | flops 7077888 | bytes 1327232 | tf_op jit(solution)/shard_map/k,kij->ij/dot_general | solution.py:38
  4.7 0.6 %convolution_negate_fusion = f32[64,4,6,64]{3,0,2,1:T(8,128)S(1)} fusion(f32[4,6,64,64]{3,2,1,0:T(8,128)S(1)} %reshape_reshape.3), kind=kOutput, calls=%fused_computation.8 | convolution fusion | flops 37904384 | bytes 786432 | tf_op jit(solution)/shard_map/bwnq,fn->bwfq/dot_general | solution.py:53
  5.9 1.2 %fusion.10 = f32[32,4,6,64]{3,0,2,1:T(8,128)S(1)} fusion(f32[64,4,6,64]{3,0,2,1:T(8,128)S(1)} %fusion.23, f32[64,4,6,64]{3,0,2,1:T(8,128)S(1)} %convolution_negate_fusion, f32[64,64]{1,0:T(8,128)S(1)} %get-tuple-element.14, f32[64,64]{1,0:T(8,128)S(1)} %get-tuple-element.15), kind=kOutput, calls=%fused_computation.25 | convolution fusion | flops 19197952 | bytes 1015808 | tf_op jit(solution)/shard_map/bwfq,gq->bwgf/dot_general | solution.py:61
  7.1 1.2 %fusion.14 = f32[32,4,6,64]{3,0,2,1:T(8,128)S(1)} fusion(f32[64,4,6,64]{3,0,2,1:T(8,128)S(1)} %convolution_negate_fusion, f32[64,4,6,64]{3,0,2,1:T(8,128)S(1)} %fusion.23, f32[64,64]{1,0:T(8,128)S(1)} %get-tuple-element.14, f32[64,64]{1,0:T(8,128)S(1)} %get-tuple-element.15), kind=kOutput, calls=%fused_computation.29 | convolution fusion | flops 19197952 | bytes 1015808 | tf_op jit(solution)/shard_map/bwfq,gq->bwgf/dot_general | solution.py:58
  8.3 1.2 %fusion.3 = f32[4,6,32,64]{3,2,1,0:T(8,128)S(1)} fusion(f32[32,4,6,64]{3,0,2,1:T(8,128)S(1)} %fusion.14, f32[64,4,6,64]{3,0,2,1:T(8,128)S(1)} %fusion.23, f32[64,4,6,64]{3,0,2,1:T(8,128)S(1)} %convolution_negate_fusion, f32[64,64]{1,0:T(8,128)S(1)} %get-tuple-element.14, f32[64,64]{1,0:T(8,128)S(1)} %get-tuple-element.15), kind=kOutput, calls=%fused_computation.14 | convolution fusion | flops 19247104 | bytes 1212416 | tf_op jit(solution)/shard_map/bwfq,gq->bwgf/dot_general | solution.py:60
  9.6 1.3 %add_reduce_fusion = (f32[4,6,32]{2,1,0:T(8,128)S(1)}, f32[4,6,32,64]{3,2,1,0:T(8,128)S(1)}) fusion(f32[4,6,32,64]{3,2,1,0:T(8,128)S(1)} %fusion.3, f32[32,4,6,64]{3,0,2,1:T(8,128)S(1)} %fusion.10, f32[64,4,6,64]{3,0,2,1:T(8,128)S(1)} %convolution_negate_fusion, f32[64,64]{1,0:T(8,128)S(1)} %get-tuple-element.14, f32[64,4,6,64]{3,0,2,1:T(8,128)S(1)} %fusion.23, ...), kind=kOutput, calls=%fused_computation.35 | convolution fusion | flops 19442944 | bytes 1412096 | tf_op jit(solution)/shard_map/bwfq,gq->bwgf/dot_general | solution.py:63
  11.8 4.1 %collective-permute-start.7 = (bf16[6,4,4096]{2,1,0:T(4,128)(2,1)S(1)}, bf16[6,4,4096]{2,1,0:T(4,128)(2,1)S(1)}, u32[]{:S(2)}, u32[]{:S(2)}) collective-permute-start(bf16[6,4,4096]{2,1,0:T(4,128)(2,1)S(1)} %maximum_bitcast_fusion.refs_3_.refs_4_), channel_id=1, source_target_pairs={{0,2},{1,3},{2,0},{3,1},{4,6},{5,7},{6,4},{7,5},{8,10},{9,11},{10,... | collective-permute-start | bytes 589832 | tf_op jit(solution)/shard_map/ppermute | solution.py:169
  15.9 1.3 %collective-permute-start.6 = (bf16[6,4,4096]{2,1,0:T(4,128)(2,1)S(1)}, bf16[6,4,4096]{2,1,0:T(4,128)(2,1)S(1)}, u32[]{:S(2)}, u32[]{:S(2)}) collective-permute-start(bf16[6,4,4096]{2,1,0:T(4,128)(2,1)S(1)} %maximum_bitcast_fusion.refs_3_.refs_4_), channel_id=1, source_target_pairs={{0,3},{1,2},{2,1},{3,0},{4,7},{5,6},{6,5},{7,4},{8,11},{9,10},{10,... | collective-permute-start | bytes 589832 | tf_op jit(solution)/shard_map/ppermute | solution.py:169
  17.2 2.5 %collective-permute-start.2 = (bf16[6,4,4096]{2,1,0:T(4,128)(2,1)S(1)}, bf16[6,4,4096]{2,1,0:T(4,128)(2,1)S(1)}, u32[]{:S(2)}, u32[]{:S(2)}) collective-permute-start(bf16[6,4,4096]{2,1,0:T(4,128)(2,1)S(1)} %maximum_bitcast_fusion.refs_3_.refs_4_), channel_id=1, source_target_pairs={{0,24},{4,28},{8,16},{12,20},{16,8},{20,12},{24,0},{28,4},{1,25},{... | collective-permute-start | bytes 589832 | tf_op jit(solution)/shard_map/ppermute | solution.py:181
  20.8 0.7 %gather_fusion = s32[16]{0:T(128)S(1)} fusion(s32[4]{0:T(128)S(1)} %iota_xor_fusion.1, s32[1024]{0:T(1024)S(1)} %pad_clamp_fusion.1), kind=kCustom, calls=%fused_computation | custom fusion | bytes 192 | tf_op jit(solution)/shard_map/gather | solution.py:220
  21.5 0.7 %gather_fusion.1 = s32[32]{0:T(128)S(1)} fusion(s32[8]{0:T(128)S(1)} %iota_xor_fusion, s32[1024]{0:T(1024)S(1)} %pad_clamp_fusion), kind=kCustom, calls=%fused_computation.1 | custom fusion | bytes 384 | tf_op jit(solution)/shard_map/gather | solution.py:222
  22.2 0.7 %fusion.48.refs_13_ = bf16[32,32]{1,0:T(8,128)(2,1)} fusion(s32[32]{0:T(128)S(1)} %fusion.57), kind=kLoop, calls=%fused_computation.83 | loop fusion | flops 2048 | bytes 2176 | tf_op jit(solution)/shard_map/convert_element_type | solution.py:224
  22.8 4.4 %cosine_convert_fusion = (bf16[2048,128]{1,0:T(8,128)(2,1)S(1)}, bf16[2048,128]{1,0:T(8,128)(2,1)S(1)}) fusion(s32[128]{0:T(128)S(1)} %iota_add_fusion), kind=kLoop, calls=%fused_computation.20 | loop fusion | flops 4194304 | bytes 1049088 | tf_op jit(solution)/shard_map/convert
  27.2 0.7 %fusion.55.refs_12_ = bf16[16,16]{1,0:T(8,128)(2,1)} fusion(s32[16]{0:T(128)S(1)} %fusion.56), kind=kLoop, calls=%fused_computation.87 | loop fusion | flops 512 | bytes 576 | tf_op jit(solution)/shard_map/convert_element_type | solution.py:223
  29.4 1.1 %pad_maximum_fusion.refs_14_ = bf16[4096,128]{1,0:T(8,128)(2,1)} fusion(bf16[2048,128]{1,0:T(8,128)(2,1)S(1)} %get-tuple-element.11, bf16[2048,128]{1,0:T(8,128)(2,1)S(1)} %get-tuple-element.10), kind=kLoop, calls=%fused_computation.18 | loop fusion | flops 2097152 | bytes 2097152 | tf_op jit(solution)/shard_map/concatenate | solution.py:205
  30.5 0.8 %collective-permute-done.3 = bf16[6,12,4096]{2,1,0:T(8,128)(2,1)S(1)} collective-permute-done((bf16[6,12,4096]{2,1,0:T(8,128)(2,1)S(1)}, bf16[6,12,4096]{2,1,0:T(8,128)(2,1)S(1)}, u32[]{:S(2)}, u32[]{:S(2)}) %collective-permute-start.3) | collective-permute-done | bytes 589856 | tf_op jit(solution)/shard_map/ppermute | solution.py:185
  31.3 1.0 %fusion.88 = (bf16[6,4,4096]{2,1,0:T(4,128)(2,1)}, bf16[6,4,4096]{2,1,0:T(4,128)(2,1)}, bf16[6,4,4096]{2,1,0:T(4,128)(2,1)}) fusion(bf16[6,12,4096]{2,1,0:T(8,128)(2,1)S(1)} %collective-permute-done.3), kind=kLoop, calls=%fused_computation.139 | loop fusion | bytes 1179648 | tf_op jit(solution)/shard_map/slice | solution.py:188
  32.3 1.4 %collective-permute-done.5.refs_7_ = bf16[6,4,4096]{2,1,0:T(4,128)(2,1)S(1)} collective-permute-done((bf16[6,4,4096]{2,1,0:T(4,128)(2,1)S(1)}, bf16[6,4,4096]{2,1,0:T(4,128)(2,1)S(1)}, u32[]{:S(2)}, u32[]{:S(2)}) %collective-permute-start.5) | collective-permute-done | bytes 196640 | tf_op jit(solution)/shard_map/ppermute | solution.py:169
  33.7 0.6 %copy-done.7 = bf16[6,4,4096]{2,1,0:T(4,128)(2,1)} copy-done((bf16[6,4,4096]{2,1,0:T(4,128)(2,1)}, bf16[6,4,4096]{2,1,0:T(4,128)(2,1)S(1)}, u32[]{:S(2)}) %copy-start.7) | copy-done | bytes 196632
  34.5 13.9 %shard_map.37 = f32[512,128]{1,0:T(8,128)} custom-call(bf16[6,4,4096]{2,1,0:T(4,128)(2,1)} %get-tuple-element.7.refs_0_, bf16[6,4,4096]{2,1,0:T(4,128)(2,1)} %get-tuple-element.6.refs_1_, bf16[6,4,4096]{2,1,0:T(4,128)(2,1)} %get-tuple-element.5.refs_2_, bf16[6,4,4096]{2,1,0:T(4,128)(2,1)} %copy-done.1, bf16[6,4,4096]{2,1,0:T(4,128)(2,1)} %copy-done.1, ...), custom_call_target="tpu_custom_call" | custom-call | flops 587202560 | bytes 3670016 | tf_op jit(solution)/shard_map/pallas_call | solution.py:143
  48.3 1.0 %broadcast_multiply_fusion = f32[512,128]{1,0:T(8,128)S(1)} fusion(f32[512,128]{1,0:T(8,128)} %shard_map.37), kind=kLoop, calls=%fused_computation.41 | loop fusion | flops 65536 | bytes 524288 | tf_op jit(solution)/shard_map/mul | solution.py:228
  49.3 0.8 %fusion.17 = f32[16,1,32,128]{3,2,1,0:T(8,128)} fusion(f32[32,16,128]{2,1,0:T(8,128)S(1)} %bitcast.80, pred[16,128]{1,0:T(8,128)(4,1)S(1)} %broadcast_compare_fusion), kind=kLoop, calls=%fused_computation.38 | loop fusion | flops 65536 | bytes 526336 | tf_op jit(solution)/shard_map/broadcast_in_dim | solution.py:232
  (56 shorter events, 5.4 us)
Async XLA Ops:
  0.0 2.5 %copy-start = (f32[32]{0:T(128)S(1)}, f32[32]{0:T(128)}, u32[]{:S(2)}) copy-start(f32[32]{0:T(128)} %param.4) | copy-start | bytes 388
  11.8 17.1 %copy-start.1 = (bf16[6,4,4096]{2,1,0:T(4,128)(2,1)}, bf16[6,4,4096]{2,1,0:T(4,128)(2,1)S(1)}, u32[]{:S(2)}) copy-start(bf16[6,4,4096]{2,1,0:T(4,128)(2,1)S(1)} %maximum_bitcast_fusion.refs_3_.refs_4_) | copy-start | bytes 589828
  11.8 20.5 %collective-permute-start.7 = (bf16[6,4,4096]{2,1,0:T(4,128)(2,1)S(1)}, bf16[6,4,4096]{2,1,0:T(4,128)(2,1)S(1)}, u32[]{:S(2)}, u32[]{:S(2)}) collective-permute-start(bf16[6,4,4096]{2,1,0:T(4,128)(2,1)S(1)} %maximum_bitcast_fusion.refs_3_.refs_4_), channel_id=1, source_target_pairs={{0,2},{1,3},{2,0},{3,1},{4,6},{5,7},{6,4},{7,5},{8,10},{9,11},{10,... | collective-permute-start | bytes 589832 | tf_op jit(solution)/shard_map/ppermute | solution.py:169
  15.9 16.4 %collective-permute-start.6 = (bf16[6,4,4096]{2,1,0:T(4,128)(2,1)S(1)}, bf16[6,4,4096]{2,1,0:T(4,128)(2,1)S(1)}, u32[]{:S(2)}, u32[]{:S(2)}) collective-permute-start(bf16[6,4,4096]{2,1,0:T(4,128)(2,1)S(1)} %maximum_bitcast_fusion.refs_3_.refs_4_), channel_id=1, source_target_pairs={{0,3},{1,2},{2,1},{3,0},{4,7},{5,6},{6,5},{7,4},{8,11},{9,10},{10,... | collective-permute-start | bytes 589832 | tf_op jit(solution)/shard_map/ppermute | solution.py:169
  17.2 10.7 %collective-permute-start.2 = (bf16[6,4,4096]{2,1,0:T(4,128)(2,1)S(1)}, bf16[6,4,4096]{2,1,0:T(4,128)(2,1)S(1)}, u32[]{:S(2)}, u32[]{:S(2)}) collective-permute-start(bf16[6,4,4096]{2,1,0:T(4,128)(2,1)S(1)} %maximum_bitcast_fusion.refs_3_.refs_4_), channel_id=1, source_target_pairs={{0,24},{4,28},{8,16},{12,20},{16,8},{20,12},{24,0},{28,4},{1,25},{... | collective-permute-start | bytes 589832 | tf_op jit(solution)/shard_map/ppermute | solution.py:181
  19.7 8.8 %collective-permute-start.1 = (bf16[6,4,4096]{2,1,0:T(4,128)(2,1)S(1)}, bf16[6,4,4096]{2,1,0:T(4,128)(2,1)S(1)}, u32[]{:S(2)}, u32[]{:S(2)}) collective-permute-start(bf16[6,4,4096]{2,1,0:T(4,128)(2,1)S(1)} %maximum_bitcast_fusion.refs_3_.refs_4_), channel_id=1, source_target_pairs={{0,16},{4,20},{8,24},{12,28},{16,0},{20,4},{24,8},{28,12},{1,17},{... | collective-permute-start | bytes 589832 | tf_op jit(solution)/shard_map/ppermute | solution.py:181
  20.2 8.4 %collective-permute-start = (bf16[6,4,4096]{2,1,0:T(4,128)(2,1)S(1)}, bf16[6,4,4096]{2,1,0:T(4,128)(2,1)S(1)}, u32[]{:S(2)}, u32[]{:S(2)}) collective-permute-start(bf16[6,4,4096]{2,1,0:T(4,128)(2,1)S(1)} %maximum_bitcast_fusion.refs_3_.refs_4_), channel_id=1, source_target_pairs={{0,8},{4,12},{8,0},{12,4},{16,24},{20,28},{24,16},{28,20},{1,9},{5... | collective-permute-start | bytes 589832 | tf_op jit(solution)/shard_map/ppermute | solution.py:181
  22.8 6.5 %copy-start.9 = (s32[16]{0:T(128)S(1)}, s32[16]{0:T(128)}, u32[]{:S(2)}) copy-start(s32[16]{0:T(128)} %param.5) | copy-start | bytes 196
  27.9 2.6 %copy-start.2 = (bf16[6,4,4096]{2,1,0:T(4,128)(2,1)}, bf16[6,4,4096]{2,1,0:T(4,128)(2,1)S(1)}, u32[]{:S(2)}) copy-start(bf16[6,4,4096]{2,1,0:T(4,128)(2,1)S(1)} %collective-permute-done.2.refs_9_) | copy-start | bytes 589828
  27.9 5.8 %collective-permute-start.5 = (bf16[6,4,4096]{2,1,0:T(4,128)(2,1)S(1)}, bf16[6,4,4096]{2,1,0:T(4,128)(2,1)S(1)}, u32[]{:S(2)}, u32[]{:S(2)}) collective-permute-start(bf16[6,4,4096]{2,1,0:T(4,128)(2,1)S(1)} %maximum_bitcast_fusion.refs_3_.refs_4_), channel_id=1, source_target_pairs={{0,1},{1,0},{2,3},{3,2},{4,5},{5,4},{6,7},{7,6},{8,9},{9,8},{10,11... | collective-permute-start | bytes 589832 | tf_op jit(solution)/shard_map/ppermute | solution.py:169
  28.4 2.1 %copy-start.3 = (bf16[6,4,4096]{2,1,0:T(4,128)(2,1)}, bf16[6,4,4096]{2,1,0:T(4,128)(2,1)S(1)}, u32[]{:S(2)}) copy-start(bf16[6,4,4096]{2,1,0:T(4,128)(2,1)S(1)} %collective-permute-done.1.refs_8_) | copy-start | bytes 589828
  28.4 5.3 %collective-permute-start.4 = (bf16[6,4,4096]{2,1,0:T(4,128)(2,1)S(1)}, bf16[6,4,4096]{2,1,0:T(4,128)(2,1)S(1)}, u32[]{:S(2)}, u32[]{:S(2)}) collective-permute-start(bf16[6,4,4096]{2,1,0:T(4,128)(2,1)S(1)} %maximum_bitcast_fusion.refs_3_.refs_4_), channel_id=1, source_target_pairs={{0,4},{4,0},{8,12},{12,8},{16,20},{20,16},{24,28},{28,24},{1,5},{5... | collective-permute-start | bytes 589832 | tf_op jit(solution)/shard_map/ppermute | solution.py:183
  28.5 2.0 %copy-start.4 = (bf16[6,4,4096]{2,1,0:T(4,128)(2,1)}, bf16[6,4,4096]{2,1,0:T(4,128)(2,1)S(1)}, u32[]{:S(2)}) copy-start(bf16[6,4,4096]{2,1,0:T(4,128)(2,1)S(1)} %collective-permute-done.refs_6_) | copy-start | bytes 589828
  28.9 2.4 %collective-permute-start.3 = (bf16[6,12,4096]{2,1,0:T(8,128)(2,1)S(1)}, bf16[6,12,4096]{2,1,0:T(8,128)(2,1)S(1)}, u32[]{:S(2)}, u32[]{:S(2)}) collective-permute-start(bf16[6,12,4096]{2,1,0:T(8,128)(2,1)S(1)} %pad_maximum_fusion.1), channel_id=1, source_target_pairs={{0,4},{4,0},{8,12},{12,8},{16,20},{20,16},{24,28},{28,24},{1,5},{5... | collective-permute-start | bytes 1769480 | tf_op jit(solution)/shard_map/ppermute | solution.py:185
  32.3 1.4 %copy-start.5 = (bf16[6,4,4096]{2,1,0:T(4,128)(2,1)}, bf16[6,4,4096]{2,1,0:T(4,128)(2,1)S(1)}, u32[]{:S(2)}) copy-start(bf16[6,4,4096]{2,1,0:T(4,128)(2,1)S(1)} %collective-permute-done.7.refs_11_) | copy-start | bytes 589828
  32.3 1.4 %copy-start.6 = (bf16[6,4,4096]{2,1,0:T(4,128)(2,1)}, bf16[6,4,4096]{2,1,0:T(4,128)(2,1)S(1)}, u32[]{:S(2)}) copy-start(bf16[6,4,4096]{2,1,0:T(4,128)(2,1)S(1)} %collective-permute-done.6.refs_10_) | copy-start | bytes 589828
  33.7 0.7 %copy-start.7 = (bf16[6,4,4096]{2,1,0:T(4,128)(2,1)}, bf16[6,4,4096]{2,1,0:T(4,128)(2,1)S(1)}, u32[]{:S(2)}) copy-start(bf16[6,4,4096]{2,1,0:T(4,128)(2,1)S(1)} %collective-permute-done.5.refs_7_) | copy-start | bytes 589828
  33.7 0.8 %copy-start.8 = (bf16[6,4,4096]{2,1,0:T(4,128)(2,1)}, bf16[6,4,4096]{2,1,0:T(4,128)(2,1)S(1)}, u32[]{:S(2)}) copy-start(bf16[6,4,4096]{2,1,0:T(4,128)(2,1)S(1)} %collective-permute-done.4.refs_5_) | copy-start | bytes 589828

commit v20 on v19

--- a/solution.py
+++ b/solution.py
@@ -31,11 +31,12 @@
     blocks = records.reshape(lead_dims + (block_count, in_block))
     tails = blocks[:, :, :-1, in_block - tap_count :]
     tails = jnp.concatenate([jnp.zeros(lead_dims + (1, tap_count), records.dtype), tails], axis=2)
-    tap_ids = jnp.arange(tap_count, dtype=jnp.int32)[:, None, None]
-    in_ids = jnp.arange(in_block + tap_count, dtype=jnp.int32)[None, :, None]
-    out_ids = jnp.arange(out_block, dtype=jnp.int32)[None, None, :]
-    onehot = (in_ids == DECIM * out_ids + tap_count - tap_ids).astype(jnp.float32)
-    band_matrix = jnp.einsum("k,kij->ij", fir_taps, onehot, precision=lax.Precision.HIGH)
+    in_ids = jnp.arange(in_block + tap_count, dtype=jnp.int32)[:, None]
+    out_ids = jnp.arange(out_block, dtype=jnp.int32)[None, :]
+    tap_index = DECIM * out_ids + tap_count - in_ids
+    band_matrix = jnp.zeros(tap_index.shape, jnp.float32)
+    for tap in range(tap_count):
+        band_matrix = jnp.where(tap_index == tap, fir_taps[tap], band_matrix)
     summed = jnp.einsum(
         "swbi,ij->swbj", blocks, band_matrix[tap_count:], precision=lax.Precision.HIGH
     ) + jnp.einsum("swbi,ij->swbj", tails, band_matrix[:tap_count], precision=lax.Precision.HIGH)
@@ -211,7 +212,7 @@
     fetches = [(1, index) for index in range(len(piece_rows)) if index > 1 and index % 2 == 0]
     far = [(0, index) for index in range(2, len(left_by_window))]
     issue_order = [slot for slot in late_first + near[:2] + near[3:] + fetches[:1] + near[2:3] + fetches[1:] + far[::-1]]
-    issue_order = sorted(set(issue_order), key=issue_order.index)
+    issue_order = sorted(set(issue_order), key=issue_order.index)[::-1]
     assert len(issue_order) == len(left_by_window) + len(piece_rows)
     piece = block_size
     left_pos = jnp.arange(group_rows, dtype=jnp.int32)

time: 50.3 us -> 75.3 us (1.50)
  other arithmetic: 10.1 us -> 29.7 us
  local copies, waits for them, and re-layouts: 5.51 us -> 9.42 us
  waiting for transfers between devices: 2.59 us -> 4.77 us
  matrix products: 8.14 us -> 7.04 us
    select_n x0 -> x1, other arithmetic: none -> 20.3 us  [decimate(): band_matrix = jnp.where(tap_index == tap, fir_taps[tap], band_matrix)]
    slice x0 -> x2, local copies, waits for them, and re-layouts: none -> 3.89 us  [decimate(): band_matrix = jnp.where(tap_index == tap, fir_taps[tap], band_matrix)]
    ppermute x3, waiting for transfers between devices: 1.39 us -> 3.99 us  [xor_gather(): pieces.append(lax.ppermute(block, axis_name, pairs))]
    ppermute x3, starting transfers between devices: 5.69 us -> 4.57 us  [xor_gather(): pieces.append(lax.ppermute(block, axis_name, pairs))]
    ppermute x3, starting transfers between devices: 3.49 us -> 4.6 us  [chip_gather(): fetched.append(lax.ppermute(block, axis_name, pairs))]
    dot_general x1 -> x0, matrix products: 1.06 us -> none  [decimate(): jnp.einsum('k,kij->ij', fir_taps, onehot, precision=lax.Precision.HIGH)]
  transfers between devices with their start and end apart: 8 -> 8, of which waited for: 4 -> 3; matrix products, arithmetic and copies ran while one was open for 19% -> 13% of each run, Pallas kernels for 0% -> 0%
where the time goes in v20:
time: 75.3 us; the launch traced here: 74.8 us
  other arithmetic  29.7 us (39%)
  Pallas kernels  13.8 us (18%)
  starting transfers between devices  9.77 us (13%)
  local copies, waits for them, and re-layouts  9.42 us (13%)
  matrix products  7.04 us (9%)
  waiting for transfers between devices  4.77 us (6%)
    select_n x1, other arithmetic, decimate(): band_matrix = jnp.where(tap_index == tap, fir_taps[tap], band_matrix)  20.3 us
    pallas_call x1, Pallas kernels, pair_block(): pl.pallas_call(functools.partial(cross_kernel, tuple(issue_order)), out_s...  13.8 us
    ppermute x3, starting transfers between devices, chip_gather(): fetched.append(lax.ppermute(block, axis_name, pairs))  4.6 us
    ppermute x3, starting transfers between devices, xor_gather(): pieces.append(lax.ppermute(block, axis_name, pairs))  4.57 us
    another operation x2, other arithmetic  4.55 us
    ppermute x3, waiting for transfers between devices, xor_gather(): pieces.append(lax.ppermute(block, axis_name, pairs))  3.99 us
    slice x2, local copies, waits for them, and re-layouts, decimate(): band_matrix = jnp.where(tap_index == tap, fir_taps[tap], band_matrix)  3.89 us
    reshape x1, local copies, waits for them, and re-layouts, decimate(): blocks = records.reshape(lead_dims + (block_count, in_block))  1.68 us
  transfers between devices with their start and end apart: 8, of which 3 were waited for; matrix products, arithmetic and copies ran while one was open for 13% of the time, Pallas kernels for 0%

profile of v20, /device:TPU:0, one launch (start us, length us, event | category | flops | bytes accessed | tf_op | source)
XLA Modules:
  0.0 74.8 jit_solution(10089081228661642344)
XLA Ops:
  0.0 2.1 %fusion.118 = (f32[1]{0:T(128)}, f32[1]{0:T(128)}, f32[1]{0:T(128)}, f32[1]{0:T(128)}, f32[1]{0:T(128)}, /*index=5*/f32[1]{0:T(128)}, f32[1]{0:T(128)}, f32[1]{0...) fusion(f32[32]{0:T(128)} %param.4), kind=kLoop, calls=%fused_computation.169 | loop fusion | bytes 152 | tf_op jit(solution)/shard_map/slice | solution.py:39
  2.1 1.8 %fusion.119 = (f32[1]{0:T(128)}, f32[1]{0:T(128)}, f32[1]{0:T(128)}, f32[1]{0:T(128)}, f32[1]{0:T(128)}, /*index=5*/f32[1]{0:T(128)}, f32[1]{0:T(128)}, f32[1]{0...) fusion(f32[32]{0:T(128)} %param.4), kind=kLoop, calls=%fused_computation.170 | loop fusion | bytes 104 | tf_op jit(solution)/shard_map/slice | solution.py:39
  3.9 1.7 %reshape.214 = f32[4,6,32,256]{3,2,0,1:T(8,128)S(1)} reshape(f32[4,6,8192]{2,0,1:T(4,128)} %param.3) | data formatting | bytes 1572864 | tf_op jit(solution)/shard_map/reshape | solution.py:31
  5.6 20.3 %select_select_fusion = f32[288,128]{1,0:T(8,128)S(1)} fusion(f32[]{:T(128)} %bitcast.35, f32[]{:T(128)} %bitcast.34, f32[]{:T(128)} %bitcast.33, f32[]{:T(128)} %bitcast.32, f32[]{:T(128)} %bitcast.31, f32[]{:T(128)} %bitcast.30, f32[]{:T(128)} %bitcast.29, f32[]{:T(128)} %bitcast.28, f32[]{:T(128)} %bitcast.27, f32[]{:T(128)} %bitcast.26, f32[]{:T(128)} %bitcast.25, ...), kind=kLoop, calls=%fused_computation.37 | loop fusion | flops 2396160 | bytes 148096 | tf_op jit(solution)/shard_map/jit(_where)/select_n | solution.py:39
  28.3 1.2 %fusion.8 = f32[32,4,6,64]{3,0,2,1:T(8,128)S(1)} fusion(f32[64,4,6,64]{3,0,2,1:T(8,128)S(1)} %fusion.53, f32[64,4,6,64]{3,0,2,1:T(8,128)S(1)} %convolution_negate_fusion, f32[64,64]{1,0:T(8,128)S(1)} %get-tuple-element.46, f32[64,64]{1,0:T(8,128)S(1)} %get-tuple-element.47), kind=kOutput, calls=%fused_computation.22 | convolution fusion | flops 19197952 | bytes 1015808 | tf_op jit(solution)/shard_map/bwfq,gq->bwgf/dot_general | solution.py:62
  29.5 1.2 %fusion.12 = f32[32,4,6,64]{3,0,2,1:T(8,128)S(1)} fusion(f32[64,4,6,64]{3,0,2,1:T(8,128)S(1)} %convolution_negate_fusion, f32[64,4,6,64]{3,0,2,1:T(8,128)S(1)} %fusion.53, f32[64,64]{1,0:T(8,128)S(1)} %get-tuple-element.46, f32[64,64]{1,0:T(8,128)S(1)} %get-tuple-element.47), kind=kOutput, calls=%fused_computation.26 | convolution fusion | flops 19197952 | bytes 1015808 | tf_op jit(solution)/shard_map/bwfq,gq->bwgf/dot_general | solution.py:59
  30.7 1.2 %fusion.1 = f32[4,6,32,64]{3,2,1,0:T(8,128)S(1)} fusion(f32[32,4,6,64]{3,0,2,1:T(8,128)S(1)} %fusion.12, f32[64,4,6,64]{3,0,2,1:T(8,128)S(1)} %fusion.53, f32[64,4,6,64]{3,0,2,1:T(8,128)S(1)} %convolution_negate_fusion, f32[64,64]{1,0:T(8,128)S(1)} %get-tuple-element.46, f32[64,64]{1,0:T(8,128)S(1)} %get-tuple-element.47), kind=kOutput, calls=%fused_computation.11 | convolution fusion | flops 19247104 | bytes 1212416 | tf_op jit(solution)/shard_map/bwfq,gq->bwgf/dot_general | solution.py:61
  32.0 1.3 %add_reduce_fusion = (f32[4,6,32]{2,1,0:T(8,128)S(1)}, f32[4,6,32,64]{3,2,1,0:T(8,128)S(1)}) fusion(f32[4,6,32,64]{3,2,1,0:T(8,128)S(1)} %fusion.1, f32[32,4,6,64]{3,0,2,1:T(8,128)S(1)} %fusion.8, f32[64,4,6,64]{3,0,2,1:T(8,128)S(1)} %convolution_negate_fusion, f32[64,64]{1,0:T(8,128)S(1)} %get-tuple-element.46, f32[64,4,6,64]{3,0,2,1:T(8,128)S(1)} %fusion.53, ...), kind=kOutput, calls=%fused_computation.32 | convolution fusion | flops 19442944 | bytes 1412096 | tf_op jit(solution)/shard_map/bwfq,gq->bwgf/dot_general | solution.py:64
  34.2 4.0 %collective-permute-start.2 = (bf16[6,4,4096]{2,1,0:T(4,128)(2,1)S(1)}, bf16[6,4,4096]{2,1,0:T(4,128)(2,1)S(1)}, u32[]{:S(2)}, u32[]{:S(2)}) collective-permute-start(bf16[6,4,4096]{2,1,0:T(4,128)(2,1)S(1)} %maximum_bitcast_fusion.refs_7_.refs_8_), channel_id=1, source_target_pairs={{0,24},{4,28},{8,16},{12,20},{16,8},{20,12},{24,0},{28,4},{1,25},{... | collective-permute-start | bytes 589832 | tf_op jit(solution)/shard_map/ppermute | solution.py:182
  38.8 3.0 %collective-permute-start = (bf16[6,4,4096]{2,1,0:T(4,128)(2,1)S(1)}, bf16[6,4,4096]{2,1,0:T(4,128)(2,1)S(1)}, u32[]{:S(2)}, u32[]{:S(2)}) collective-permute-start(bf16[6,4,4096]{2,1,0:T(4,128)(2,1)S(1)} %maximum_bitcast_fusion.refs_7_.refs_8_), channel_id=1, source_target_pairs={{0,2},{1,3},{2,0},{3,1},{4,6},{5,7},{6,4},{7,5},{8,10},{9,11},{10,... | collective-permute-start | bytes 589832 | tf_op jit(solution)/shard_map/ppermute | solution.py:170
  41.7 1.3 %collective-permute-start.1 = (bf16[6,4,4096]{2,1,0:T(4,128)(2,1)S(1)}, bf16[6,4,4096]{2,1,0:T(4,128)(2,1)S(1)}, u32[]{:S(2)}, u32[]{:S(2)}) collective-permute-start(bf16[6,4,4096]{2,1,0:T(4,128)(2,1)S(1)} %maximum_bitcast_fusion.refs_7_.refs_8_), channel_id=1, source_target_pairs={{0,3},{1,2},{2,1},{3,0},{4,7},{5,6},{6,5},{7,4},{8,11},{9,10},{10,... | collective-permute-start | bytes 589832 | tf_op jit(solution)/shard_map/ppermute | solution.py:170
  43.1 4.4 %cosine_convert_fusion = (bf16[2048,128]{1,0:T(8,128)(2,1)S(1)}, bf16[2048,128]{1,0:T(8,128)(2,1)S(1)}) fusion(s32[128]{0:T(128)S(1)} %iota_add_fusion), kind=kLoop, calls=%fused_computation.17 | loop fusion | flops 4194304 | bytes 1049088 | tf_op jit(solution)/shard_map/convert
  47.5 0.7 gather_fusion.1
  48.3 0.7 fusion.78.refs_13_
  49.6 0.7 fusion.85.refs_12_
  51.6 1.1 %pad_maximum_fusion.refs_14_ = bf16[4096,128]{1,0:T(8,128)(2,1)} fusion(bf16[2048,128]{1,0:T(8,128)(2,1)S(1)} %get-tuple-element.11, bf16[2048,128]{1,0:T(8,128)(2,1)S(1)} %get-tuple-element.10), kind=kLoop, calls=%fused_computation.15 | loop fusion | flops 2097152 | bytes 2097152 | tf_op jit(solution)/shard_map/concatenate | solution.py:206
  52.7 0.8 %collective-permute-done.7 = bf16[6,12,4096]{2,1,0:T(8,128)(2,1)S(1)} collective-permute-done((bf16[6,12,4096]{2,1,0:T(8,128)(2,1)S(1)}, bf16[6,12,4096]{2,1,0:T(8,128)(2,1)S(1)}, u32[]{:S(2)}, u32[]{:S(2)}) %collective-permute-start.7) | collective-permute-done | bytes 589856 | tf_op jit(solution)/shard_map/ppermute | solution.py:186
  53.4 1.0 %fusion.117 = (bf16[6,4,4096]{2,1,0:T(4,128)(2,1)}, bf16[6,4,4096]{2,1,0:T(4,128)(2,1)}, bf16[6,4,4096]{2,1,0:T(4,128)(2,1)}) fusion(bf16[6,12,4096]{2,1,0:T(8,128)(2,1)S(1)} %collective-permute-done.7), kind=kLoop, calls=%fused_computation.168 | loop fusion | bytes 1179648 | tf_op jit(solution)/shard_map/slice | solution.py:189
  54.5 1.0 %collective-permute-done.refs_0_ = bf16[6,4,4096]{2,1,0:T(4,128)(2,1)S(1)} collective-permute-done((bf16[6,4,4096]{2,1,0:T(4,128)(2,1)S(1)}, bf16[6,4,4096]{2,1,0:T(4,128)(2,1)S(1)}, u32[]{:S(2)}, u32[]{:S(2)}) %collective-permute-start) | collective-permute-done | bytes 196640 | tf_op jit(solution)/shard_map/ppermute | solution.py:170
  55.5 3.0 %collective-permute-done.4.refs_4_ = bf16[6,4,4096]{2,1,0:T(4,128)(2,1)S(1)} collective-permute-done((bf16[6,4,4096]{2,1,0:T(4,128)(2,1)S(1)}, bf16[6,4,4096]{2,1,0:T(4,128)(2,1)S(1)}, u32[]{:S(2)}, u32[]{:S(2)}) %collective-permute-start.4) | collective-permute-done | bytes 196640 | tf_op jit(solution)/shard_map/ppermute | solution.py:170
  58.5 0.7 copy-done.6
  59.2 13.8 %shard_map.37 = f32[512,128]{1,0:T(8,128)} custom-call(bf16[6,4,4096]{2,1,0:T(4,128)(2,1)} %copy-done.4, bf16[6,4,4096]{2,1,0:T(4,128)(2,1)} %copy-done.5, bf16[6,4,4096]{2,1,0:T(4,128)(2,1)} %copy-done.1, bf16[6,4,4096]{2,1,0:T(4,128)(2,1)} %copy-done.2, bf16[6,4,4096]{2,1,0:T(4,128)(2,1)} %copy-done.6, bf16[6,4,4096]{2,1,0:T(4,128)(2,1)} %copy-done.3, ...), custom_call_target="tpu_custom_call" | custom-call | flops 587202560 | bytes 3670016 | tf_op jit(solution)/shard_map/pallas_call | solution.py:144
  73.0 1.0 %broadcast_multiply_fusion = f32[512,128]{1,0:T(8,128)S(1)} fusion(f32[512,128]{1,0:T(8,128)} %shard_map.37), kind=kLoop, calls=%fused_computation.72 | loop fusion | flops 65536 | bytes 524288 | tf_op jit(solution)/shard_map/mul | solution.py:229
  74.0 0.8 %fusion.15 = f32[16,1,32,128]{3,2,1,0:T(8,128)} fusion(f32[32,16,128]{2,1,0:T(8,128)S(1)} %bitcast.107, pred[16,128]{1,0:T(8,128)(4,1)S(1)} %broadcast_compare_fusion), kind=kLoop, calls=%fused_computation.35 | loop fusion | flops 65536 | bytes 526336 | tf_op jit(solution)/shard_map/broadcast_in_dim | solution.py:233
  (54 shorter events, 5.9 us)
Async XLA Ops:
  34.1 16.4 %copy-start = (bf16[6,4,4096]{2,1,0:T(4,128)(2,1)}, bf16[6,4,4096]{2,1,0:T(4,128)(2,1)S(1)}, u32[]{:S(2)}) copy-start(bf16[6,4,4096]{2,1,0:T(4,128)(2,1)S(1)} %maximum_bitcast_fusion.refs_7_.refs_8_) | copy-start | bytes 589828
  34.2 16.1 %collective-permute-start.2 = (bf16[6,4,4096]{2,1,0:T(4,128)(2,1)S(1)}, bf16[6,4,4096]{2,1,0:T(4,128)(2,1)S(1)}, u32[]{:S(2)}, u32[]{:S(2)}) collective-permute-start(bf16[6,4,4096]{2,1,0:T(4,128)(2,1)S(1)} %maximum_bitcast_fusion.refs_7_.refs_8_), channel_id=1, source_target_pairs={{0,24},{4,28},{8,16},{12,20},{16,8},{20,12},{24,0},{28,4},{1,25},{... | collective-permute-start | bytes 589832 | tf_op jit(solution)/shard_map/ppermute | solution.py:182
  38.1 12.4 %collective-permute-start.3 = (bf16[6,4,4096]{2,1,0:T(4,128)(2,1)S(1)}, bf16[6,4,4096]{2,1,0:T(4,128)(2,1)S(1)}, u32[]{:S(2)}, u32[]{:S(2)}) collective-permute-start(bf16[6,4,4096]{2,1,0:T(4,128)(2,1)S(1)} %maximum_bitcast_fusion.refs_7_.refs_8_), channel_id=1, source_target_pairs={{0,16},{4,20},{8,24},{12,28},{16,0},{20,4},{24,8},{28,12},{1,17},{... | collective-permute-start | bytes 589832 | tf_op jit(solution)/shard_map/ppermute | solution.py:182
  38.6 12.0 %collective-permute-start.5 = (bf16[6,4,4096]{2,1,0:T(4,128)(2,1)S(1)}, bf16[6,4,4096]{2,1,0:T(4,128)(2,1)S(1)}, u32[]{:S(2)}, u32[]{:S(2)}) collective-permute-start(bf16[6,4,4096]{2,1,0:T(4,128)(2,1)S(1)} %maximum_bitcast_fusion.refs_7_.refs_8_), channel_id=1, source_target_pairs={{0,8},{4,12},{8,0},{12,4},{16,24},{20,28},{24,16},{28,20},{1,9},{5... | collective-permute-start | bytes 589832 | tf_op jit(solution)/shard_map/ppermute | solution.py:182
  38.8 16.7 %collective-permute-start = (bf16[6,4,4096]{2,1,0:T(4,128)(2,1)S(1)}, bf16[6,4,4096]{2,1,0:T(4,128)(2,1)S(1)}, u32[]{:S(2)}, u32[]{:S(2)}) collective-permute-start(bf16[6,4,4096]{2,1,0:T(4,128)(2,1)S(1)} %maximum_bitcast_fusion.refs_7_.refs_8_), channel_id=1, source_target_pairs={{0,2},{1,3},{2,0},{3,1},{4,6},{5,7},{6,4},{7,5},{8,10},{9,11},{10,... | collective-permute-start | bytes 589832 | tf_op jit(solution)/shard_map/ppermute | solution.py:170
  41.7 13.7 %collective-permute-start.1 = (bf16[6,4,4096]{2,1,0:T(4,128)(2,1)S(1)}, bf16[6,4,4096]{2,1,0:T(4,128)(2,1)S(1)}, u32[]{:S(2)}, u32[]{:S(2)}) collective-permute-start(bf16[6,4,4096]{2,1,0:T(4,128)(2,1)S(1)} %maximum_bitcast_fusion.refs_7_.refs_8_), channel_id=1, source_target_pairs={{0,3},{1,2},{2,1},{3,0},{4,7},{5,6},{6,5},{7,4},{8,11},{9,10},{10,... | collective-permute-start | bytes 589832 | tf_op jit(solution)/shard_map/ppermute | solution.py:170
  48.2 3.3 %copy-start.8 = (s32[16]{0:T(128)S(1)}, s32[16]{0:T(128)}, u32[]{:S(2)}) copy-start(s32[16]{0:T(128)} %param.5) | copy-start | bytes 196
  50.3 2.4 %copy-start.1 = (bf16[6,4,4096]{2,1,0:T(4,128)(2,1)}, bf16[6,4,4096]{2,1,0:T(4,128)(2,1)S(1)}, u32[]{:S(2)}) copy-start(bf16[6,4,4096]{2,1,0:T(4,128)(2,1)S(1)} %collective-permute-done.2.refs_2_) | copy-start | bytes 589828
  50.3 8.2 %collective-permute-start.4 = (bf16[6,4,4096]{2,1,0:T(4,128)(2,1)S(1)}, bf16[6,4,4096]{2,1,0:T(4,128)(2,1)S(1)}, u32[]{:S(2)}, u32[]{:S(2)}) collective-permute-start(bf16[6,4,4096]{2,1,0:T(4,128)(2,1)S(1)} %maximum_bitcast_fusion.refs_7_.refs_8_), channel_id=1, source_target_pairs={{0,1},{1,0},{2,3},{3,2},{4,5},{5,4},{6,7},{7,6},{8,9},{9,8},{10,11... | collective-permute-start | bytes 589832 | tf_op jit(solution)/shard_map/ppermute | solution.py:170
  50.5 2.1 %copy-start.2 = (bf16[6,4,4096]{2,1,0:T(4,128)(2,1)}, bf16[6,4,4096]{2,1,0:T(4,128)(2,1)S(1)}, u32[]{:S(2)}) copy-start(bf16[6,4,4096]{2,1,0:T(4,128)(2,1)S(1)} %collective-permute-done.3.refs_3_) | copy-start | bytes 589828
  50.5 7.9 %collective-permute-start.6 = (bf16[6,4,4096]{2,1,0:T(4,128)(2,1)S(1)}, bf16[6,4,4096]{2,1,0:T(4,128)(2,1)S(1)}, u32[]{:S(2)}, u32[]{:S(2)}) collective-permute-start(bf16[6,4,4096]{2,1,0:T(4,128)(2,1)S(1)} %maximum_bitcast_fusion.refs_7_.refs_8_), channel_id=1, source_target_pairs={{0,4},{4,0},{8,12},{12,8},{16,20},{20,16},{24,28},{28,24},{1,5},{5... | collective-permute-start | bytes 589832 | tf_op jit(solution)/shard_map/ppermute | solution.py:184
  50.6 2.0 %copy-start.3 = (bf16[6,4,4096]{2,1,0:T(4,128)(2,1)}, bf16[6,4,4096]{2,1,0:T(4,128)(2,1)S(1)}, u32[]{:S(2)}) copy-start(bf16[6,4,4096]{2,1,0:T(4,128)(2,1)S(1)} %collective-permute-done.5.refs_5_) | copy-start | bytes 589828
  51.0 2.5 %collective-permute-start.7 = (bf16[6,12,4096]{2,1,0:T(8,128)(2,1)S(1)}, bf16[6,12,4096]{2,1,0:T(8,128)(2,1)S(1)}, u32[]{:S(2)}, u32[]{:S(2)}) collective-permute-start(bf16[6,12,4096]{2,1,0:T(8,128)(2,1)S(1)} %pad_maximum_fusion.1), channel_id=1, source_target_pairs={{0,4},{4,0},{8,12},{12,8},{16,20},{20,16},{24,28},{28,24},{1,5},{5... | collective-permute-start | bytes 1769480 | tf_op jit(solution)/shard_map/ppermute | solution.py:186
  55.5 3.0 %copy-start.4 = (bf16[6,4,4096]{2,1,0:T(4,128)(2,1)}, bf16[6,4,4096]{2,1,0:T(4,128)(2,1)S(1)}, u32[]{:S(2)}) copy-start(bf16[6,4,4096]{2,1,0:T(4,128)(2,1)S(1)} %collective-permute-done.refs_0_) | copy-start | bytes 589828
  55.5 3.0 %copy-start.5 = (bf16[6,4,4096]{2,1,0:T(4,128)(2,1)}, bf16[6,4,4096]{2,1,0:T(4,128)(2,1)S(1)}, u32[]{:S(2)}) copy-start(bf16[6,4,4096]{2,1,0:T(4,128)(2,1)S(1)} %collective-permute-done.1.refs_1_) | copy-start | bytes 589828
  58.4 0.7 copy-start.6
  58.5 0.7 copy-start.7

commit v21 on v19

--- a/solution.py
+++ b/solution.py
@@ -135,7 +135,7 @@
     rows_left = left_count * piece
     visit_rows = visit_count * piece
     lag_count = lag_table.shape[1]
-    group = max(1, min(visit_count, 256 // (piece * rows_left)))
+    group = max(1, min(visit_count, 512 // (piece * rows_left)))
     while visit_count % group:
         group -= 1
     flops = visit_rows * rows_left * width * (4 * window_count + 2 * lag_count)

time: 50.3 us -> 50.1 us (level)
  no operation moved by 1% of the time
where the time goes in v21:
time: 50.1 us; the launch traced here: 49.9 us
  Pallas kernels  13.7 us (27%)
  other arithmetic  10.1 us (20%)
  starting transfers between devices  9.66 us (19%)
  matrix products  8.14 us (16%)
  local copies, waits for them, and re-layouts  5.51 us (11%)
  waiting for transfers between devices  2.59 us (5%)
    pallas_call x1, Pallas kernels, pair_block(): pl.pallas_call(functools.partial(cross_kernel, tuple(issue_order)), out_s...  13.7 us
    ppermute x3, starting transfers between devices, xor_gather(): pieces.append(lax.ppermute(block, axis_name, pairs))  5.69 us
    another operation x2, other arithmetic  4.53 us
    ppermute x3, starting transfers between devices, chip_gather(): fetched.append(lax.ppermute(block, axis_name, pairs))  3.49 us
    reshape x1, local copies, waits for them, and re-layouts, decimate(): blocks = records.reshape(lead_dims + (block_count, in_block))  1.68 us
    ppermute x3, waiting for transfers between devices, xor_gather(): pieces.append(lax.ppermute(block, axis_name, pairs))  1.39 us
    dot_general x1, matrix products, spectrum(): jnp.einsum('bwfq,gq->bwgf', real_t, sin_three, precision=lax.Precision.HIGH)  1.31 us
    dot_general x1, matrix products, spectrum(): jnp.einsum('bwfq,gq->bwgf', imag_t, sin_three, precision=lax.Precision.HIGH)  1.24 us
  transfers between devices with their start and end apart: 8, of which 4 were waited for; matrix products, arithmetic and copies ran while one was open for 19% of the time, Pallas kernels for 0%

profile of v21, /device:TPU:0, one launch (start us, length us, event | category | flops | bytes accessed | tf_op | source)
XLA Modules:
  0.0 49.9 jit_solution(8064275994079561197)
XLA Ops:
  0.2 1.7 %reshape.236 = f32[4,6,32,256]{3,2,0,1:T(8,128)S(1)} reshape(f32[4,6,8192]{2,0,1:T(4,128)} %param.3) | data formatting | bytes 1572864 | tf_op jit(solution)/shard_map/reshape | solution.py:31
  1.8 0.7 %iota_compare_fusion = pred[32,288,128]{2,1,0:T(32,128)(4,1)S(1)} fusion(s32[32,128]{1,0:T(8,128)S(1)} %iota_subtract_fusion), kind=kLoop, calls=%fused_computation.2 | loop fusion | flops 1179648 | bytes 1196032 | tf_op jit(solution)/shard_map/eq | solution.py:37
  2.5 1.1 %fusion = f32[1,288,128]{2,0,1:T(1,128)S(1)} fusion(pred[32,288,128]{2,1,0:T(32,128)(4,1)S(1)} %iota_compare_fusion, f32[32]{0:T(128)S(1)} %copy-done), kind=kOutput, calls=%fused_computation.3 | convolution fusion | flops 7077888 | bytes 1327232 | tf_op jit(solution)/shard_map/k,kij->ij/dot_general | solution.py:38
  4.7 0.6 %convolution_negate_fusion = f32[64,4,6,64]{3,0,2,1:T(8,128)S(1)} fusion(f32[4,6,64,64]{3,2,1,0:T(8,128)S(1)} %reshape_reshape.3), kind=kOutput, calls=%fused_computation.8 | convolution fusion | flops 37904384 | bytes 786432 | tf_op jit(solution)/shard_map/bwnq,fn->bwfq/dot_general | solution.py:53
  5.9 1.2 %fusion.10 = f32[32,4,6,64]{3,0,2,1:T(8,128)S(1)} fusion(f32[64,4,6,64]{3,0,2,1:T(8,128)S(1)} %fusion.23, f32[64,4,6,64]{3,0,2,1:T(8,128)S(1)} %convolution_negate_fusion, f32[64,64]{1,0:T(8,128)S(1)} %get-tuple-element.14, f32[64,64]{1,0:T(8,128)S(1)} %get-tuple-element.15), kind=kOutput, calls=%fused_computation.25 | convolution fusion | flops 19197952 | bytes 1015808 | tf_op jit(solution)/shard_map/bwfq,gq->bwgf/dot_general | solution.py:61
  7.1 1.2 %fusion.14 = f32[32,4,6,64]{3,0,2,1:T(8,128)S(1)} fusion(f32[64,4,6,64]{3,0,2,1:T(8,128)S(1)} %convolution_negate_fusion, f32[64,4,6,64]{3,0,2,1:T(8,128)S(1)} %fusion.23, f32[64,64]{1,0:T(8,128)S(1)} %get-tuple-element.14, f32[64,64]{1,0:T(8,128)S(1)} %get-tuple-element.15), kind=kOutput, calls=%fused_computation.29 | convolution fusion | flops 19197952 | bytes 1015808 | tf_op jit(solution)/shard_map/bwfq,gq->bwgf/dot_general | solution.py:58
  8.3 1.2 %fusion.3 = f32[4,6,32,64]{3,2,1,0:T(8,128)S(1)} fusion(f32[32,4,6,64]{3,0,2,1:T(8,128)S(1)} %fusion.14, f32[64,4,6,64]{3,0,2,1:T(8,128)S(1)} %fusion.23, f32[64,4,6,64]{3,0,2,1:T(8,128)S(1)} %convolution_negate_fusion, f32[64,64]{1,0:T(8,128)S(1)} %get-tuple-element.14, f32[64,64]{1,0:T(8,128)S(1)} %get-tuple-element.15), kind=kOutput, calls=%fused_computation.14 | convolution fusion | flops 19247104 | bytes 1212416 | tf_op jit(solution)/shard_map/bwfq,gq->bwgf/dot_general | solution.py:60
  9.6 1.3 %add_reduce_fusion = (f32[4,6,32]{2,1,0:T(8,128)S(1)}, f32[4,6,32,64]{3,2,1,0:T(8,128)S(1)}) fusion(f32[4,6,32,64]{3,2,1,0:T(8,128)S(1)} %fusion.3, f32[32,4,6,64]{3,0,2,1:T(8,128)S(1)} %fusion.10, f32[64,4,6,64]{3,0,2,1:T(8,128)S(1)} %convolution_negate_fusion, f32[64,64]{1,0:T(8,128)S(1)} %get-tuple-element.14, f32[64,4,6,64]{3,0,2,1:T(8,128)S(1)} %fusion.23, ...), kind=kOutput, calls=%fused_computation.35 | convolution fusion | flops 19442944 | bytes 1412096 | tf_op jit(solution)/shard_map/bwfq,gq->bwgf/dot_general | solution.py:63
  11.8 4.1 %collective-permute-start.7 = (bf16[6,4,4096]{2,1,0:T(4,128)(2,1)S(1)}, bf16[6,4,4096]{2,1,0:T(4,128)(2,1)S(1)}, u32[]{:S(2)}, u32[]{:S(2)}) collective-permute-start(bf16[6,4,4096]{2,1,0:T(4,128)(2,1)S(1)} %maximum_bitcast_fusion.refs_3_.refs_4_), channel_id=1, source_target_pairs={{0,2},{1,3},{2,0},{3,1},{4,6},{5,7},{6,4},{7,5},{8,10},{9,11},{10,... | collective-permute-start | bytes 589832 | tf_op jit(solution)/shard_map/ppermute | solution.py:169
  15.9 1.3 %collective-permute-start.6 = (bf16[6,4,4096]{2,1,0:T(4,128)(2,1)S(1)}, bf16[6,4,4096]{2,1,0:T(4,128)(2,1)S(1)}, u32[]{:S(2)}, u32[]{:S(2)}) collective-permute-start(bf16[6,4,4096]{2,1,0:T(4,128)(2,1)S(1)} %maximum_bitcast_fusion.refs_3_.refs_4_), channel_id=1, source_target_pairs={{0,3},{1,2},{2,1},{3,0},{4,7},{5,6},{6,5},{7,4},{8,11},{9,10},{10,... | collective-permute-start | bytes 589832 | tf_op jit(solution)/shard_map/ppermute | solution.py:169
  17.2 2.5 %collective-permute-start.2 = (bf16[6,4,4096]{2,1,0:T(4,128)(2,1)S(1)}, bf16[6,4,4096]{2,1,0:T(4,128)(2,1)S(1)}, u32[]{:S(2)}, u32[]{:S(2)}) collective-permute-start(bf16[6,4,4096]{2,1,0:T(4,128)(2,1)S(1)} %maximum_bitcast_fusion.refs_3_.refs_4_), channel_id=1, source_target_pairs={{0,24},{4,28},{8,16},{12,20},{16,8},{20,12},{24,0},{28,4},{1,25},{... | collective-permute-start | bytes 589832 | tf_op jit(solution)/shard_map/ppermute | solution.py:181
  20.8 0.7 %gather_fusion = s32[16]{0:T(128)S(1)} fusion(s32[4]{0:T(128)S(1)} %iota_xor_fusion.1, s32[1024]{0:T(1024)S(1)} %pad_clamp_fusion.1), kind=kCustom, calls=%fused_computation | custom fusion | bytes 192 | tf_op jit(solution)/shard_map/gather | solution.py:220
  21.5 0.7 %gather_fusion.1 = s32[32]{0:T(128)S(1)} fusion(s32[8]{0:T(128)S(1)} %iota_xor_fusion, s32[1024]{0:T(1024)S(1)} %pad_clamp_fusion), kind=kCustom, calls=%fused_computation.1 | custom fusion | bytes 384 | tf_op jit(solution)/shard_map/gather | solution.py:222
  22.2 0.7 %fusion.48.refs_13_ = bf16[32,32]{1,0:T(8,128)(2,1)} fusion(s32[32]{0:T(128)S(1)} %fusion.57), kind=kLoop, calls=%fused_computation.83 | loop fusion | flops 2048 | bytes 2176 | tf_op jit(solution)/shard_map/convert_element_type | solution.py:224
  22.8 4.4 %cosine_convert_fusion = (bf16[2048,128]{1,0:T(8,128)(2,1)S(1)}, bf16[2048,128]{1,0:T(8,128)(2,1)S(1)}) fusion(s32[128]{0:T(128)S(1)} %iota_add_fusion), kind=kLoop, calls=%fused_computation.20 | loop fusion | flops 4194304 | bytes 1049088 | tf_op jit(solution)/shard_map/convert
  27.2 0.7 %fusion.55.refs_12_ = bf16[16,16]{1,0:T(8,128)(2,1)} fusion(s32[16]{0:T(128)S(1)} %fusion.56), kind=kLoop, calls=%fused_computation.87 | loop fusion | flops 512 | bytes 576 | tf_op jit(solution)/shard_map/convert_element_type | solution.py:223
  29.4 1.1 %pad_maximum_fusion.refs_14_ = bf16[4096,128]{1,0:T(8,128)(2,1)} fusion(bf16[2048,128]{1,0:T(8,128)(2,1)S(1)} %get-tuple-element.11, bf16[2048,128]{1,0:T(8,128)(2,1)S(1)} %get-tuple-element.10), kind=kLoop, calls=%fused_computation.18 | loop fusion | flops 2097152 | bytes 2097152 | tf_op jit(solution)/shard_map/concatenate | solution.py:205
  30.5 0.8 %collective-permute-done.3 = bf16[6,12,4096]{2,1,0:T(8,128)(2,1)S(1)} collective-permute-done((bf16[6,12,4096]{2,1,0:T(8,128)(2,1)S(1)}, bf16[6,12,4096]{2,1,0:T(8,128)(2,1)S(1)}, u32[]{:S(2)}, u32[]{:S(2)}) %collective-permute-start.3) | collective-permute-done | bytes 589856 | tf_op jit(solution)/shard_map/ppermute | solution.py:185
  31.3 1.0 %fusion.88 = (bf16[6,4,4096]{2,1,0:T(4,128)(2,1)}, bf16[6,4,4096]{2,1,0:T(4,128)(2,1)}, bf16[6,4,4096]{2,1,0:T(4,128)(2,1)}) fusion(bf16[6,12,4096]{2,1,0:T(8,128)(2,1)S(1)} %collective-permute-done.3), kind=kLoop, calls=%fused_computation.139 | loop fusion | bytes 1179648 | tf_op jit(solution)/shard_map/slice | solution.py:188
  32.3 1.4 %collective-permute-done.5.refs_7_ = bf16[6,4,4096]{2,1,0:T(4,128)(2,1)S(1)} collective-permute-done((bf16[6,4,4096]{2,1,0:T(4,128)(2,1)S(1)}, bf16[6,4,4096]{2,1,0:T(4,128)(2,1)S(1)}, u32[]{:S(2)}, u32[]{:S(2)}) %collective-permute-start.5) | collective-permute-done | bytes 196640 | tf_op jit(solution)/shard_map/ppermute | solution.py:169
  33.7 0.6 %copy-done.7 = bf16[6,4,4096]{2,1,0:T(4,128)(2,1)} copy-done((bf16[6,4,4096]{2,1,0:T(4,128)(2,1)}, bf16[6,4,4096]{2,1,0:T(4,128)(2,1)S(1)}, u32[]{:S(2)}) %copy-start.7) | copy-done | bytes 196632
  34.5 13.7 %shard_map.37 = f32[512,128]{1,0:T(8,128)} custom-call(bf16[6,4,4096]{2,1,0:T(4,128)(2,1)} %get-tuple-element.7.refs_0_, bf16[6,4,4096]{2,1,0:T(4,128)(2,1)} %get-tuple-element.6.refs_1_, bf16[6,4,4096]{2,1,0:T(4,128)(2,1)} %get-tuple-element.5.refs_2_, bf16[6,4,4096]{2,1,0:T(4,128)(2,1)} %copy-done.1, bf16[6,4,4096]{2,1,0:T(4,128)(2,1)} %copy-done.1, ...), custom_call_target="tpu_custom_call" | custom-call | flops 587202560 | bytes 3670016 | tf_op jit(solution)/shard_map/pallas_call | solution.py:143
  48.1 1.0 %broadcast_multiply_fusion = f32[512,128]{1,0:T(8,128)S(1)} fusion(f32[512,128]{1,0:T(8,128)} %shard_map.37), kind=kLoop, calls=%fused_computation.41 | loop fusion | flops 65536 | bytes 524288 | tf_op jit(solution)/shard_map/mul | solution.py:228
  49.1 0.8 %fusion.17 = f32[16,1,32,128]{3,2,1,0:T(8,128)} fusion(f32[32,16,128]{2,1,0:T(8,128)S(1)} %bitcast.80, pred[16,128]{1,0:T(8,128)(4,1)S(1)} %broadcast_compare_fusion), kind=kLoop, calls=%fused_computation.38 | loop fusion | flops 65536 | bytes 526336 | tf_op jit(solution)/shard_map/broadcast_in_dim | solution.py:232
  (56 shorter events, 5.4 us)
Async XLA Ops:
  0.0 2.5 %copy-start = (f32[32]{0:T(128)S(1)}, f32[32]{0:T(128)}, u32[]{:S(2)}) copy-start(f32[32]{0:T(128)} %param.4) | copy-start | bytes 388
  11.8 17.1 %copy-start.1 = (bf16[6,4,4096]{2,1,0:T(4,128)(2,1)}, bf16[6,4,4096]{2,1,0:T(4,128)(2,1)S(1)}, u32[]{:S(2)}) copy-start(bf16[6,4,4096]{2,1,0:T(4,128)(2,1)S(1)} %maximum_bitcast_fusion.refs_3_.refs_4_) | copy-start | bytes 589828
  11.8 20.5 %collective-permute-start.7 = (bf16[6,4,4096]{2,1,0:T(4,128)(2,1)S(1)}, bf16[6,4,4096]{2,1,0:T(4,128)(2,1)S(1)}, u32[]{:S(2)}, u32[]{:S(2)}) collective-permute-start(bf16[6,4,4096]{2,1,0:T(4,128)(2,1)S(1)} %maximum_bitcast_fusion.refs_3_.refs_4_), channel_id=1, source_target_pairs={{0,2},{1,3},{2,0},{3,1},{4,6},{5,7},{6,4},{7,5},{8,10},{9,11},{10,... | collective-permute-start | bytes 589832 | tf_op jit(solution)/shard_map/ppermute | solution.py:169
  15.9 16.4 %collective-permute-start.6 = (bf16[6,4,4096]{2,1,0:T(4,128)(2,1)S(1)}, bf16[6,4,4096]{2,1,0:T(4,128)(2,1)S(1)}, u32[]{:S(2)}, u32[]{:S(2)}) collective-permute-start(bf16[6,4,4096]{2,1,0:T(4,128)(2,1)S(1)} %maximum_bitcast_fusion.refs_3_.refs_4_), channel_id=1, source_target_pairs={{0,3},{1,2},{2,1},{3,0},{4,7},{5,6},{6,5},{7,4},{8,11},{9,10},{10,... | collective-permute-start | bytes 589832 | tf_op jit(solution)/shard_map/ppermute | solution.py:169
  17.2 10.7 %collective-permute-start.2 = (bf16[6,4,4096]{2,1,0:T(4,128)(2,1)S(1)}, bf16[6,4,4096]{2,1,0:T(4,128)(2,1)S(1)}, u32[]{:S(2)}, u32[]{:S(2)}) collective-permute-start(bf16[6,4,4096]{2,1,0:T(4,128)(2,1)S(1)} %maximum_bitcast_fusion.refs_3_.refs_4_), channel_id=1, source_target_pairs={{0,24},{4,28},{8,16},{12,20},{16,8},{20,12},{24,0},{28,4},{1,25},{... | collective-permute-start | bytes 589832 | tf_op jit(solution)/shard_map/ppermute | solution.py:181
  19.7 8.8 %collective-permute-start.1 = (bf16[6,4,4096]{2,1,0:T(4,128)(2,1)S(1)}, bf16[6,4,4096]{2,1,0:T(4,128)(2,1)S(1)}, u32[]{:S(2)}, u32[]{:S(2)}) collective-permute-start(bf16[6,4,4096]{2,1,0:T(4,128)(2,1)S(1)} %maximum_bitcast_fusion.refs_3_.refs_4_), channel_id=1, source_target_pairs={{0,16},{4,20},{8,24},{12,28},{16,0},{20,4},{24,8},{28,12},{1,17},{... | collective-permute-start | bytes 589832 | tf_op jit(solution)/shard_map/ppermute | solution.py:181
  20.2 8.4 %collective-permute-start = (bf16[6,4,4096]{2,1,0:T(4,128)(2,1)S(1)}, bf16[6,4,4096]{2,1,0:T(4,128)(2,1)S(1)}, u32[]{:S(2)}, u32[]{:S(2)}) collective-permute-start(bf16[6,4,4096]{2,1,0:T(4,128)(2,1)S(1)} %maximum_bitcast_fusion.refs_3_.refs_4_), channel_id=1, source_target_pairs={{0,8},{4,12},{8,0},{12,4},{16,24},{20,28},{24,16},{28,20},{1,9},{5... | collective-permute-start | bytes 589832 | tf_op jit(solution)/shard_map/ppermute | solution.py:181
  22.8 6.5 %copy-start.9 = (s32[16]{0:T(128)S(1)}, s32[16]{0:T(128)}, u32[]{:S(2)}) copy-start(s32[16]{0:T(128)} %param.5) | copy-start | bytes 196
  27.9 2.6 %copy-start.2 = (bf16[6,4,4096]{2,1,0:T(4,128)(2,1)}, bf16[6,4,4096]{2,1,0:T(4,128)(2,1)S(1)}, u32[]{:S(2)}) copy-start(bf16[6,4,4096]{2,1,0:T(4,128)(2,1)S(1)} %collective-permute-done.2.refs_9_) | copy-start | bytes 589828
  27.9 5.8 %collective-permute-start.5 = (bf16[6,4,4096]{2,1,0:T(4,128)(2,1)S(1)}, bf16[6,4,4096]{2,1,0:T(4,128)(2,1)S(1)}, u32[]{:S(2)}, u32[]{:S(2)}) collective-permute-start(bf16[6,4,4096]{2,1,0:T(4,128)(2,1)S(1)} %maximum_bitcast_fusion.refs_3_.refs_4_), channel_id=1, source_target_pairs={{0,1},{1,0},{2,3},{3,2},{4,5},{5,4},{6,7},{7,6},{8,9},{9,8},{10,11... | collective-permute-start | bytes 589832 | tf_op jit(solution)/shard_map/ppermute | solution.py:169
  28.4 2.1 %copy-start.3 = (bf16[6,4,4096]{2,1,0:T(4,128)(2,1)}, bf16[6,4,4096]{2,1,0:T(4,128)(2,1)S(1)}, u32[]{:S(2)}) copy-start(bf16[6,4,4096]{2,1,0:T(4,128)(2,1)S(1)} %collective-permute-done.1.refs_8_) | copy-start | bytes 589828
  28.4 5.3 %collective-permute-start.4 = (bf16[6,4,4096]{2,1,0:T(4,128)(2,1)S(1)}, bf16[6,4,4096]{2,1,0:T(4,128)(2,1)S(1)}, u32[]{:S(2)}, u32[]{:S(2)}) collective-permute-start(bf16[6,4,4096]{2,1,0:T(4,128)(2,1)S(1)} %maximum_bitcast_fusion.refs_3_.refs_4_), channel_id=1, source_target_pairs={{0,4},{4,0},{8,12},{12,8},{16,20},{20,16},{24,28},{28,24},{1,5},{5... | collective-permute-start | bytes 589832 | tf_op jit(solution)/shard_map/ppermute | solution.py:183
  28.5 2.0 %copy-start.4 = (bf16[6,4,4096]{2,1,0:T(4,128)(2,1)}, bf16[6,4,4096]{2,1,0:T(4,128)(2,1)S(1)}, u32[]{:S(2)}) copy-start(bf16[6,4,4096]{2,1,0:T(4,128)(2,1)S(1)} %collective-permute-done.refs_6_) | copy-start | bytes 589828
  28.9 2.4 %collective-permute-start.3 = (bf16[6,12,4096]{2,1,0:T(8,128)(2,1)S(1)}, bf16[6,12,4096]{2,1,0:T(8,128)(2,1)S(1)}, u32[]{:S(2)}, u32[]{:S(2)}) collective-permute-start(bf16[6,12,4096]{2,1,0:T(8,128)(2,1)S(1)} %pad_maximum_fusion.1), channel_id=1, source_target_pairs={{0,4},{4,0},{8,12},{12,8},{16,20},{20,16},{24,28},{28,24},{1,5},{5... | collective-permute-start | bytes 1769480 | tf_op jit(solution)/shard_map/ppermute | solution.py:185
  32.3 1.4 %copy-start.5 = (bf16[6,4,4096]{2,1,0:T(4,128)(2,1)}, bf16[6,4,4096]{2,1,0:T(4,128)(2,1)S(1)}, u32[]{:S(2)}) copy-start(bf16[6,4,4096]{2,1,0:T(4,128)(2,1)S(1)} %collective-permute-done.7.refs_11_) | copy-start | bytes 589828
  32.3 1.4 %copy-start.6 = (bf16[6,4,4096]{2,1,0:T(4,128)(2,1)}, bf16[6,4,4096]{2,1,0:T(4,128)(2,1)S(1)}, u32[]{:S(2)}) copy-start(bf16[6,4,4096]{2,1,0:T(4,128)(2,1)S(1)} %collective-permute-done.6.refs_10_) | copy-start | bytes 589828
  33.7 0.7 %copy-start.7 = (bf16[6,4,4096]{2,1,0:T(4,128)(2,1)}, bf16[6,4,4096]{2,1,0:T(4,128)(2,1)S(1)}, u32[]{:S(2)}) copy-start(bf16[6,4,4096]{2,1,0:T(4,128)(2,1)S(1)} %collective-permute-done.5.refs_7_) | copy-start | bytes 589828
  33.7 0.8 %copy-start.8 = (bf16[6,4,4096]{2,1,0:T(4,128)(2,1)}, bf16[6,4,4096]{2,1,0:T(4,128)(2,1)S(1)}, u32[]{:S(2)}) copy-start(bf16[6,4,4096]{2,1,0:T(4,128)(2,1)S(1)} %collective-permute-done.4.refs_5_) | copy-start | bytes 589828

commit v22 on v21

--- a/solution.py
+++ b/solution.py
@@ -201,7 +201,11 @@
     col_size = lax.axis_size("col")
     row_size = lax.axis_size("row")
     left_by_window, left_order = xor_gather(white_by_window, "col", col_size)
-    cos_lag, sin_lag = angle_table(LAGS, bin_count, out_length, -LH)
+    step = out_length // BAND
+    cos_hi, sin_hi = angle_table(LAGS, bin_count // BAND, step, -LH)
+    cos_lo, sin_lo = angle_table(LAGS, BAND, out_length, -LH)
+    cos_lag = (cos_hi[:, :, None] * cos_lo[:, None, :] - sin_hi[:, :, None] * sin_lo[:, None, :]).reshape(LAGS, bin_count)
+    sin_lag = (sin_hi[:, :, None] * cos_lo[:, None, :] + cos_hi[:, :, None] * sin_lo[:, None, :]).reshape(LAGS, bin_count)
     lag_table = jnp.concatenate([cos_lag.T, sin_lag.T], axis=0).astype(jnp.bfloat16)
     group_rows = sum(piece.shape[1] for piece in left_by_window)
     piece_rows, visit_order = chip_gather(white_by_window, "row", row_size)

time: 50.1 us -> 49.8 us (level)
  other arithmetic: 10.1 us -> 6.27 us
  waiting for transfers between devices: 2.59 us -> 6.14 us
    another operation x2, other arithmetic: 4.53 us -> 0.46 us
    ppermute x3, waiting for transfers between devices: 0.43 us -> 4.26 us  [chip_gather(): fetched.append(lax.ppermute(block, axis_name, pairs))]
  transfers between devices with their start and end apart: 8 -> 8, of which waited for: 4 -> 5; matrix products, arithmetic and copies ran while one was open for 19% -> 12% of each run, Pallas kernels for 0% -> 0%
where the time goes in v22:
time: 49.8 us; the launch traced here: 49.6 us
  Pallas kernels  13.7 us (28%)
  starting transfers between devices  9.64 us (19%)
  matrix products  8.15 us (16%)
  other arithmetic  6.27 us (13%)
  waiting for transfers between devices  6.14 us (12%)
  local copies, waits for them, and re-layouts  5.51 us (11%)
    pallas_call x1, Pallas kernels, pair_block(): pl.pallas_call(functools.partial(cross_kernel, tuple(issue_order)), out_s...  13.7 us
    ppermute x3, starting transfers between devices, xor_gather(): pieces.append(lax.ppermute(block, axis_name, pairs))  5.67 us
    ppermute x3, waiting for transfers between devices, chip_gather(): fetched.append(lax.ppermute(block, axis_name, pairs))  4.26 us
    ppermute x3, starting transfers between devices, chip_gather(): fetched.append(lax.ppermute(block, axis_name, pairs))  3.49 us
    reshape x1, local copies, waits for them, and re-layouts, decimate(): blocks = records.reshape(lead_dims + (block_count, in_block))  1.68 us
    dot_general x1, matrix products, spectrum(): jnp.einsum('bwfq,gq->bwgf', real_t, sin_three, precision=lax.Precision.HIGH)  1.31 us
    dot_general x1, matrix products, spectrum(): jnp.einsum('bwfq,gq->bwgf', imag_t, sin_three, precision=lax.Precision.HIGH)  1.24 us
    dot_general x1, matrix products, spectrum(): jnp.einsum('bwfq,gq->bwgf', real_t, cos_three, precision=lax.Precision.HIGH)  1.22 us
  transfers between devices with their start and end apart: 8, of which 5 were waited for; matrix products, arithmetic and copies ran while one was open for 12% of the time, Pallas kernels for 0%

profile of v22, /device:TPU:0, one launch (start us, length us, event | category | flops | bytes accessed | tf_op | source)
XLA Modules:
  0.0 49.6 jit_solution(11044996388083411726)
XLA Ops:
  0.2 1.7 %reshape.354 = f32[4,6,32,256]{3,2,0,1:T(8,128)S(1)} reshape(f32[4,6,8192]{2,0,1:T(4,128)} %param.3) | data formatting | bytes 1572864 | tf_op jit(solution)/shard_map/reshape | solution.py:31
  1.8 0.7 %iota_compare_fusion = pred[32,288,128]{2,1,0:T(32,128)(4,1)S(1)} fusion(s32[32,128]{1,0:T(8,128)S(1)} %iota_subtract_fusion), kind=kLoop, calls=%fused_computation.2 | loop fusion | flops 1179648 | bytes 1196032 | tf_op jit(solution)/shard_map/eq | solution.py:37
  2.5 1.1 %fusion = f32[1,288,128]{2,0,1:T(1,128)S(1)} fusion(pred[32,288,128]{2,1,0:T(32,128)(4,1)S(1)} %iota_compare_fusion, f32[32]{0:T(128)S(1)} %copy-done), kind=kOutput, calls=%fused_computation.3 | convolution fusion | flops 7077888 | bytes 1327232 | tf_op jit(solution)/shard_map/k,kij->ij/dot_general | solution.py:38
  5.9 1.2 %fusion.4 = f32[32,4,6,64]{3,0,2,1:T(8,128)S(1)} fusion(f32[64,4,6,64]{3,0,2,1:T(8,128)S(1)} %fusion.20, f32[64,4,6,64]{3,0,2,1:T(8,128)S(1)} %convolution_negate_fusion, f32[64,64]{1,0:T(8,128)S(1)} %get-tuple-element.18, f32[64,64]{1,0:T(8,128)S(1)} %get-tuple-element.19), kind=kOutput, calls=%fused_computation.16 | convolution fusion | flops 19197952 | bytes 1015808 | tf_op jit(solution)/shard_map/bwfq,gq->bwgf/dot_general | solution.py:61
  7.1 1.2 %fusion.8 = f32[32,4,6,64]{3,0,2,1:T(8,128)S(1)} fusion(f32[64,4,6,64]{3,0,2,1:T(8,128)S(1)} %convolution_negate_fusion, f32[64,4,6,64]{3,0,2,1:T(8,128)S(1)} %fusion.20, f32[64,64]{1,0:T(8,128)S(1)} %get-tuple-element.18, f32[64,64]{1,0:T(8,128)S(1)} %get-tuple-element.19), kind=kOutput, calls=%fused_computation.20 | convolution fusion | flops 19197952 | bytes 1015808 | tf_op jit(solution)/shard_map/bwfq,gq->bwgf/dot_general | solution.py:58
  8.4 1.2 %fusion.3 = f32[4,6,32,64]{3,2,1,0:T(8,128)S(1)} fusion(f32[32,4,6,64]{3,0,2,1:T(8,128)S(1)} %fusion.8, f32[64,4,6,64]{3,0,2,1:T(8,128)S(1)} %fusion.20, f32[64,4,6,64]{3,0,2,1:T(8,128)S(1)} %convolution_negate_fusion, f32[64,64]{1,0:T(8,128)S(1)} %get-tuple-element.18, f32[64,64]{1,0:T(8,128)S(1)} %get-tuple-element.19), kind=kOutput, calls=%fused_computation.11 | convolution fusion | flops 19247104 | bytes 1212416 | tf_op jit(solution)/shard_map/bwfq,gq->bwgf/dot_general | solution.py:60
  9.6 1.3 %add_reduce_fusion = (f32[4,6,32]{2,1,0:T(8,128)S(1)}, f32[4,6,32,64]{3,2,1,0:T(8,128)S(1)}) fusion(f32[4,6,32,64]{3,2,1,0:T(8,128)S(1)} %fusion.3, f32[32,4,6,64]{3,0,2,1:T(8,128)S(1)} %fusion.4, f32[64,4,6,64]{3,0,2,1:T(8,128)S(1)} %convolution_negate_fusion, f32[64,64]{1,0:T(8,128)S(1)} %get-tuple-element.18, f32[64,4,6,64]{3,0,2,1:T(8,128)S(1)} %fusion.20, ...), kind=kOutput, calls=%fused_computation.26 | convolution fusion | flops 19442944 | bytes 1412096 | tf_op jit(solution)/shard_map/bwfq,gq->bwgf/dot_general | solution.py:63
  11.8 4.1 %collective-permute-start.7 = (bf16[6,4,4096]{2,1,0:T(4,128)(2,1)S(1)}, bf16[6,4,4096]{2,1,0:T(4,128)(2,1)S(1)}, u32[]{:S(2)}, u32[]{:S(2)}) collective-permute-start(bf16[6,4,4096]{2,1,0:T(4,128)(2,1)S(1)} %maximum_bitcast_fusion.refs_3_.refs_4_), channel_id=1, source_target_pairs={{0,2},{1,3},{2,0},{3,1},{4,6},{5,7},{6,4},{7,5},{8,10},{9,11},{10,... | collective-permute-start | bytes 589832 | tf_op jit(solution)/shard_map/ppermute | solution.py:169
  15.9 1.3 %collective-permute-start.6 = (bf16[6,4,4096]{2,1,0:T(4,128)(2,1)S(1)}, bf16[6,4,4096]{2,1,0:T(4,128)(2,1)S(1)}, u32[]{:S(2)}, u32[]{:S(2)}) collective-permute-start(bf16[6,4,4096]{2,1,0:T(4,128)(2,1)S(1)} %maximum_bitcast_fusion.refs_3_.refs_4_), channel_id=1, source_target_pairs={{0,3},{1,2},{2,1},{3,0},{4,7},{5,6},{6,5},{7,4},{8,11},{9,10},{10,... | collective-permute-start | bytes 589832 | tf_op jit(solution)/shard_map/ppermute | solution.py:169
  17.2 2.5 %collective-permute-start.2 = (bf16[6,4,4096]{2,1,0:T(4,128)(2,1)S(1)}, bf16[6,4,4096]{2,1,0:T(4,128)(2,1)S(1)}, u32[]{:S(2)}, u32[]{:S(2)}) collective-permute-start(bf16[6,4,4096]{2,1,0:T(4,128)(2,1)S(1)} %maximum_bitcast_fusion.refs_3_.refs_4_), channel_id=1, source_target_pairs={{0,24},{4,28},{8,16},{12,20},{16,8},{20,12},{24,0},{28,4},{1,25},{... | collective-permute-start | bytes 589832 | tf_op jit(solution)/shard_map/ppermute | solution.py:181
  21.0 0.7 %gather_fusion = s32[16]{0:T(128)S(1)} fusion(s32[4]{0:T(128)S(1)} %iota_xor_fusion.1, s32[1024]{0:T(1024)S(1)} %pad_clamp_fusion.1), kind=kCustom, calls=%fused_computation | custom fusion | bytes 192 | tf_op jit(solution)/shard_map/gather | solution.py:224
  21.7 0.7 %gather_fusion.1 = s32[32]{0:T(128)S(1)} fusion(s32[8]{0:T(128)S(1)} %iota_xor_fusion, s32[1024]{0:T(1024)S(1)} %pad_clamp_fusion), kind=kCustom, calls=%fused_computation.1 | custom fusion | bytes 384 | tf_op jit(solution)/shard_map/gather | solution.py:226
  22.4 0.7 %fusion.56.refs_13_ = bf16[32,32]{1,0:T(8,128)(2,1)} fusion(s32[32]{0:T(128)S(1)} %fusion.67), kind=kLoop, calls=%fused_computation.94 | loop fusion | flops 2048 | bytes 2176 | tf_op jit(solution)/shard_map/convert_element_type | solution.py:228
  23.4 0.7 %fusion.65.refs_12_ = bf16[16,16]{1,0:T(8,128)(2,1)} fusion(s32[16]{0:T(128)S(1)} %fusion.66), kind=kLoop, calls=%fused_computation.100 | loop fusion | flops 512 | bytes 576 | tf_op jit(solution)/shard_map/convert_element_type | solution.py:227
  24.1 1.9 %collective-permute-done.2.refs_9_ = bf16[6,4,4096]{2,1,0:T(4,128)(2,1)S(1)} collective-permute-done((bf16[6,4,4096]{2,1,0:T(4,128)(2,1)S(1)}, bf16[6,4,4096]{2,1,0:T(4,128)(2,1)S(1)}, u32[]{:S(2)}, u32[]{:S(2)}) %collective-permute-start.2) | collective-permute-done | bytes 196640 | tf_op jit(solution)/shard_map/ppermute | solution.py:181
  26.2 2.3 %collective-permute-done.1.refs_8_ = bf16[6,4,4096]{2,1,0:T(4,128)(2,1)S(1)} collective-permute-done((bf16[6,4,4096]{2,1,0:T(4,128)(2,1)S(1)}, bf16[6,4,4096]{2,1,0:T(4,128)(2,1)S(1)}, u32[]{:S(2)}, u32[]{:S(2)}) %collective-permute-start.1) | collective-permute-done | bytes 196640 | tf_op jit(solution)/shard_map/ppermute | solution.py:181
  29.5 1.1 %pad_maximum_fusion.refs_14_ = bf16[4096,128]{1,0:T(8,128)(2,1)} fusion(bf16[2048,128]{1,0:T(8,128)(2,1)S(1)} %bitcast.87, bf16[2048,128]{1,0:T(8,128)(2,1)S(1)} %bitcast.86), kind=kLoop, calls=%fused_computation.12 | loop fusion | flops 2097152 | bytes 2097152 | tf_op jit(solution)/shard_map/concatenate | solution.py:209
  30.5 0.8 %collective-permute-done.3 = bf16[6,12,4096]{2,1,0:T(8,128)(2,1)S(1)} collective-permute-done((bf16[6,12,4096]{2,1,0:T(8,128)(2,1)S(1)}, bf16[6,12,4096]{2,1,0:T(8,128)(2,1)S(1)}, u32[]{:S(2)}, u32[]{:S(2)}) %collective-permute-start.3) | collective-permute-done | bytes 589856 | tf_op jit(solution)/shard_map/ppermute | solution.py:185
  31.3 1.0 %fusion.98 = (bf16[6,4,4096]{2,1,0:T(4,128)(2,1)}, bf16[6,4,4096]{2,1,0:T(4,128)(2,1)}, bf16[6,4,4096]{2,1,0:T(4,128)(2,1)}) fusion(bf16[6,12,4096]{2,1,0:T(8,128)(2,1)S(1)} %collective-permute-done.3), kind=kLoop, calls=%fused_computation.152 | loop fusion | bytes 1179648 | tf_op jit(solution)/shard_map/slice | solution.py:188
  32.3 1.1 %collective-permute-done.5.refs_7_ = bf16[6,4,4096]{2,1,0:T(4,128)(2,1)S(1)} collective-permute-done((bf16[6,4,4096]{2,1,0:T(4,128)(2,1)S(1)}, bf16[6,4,4096]{2,1,0:T(4,128)(2,1)S(1)}, u32[]{:S(2)}, u32[]{:S(2)}) %collective-permute-start.5) | collective-permute-done | bytes 196640 | tf_op jit(solution)/shard_map/ppermute | solution.py:169
  33.4 0.7 %copy-done.7 = bf16[6,4,4096]{2,1,0:T(4,128)(2,1)} copy-done((bf16[6,4,4096]{2,1,0:T(4,128)(2,1)}, bf16[6,4,4096]{2,1,0:T(4,128)(2,1)S(1)}, u32[]{:S(2)}) %copy-start.7) | copy-done | bytes 196632
  34.2 13.7 %shard_map.37 = f32[512,128]{1,0:T(8,128)} custom-call(bf16[6,4,4096]{2,1,0:T(4,128)(2,1)} %get-tuple-element.7.refs_0_, bf16[6,4,4096]{2,1,0:T(4,128)(2,1)} %get-tuple-element.6.refs_1_, bf16[6,4,4096]{2,1,0:T(4,128)(2,1)} %get-tuple-element.5.refs_2_, bf16[6,4,4096]{2,1,0:T(4,128)(2,1)} %copy-done.1, bf16[6,4,4096]{2,1,0:T(4,128)(2,1)} %copy-done.1, ...), custom_call_target="tpu_custom_call" | custom-call | flops 587202560 | bytes 3670016 | tf_op jit(solution)/shard_map/pallas_call | solution.py:143
  47.9 1.0 %broadcast_multiply_fusion = f32[512,128]{1,0:T(8,128)S(1)} fusion(f32[512,128]{1,0:T(8,128)} %shard_map.37), kind=kLoop, calls=%fused_computation.32 | loop fusion | flops 65536 | bytes 524288 | tf_op jit(solution)/shard_map/mul | solution.py:232
  48.8 0.8 %fusion.11 = f32[16,1,32,128]{3,2,1,0:T(8,128)} fusion(f32[32,16,128]{2,1,0:T(8,128)S(1)} %bitcast.88, pred[16,128]{1,0:T(8,128)(4,1)S(1)} %broadcast_compare_fusion), kind=kLoop, calls=%fused_computation.29 | loop fusion | flops 65536 | bytes 526336 | tf_op jit(solution)/shard_map/broadcast_in_dim | solution.py:236
  (58 shorter events, 6.2 us)
Async XLA Ops:
  0.0 2.5 %copy-start = (f32[32]{0:T(128)S(1)}, f32[32]{0:T(128)}, u32[]{:S(2)}) copy-start(f32[32]{0:T(128)} %param.4) | copy-start | bytes 388
  11.8 17.1 %copy-start.1 = (bf16[6,4,4096]{2,1,0:T(4,128)(2,1)}, bf16[6,4,4096]{2,1,0:T(4,128)(2,1)S(1)}, u32[]{:S(2)}) copy-start(bf16[6,4,4096]{2,1,0:T(4,128)(2,1)S(1)} %maximum_bitcast_fusion.refs_3_.refs_4_) | copy-start | bytes 589828
  11.8 20.5 %collective-permute-start.7 = (bf16[6,4,4096]{2,1,0:T(4,128)(2,1)S(1)}, bf16[6,4,4096]{2,1,0:T(4,128)(2,1)S(1)}, u32[]{:S(2)}, u32[]{:S(2)}) collective-permute-start(bf16[6,4,4096]{2,1,0:T(4,128)(2,1)S(1)} %maximum_bitcast_fusion.refs_3_.refs_4_), channel_id=1, source_target_pairs={{0,2},{1,3},{2,0},{3,1},{4,6},{5,7},{6,4},{7,5},{8,10},{9,11},{10,... | collective-permute-start | bytes 589832 | tf_op jit(solution)/shard_map/ppermute | solution.py:169
  15.9 16.4 %collective-permute-start.6 = (bf16[6,4,4096]{2,1,0:T(4,128)(2,1)S(1)}, bf16[6,4,4096]{2,1,0:T(4,128)(2,1)S(1)}, u32[]{:S(2)}, u32[]{:S(2)}) collective-permute-start(bf16[6,4,4096]{2,1,0:T(4,128)(2,1)S(1)} %maximum_bitcast_fusion.refs_3_.refs_4_), channel_id=1, source_target_pairs={{0,3},{1,2},{2,1},{3,0},{4,7},{5,6},{6,5},{7,4},{8,11},{9,10},{10,... | collective-permute-start | bytes 589832 | tf_op jit(solution)/shard_map/ppermute | solution.py:169
  17.2 8.7 %collective-permute-start.2 = (bf16[6,4,4096]{2,1,0:T(4,128)(2,1)S(1)}, bf16[6,4,4096]{2,1,0:T(4,128)(2,1)S(1)}, u32[]{:S(2)}, u32[]{:S(2)}) collective-permute-start(bf16[6,4,4096]{2,1,0:T(4,128)(2,1)S(1)} %maximum_bitcast_fusion.refs_3_.refs_4_), channel_id=1, source_target_pairs={{0,24},{4,28},{8,16},{12,20},{16,8},{20,12},{24,0},{28,4},{1,25},{... | collective-permute-start | bytes 589832 | tf_op jit(solution)/shard_map/ppermute | solution.py:181
  19.7 8.8 %collective-permute-start.1 = (bf16[6,4,4096]{2,1,0:T(4,128)(2,1)S(1)}, bf16[6,4,4096]{2,1,0:T(4,128)(2,1)S(1)}, u32[]{:S(2)}, u32[]{:S(2)}) collective-permute-start(bf16[6,4,4096]{2,1,0:T(4,128)(2,1)S(1)} %maximum_bitcast_fusion.refs_3_.refs_4_), channel_id=1, source_target_pairs={{0,16},{4,20},{8,24},{12,28},{16,0},{20,4},{24,8},{28,12},{1,17},{... | collective-permute-start | bytes 589832 | tf_op jit(solution)/shard_map/ppermute | solution.py:181
  20.2 8.4 %collective-permute-start = (bf16[6,4,4096]{2,1,0:T(4,128)(2,1)S(1)}, bf16[6,4,4096]{2,1,0:T(4,128)(2,1)S(1)}, u32[]{:S(2)}, u32[]{:S(2)}) collective-permute-start(bf16[6,4,4096]{2,1,0:T(4,128)(2,1)S(1)} %maximum_bitcast_fusion.refs_3_.refs_4_), channel_id=1, source_target_pairs={{0,8},{4,12},{8,0},{12,4},{16,24},{20,28},{24,16},{28,20},{1,9},{5... | collective-permute-start | bytes 589832 | tf_op jit(solution)/shard_map/ppermute | solution.py:181
  23.1 6.3 %copy-start.9 = (s32[16]{0:T(128)S(1)}, s32[16]{0:T(128)}, u32[]{:S(2)}) copy-start(s32[16]{0:T(128)} %param.5) | copy-start | bytes 196
  26.0 4.6 %copy-start.2 = (bf16[6,4,4096]{2,1,0:T(4,128)(2,1)}, bf16[6,4,4096]{2,1,0:T(4,128)(2,1)S(1)}, u32[]{:S(2)}) copy-start(bf16[6,4,4096]{2,1,0:T(4,128)(2,1)S(1)} %collective-permute-done.2.refs_9_) | copy-start | bytes 589828
  26.0 7.5 %collective-permute-start.5 = (bf16[6,4,4096]{2,1,0:T(4,128)(2,1)S(1)}, bf16[6,4,4096]{2,1,0:T(4,128)(2,1)S(1)}, u32[]{:S(2)}, u32[]{:S(2)}) collective-permute-start(bf16[6,4,4096]{2,1,0:T(4,128)(2,1)S(1)} %maximum_bitcast_fusion.refs_3_.refs_4_), channel_id=1, source_target_pairs={{0,1},{1,0},{2,3},{3,2},{4,5},{5,4},{6,7},{7,6},{8,9},{9,8},{10,11... | collective-permute-start | bytes 589832 | tf_op jit(solution)/shard_map/ppermute | solution.py:169
  28.4 2.1 %copy-start.3 = (bf16[6,4,4096]{2,1,0:T(4,128)(2,1)}, bf16[6,4,4096]{2,1,0:T(4,128)(2,1)S(1)}, u32[]{:S(2)}) copy-start(bf16[6,4,4096]{2,1,0:T(4,128)(2,1)S(1)} %collective-permute-done.1.refs_8_) | copy-start | bytes 589828
  28.4 5.0 %collective-permute-start.4 = (bf16[6,4,4096]{2,1,0:T(4,128)(2,1)S(1)}, bf16[6,4,4096]{2,1,0:T(4,128)(2,1)S(1)}, u32[]{:S(2)}, u32[]{:S(2)}) collective-permute-start(bf16[6,4,4096]{2,1,0:T(4,128)(2,1)S(1)} %maximum_bitcast_fusion.refs_3_.refs_4_), channel_id=1, source_target_pairs={{0,4},{4,0},{8,12},{12,8},{16,20},{20,16},{24,28},{28,24},{1,5},{5... | collective-permute-start | bytes 589832 | tf_op jit(solution)/shard_map/ppermute | solution.py:183
  28.5 2.0 %copy-start.4 = (bf16[6,4,4096]{2,1,0:T(4,128)(2,1)}, bf16[6,4,4096]{2,1,0:T(4,128)(2,1)S(1)}, u32[]{:S(2)}) copy-start(bf16[6,4,4096]{2,1,0:T(4,128)(2,1)S(1)} %collective-permute-done.refs_6_) | copy-start | bytes 589828
  28.9 2.4 %collective-permute-start.3 = (bf16[6,12,4096]{2,1,0:T(8,128)(2,1)S(1)}, bf16[6,12,4096]{2,1,0:T(8,128)(2,1)S(1)}, u32[]{:S(2)}, u32[]{:S(2)}) collective-permute-start(bf16[6,12,4096]{2,1,0:T(8,128)(2,1)S(1)} %pad_maximum_fusion.1), channel_id=1, source_target_pairs={{0,4},{4,0},{8,12},{12,8},{16,20},{20,16},{24,28},{28,24},{1,5},{5... | collective-permute-start | bytes 1769480 | tf_op jit(solution)/shard_map/ppermute | solution.py:185
  32.3 1.1 %copy-start.5 = (bf16[6,4,4096]{2,1,0:T(4,128)(2,1)}, bf16[6,4,4096]{2,1,0:T(4,128)(2,1)S(1)}, u32[]{:S(2)}) copy-start(bf16[6,4,4096]{2,1,0:T(4,128)(2,1)S(1)} %collective-permute-done.7.refs_11_) | copy-start | bytes 589828
  32.3 1.1 %copy-start.6 = (bf16[6,4,4096]{2,1,0:T(4,128)(2,1)}, bf16[6,4,4096]{2,1,0:T(4,128)(2,1)S(1)}, u32[]{:S(2)}) copy-start(bf16[6,4,4096]{2,1,0:T(4,128)(2,1)S(1)} %collective-permute-done.6.refs_10_) | copy-start | bytes 589828
  33.4 0.7 %copy-start.7 = (bf16[6,4,4096]{2,1,0:T(4,128)(2,1)}, bf16[6,4,4096]{2,1,0:T(4,128)(2,1)S(1)}, u32[]{:S(2)}) copy-start(bf16[6,4,4096]{2,1,0:T(4,128)(2,1)S(1)} %collective-permute-done.5.refs_7_) | copy-start | bytes 589828
  33.4 0.8 %copy-start.8 = (bf16[6,4,4096]{2,1,0:T(4,128)(2,1)}, bf16[6,4,4096]{2,1,0:T(4,128)(2,1)S(1)}, u32[]{:S(2)}) copy-start(bf16[6,4,4096]{2,1,0:T(4,128)(2,1)S(1)} %collective-permute-done.4.refs_5_) | copy-start | bytes 589828
